TPU v7x, 32 devices: a whole 2x2x4 slice. The times are simulated.
32 devices in a mesh: mesh: 8 (over z, x), view: 4 (over y, core).
Axes of the slice: x: 2, y: 2, z: 4, core: 2. Of those that a mesh axis runs over, the one named last changes fastest.
Arguments:
- queries: bfloat16 [6144, 1280], P(('mesh', 'view')), may hold values from -6 to 6
- keys: bfloat16 [6144, 1280], P(('mesh', 'view')), may hold values from -6 to 6
- values: bfloat16 [6144, 1280], P(('mesh', 'view')), may hold values from -6 to 6
- ref_keys: bfloat16 [1024, 1280], P(('mesh', 'view')), may hold values from -6 to 6
- ref_values: bfloat16 [1024, 1280], P(('mesh', 'view')), may hold values from -6 to 6
- out_weight: bfloat16 [1280, 1280], replicated, may hold values from -0.15625 to 0.15625
- adjacency: int32 [48, 3], P('mesh'), may hold values from 0 to 5, as said below
- ref_source: int32 [1], replicated, may hold values from 0 to 7
Outputs:
- blended: bfloat16 [6144, 1280], P(('mesh', 'view'))
Inputs may be any that keep to these rules, and one draw needn't show every extreme that they name: `adjacency`: each row lists 3 different views of the same mesh, never the row's own view.
All inputs are finite; a program needn't handle non-finite values.
Results may differ from a plain program's by a relative error of at most 0.0055.
Values may be sent and summed in bfloat16 or wider, within the bound.
No kernel may reach another device: no remote copies, remote signals or barrier semaphores. Data moves between devices by JAX's collectives and lax.ppermute only.
A program may use at most 128 MiB of HBM per device.

v0:
```python
import math

import jax
import jax.numpy as jnp
from jax import lax
from jax.sharding import PartitionSpec as P

HEADS = 20
HEAD_DIM = 64
VIEWS = 6


SCALE = 0.125


def broadcast(value, axis, source):
    kept = jnp.where(lax.axis_index(axis) == source, value, 0).astype(value.dtype)
    return lax.psum(kept, axis)


def absorb(carried, pieces, first_row, query_heads, query_table, view_tok):
    running_peak, totals, summed = carried
    piece_keys, piece_values = pieces
    key_count = piece_keys.shape[0]
    key_heads = piece_keys.reshape(key_count, HEADS, HEAD_DIM)
    value_heads = piece_values.reshape(key_count, HEADS, HEAD_DIM)
    scores = (
        jnp.einsum("qhd,khd->hqk", query_heads, key_heads, preferred_element_type=jnp.float32)
        * SCALE
    )
    if query_table is not None:
        key_views = (first_row + jnp.arange(key_count, dtype=jnp.int32)) // view_tok
        key_onehot = (key_views[:, None] == jnp.arange(VIEWS, dtype=jnp.int32)[None, :]).astype(
            jnp.float32
        )
        keep_mask = jnp.dot(query_table, jnp.transpose(key_onehot)) > 0.5
        scores = jnp.where(keep_mask[None, :, :], scores, -jnp.inf)
    new_peak = jnp.maximum(running_peak, jnp.max(scores, axis=-1))
    factor = jnp.exp(running_peak - new_peak)
    weights = jnp.exp(scores - new_peak[:, :, None])
    totals = totals * factor + jnp.sum(weights, axis=-1)
    rounded = weights.astype(jnp.bfloat16)
    summed = summed * jnp.transpose(factor)[:, :, None] + jnp.einsum(
        "hqk,khd->qhd", rounded, value_heads, preferred_element_type=jnp.float32
    )
    return (new_peak, totals, summed)


def absorb_needed(carried, pieces, first_row, query_heads, query_table, view_tok):
    key_count = pieces[0].shape[0]
    key_views = (first_row + jnp.arange(key_count, dtype=jnp.int32)) // view_tok
    key_onehot = (key_views[:, None] == jnp.arange(VIEWS, dtype=jnp.int32)[None, :]).astype(
        jnp.float32
    )
    needed = jnp.any(jnp.dot(query_table, jnp.transpose(key_onehot)) > 0.5)

    def compute(state):
        return absorb(state, pieces, first_row, query_heads, query_table, view_tok)

    def passing(state):
        return state

    return lax.cond(needed, compute, passing, carried)


def finish(carried):
    running_peak, totals, summed = carried
    return summed / jnp.transpose(totals)[:, :, None]


def body(queries, keys, values, ref_keys, ref_values, out_weight, adjacency, ref_source):
    shard_rows = queries.shape[0]
    width = queries.shape[1]
    view_count = lax.axis_size("view")
    view_index = lax.axis_index("view")
    view_tok = shard_rows * view_count // VIEWS
    query_heads = queries.reshape(shard_rows, HEADS, HEAD_DIM)
    view_ids = jnp.arange(VIEWS, dtype=jnp.int32)
    listed = jnp.any(adjacency[:, :, None] == view_ids[None, None, :], axis=1)
    allowed_table = (listed | (view_ids[:, None] == view_ids[None, :])).astype(jnp.float32)
    query_views = (view_index * shard_rows + jnp.arange(shard_rows, dtype=jnp.int32)) // view_tok
    query_onehot = (query_views[:, None] == view_ids[None, :]).astype(jnp.float32)
    query_table = jnp.dot(query_onehot, allowed_table)
    initial = (
        jnp.full((HEADS, shard_rows), -1e30, jnp.float32),
        jnp.zeros((HEADS, shard_rows), jnp.float32),
        jnp.zeros((shard_rows, HEADS, HEAD_DIM), jnp.float32),
    )
    gathered_keys, gathered_values = (
        lax.all_gather(keys, "view", axis=0, tiled=True),
        lax.all_gather(values, "view", axis=0, tiled=True),
    )
    group_size = math.gcd(view_count, max(1, 512 // shard_rows))
    block_rows = shard_rows * group_size
    blocks = view_count // group_size
    stacked_keys = gathered_keys.reshape(blocks, block_rows, width)
    stacked_values = gathered_values.reshape(blocks, block_rows, width)

    def advance(carried, inputs):
        block_keys, block_values, block_index = inputs
        updated = absorb_needed(
            carried,
            (block_keys, block_values),
            block_index * block_rows,
            query_heads,
            query_table,
            view_tok,
        )
        return (updated, None)

    view_state, unused = lax.scan(
        advance, initial, (stacked_keys, stacked_values, jnp.arange(blocks, dtype=jnp.int32))
    )
    root_mesh = ref_source[0]
    shared_keys, shared_values = (
        broadcast(ref_keys, "mesh", root_mesh),
        broadcast(ref_values, "mesh", root_mesh),
    )
    whole_keys, whole_values = (
        lax.all_gather(shared_keys, "view", axis=0, tiled=True),
        lax.all_gather(shared_values, "view", axis=0, tiled=True),
    )
    ref_state = absorb(initial, (whole_keys, whole_values), 0, query_heads, None, view_tok)
    mixed = (finish(view_state) + finish(ref_state)).reshape(shard_rows, width).astype(jnp.bfloat16)
    return jnp.dot(mixed, out_weight, preferred_element_type=jnp.float32).astype(jnp.bfloat16)


def solution(mesh):
    return jax.shard_map(
        body,
        mesh=mesh,
        in_specs=(
            P(("mesh", "view"), None),
            P(("mesh", "view"), None),
            P(("mesh", "view"), None),
            P(("mesh", "view"), None),
            P(("mesh", "view"), None),
            P(),
            P("mesh", None),
            P(),
        ),
        out_specs=P(("mesh", "view"), None),
        check_vma=False,
    )
```

profile of v0, /device:TPU:0, one launch (start us, length us, event | category | flops | bytes accessed | tf_op | source)
XLA Modules:
  0.0 151.8 jit_solution(6824898080280562233)
XLA Ops:
  10.1 2.2 %copy.19 = bf16[192,1280]{0,1:T(8,128)(2,1)} copy(bf16[192,1280]{1,0:T(8,128)(2,1)} %param.12) | data formatting | bytes 983040 | tf_op args[0]
  12.5 71.4 %all-reduce.3.cloned.1.call-done = (bf16[32,1280]{1,0:T(8,128)(2,1)}, bf16[32,1280]{1,0:T(8,128)(2,1)}) async-done(((bf16[32,1280]{1,0:T(8,128)(2,1)}, bf16[32,1280]{1,0:T(8,128)(2,1)}), (bf16[32,1280]{1,0:T(8,128)(2,1)}, bf16[32,1280]{1,0:T(8,128)(2,1)})) %all-reduce.3.cloned.1.call-update) | async-done | bytes 163856 | tf_op jit(solution)/shard_map/psum | solution.py:18
  83.9 7.6 %all_gather.15 = bf16[128,1280]{1,0:T(8,128)(2,1)} all-gather(bf16[32,1280]{1,0:T(8,128)(2,1)} %get-tuple-element.247), channel_id=1, replica_groups=mesh['mesh'=8,'view'=4] {'view'}, dimensions={0}, use_global_device_ids=true | all-gather | bytes 409600 | tf_op jit(solution)/shard_map/all_gather | solution.py:121
  91.5 1.9 %copy.23 = bf16[128,1280]{0,1:T(8,128)(2,1)} copy(bf16[128,1280]{1,0:T(8,128)(2,1)} %all_gather.15) | data formatting | bytes 655360 | tf_op jit(solution)/shard_map/all_gather | solution.py:121
  93.4 7.2 %all_gather.14 = bf16[128,1280]{1,0:T(8,128)(2,1)} all-gather(bf16[32,1280]{1,0:T(8,128)(2,1)} %get-tuple-element.248), channel_id=1, replica_groups=mesh['mesh'=8,'view'=4] {'view'}, dimensions={0}, use_global_device_ids=true | all-gather | bytes 409600 | tf_op jit(solution)/shard_map/all_gather | solution.py:120
  100.5 1.9 %copy.22 = bf16[128,1280]{0,1:T(8,128)(2,1)} copy(bf16[128,1280]{1,0:T(8,128)(2,1)} %all_gather.14) | data formatting | bytes 655360 | tf_op jit(solution)/shard_map/all_gather | solution.py:120
  102.4 2.2 %bitcast_reduce_fusion = (f32[20,192]{1,0:T(8,128)S(1)}, f32[20,128,192]{1,2,0:T(8,128)S(1)}) fusion(bf16[128,20,64]{0,2,1:T(8,128)(2,1)} %bitcast.79, bf16[192,20,64]{0,2,1:T(8,128)(2,1)} %bitcast.74), kind=kOutput, calls=%fused_computation.47 | convolution fusion | flops 63893760 | bytes 2800640 | tf_op jit(solution)/shard_map/qhd,khd->hqk/dot_general | solution.py:28
  104.7 1.3 copy-done.2
  106.0 1.5 fusion.29
  107.5 4.0 %copy.20 = bf16[2,384,1280]{1,2,0:T(8,128)(2,1)} copy(bf16[2,384,1280]{2,1,0:T(8,128)(2,1)} %bitcast.77) | data formatting | bytes 3932160 | tf_op jit(solution)/shard_map/while | solution.py:111
  111.5 4.0 %copy.21 = bf16[2,384,1280]{1,2,0:T(8,128)(2,1)} copy(bf16[2,384,1280]{2,1,0:T(8,128)(2,1)} %bitcast.78) | data formatting | bytes 3932160 | tf_op jit(solution)/shard_map/while | solution.py:111
  116.8 23.0 %while.16 = (s32[]{:T(128)}, f32[20,192]{1,0:T(8,128)S(1)}, f32[20,192]{1,0:T(8,128)S(1)}, f32[192,20,64]{0,2,1:T(8,128)}, s32[2]{0:T(128)S(1)}, /*index=5*/bf16...) while((s32[]{:T(128)}, f32[20,192]{1,0:T(8,128)S(1)}, ...), condition=%wide.region_7.8_spmd, body=%wide.region_1.7_spmd.sunk | while | flops 396218112 | bytes 36432752 | solution.py:111
  119.6 8.7 %conditional.2 = ((f32[20,192]{1,0:T(8,128)S(1)}, f32[20,192]{1,0:T(8,128)S(1)}, f32[192,20,64]{0,2,1:T(8,128)})) conditional(s32[]{:T(128)} %convert_element_type.45, (f32[20,192]{1,0:T(8,128)S(1)}, f32[20,192]{1,0:T(8,128)S(1)}, f32[192,20,64]{0,2,1:T(8,128)}) %tuple.49, (s32[]{:T(128)}, bf16[192,6]{0,1:T(8,128)(2,1)S(1)}, ...), branch_computations={%region_3.3_spmd, %region_4.6_spmd} | conditional | flops 395177472 | bytes 36427132 | solution.py:63
  120.0 1.8 %constant_dynamic-slice_fusion = (bf16[1,384,1280]{1,2,0:T(8,128)(2,1)S(1)}, bf16[1,384,1280]{1,2,0:T(8,128)(2,1)S(1)}) fusion(bf16[2,384,1280]{1,2,0:T(8,128)(2,1)} %get-tuple-element.193, s32[]{:T(128)} %get-tuple-element.189, bf16[2,384,1280]{1,2,0:T(8,128)(2,1)} %get-tuple-element.188), kind=kLoop, calls=%fused_computation.28 | loop fusion | bytes 3932164 | tf_op jit(solution)/shard_map/while/body/jit(dynamic_index_in_dim)/dynamic_slice | solution.py:111
  121.8 1.3 fusion.2
  123.1 2.2 %fusion.1 = f32[20,192]{1,0:T(8,128)S(1)} fusion(f32[20,384,192]{1,2,0:T(8,128)S(1)} %get-tuple-element.252, f32[20,192]{1,0:T(8,128)S(1)} %get-tuple-element.325, pred[192,384]{1,0:T(8,128)(4,1)S(1)} %fusion.15), kind=kLoop, calls=%fused_computation.3 | loop fusion | flops 5894400 | bytes 6002688 | tf_op jit(solution)/shard_map/while/body/eval_jaxpr/cond/branch_1_fun/reduce_sum | solution.py:41
  125.3 1.9 %fusion.12 = f32[192,20,64]{0,2,1:T(8,128)S(1)} fusion(bf16[384,20,64]{0,2,1:T(8,128)(2,1)S(1)} %bitcast.76, f32[20,384,192]{1,2,0:T(8,128)S(1)} %get-tuple-element.252, f32[20,192]{1,0:T(8,128)S(1)} %get-tuple-element.325, pred[192,384]{1,0:T(8,128)(4,1)S(1)} %fusion.15, f32[192,20,64]{0,2,1:T(8,128)S(1)} %copy-done.3, f32[192,20]{0,1:T(8,128)S(1)} %get-tuple-element.249), kind=kOutput, calls=%fused_computation.11 | convolution fusion | flops 195133440 | bytes 8951808 | tf_op jit(solution)/shard_map/while/body/eval_jaxpr/cond/branch_1_fun/hqk,khd->qhd/dot_general | solution.py:43
  131.2 8.7 %conditional.2 = ((f32[20,192]{1,0:T(8,128)S(1)}, f32[20,192]{1,0:T(8,128)S(1)}, f32[192,20,64]{0,2,1:T(8,128)})) conditional(s32[]{:T(128)} %convert_element_type.45, (f32[20,192]{1,0:T(8,128)S(1)}, f32[20,192]{1,0:T(8,128)S(1)}, f32[192,20,64]{0,2,1:T(8,128)}) %tuple.49, (s32[]{:T(128)}, bf16[192,6]{0,1:T(8,128)(2,1)S(1)}, ...), branch_computations={%region_3.3_spmd, %region_4.6_spmd} | conditional | flops 395177472 | bytes 36427132 | solution.py:63
  131.5 1.8 %constant_dynamic-slice_fusion = (bf16[1,384,1280]{1,2,0:T(8,128)(2,1)S(1)}, bf16[1,384,1280]{1,2,0:T(8,128)(2,1)S(1)}) fusion(bf16[2,384,1280]{1,2,0:T(8,128)(2,1)} %get-tuple-element.193, s32[]{:T(128)} %get-tuple-element.189, bf16[2,384,1280]{1,2,0:T(8,128)(2,1)} %get-tuple-element.188), kind=kLoop, calls=%fused_computation.28 | loop fusion | bytes 3932164 | tf_op jit(solution)/shard_map/while/body/jit(dynamic_index_in_dim)/dynamic_slice | solution.py:111
  133.3 1.3 fusion.2
  134.6 2.2 %fusion.1 = f32[20,192]{1,0:T(8,128)S(1)} fusion(f32[20,384,192]{1,2,0:T(8,128)S(1)} %get-tuple-element.252, f32[20,192]{1,0:T(8,128)S(1)} %get-tuple-element.325, pred[192,384]{1,0:T(8,128)(4,1)S(1)} %fusion.15), kind=kLoop, calls=%fused_computation.3 | loop fusion | flops 5894400 | bytes 6002688 | tf_op jit(solution)/shard_map/while/body/eval_jaxpr/cond/branch_1_fun/reduce_sum | solution.py:41
  136.9 1.9 %fusion.12 = f32[192,20,64]{0,2,1:T(8,128)S(1)} fusion(bf16[384,20,64]{0,2,1:T(8,128)(2,1)S(1)} %bitcast.76, f32[20,384,192]{1,2,0:T(8,128)S(1)} %get-tuple-element.252, f32[20,192]{1,0:T(8,128)S(1)} %get-tuple-element.325, pred[192,384]{1,0:T(8,128)(4,1)S(1)} %fusion.15, f32[192,20,64]{0,2,1:T(8,128)S(1)} %copy-done.3, f32[192,20]{0,1:T(8,128)S(1)} %get-tuple-element.249), kind=kOutput, calls=%fused_computation.11 | convolution fusion | flops 195133440 | bytes 8951808 | tf_op jit(solution)/shard_map/while/body/eval_jaxpr/cond/branch_1_fun/hqk,khd->qhd/dot_general | solution.py:43
  139.9 2.9 %fusion.34 = bf16[192,20,64]{0,2,1:T(8,128)(2,1)S(1)} fusion(bf16[128,20,64]{0,2,1:T(8,128)(2,1)} %bitcast.81, f32[192,20,64]{0,2,1:T(8,128)} %get-tuple-element.209, f32[20,128,192]{1,2,0:T(8,128)} %copy-done.2, f32[20,192]{1,0:T(8,128)S(1)} %get-tuple-element.256, f32[192,20]{0,1:T(8,128)S(1)} %bitcast_add_fusion, f32[192,20]{0,1:T(8,128)S(1)} %get-tuple-element.255, ...), kind=kOutput, calls=%fused_computation.55 | convolution fusion | flops 65617920 | bytes 3829760 | tf_op jit(solution)/shard_map/hqk,khd->qhd/dot_general | solution.py:43
  142.8 1.6 %convolution_convert_fusion = bf16[192,1280]{1,0:T(8,128)(2,1)} fusion(bf16[192,1280]{0,1:T(8,128)(2,1)S(1)} %bitcast.82, bf16[1280,1280]{1,0:T(8,128)(2,1)S(1)} %copy-done), kind=kOutput, calls=%fused_computation.45 | convolution fusion | flops 629391360 | bytes 4259840 | tf_op jit(solution)/shard_map/dot_general | solution.py:125
  (51 shorter events, 9.6 us)
Async XLA Ops:
  7.4 135.4 %copy-start = (bf16[1280,1280]{1,0:T(8,128)(2,1)S(1)}, bf16[1280,1280]{1,0:T(8,128)(2,1)}, u32[]{:S(2)}) copy-start(bf16[1280,1280]{1,0:T(8,128)(2,1)} %param.17) | copy-start | bytes 9830404
  7.4 4.9 %copy-start.5 = (s32[6,3]{0,1:T(4,128)S(1)}, s32[6,3]{0,1:T(4,128)}, u32[]{:S(2)}) copy-start(s32[6,3]{0,1:T(4,128)} %param.18) | copy-start | bytes 220
  7.4 76.5 %all-reduce.3.cloned.1.call-start = ((), (), s32[]{:S(2)}) async-start(), calls=%async_computation.2 | async-start | bytes 327680 | tf_op jit(solution)/shard_map/psum | solution.py:18
  8.9 98.6 %all-gather.3.cloned.1.call-start = ((), (), s32[]{:S(2)}) async-start(), calls=%async_computation | async-start | bytes 2457600 | tf_op jit(solution)/shard_map/all_gather | solution.py:90
  9.5 102.1 %all-gather.5.cloned.1.call-start = ((), (), s32[]{:S(2)}) async-start(), calls=%async_computation.1 | async-start | bytes 2457600 | tf_op jit(solution)/shard_map/all_gather | solution.py:91
  104.6 1.3 copy-start.2
  120.0 1.8 %copy-start.1 = (bf16[192,20,64]{0,2,1:T(8,128)(2,1)S(1)}, bf16[192,20,64]{0,2,1:T(8,128)(2,1)}, u32[]{:S(2)}) copy-start(bf16[192,20,64]{0,2,1:T(8,128)(2,1)} %get-tuple-element.190) | copy-start | bytes 1474564 | tf_op jit(solution)/shard_map/while/body/eval_jaxpr/cond
  123.1 2.3 %copy-start.3 = (f32[192,20,64]{0,2,1:T(8,128)S(1)}, f32[192,20,64]{0,2,1:T(8,128)}, u32[]{:S(2)}) copy-start(f32[192,20,64]{0,2,1:T(8,128)} %get-tuple-element.192) | copy-start | bytes 2949124 | tf_op jit(solution)/shard_map/while/body/eval_jaxpr/cond
  127.3 1.1 copy-start.4
  131.5 1.8 %copy-start.1 = (bf16[192,20,64]{0,2,1:T(8,128)(2,1)S(1)}, bf16[192,20,64]{0,2,1:T(8,128)(2,1)}, u32[]{:S(2)}) copy-start(bf16[192,20,64]{0,2,1:T(8,128)(2,1)} %get-tuple-element.190) | copy-start | bytes 1474564 | tf_op jit(solution)/shard_map/while/body/eval_jaxpr/cond
  134.6 2.3 %copy-start.3 = (f32[192,20,64]{0,2,1:T(8,128)S(1)}, f32[192,20,64]{0,2,1:T(8,128)}, u32[]{:S(2)}) copy-start(f32[192,20,64]{0,2,1:T(8,128)} %get-tuple-element.192) | copy-start | bytes 2949124 | tf_op jit(solution)/shard_map/while/body/eval_jaxpr/cond
  138.8 1.1 copy-start.4
Sparse Core Ops, SparseCore 0:
  11.6 72.2 all-reduce.2
Sparse Core Ops, SparseCore 1:
  11.0 24.6 all-gather.2
  37.1 21.7 all-gather.4
where the time goes:
time: 152 us
  waiting for transfers between devices  72.5 us (48%)
  local copies, waits for them, and re-layouts  23.5 us (15%)
  matrix products  15.8 us (10%)
  between operations  15.7 us (10%)
  blocking collectives  14.8 us (10%)
  other arithmetic  6.79 us (4%)
  loops' own time  2.63 us (2%)
    psum x1, waiting for transfers between devices, broadcast(): return lax.psum(kept, axis)  71.4 us
    while x2, local copies, waits for them, and re-layouts, body(): lax.scan(advance, initial, (stacked_keys, stacked_values, jnp.arange(bloc...  8.07 us
    all_gather x1, blocking collectives, body(): lax.all_gather(shared_values, 'view', axis=0, tiled=True)  7.57 us
    all_gather x1, blocking collectives, body(): lax.all_gather(shared_keys, 'view', axis=0, tiled=True)  7.18 us
    dot_general x3, matrix products, absorb(): jnp.einsum('hqk,khd->qhd', rounded, value_heads, preferred_element_type=j...  6.68 us
    reduce_sum x3, other arithmetic, absorb(): totals = totals * factor + jnp.sum(weights, axis=-1)  5.88 us
    dynamic_slice x4, local copies, waits for them, and re-layouts, body(): lax.scan(advance, initial, (stacked_keys, stacked_values, jnp.arange(bloc...  4.76 us
    dot_general x3, matrix products, absorb(): jnp.einsum('qhd,khd->hqk', query_heads, key_heads, preferred_element_type...  4.75 us
  transfers between devices with their start and end apart: 3, of which 1 were waited for; matrix products, arithmetic and copies ran while one was open for 9% of the time, Pallas kernels for 0%

commit v1 on v0

v1 whole, which is shorter than its diff:
```python
import functools

import jax
import jax.numpy as jnp
from jax import lax
from jax.experimental import pallas as pl
from jax.experimental.pallas import tpu as pltpu
from jax.sharding import PartitionSpec as P

HEADS = 20
HEAD_DIM = 64
VIEWS = 6
ADJ = 3
SCALE = 0.125
LANES = 128


def tree_broadcast(value, axis, source):
    count = lax.axis_size(axis)
    index = lax.axis_index(axis)
    if count & (count - 1):
        kept = jnp.where(index == source, value, jnp.zeros_like(value))
        return lax.psum(kept, axis)
    distance = 1
    while distance < count:
        pairs = [(i, i ^ distance) for i in range(count)]
        received = lax.ppermute(value, axis, pairs)
        partner_has = ((index ^ distance) // distance) == (source // distance)
        value = jnp.where(partner_has, received, value)
        distance *= 2
    return value


def gather_pieces(value, axis):
    count = lax.axis_size(axis)
    index = lax.axis_index(axis)
    if count == 4:
        across = lax.ppermute(value, axis, [(i, i ^ 2) for i in range(count)])
        both = jnp.concatenate([value, across], axis=0)
        near = lax.ppermute(both, axis, [(i, i ^ 1) for i in range(count)])
        positions = jnp.stack([index, index ^ 2, index ^ 1, index ^ 3])
        return [both, near], positions
    whole = lax.all_gather(value, axis, axis=0, tiled=True)
    return [whole], jnp.arange(count, dtype=jnp.int32)


def attention_kernel(piece_count, q_ref, *refs):
    key_refs = refs[: 2 * piece_count]
    rk_ref, rv_ref, bias_ref, out_ref = refs[2 * piece_count :]
    queries = q_ref[...]
    lane = lax.broadcasted_iota(jnp.int32, (1, LANES), 1)
    bias = bias_ref[...]
    dims = (((1,), (1,)), ((), ()))
    results = []
    for head in range(LANES // HEAD_DIM):
        own = (lane // HEAD_DIM) == head
        q_head = jnp.where(own, queries, jnp.zeros_like(queries))
        scores = [
            lax.dot_general(q_head, key_refs[2 * p][...], dims, preferred_element_type=jnp.float32)
            for p in range(piece_count)
        ]
        scores = jnp.concatenate(scores, axis=1) * SCALE + bias
        peak = jnp.max(scores, axis=1, keepdims=True)
        weights = jnp.exp(scores - peak)
        total = jnp.sum(weights, axis=1, keepdims=True)
        rounded = weights.astype(jnp.bfloat16)
        summed = None
        start = 0
        for p in range(piece_count):
            values = key_refs[2 * p + 1][...]
            rows = values.shape[0]
            part = jnp.dot(rounded[:, start : start + rows], values, preferred_element_type=jnp.float32)
            summed = part if summed is None else summed + part
            start += rows
        view_part = summed / total
        ref_scores = (
            lax.dot_general(q_head, rk_ref[...], dims, preferred_element_type=jnp.float32) * SCALE
        )
        ref_peak = jnp.max(ref_scores, axis=1, keepdims=True)
        ref_weights = jnp.exp(ref_scores - ref_peak)
        ref_total = jnp.sum(ref_weights, axis=1, keepdims=True)
        ref_summed = jnp.dot(
            ref_weights.astype(jnp.bfloat16), rv_ref[...], preferred_element_type=jnp.float32
        )
        results.append((own, view_part + ref_summed / ref_total))
    mixed = results[-1][1]
    for own, value in results[:-1]:
        mixed = jnp.where(own, value, mixed)
    out_ref[...] = mixed.astype(out_ref.dtype)


def attention(queries, pieces, ref_both, bias, width):
    rows = queries.shape[0]
    blocks = width // LANES
    in_specs = [pl.BlockSpec((rows, LANES), lambda j: (0, j))]
    operands = [queries]
    for piece in pieces:
        in_specs.append(pl.BlockSpec((piece.shape[0], LANES), lambda j: (0, j)))
        in_specs.append(pl.BlockSpec((piece.shape[0], LANES), lambda j: (0, j + blocks)))
        operands += [piece, piece]
    ref_rows = ref_both.shape[0]
    in_specs.append(pl.BlockSpec((ref_rows, LANES), lambda j: (0, j)))
    in_specs.append(pl.BlockSpec((ref_rows, LANES), lambda j: (0, j + blocks)))
    operands += [ref_both, ref_both]
    in_specs.append(pl.BlockSpec(bias.shape, lambda j: (0, 0)))
    operands.append(bias)
    keys = sum(piece.shape[0] for piece in pieces)
    flops = 4 * rows * (keys + ref_rows) * width * 2
    return pl.pallas_call(
        functools.partial(attention_kernel, len(pieces)),
        grid=(blocks,),
        in_specs=in_specs,
        out_specs=pl.BlockSpec((rows, LANES), lambda j: (0, j)),
        out_shape=jax.ShapeDtypeStruct((rows, width), jnp.bfloat16),
        compiler_params=pltpu.CompilerParams(
            dimension_semantics=("arbitrary",), vmem_limit_bytes=48 * 1024 * 1024
        ),
        cost_estimate=pl.CostEstimate(
            flops=flops,
            transcendentals=2 * rows * (keys + ref_rows) * HEADS,
            bytes_accessed=2 * (rows * width * 2 + (keys + ref_rows) * width * 2) + 4 * rows * keys,
        ),
    )(*operands)


def body(queries, keys, values, ref_keys, ref_values, out_weight, adjacency, ref_source):
    shard_rows, width = queries.shape
    view_count = lax.axis_size("view")
    view_index = lax.axis_index("view")
    view_tok = shard_rows * view_count // VIEWS

    ref_both = jnp.concatenate([ref_keys, ref_values], axis=1)
    ref_shared = tree_broadcast(ref_both, "mesh", ref_source[0])
    ref_pieces, unused = gather_pieces(ref_shared, "view")
    ref_all = ref_pieces[0] if len(ref_pieces) == 1 else jnp.concatenate(ref_pieces, axis=0)

    both = jnp.concatenate([keys, values], axis=1)
    pieces, positions = gather_pieces(both, "view")

    view_ids = jnp.arange(VIEWS, dtype=jnp.int32)
    listed = jnp.any(adjacency[:, :, None] == view_ids[None, None, :], axis=1)
    allowed = listed | (view_ids[:, None] == view_ids[None, :])
    query_views = (view_index * shard_rows + jnp.arange(shard_rows, dtype=jnp.int32)) // view_tok
    key_rows = (positions[:, None] * shard_rows + jnp.arange(shard_rows, dtype=jnp.int32)[None, :]).reshape(-1)
    key_views = key_rows // view_tok
    keep = allowed[query_views[:, None], key_views[None, :]]
    bias = jnp.where(keep, 0.0, -jnp.inf).astype(jnp.float32)

    mixed = attention(queries, pieces, ref_all, bias, width)
    return jnp.dot(mixed, out_weight, preferred_element_type=jnp.float32).astype(jnp.bfloat16)


def solution(mesh):
    return jax.shard_map(
        body,
        mesh=mesh,
        in_specs=(
            P(("mesh", "view"), None),
            P(("mesh", "view"), None),
            P(("mesh", "view"), None),
            P(("mesh", "view"), None),
            P(("mesh", "view"), None),
            P(),
            P("mesh", None),
            P(),
        ),
        out_specs=P(("mesh", "view"), None),
        check_vma=False,
    )
```

time: 152 us -> 1880 us (12.37)
  local copies, waits for them, and re-layouts: 23.5 us -> 1840 us
  waiting for transfers between devices: 72.5 us -> 7.28 us
    gather x0 -> x1, local copies, waits for them, and re-layouts: none -> 1830 us  [body(): keep = allowed[query_views[:, None], key_views[None, :]]]
    psum x1 -> x0, waiting for transfers between devices: 71.4 us -> none  [broadcast(): return lax.psum(kept, axis)]
  transfers between devices with their start and end apart: 3 -> 7, of which waited for: 1 -> 2; matrix products, arithmetic and copies ran while one was open for 9% -> 98% of each run, Pallas kernels for 0% -> 0%
where the time goes in v1:
time: 1880 us
  local copies, waits for them, and re-layouts  1840 us (98%)
    gather x1, local copies, waits for them, and re-layouts, body(): keep = allowed[query_views[:, None], key_views[None, :]]  1830 us
  transfers between devices with their start and end apart: 7, of which 2 were waited for; matrix products, arithmetic and copies ran while one was open for 98% of the time, Pallas kernels for 0%

profile of v1, /device:TPU:0, one launch (start us, length us, event | category | flops | bytes accessed | tf_op | source)
XLA Modules:
  0.0 1882.3 jit_solution(13916729701147797404)
XLA Ops:
  0.0 1.1 constant_dynamic-update-slice_fusion.3
  1.1 0.9 constant_dynamic-update-slice_fusion.2
  2.0 2.9 collective-permute-start.2
  4.9 1.9 constant_dynamic-update-slice_fusion.1
  6.7 1.9 constant_dynamic-update-slice_fusion
  8.6 1.5 collective-permute-start
  11.0 0.9 broadcast_select_fusion.1
  12.0 1.6 collective-permute-start.3
  13.7 3.8 collective-permute-done.3
  17.5 0.9 broadcast_select_fusion.2
  18.5 2.7 collective-permute-start.4
  21.1 0.9 broadcast_or_fusion
  22.1 1.9 reshape.79
  24.1 3.5 collective-permute-done.4
  27.5 0.9 broadcast_select_fusion.3
  29.0 1825.6 %gather_fusion = pred[147456]{0:T(1024)(128)(4,1)} fusion(pred[6,6]{1,0:T(8,128)(4,1)S(1)} %fusion.4, s32[147456]{0:T(1024)} %reshape.79), kind=kCustom, calls=%fused_computation | custom fusion | bytes 1474560 | tf_op jit(solution)/shard_map/gather | solution.py:146
  1854.7 1.7 pad_maximum_fusion.2
  1856.4 2.9 pad_maximum_fusion.refs_0_.refs_1_
  1860.7 2.0 reshape.87.refs_6_
  1862.7 1.1 pad_maximum_fusion.1.refs_4_.refs_5_
  1863.8 1.1 copy-done.1
  1864.8 1.0 copy-done.2
  1865.8 14.8 shard_map.82
  1880.7 1.6 convolution_convert_fusion
  (30 shorter events, 2.4 us)
Async XLA Ops:
  0.0 1880.7 %copy-start = (bf16[1280,1280]{1,0:T(8,128)(2,1)S(1)}, bf16[1280,1280]{1,0:T(8,128)(2,1)}, u32[]{:S(2)}) copy-start(bf16[1280,1280]{1,0:T(8,128)(2,1)} %param.13) | copy-start | bytes 9830404
  0.0 24.0 %copy-start.7 = (s32[6,3]{0,1:T(4,128)S(1)}, s32[6,3]{0,1:T(4,128)}, u32[]{:S(2)}) copy-start(s32[6,3]{0,1:T(4,128)} %param.14) | copy-start | bytes 220
  2.0 9.1 copy-start.6
  2.0 9.1 collective-permute-start.2
  8.6 1847.8 %collective-permute-start = (bf16[192,2560]{1,0:T(8,128)(2,1)}, bf16[192,2560]{1,0:T(8,128)(2,1)}, u32[]{:S(2)}, u32[]{:S(2)}) collective-permute-start(bf16[192,2560]{1,0:T(8,128)(2,1)} %constant_dynamic-update-slice_fusion), channel_id=1, source_target_pairs={{0,2},{1,3},{2,0},{3,1},{4,6},{5,7},{6,4},{7,5},{8,10},{9,11},{10,... | collective-permute-start | bytes 2949128 | tf_op jit(solution)/shard_map/ppermute | solution.py:38
  12.0 1.7 copy-start.4
  12.0 5.5 collective-permute-start.3
  18.5 5.6 copy-start.3
  18.5 9.0 collective-permute-start.4
  28.5 1826.2 %collective-permute-start.5 = (bf16[32,2560]{1,0:T(8,128)(2,1)S(1)}, bf16[32,2560]{1,0:T(8,128)(2,1)}, u32[]{:S(2)}, u32[]{:S(2)}) collective-permute-start(bf16[32,2560]{1,0:T(8,128)(2,1)S(1)} %broadcast_select_fusion.3), channel_id=1, source_target_pairs={{0,2},{1,3},{2,0},{3,1},{4,6},{5,7},{6,4},{7,5},{8,10},{9,11},{10,... | collective-permute-start | bytes 491528 | tf_op jit(solution)/shard_map/ppermute | solution.py:38
  1854.7 5.1 copy-start.5
  1856.4 6.3 collective-permute-start.6
  1859.3 4.5 collective-permute-start.1
  1863.7 1.1 copy-start.1
  1864.8 1.0 copy-start.2

commit v2 on v1

--- a/solution.py
+++ b/solution.py
@@ -138,12 +138,14 @@
     pieces, positions = gather_pieces(both, "view")
 
     view_ids = jnp.arange(VIEWS, dtype=jnp.int32)
-    listed = jnp.any(adjacency[:, :, None] == view_ids[None, None, :], axis=1)
-    allowed = listed | (view_ids[:, None] == view_ids[None, :])
     query_views = (view_index * shard_rows + jnp.arange(shard_rows, dtype=jnp.int32)) // view_tok
     key_rows = (positions[:, None] * shard_rows + jnp.arange(shard_rows, dtype=jnp.int32)[None, :]).reshape(-1)
     key_views = key_rows // view_tok
-    keep = allowed[query_views[:, None], key_views[None, :]]
+    query_onehot = (query_views[:, None] == view_ids[None, :]).astype(jnp.float32)
+    query_adjacent = jnp.dot(query_onehot, adjacency.astype(jnp.float32))
+    keep = query_views[:, None] == key_views[None, :]
+    for slot in range(ADJ):
+        keep = keep | (query_adjacent[:, slot : slot + 1] == key_views[None, :].astype(jnp.float32))
     bias = jnp.where(keep, 0.0, -jnp.inf).astype(jnp.float32)
 
     mixed = attention(queries, pieces, ref_all, bias, width)

time: 1880 us -> 58.6 us (0.03)
  local copies, waits for them, and re-layouts: 1840 us -> 5.81 us
    gather x1 -> x0, local copies, waits for them, and re-layouts: 1830 us -> none  [body(): keep = allowed[query_views[:, None], key_views[None, :]]]
  transfers between devices with their start and end apart: 7 -> 7, of which waited for: 2 -> 4; matrix products, arithmetic and copies ran while one was open for 98% -> 12% of each run, Pallas kernels for 0% -> 0%
where the time goes in v2:
time: 58.6 us; the launch traced here: 58.4 us
  waiting for transfers between devices  21 us (36%)
  Pallas kernels  14.4 us (25%)
  starting transfers between devices  11.4 us (19%)
  local copies, waits for them, and re-layouts  5.81 us (10%)
  other arithmetic  3.16 us (5%)
  matrix products  1.8 us (3%)
  between operations  0.87 us (1%)
    ppermute x2, waiting for transfers between devices, gather_pieces(): across = lax.ppermute(value, axis, [(i, i ^ 2) for i in range(count)])  15.9 us
    pallas_call x1, Pallas kernels, attention(): pl.pallas_call(functools.partial(attention_kernel, len(pieces)), grid=(bl...  14.4 us
    ppermute x3, starting transfers between devices, tree_broadcast(): received = lax.ppermute(value, axis, pairs)  8.15 us
    ppermute x3, waiting for transfers between devices, tree_broadcast(): received = lax.ppermute(value, axis, pairs)  3.8 us
    ppermute x2, starting transfers between devices, gather_pieces(): across = lax.ppermute(value, axis, [(i, i ^ 2) for i in range(count)])  3.1 us
    unnamed x10, local copies, waits for them, and re-layouts  2.95 us
    concatenate x1, local copies, waits for them, and re-layouts, body(): both = jnp.concatenate([keys, values], axis=1)  1.88 us
    concatenate x2, other arithmetic, gather_pieces(): both = jnp.concatenate([value, across], axis=0)  1.65 us
  transfers between devices with their start and end apart: 7, of which 4 were waited for; matrix products, arithmetic and copies ran while one was open for 12% of the time, Pallas kernels for 0%

profile of v2, /device:TPU:0, one launch (start us, length us, event | category | flops | bytes accessed | tf_op | source)
XLA Modules:
  0.0 58.4 jit_solution(15779356869783213959)
XLA Ops:
  0.0 1.0 %constant_dynamic-update-slice_fusion.3 = bf16[32,2560]{1,0:T(8,128)(2,1)S(1)} fusion(bf16[32,1280]{1,0:T(8,128)(2,1)} %param.11), kind=kLoop, calls=%fused_computation.14 | loop fusion | bytes 163840
  1.0 0.9 %constant_dynamic-update-slice_fusion.2 = bf16[32,2560]{1,0:T(8,128)(2,1)S(1)} fusion(bf16[32,2560]{1,0:T(8,128)(2,1)S(1)} %constant_dynamic-update-slice_fusion.3, bf16[32,1280]{1,0:T(8,128)(2,1)} %param.12), kind=kLoop, calls=%fused_computation.13 | loop fusion | bytes 163840 | tf_op jit(solution)/shard_map/concatenate | solution.py:132
  1.9 2.9 %collective-permute-start.2 = (bf16[32,2560]{1,0:T(8,128)(2,1)S(1)}, bf16[32,2560]{1,0:T(8,128)(2,1)}, u32[]{:S(2)}, u32[]{:S(2)}) collective-permute-start(bf16[32,2560]{1,0:T(8,128)(2,1)S(1)} %constant_dynamic-update-slice_fusion.2), channel_id=1, source_target_pairs={{0,4},{4,0},{8,12},{12,8},{16,20},{20,16},{24,28},{28,24},{1,5},{5... | collective-permute-start | bytes 491528 | tf_op jit(solution)/shard_map/ppermute | solution.py:27
  4.9 1.9 %constant_dynamic-update-slice_fusion.1 = bf16[192,2560]{1,0:T(8,128)(2,1)} fusion(bf16[192,1280]{1,0:T(8,128)(2,1)} %param.9), kind=kLoop, calls=%fused_computation.12 | loop fusion | bytes 983040
  6.8 1.9 %constant_dynamic-update-slice_fusion = bf16[192,2560]{1,0:T(8,128)(2,1)} fusion(bf16[192,2560]{1,0:T(8,128)(2,1)} %constant_dynamic-update-slice_fusion.1, bf16[192,1280]{1,0:T(8,128)(2,1)} %param.10), kind=kLoop, calls=%fused_computation.11 | loop fusion | bytes 983040 | tf_op jit(solution)/shard_map/concatenate | solution.py:137
  8.6 1.5 %collective-permute-start = (bf16[192,2560]{1,0:T(8,128)(2,1)}, bf16[192,2560]{1,0:T(8,128)(2,1)}, u32[]{:S(2)}, u32[]{:S(2)}) collective-permute-start(bf16[192,2560]{1,0:T(8,128)(2,1)} %constant_dynamic-update-slice_fusion), channel_id=1, source_target_pairs={{0,2},{1,3},{2,0},{3,1},{4,6},{5,7},{6,4},{7,5},{8,10},{9,11},{10,... | collective-permute-start | bytes 2949128 | tf_op jit(solution)/shard_map/ppermute | solution.py:38
  10.8 0.1 add_multiply_fusion
  10.9 0.1 iota_add_fusion
  11.0 0.1 add.58
  11.1 0.9 %broadcast_select_fusion = bf16[32,2560]{1,0:T(8,128)(2,1)S(1)} fusion(bf16[32,2560]{1,0:T(8,128)(2,1)} %collective-permute-done.2, bf16[32,2560]{1,0:T(8,128)(2,1)} %copy-done.2, pred[]{:T(512)S(6)} %eq.78), kind=kLoop, calls=%fused_computation.5 | loop fusion | flops 81920 | bytes 491521 | tf_op jit(solution)/shard_map/jit(_where)/select_n | solution.py:29
  12.0 1.6 %collective-permute-start.3 = (bf16[32,2560]{1,0:T(8,128)(2,1)S(1)}, bf16[32,2560]{1,0:T(8,128)(2,1)}, u32[]{:S(2)}, u32[]{:S(2)}) collective-permute-start(bf16[32,2560]{1,0:T(8,128)(2,1)S(1)} %broadcast_select_fusion), channel_id=1, source_target_pairs={{0,8},{4,12},{8,0},{12,4},{16,24},{20,28},{24,16},{28,20},{1,9},{5... | collective-permute-start | bytes 491528 | tf_op jit(solution)/shard_map/ppermute | solution.py:27
  13.8 3.8 %collective-permute-done.3 = bf16[32,2560]{1,0:T(8,128)(2,1)} collective-permute-done((bf16[32,2560]{1,0:T(8,128)(2,1)S(1)}, bf16[32,2560]{1,0:T(8,128)(2,1)}, u32[]{:S(2)}, u32[]{:S(2)}) %collective-permute-start.3) | collective-permute-done | bytes 163872 | tf_op jit(solution)/shard_map/ppermute | solution.py:27
  17.6 3.6 %collective-permute-start.4 = (bf16[32,2560]{1,0:T(8,128)(2,1)S(1)}, bf16[32,2560]{1,0:T(8,128)(2,1)S(1)}, u32[]{:S(2)}, u32[]{:S(2)}) collective-permute-start(bf16[32,2560]{1,0:T(8,128)(2,1)S(1)} %broadcast_select_fusion.1), channel_id=1, source_target_pairs={{0,16},{4,20},{8,24},{12,28},{16,0},{20,4},{24,8},{28,12},{1,17},{... | collective-permute-start | bytes 491528 | tf_op jit(solution)/shard_map/ppermute | solution.py:27
  21.2 11.0 %collective-permute-done = bf16[192,2560]{1,0:T(8,128)(2,1)} collective-permute-done((bf16[192,2560]{1,0:T(8,128)(2,1)}, bf16[192,2560]{1,0:T(8,128)(2,1)}, u32[]{:S(2)}, u32[]{:S(2)}) %collective-permute-start) | collective-permute-done | bytes 983072 | tf_op jit(solution)/shard_map/ppermute | solution.py:38
  32.2 1.6 %pad_maximum_fusion.refs_0_.refs_1_ = bf16[384,2560]{1,0:T(8,128)(2,1)S(1)} fusion(bf16[192,2560]{1,0:T(8,128)(2,1)} %collective-permute-done, bf16[192,2560]{1,0:T(8,128)(2,1)} %constant_dynamic-update-slice_fusion), kind=kLoop, calls=%fused_computation.1 | loop fusion | flops 3932160 | bytes 3932160 | tf_op jit(solution)/shard_map/concatenate | solution.py:39
  33.8 0.1 collective-permute-start.1
  33.9 1.6 %collective-permute-start.5 = (bf16[32,2560]{1,0:T(8,128)(2,1)S(1)}, bf16[32,2560]{1,0:T(8,128)(2,1)S(1)}, u32[]{:S(2)}, u32[]{:S(2)}) collective-permute-start(bf16[32,2560]{1,0:T(8,128)(2,1)S(1)} %broadcast_select_fusion.2), channel_id=1, source_target_pairs={{0,2},{1,3},{2,0},{3,1},{4,6},{5,7},{6,4},{7,5},{8,10},{9,11},{10,... | collective-permute-start | bytes 491528 | tf_op jit(solution)/shard_map/ppermute | solution.py:38
  35.5 0.2 fusion
  35.7 4.9 %collective-permute-done.5 = bf16[32,2560]{1,0:T(8,128)(2,1)S(1)} collective-permute-done((bf16[32,2560]{1,0:T(8,128)(2,1)S(1)}, bf16[32,2560]{1,0:T(8,128)(2,1)S(1)}, u32[]{:S(2)}, u32[]{:S(2)}) %collective-permute-start.5) | collective-permute-done | bytes 163872 | tf_op jit(solution)/shard_map/ppermute | solution.py:38
  40.6 0.1 collective-permute-start.6
  40.7 0.3 or_select_fusion.refs_6_
  41.0 1.3 %collective-permute-done.6 = bf16[64,2560]{1,0:T(8,128)(2,1)S(1)} collective-permute-done((bf16[64,2560]{1,0:T(8,128)(2,1)S(1)}, bf16[64,2560]{1,0:T(8,128)(2,1)S(1)}, u32[]{:S(2)}, u32[]{:S(2)}) %collective-permute-start.6) | collective-permute-done | bytes 327712 | tf_op jit(solution)/shard_map/ppermute | solution.py:40
  42.4 14.4 %shard_map.82 = bf16[192,1280]{1,0:T(8,128)(2,1)S(1)} custom-call(bf16[192,1280]{1,0:T(8,128)(2,1)S(1)} %copy-done.1, bf16[384,2560]{1,0:T(8,128)(2,1)S(1)} %pad_maximum_fusion.refs_0_.refs_1_, bf16[384,2560]{1,0:T(8,128)(2,1)S(1)} %pad_maximum_fusion.refs_0_.refs_1_, bf16[384,2560]{1,0:T(8,128)(2,1)S(1)} %collective-permute-done.1.refs_2_.refs_3_, ...), custom_call_target="tpu_custom_call" | custom-call | flops 1761607680 | bytes 6160384 | tf_op jit(solution)/shard_map/pallas_call | solution.py:109
  56.8 1.6 %convolution_convert_fusion = bf16[192,1280]{1,0:T(8,128)(2,1)} fusion(bf16[192,1280]{1,0:T(8,128)(2,1)S(1)} %shard_map.82, bf16[1280,1280]{1,0:T(8,128)(2,1)S(1)} %copy-done), kind=kOutput, calls=%fused_computation | convolution fusion | flops 629391360 | bytes 4259840 | tf_op jit(solution)/shard_map/dot_general | solution.py:152
  (18 shorter events, 0.2 us)
Async XLA Ops:
  0.0 56.8 %copy-start = (bf16[1280,1280]{1,0:T(8,128)(2,1)S(1)}, bf16[1280,1280]{1,0:T(8,128)(2,1)}, u32[]{:S(2)}) copy-start(bf16[1280,1280]{1,0:T(8,128)(2,1)} %param.13) | copy-start | bytes 9830404
  1.9 9.1 %copy-start.2 = (bf16[32,2560]{1,0:T(8,128)(2,1)}, bf16[32,2560]{1,0:T(8,128)(2,1)S(1)}, u32[]{:S(2)}) copy-start(bf16[32,2560]{1,0:T(8,128)(2,1)S(1)} %constant_dynamic-update-slice_fusion.2) | copy-start | bytes 491524
  1.9 9.1 %collective-permute-start.2 = (bf16[32,2560]{1,0:T(8,128)(2,1)S(1)}, bf16[32,2560]{1,0:T(8,128)(2,1)}, u32[]{:S(2)}, u32[]{:S(2)}) collective-permute-start(bf16[32,2560]{1,0:T(8,128)(2,1)S(1)} %constant_dynamic-update-slice_fusion.2), channel_id=1, source_target_pairs={{0,4},{4,0},{8,12},{12,8},{16,20},{20,16},{24,28},{28,24},{1,5},{5... | collective-permute-start | bytes 491528 | tf_op jit(solution)/shard_map/ppermute | solution.py:27
  8.6 23.5 %collective-permute-start = (bf16[192,2560]{1,0:T(8,128)(2,1)}, bf16[192,2560]{1,0:T(8,128)(2,1)}, u32[]{:S(2)}, u32[]{:S(2)}) collective-permute-start(bf16[192,2560]{1,0:T(8,128)(2,1)} %constant_dynamic-update-slice_fusion), channel_id=1, source_target_pairs={{0,2},{1,3},{2,0},{3,1},{4,6},{5,7},{6,4},{7,5},{8,10},{9,11},{10,... | collective-permute-start | bytes 2949128 | tf_op jit(solution)/shard_map/ppermute | solution.py:38
  12.0 5.5 %collective-permute-start.3 = (bf16[32,2560]{1,0:T(8,128)(2,1)S(1)}, bf16[32,2560]{1,0:T(8,128)(2,1)}, u32[]{:S(2)}, u32[]{:S(2)}) collective-permute-start(bf16[32,2560]{1,0:T(8,128)(2,1)S(1)} %broadcast_select_fusion), channel_id=1, source_target_pairs={{0,8},{4,12},{8,0},{12,4},{16,24},{20,28},{24,16},{28,20},{1,9},{5... | collective-permute-start | bytes 491528 | tf_op jit(solution)/shard_map/ppermute | solution.py:27
  17.6 17.9 %copy-start.3 = (s32[6,3]{0,1:T(4,128)S(1)}, s32[6,3]{0,1:T(4,128)}, u32[]{:S(2)}) copy-start(s32[6,3]{0,1:T(4,128)} %param.14) | copy-start | bytes 220
  17.6 16.3 %collective-permute-start.4 = (bf16[32,2560]{1,0:T(8,128)(2,1)S(1)}, bf16[32,2560]{1,0:T(8,128)(2,1)S(1)}, u32[]{:S(2)}, u32[]{:S(2)}) collective-permute-start(bf16[32,2560]{1,0:T(8,128)(2,1)S(1)} %broadcast_select_fusion.1), channel_id=1, source_target_pairs={{0,16},{4,20},{8,24},{12,28},{16,0},{20,4},{24,8},{28,12},{1,17},{... | collective-permute-start | bytes 491528 | tf_op jit(solution)/shard_map/ppermute | solution.py:27
  33.8 8.6 %copy-start.1 = (bf16[192,1280]{1,0:T(8,128)(2,1)S(1)}, bf16[192,1280]{1,0:T(8,128)(2,1)}, u32[]{:S(2)}) copy-start(bf16[192,1280]{1,0:T(8,128)(2,1)} %q_ref.1) | copy-start | bytes 1474564
  33.8 8.5 %collective-permute-start.1 = (bf16[384,2560]{1,0:T(8,128)(2,1)S(1)}, bf16[384,2560]{1,0:T(8,128)(2,1)S(1)}, u32[]{:S(2)}, u32[]{:S(2)}) collective-permute-start(bf16[384,2560]{1,0:T(8,128)(2,1)S(1)} %pad_maximum_fusion.refs_0_.refs_1_), channel_id=1, source_target_pairs={{0,1},{1,0},{2,3},{3,2},{4,5},{5,4},{6,7},{7,6},{8,9},{9,8},{10,11... | collective-permute-start | bytes 5898248 | tf_op jit(solution)/shard_map/ppermute | solution.py:40
  33.9 6.7 %collective-permute-start.5 = (bf16[32,2560]{1,0:T(8,128)(2,1)S(1)}, bf16[32,2560]{1,0:T(8,128)(2,1)S(1)}, u32[]{:S(2)}, u32[]{:S(2)}) collective-permute-start(bf16[32,2560]{1,0:T(8,128)(2,1)S(1)} %broadcast_select_fusion.2), channel_id=1, source_target_pairs={{0,2},{1,3},{2,0},{3,1},{4,6},{5,7},{6,4},{7,5},{8,10},{9,11},{10,... | collective-permute-start | bytes 491528 | tf_op jit(solution)/shard_map/ppermute | solution.py:38
  40.6 1.7 %collective-permute-start.6 = (bf16[64,2560]{1,0:T(8,128)(2,1)S(1)}, bf16[64,2560]{1,0:T(8,128)(2,1)S(1)}, u32[]{:S(2)}, u32[]{:S(2)}) collective-permute-start(bf16[64,2560]{1,0:T(8,128)(2,1)S(1)} %pad_maximum_fusion.2), channel_id=1, source_target_pairs={{0,1},{1,0},{2,3},{3,2},{4,5},{5,4},{6,7},{7,6},{8,9},{9,8},{10,11... | collective-permute-start | bytes 983048 | tf_op jit(solution)/shard_map/ppermute | solution.py:40

commit v3 on v2

v3 whole, which is shorter than its diff:
```python
import functools

import jax
import jax.numpy as jnp
from jax import lax
from jax.experimental import pallas as pl
from jax.experimental.pallas import tpu as pltpu
from jax.sharding import PartitionSpec as P

HEADS = 20
HEAD_DIM = 64
VIEWS = 6
ADJ = 3
SCALE = 0.125
LANES = 128


def tree_broadcast(value, axis, source):
    count = lax.axis_size(axis)
    index = lax.axis_index(axis)
    if count & (count - 1):
        kept = jax.tree.map(lambda a: jnp.where(index == source, a, jnp.zeros_like(a)), value)
        return lax.psum(kept, axis)
    distance = 1
    while distance < count:
        pairs = [(i, i ^ distance) for i in range(count)]
        received = lax.ppermute(value, axis, pairs)
        partner_has = ((index ^ distance) // distance) == (source // distance)
        value = jax.tree.map(lambda r, a: jnp.where(partner_has, r, a), received, value)
        distance *= 2
    return value


def gather_rows(value, axis):
    count = lax.axis_size(axis)
    if count == 4:
        across = lax.ppermute(value, axis, [(i, i ^ 2) for i in range(count)])
        both = jax.tree.map(lambda a, b: jnp.concatenate([a, b], axis=0), value, across)
        near = lax.ppermute(both, axis, [(i, i ^ 1) for i in range(count)])
        return jax.tree.map(lambda a, b: jnp.concatenate([a, b], axis=0), both, near)
    return lax.all_gather(value, axis, axis=0, tiled=True)


def absorb_kernel(first, final, q_ref, k_ref, v_ref, bias_ref, *rest):
    rest = list(rest)
    if not first:
        m_in, t_in, acc_in = rest[:3]
        rest = rest[3:]
    if final:
        rk_ref, rv_ref, out_ref = rest
    else:
        m_out, t_out, acc_out = rest
    step = pl.program_id(0)
    rows = q_ref.shape[0]
    queries = q_ref[...]
    lane = lax.broadcasted_iota(jnp.int32, (1, LANES), 1)
    bias = bias_ref[...]
    dims = (((1,), (1,)), ((), ()))
    if first:
        m_cur = jnp.full((rows, LANES), -1e30, jnp.float32)
        t_cur = jnp.zeros((rows, LANES), jnp.float32)
        acc_old = jnp.zeros((rows, LANES), jnp.float32)
    else:
        m_cur = m_in[...]
        t_cur = t_in[...]
        acc_old = acc_in[...]
    keys = k_ref[...]
    values = v_ref[...]
    results = []
    for head in range(LANES // HEAD_DIM):
        own = (lane // HEAD_DIM) == head
        picked = lane == step * (LANES // HEAD_DIM) + head
        m_old = jnp.sum(jnp.where(picked, m_cur, 0.0), axis=1, keepdims=True)
        t_old = jnp.sum(jnp.where(picked, t_cur, 0.0), axis=1, keepdims=True)
        q_head = jnp.where(own, queries, jnp.zeros_like(queries))
        scores = lax.dot_general(q_head, keys, dims, preferred_element_type=jnp.float32) * SCALE + bias
        m_new = jnp.maximum(m_old, jnp.max(scores, axis=1, keepdims=True))
        alpha = jnp.exp(m_old - m_new)
        weights = jnp.exp(scores - m_new)
        t_new = alpha * t_old + jnp.sum(weights, axis=1, keepdims=True)
        summed = alpha * acc_old + jnp.dot(
            weights.astype(jnp.bfloat16), values, preferred_element_type=jnp.float32
        )
        if final:
            ref_scores = (
                lax.dot_general(q_head, rk_ref[...], dims, preferred_element_type=jnp.float32) * SCALE
            )
            ref_peak = jnp.max(ref_scores, axis=1, keepdims=True)
            ref_weights = jnp.exp(ref_scores - ref_peak)
            ref_total = jnp.sum(ref_weights, axis=1, keepdims=True)
            ref_summed = jnp.dot(
                ref_weights.astype(jnp.bfloat16), rv_ref[...], preferred_element_type=jnp.float32
            )
            results.append((own, summed / t_new + ref_summed / ref_total))
        else:
            m_cur = jnp.where(picked, m_new, m_cur)
            t_cur = jnp.where(picked, t_new, t_cur)
            results.append((own, summed))
    merged = results[-1][1]
    for own, value in results[:-1]:
        merged = jnp.where(own, value, merged)
    if final:
        out_ref[...] = merged.astype(out_ref.dtype)
    else:
        acc_out[...] = merged

        @pl.when(step == 0)
        def _():
            m_out[...] = m_cur
            t_out[...] = t_cur

        @pl.when(step > 0)
        def _():
            m_out[...] = jnp.where((lane // 2) == step, m_cur, m_out[...])
            t_out[...] = jnp.where((lane // 2) == step, t_cur, t_out[...])


def absorb(queries, piece, bias, state, ref, final):
    rows, width = queries.shape
    blocks = width // LANES
    piece_keys, piece_values = piece
    count = piece_keys.shape[0]
    column = lambda j: (0, j)
    fixed = lambda j: (0, 0)
    in_specs = [
        pl.BlockSpec((rows, LANES), column),
        pl.BlockSpec((count, LANES), column),
        pl.BlockSpec((count, LANES), column),
        pl.BlockSpec((rows, count), fixed),
    ]
    operands = [queries, piece_keys, piece_values, bias]
    if state is not None:
        in_specs += [
            pl.BlockSpec((rows, LANES), fixed),
            pl.BlockSpec((rows, LANES), fixed),
            pl.BlockSpec((rows, LANES), column),
        ]
        operands += list(state)
    ref_rows = 0
    if final:
        ref_keys, ref_values = ref
        ref_rows = ref_keys.shape[0]
        in_specs += [pl.BlockSpec((ref_rows, LANES), column), pl.BlockSpec((ref_rows, LANES), column)]
        operands += [ref_keys, ref_values]
        out_specs = pl.BlockSpec((rows, LANES), column)
        out_shape = jax.ShapeDtypeStruct((rows, width), jnp.bfloat16)
    else:
        out_specs = (
            pl.BlockSpec((rows, LANES), fixed),
            pl.BlockSpec((rows, LANES), fixed),
            pl.BlockSpec((rows, LANES), column),
        )
        out_shape = (
            jax.ShapeDtypeStruct((rows, LANES), jnp.float32),
            jax.ShapeDtypeStruct((rows, LANES), jnp.float32),
            jax.ShapeDtypeStruct((rows, width), jnp.float32),
        )
    keys = count + ref_rows
    return pl.pallas_call(
        functools.partial(absorb_kernel, state is None, final),
        grid=(blocks,),
        in_specs=in_specs,
        out_specs=out_specs,
        out_shape=out_shape,
        compiler_params=pltpu.CompilerParams(
            dimension_semantics=("arbitrary",), vmem_limit_bytes=48 * 1024 * 1024
        ),
        cost_estimate=pl.CostEstimate(
            flops=8 * rows * keys * width,
            transcendentals=2 * rows * keys * HEADS,
            bytes_accessed=2 * (rows + 2 * keys) * width + 4 * rows * (count + 3 * width),
        ),
    )(*operands)


def key_bias(query_views, query_adjacent, positions, shard_rows, view_tok):
    key_rows = (positions[:, None] * shard_rows + jnp.arange(shard_rows, dtype=jnp.int32)[None, :]).reshape(-1)
    key_views = key_rows // view_tok
    keep = query_views[:, None] == key_views[None, :]
    for slot in range(ADJ):
        keep = keep | (query_adjacent[:, slot : slot + 1] == key_views[None, :].astype(jnp.float32))
    return jnp.where(keep, 0.0, -jnp.inf).astype(jnp.float32)


def body(queries, keys, values, ref_keys, ref_values, out_weight, adjacency, ref_source):
    shard_rows, width = queries.shape
    view_count = lax.axis_size("view")
    view_index = lax.axis_index("view")
    view_tok = shard_rows * view_count // VIEWS

    view_ids = jnp.arange(VIEWS, dtype=jnp.int32)
    query_views = (view_index * shard_rows + jnp.arange(shard_rows, dtype=jnp.int32)) // view_tok
    query_onehot = (query_views[:, None] == view_ids[None, :]).astype(jnp.float32)
    query_adjacent = jnp.dot(query_onehot, adjacency.astype(jnp.float32))

    def bias_for(*positions):
        return key_bias(query_views, query_adjacent, jnp.stack(positions), shard_rows, view_tok)

    own = (keys, values)
    if view_count == 4:
        across = lax.ppermute(own, "view", [(i, i ^ 2) for i in range(view_count)])
        near = lax.ppermute(own, "view", [(i, i ^ 1) for i in range(view_count)])
        far = lax.ppermute(across, "view", [(i, i ^ 1) for i in range(view_count)])
    ref_both = jnp.concatenate([ref_keys, ref_values], axis=1)
    ref_shared = gather_rows(tree_broadcast(ref_both, "mesh", ref_source[0]), "view")
    ref_all = (ref_shared[:, :width], ref_shared[:, width:])

    if view_count == 4:
        state = absorb(queries, own, bias_for(view_index), None, None, False)
        state = absorb(queries, near, bias_for(view_index ^ 1), state, None, False)
        state = absorb(queries, across, bias_for(view_index ^ 2), state, None, False)
        mixed = absorb(queries, far, bias_for(view_index ^ 3), state, ref_all, True)
    else:
        whole = lax.all_gather(own, "view", axis=0, tiled=True)
        mixed = absorb(queries, whole, bias_for(*range(view_count)), None, ref_all, True)
    return jnp.dot(mixed, out_weight, preferred_element_type=jnp.float32).astype(jnp.bfloat16)


def solution(mesh):
    return jax.shard_map(
        body,
        mesh=mesh,
        in_specs=(
            P(("mesh", "view"), None),
            P(("mesh", "view"), None),
            P(("mesh", "view"), None),
            P(("mesh", "view"), None),
            P(("mesh", "view"), None),
            P(),
            P("mesh", None),
            P(),
        ),
        out_specs=P(("mesh", "view"), None),
        check_vma=False,
    )
```

time: 58.6 us -> 74.6 us (1.27); the launches traced: 58.4 us -> 73.3 us
  Pallas kernels: 14.4 us -> 35.7 us
  waiting for transfers between devices: 21 us -> 16.2 us
  local copies, waits for them, and re-layouts: 5.81 us -> 2.01 us
  starting transfers between devices: 11.4 us -> 12.7 us
    pallas_call x1 -> x4, Pallas kernels: 14.4 us -> 35.7 us  [absorb(): pl.pallas_call(functools.partial(absorb_kernel, state is None, final), gr...]
    ppermute x4 -> x8, waiting for transfers between devices: 17.2 us -> 5.82 us  [the longest x1 5.8 us: gather_rows(): across = lax.ppermute(value, axis, [(i, i ^ 2) for i in range(count)])]
    ppermute x3, waiting for transfers between devices: 3.8 us -> 10.4 us  [tree_broadcast(): received = lax.ppermute(value, axis, pairs)]
    unnamed x10 -> x11, local copies, waits for them, and re-layouts: 2.95 us -> 1.07 us
    concatenate x1 -> x0, local copies, waits for them, and re-layouts: 1.88 us -> none  [body(): both = jnp.concatenate([keys, values], axis=1)]
    ppermute x4 -> x8, starting transfers between devices: 3.25 us -> 4.55 us  [the longest x2 2.03 us: body(): across = lax.ppermute(own, 'view', [(i, i ^ 2) for i in range(view_count)])]
    concatenate x3 -> x2, other arithmetic: 1.69 us -> 1.9 us  [gather_rows(): jnp.concatenate([a, b], axis=0)]
  transfers between devices with their start and end apart: 7 -> 11, of which waited for: 4 -> 4; matrix products, arithmetic and copies ran while one was open for 12% -> 6% of each run, Pallas kernels for 0% -> 34%
where the time goes in v3:
time: 74.6 us; the launch traced here: 73.3 us
  Pallas kernels  35.7 us (48%)
  waiting for transfers between devices  16.2 us (22%)
  starting transfers between devices  12.7 us (17%)
  other arithmetic  3.32 us (4%)
  matrix products  2.48 us (3%)
  local copies, waits for them, and re-layouts  2.01 us (3%)
  between operations  0.9 us (1%)
    pallas_call x4, Pallas kernels, absorb(): pl.pallas_call(functools.partial(absorb_kernel, state is None, final), gr...  35.7 us
    ppermute x3, waiting for transfers between devices, tree_broadcast(): received = lax.ppermute(value, axis, pairs)  10.4 us
    ppermute x3, starting transfers between devices, tree_broadcast(): received = lax.ppermute(value, axis, pairs)  8.17 us
    ppermute x1, waiting for transfers between devices, gather_rows(): across = lax.ppermute(value, axis, [(i, i ^ 2) for i in range(count)])  5.8 us
    ppermute x2, starting transfers between devices, body(): across = lax.ppermute(own, 'view', [(i, i ^ 2) for i in range(view_count)])  2.03 us
    concatenate x2, other arithmetic, gather_rows(): jnp.concatenate([a, b], axis=0)  1.9 us
    dot_general x1, matrix products, body(): jnp.dot(mixed, out_weight, preferred_element_type=jnp.float32)  1.59 us
    ppermute x1, starting transfers between devices, gather_rows(): across = lax.ppermute(value, axis, [(i, i ^ 2) for i in range(count)])  1.58 us
  transfers between devices with their start and end apart: 11, of which 4 were waited for; matrix products, arithmetic and copies ran while one was open for 6% of the time, Pallas kernels for 34%

profile of v3, /device:TPU:0, one launch (start us, length us, event | category | flops | bytes accessed | tf_op | source)
XLA Modules:
  0.0 73.3 jit_solution(7192665733554109091)
XLA Ops:
  0.0 1.0 %constant_dynamic-update-slice_fusion.1 = bf16[32,2560]{1,0:T(8,128)(2,1)S(1)} fusion(bf16[32,1280]{1,0:T(8,128)(2,1)} %param.11), kind=kLoop, calls=%fused_computation.14 | loop fusion | bytes 163840
  1.0 0.9 %constant_dynamic-update-slice_fusion = bf16[32,2560]{1,0:T(8,128)(2,1)S(1)} fusion(bf16[32,2560]{1,0:T(8,128)(2,1)S(1)} %constant_dynamic-update-slice_fusion.1, bf16[32,1280]{1,0:T(8,128)(2,1)} %param.12), kind=kLoop, calls=%fused_computation.13 | loop fusion | bytes 163840 | tf_op jit(solution)/shard_map/concatenate | solution.py:204
  1.9 2.9 %collective-permute-start.6 = (bf16[32,2560]{1,0:T(8,128)(2,1)S(1)}, bf16[32,2560]{1,0:T(8,128)(2,1)}, u32[]{:S(2)}, u32[]{:S(2)}) collective-permute-start(bf16[32,2560]{1,0:T(8,128)(2,1)S(1)} %constant_dynamic-update-slice_fusion), channel_id=1, source_target_pairs={{0,4},{4,0},{8,12},{12,8},{16,20},{20,16},{24,28},{28,24},{1,5},{5... | collective-permute-start | bytes 491528 | tf_op jit(solution)/shard_map/ppermute | solution.py:27
  4.9 1.5 %collective-permute-start = (bf16[192,1280]{1,0:T(8,128)(2,1)}, bf16[192,1280]{1,0:T(8,128)(2,1)}, u32[]{:S(2)}, u32[]{:S(2)}) collective-permute-start(bf16[192,1280]{1,0:T(8,128)(2,1)} %k_ref.1), channel_id=1, source_target_pairs={{0,2},{1,3},{2,0},{3,1},{4,6},{5,7},{6,4},{7,5},{8,10},{9,11},{10,... | collective-permute-start | bytes 1474568 | tf_op jit(solution)/shard_map/ppermute | solution.py:201
  6.4 0.2 collective-permute-start.5
  6.6 0.5 collective-permute-start.2
  7.9 1.3 %collective-permute-done.6 = bf16[32,2560]{1,0:T(8,128)(2,1)} collective-permute-done((bf16[32,2560]{1,0:T(8,128)(2,1)S(1)}, bf16[32,2560]{1,0:T(8,128)(2,1)}, u32[]{:S(2)}, u32[]{:S(2)}) %collective-permute-start.6) | collective-permute-done | bytes 163872 | tf_op jit(solution)/shard_map/ppermute | solution.py:27
  9.2 1.9 %collective-permute-start.7 = (bf16[32,2560]{1,0:T(8,128)(2,1)S(1)}, bf16[32,2560]{1,0:T(8,128)(2,1)S(1)}, u32[]{:S(2)}, u32[]{:S(2)}) collective-permute-start(bf16[32,2560]{1,0:T(8,128)(2,1)S(1)} %broadcast_select_fusion), channel_id=1, source_target_pairs={{0,8},{4,12},{8,0},{12,4},{16,24},{20,28},{24,16},{28,20},{1,9},{5... | collective-permute-start | bytes 491528 | tf_op jit(solution)/shard_map/ppermute | solution.py:27
  11.1 0.9 %fusion = f32[192,3]{0,1:T(4,128)S(1)} fusion(s32[192]{0:T(256)S(1)} %get-tuple-element.32, s32[6,3]{0,1:T(4,128)} %param.14), kind=kOutput, calls=%fused_computation.11 | convolution fusion | flops 8082 | bytes 3144 | tf_op jit(solution)/shard_map/dot_general | solution.py:194
  12.0 2.7 %collective-permute-done.7 = bf16[32,2560]{1,0:T(8,128)(2,1)S(1)} collective-permute-done((bf16[32,2560]{1,0:T(8,128)(2,1)S(1)}, bf16[32,2560]{1,0:T(8,128)(2,1)S(1)}, u32[]{:S(2)}, u32[]{:S(2)}) %collective-permute-start.7) | collective-permute-done | bytes 163872 | tf_op jit(solution)/shard_map/ppermute | solution.py:27
  14.7 3.3 %collective-permute-start.8 = (bf16[32,2560]{1,0:T(8,128)(2,1)S(1)}, bf16[32,2560]{1,0:T(8,128)(2,1)}, u32[]{:S(2)}, u32[]{:S(2)}) collective-permute-start(bf16[32,2560]{1,0:T(8,128)(2,1)S(1)} %broadcast_select_fusion.1), channel_id=1, source_target_pairs={{0,16},{4,20},{8,24},{12,28},{16,0},{20,4},{24,8},{28,12},{1,17},{... | collective-permute-start | bytes 491528 | tf_op jit(solution)/shard_map/ppermute | solution.py:27
  18.1 6.4 %collective-permute-done.8 = bf16[32,2560]{1,0:T(8,128)(2,1)} collective-permute-done((bf16[32,2560]{1,0:T(8,128)(2,1)S(1)}, bf16[32,2560]{1,0:T(8,128)(2,1)}, u32[]{:S(2)}, u32[]{:S(2)}) %collective-permute-start.8) | collective-permute-done | bytes 163872 | tf_op jit(solution)/shard_map/ppermute | solution.py:27
  24.5 0.9 %broadcast_select_fusion.2 = bf16[32,2560]{1,0:T(8,128)(2,1)S(1)} fusion(bf16[32,2560]{1,0:T(8,128)(2,1)} %collective-permute-done.8, bf16[32,2560]{1,0:T(8,128)(2,1)} %copy-done.4, pred[]{:T(512)S(6)} %eq.108), kind=kLoop, calls=%fused_computation.9 | loop fusion | flops 81920 | bytes 491521 | tf_op jit(solution)/shard_map/jit(_where)/select_n | solution.py:29
  25.4 1.6 %collective-permute-start.9 = (bf16[32,2560]{1,0:T(8,128)(2,1)S(1)}, bf16[32,2560]{1,0:T(8,128)(2,1)}, u32[]{:S(2)}, u32[]{:S(2)}) collective-permute-start(bf16[32,2560]{1,0:T(8,128)(2,1)S(1)} %broadcast_select_fusion.2), channel_id=1, source_target_pairs={{0,2},{1,3},{2,0},{3,1},{4,6},{5,7},{6,4},{7,5},{8,10},{9,11},{10,... | collective-permute-start | bytes 491528 | tf_op jit(solution)/shard_map/ppermute | solution.py:37
  27.1 5.8 %collective-permute-done.9 = bf16[32,2560]{1,0:T(8,128)(2,1)} collective-permute-done((bf16[32,2560]{1,0:T(8,128)(2,1)S(1)}, bf16[32,2560]{1,0:T(8,128)(2,1)}, u32[]{:S(2)}, u32[]{:S(2)}) %collective-permute-start.9) | collective-permute-done | bytes 163872 | tf_op jit(solution)/shard_map/ppermute | solution.py:37
  32.9 0.9 %pad_maximum_fusion.1 = bf16[64,2560]{1,0:T(8,128)(2,1)S(1)} fusion(bf16[32,2560]{1,0:T(8,128)(2,1)} %collective-permute-done.9, bf16[32,2560]{1,0:T(8,128)(2,1)S(1)} %broadcast_select_fusion.2), kind=kLoop, calls=%fused_computation.2 | loop fusion | flops 655360 | bytes 655360 | tf_op jit(solution)/shard_map/concatenate | solution.py:38
  33.9 0.4 or_select_fusion
  34.3 7.6 %shard_map.82 = (f32[192,128]{1,0:T(8,128)S(1)}, f32[192,128]{1,0:T(8,128)S(1)}, f32[192,1280]{1,0:T(8,128)S(1)}) custom-call(bf16[192,1280]{1,0:T(8,128)(2,1)S(1)} %copy-done.1, bf16[192,1280]{1,0:T(8,128)(2,1)S(1)} %copy-done.2, bf16[192,1280]{1,0:T(8,128)(2,1)S(1)} %copy-done.3, f32[192,192]{1,0:T(8,128)S(1)} %get-tuple-element.25.bias_ref), custom_call_target="tpu_custom_call" | custom-call | flops 377487360 | bytes 4571136 | tf_op jit(solution)/shard_map/pallas_call | solution.py:159
  42.0 0.6 collective-permute-start.1
  42.6 8.8 %shard_map.83 = (f32[192,128]{1,0:T(8,128)S(1)}, f32[192,128]{1,0:T(8,128)S(1)}, f32[192,1280]{1,0:T(8,128)S(1)}) custom-call(bf16[192,1280]{1,0:T(8,128)(2,1)S(1)} %copy-done.1, bf16[192,1280]{1,0:T(8,128)(2,1)} %collective-permute-done.4.k_ref, bf16[192,1280]{1,0:T(8,128)(2,1)} %collective-permute-done.5.v_ref, f32[192,192]{1,0:T(8,128)S(1)} %get-tuple-element.26.bias_ref, ...), custom_call_target="tpu_custom_call" | custom-call | flops 377487360 | bytes 4571136 | tf_op jit(solution)/shard_map/pallas_call | solution.py:159
  51.4 8.8 %shard_map.84 = (f32[192,128]{1,0:T(8,128)S(1)}, f32[192,128]{1,0:T(8,128)S(1)}, f32[192,1280]{1,0:T(8,128)S(1)}) custom-call(bf16[192,1280]{1,0:T(8,128)(2,1)S(1)} %copy-done.1, bf16[192,1280]{1,0:T(8,128)(2,1)} %collective-permute-done.k_ref, bf16[192,1280]{1,0:T(8,128)(2,1)} %collective-permute-done.2.v_ref, f32[192,192]{1,0:T(8,128)S(1)} %get-tuple-element.27.bias_ref, ...), custom_call_target="tpu_custom_call" | custom-call | flops 377487360 | bytes 4571136 | tf_op jit(solution)/shard_map/pallas_call | solution.py:159
  60.2 1.0 %pad_maximum_fusion = bf16[128,2560]{1,0:T(8,128)(2,1)S(1)} fusion(bf16[64,2560]{1,0:T(8,128)(2,1)S(1)} %collective-permute-done.10, bf16[32,2560]{1,0:T(8,128)(2,1)} %collective-permute-done.9, bf16[32,2560]{1,0:T(8,128)(2,1)S(1)} %broadcast_select_fusion.2), kind=kLoop, calls=%fused_computation.1 | loop fusion | flops 1966080 | bytes 1310720 | tf_op jit(solution)/shard_map/concatenate | solution.py:40
  61.2 10.5 %shard_map.85 = bf16[192,1280]{1,0:T(8,128)(2,1)S(1)} custom-call(bf16[192,1280]{1,0:T(8,128)(2,1)S(1)} %copy-done.1, bf16[192,1280]{1,0:T(8,128)(2,1)S(1)} %collective-permute-done.1.k_ref, bf16[192,1280]{1,0:T(8,128)(2,1)S(1)} %collective-permute-done.3.v_ref, f32[192,192]{1,0:T(8,128)S(1)} %get-tuple-element.28.bias_ref, ...), custom_call_target="tpu_custom_call" | custom-call | flops 629145600 | bytes 5226496 | tf_op jit(solution)/shard_map/pallas_call | solution.py:159
  71.7 1.6 %convolution_convert_fusion = bf16[192,1280]{1,0:T(8,128)(2,1)} fusion(bf16[192,1280]{1,0:T(8,128)(2,1)S(1)} %shard_map.85, bf16[1280,1280]{1,0:T(8,128)(2,1)S(1)} %copy-done), kind=kOutput, calls=%fused_computation | convolution fusion | flops 629391360 | bytes 4259840 | tf_op jit(solution)/shard_map/dot_general | solution.py:216
  (28 shorter events, 0.3 us)
Async XLA Ops:
  0.0 71.7 %copy-start = (bf16[1280,1280]{1,0:T(8,128)(2,1)S(1)}, bf16[1280,1280]{1,0:T(8,128)(2,1)}, u32[]{:S(2)}) copy-start(bf16[1280,1280]{1,0:T(8,128)(2,1)} %param.13) | copy-start | bytes 9830404
  1.9 7.2 %collective-permute-start.6 = (bf16[32,2560]{1,0:T(8,128)(2,1)S(1)}, bf16[32,2560]{1,0:T(8,128)(2,1)}, u32[]{:S(2)}, u32[]{:S(2)}) collective-permute-start(bf16[32,2560]{1,0:T(8,128)(2,1)S(1)} %constant_dynamic-update-slice_fusion), channel_id=1, source_target_pairs={{0,4},{4,0},{8,12},{12,8},{16,20},{20,16},{24,28},{28,24},{1,5},{5... | collective-permute-start | bytes 491528 | tf_op jit(solution)/shard_map/ppermute | solution.py:27
  4.9 37.7 %collective-permute-start.4 = (bf16[192,1280]{1,0:T(8,128)(2,1)}, bf16[192,1280]{1,0:T(8,128)(2,1)}, u32[]{:S(2)}, u32[]{:S(2)}) collective-permute-start(bf16[192,1280]{1,0:T(8,128)(2,1)} %k_ref.1), channel_id=1, source_target_pairs={{0,1},{1,0},{2,3},{3,2},{4,5},{5,4},{6,7},{7,6},{8,9},{9,8},{10,11... | collective-permute-start | bytes 1474568 | tf_op jit(solution)/shard_map/ppermute | solution.py:202
  4.9 37.1 %collective-permute-start = (bf16[192,1280]{1,0:T(8,128)(2,1)}, bf16[192,1280]{1,0:T(8,128)(2,1)}, u32[]{:S(2)}, u32[]{:S(2)}) collective-permute-start(bf16[192,1280]{1,0:T(8,128)(2,1)} %k_ref.1), channel_id=1, source_target_pairs={{0,2},{1,3},{2,0},{3,1},{4,6},{5,7},{6,4},{7,5},{8,10},{9,11},{10,... | collective-permute-start | bytes 1474568 | tf_op jit(solution)/shard_map/ppermute | solution.py:201
  6.4 36.2 %collective-permute-start.5 = (bf16[192,1280]{1,0:T(8,128)(2,1)}, bf16[192,1280]{1,0:T(8,128)(2,1)}, u32[]{:S(2)}, u32[]{:S(2)}) collective-permute-start(bf16[192,1280]{1,0:T(8,128)(2,1)} %v_ref.1), channel_id=1, source_target_pairs={{0,1},{1,0},{2,3},{3,2},{4,5},{5,4},{6,7},{7,6},{8,9},{9,8},{10,11... | collective-permute-start | bytes 1474568 | tf_op jit(solution)/shard_map/ppermute | solution.py:202
  6.6 35.9 %collective-permute-start.2 = (bf16[192,1280]{1,0:T(8,128)(2,1)}, bf16[192,1280]{1,0:T(8,128)(2,1)}, u32[]{:S(2)}, u32[]{:S(2)}) collective-permute-start(bf16[192,1280]{1,0:T(8,128)(2,1)} %v_ref.1), channel_id=1, source_target_pairs={{0,2},{1,3},{2,0},{3,1},{4,6},{5,7},{6,4},{7,5},{8,10},{9,11},{10,... | collective-permute-start | bytes 1474568 | tf_op jit(solution)/shard_map/ppermute | solution.py:201
  9.2 5.5 %collective-permute-start.7 = (bf16[32,2560]{1,0:T(8,128)(2,1)S(1)}, bf16[32,2560]{1,0:T(8,128)(2,1)S(1)}, u32[]{:S(2)}, u32[]{:S(2)}) collective-permute-start(bf16[32,2560]{1,0:T(8,128)(2,1)S(1)} %broadcast_select_fusion), channel_id=1, source_target_pairs={{0,8},{4,12},{8,0},{12,4},{16,24},{20,28},{24,16},{28,20},{1,9},{5... | collective-permute-start | bytes 491528 | tf_op jit(solution)/shard_map/ppermute | solution.py:27
  14.7 3.4 %copy-start.4 = (bf16[32,2560]{1,0:T(8,128)(2,1)}, bf16[32,2560]{1,0:T(8,128)(2,1)S(1)}, u32[]{:S(2)}) copy-start(bf16[32,2560]{1,0:T(8,128)(2,1)S(1)} %broadcast_select_fusion.1) | copy-start | bytes 491524
  14.7 9.8 %collective-permute-start.8 = (bf16[32,2560]{1,0:T(8,128)(2,1)S(1)}, bf16[32,2560]{1,0:T(8,128)(2,1)}, u32[]{:S(2)}, u32[]{:S(2)}) collective-permute-start(bf16[32,2560]{1,0:T(8,128)(2,1)S(1)} %broadcast_select_fusion.1), channel_id=1, source_target_pairs={{0,16},{4,20},{8,24},{12,28},{16,0},{20,4},{24,8},{28,12},{1,17},{... | collective-permute-start | bytes 491528 | tf_op jit(solution)/shard_map/ppermute | solution.py:27
  25.4 7.5 %collective-permute-start.9 = (bf16[32,2560]{1,0:T(8,128)(2,1)S(1)}, bf16[32,2560]{1,0:T(8,128)(2,1)}, u32[]{:S(2)}, u32[]{:S(2)}) collective-permute-start(bf16[32,2560]{1,0:T(8,128)(2,1)S(1)} %broadcast_select_fusion.2), channel_id=1, source_target_pairs={{0,2},{1,3},{2,0},{3,1},{4,6},{5,7},{6,4},{7,5},{8,10},{9,11},{10,... | collective-permute-start | bytes 491528 | tf_op jit(solution)/shard_map/ppermute | solution.py:37
  27.0 7.3 %copy-start.1 = (bf16[192,1280]{1,0:T(8,128)(2,1)S(1)}, bf16[192,1280]{1,0:T(8,128)(2,1)}, u32[]{:S(2)}) copy-start(bf16[192,1280]{1,0:T(8,128)(2,1)} %q_ref.7) | copy-start | bytes 1474564
  27.0 7.3 %copy-start.2 = (bf16[192,1280]{1,0:T(8,128)(2,1)S(1)}, bf16[192,1280]{1,0:T(8,128)(2,1)}, u32[]{:S(2)}) copy-start(bf16[192,1280]{1,0:T(8,128)(2,1)} %k_ref.1) | copy-start | bytes 1474564
  27.0 7.3 %copy-start.3 = (bf16[192,1280]{1,0:T(8,128)(2,1)S(1)}, bf16[192,1280]{1,0:T(8,128)(2,1)}, u32[]{:S(2)}) copy-start(bf16[192,1280]{1,0:T(8,128)(2,1)} %v_ref.1) | copy-start | bytes 1474564
  33.8 26.4 %collective-permute-start.10 = (bf16[64,2560]{1,0:T(8,128)(2,1)S(1)}, bf16[64,2560]{1,0:T(8,128)(2,1)S(1)}, u32[]{:S(2)}, u32[]{:S(2)}) collective-permute-start(bf16[64,2560]{1,0:T(8,128)(2,1)S(1)} %pad_maximum_fusion.1), channel_id=1, source_target_pairs={{0,1},{1,0},{2,3},{3,2},{4,5},{5,4},{6,7},{7,6},{8,9},{9,8},{10,11... | collective-permute-start | bytes 983048 | tf_op jit(solution)/shard_map/ppermute | solution.py:39
  42.0 19.3 %collective-permute-start.1 = (bf16[192,1280]{1,0:T(8,128)(2,1)}, bf16[192,1280]{1,0:T(8,128)(2,1)S(1)}, u32[]{:S(2)}, u32[]{:S(2)}) collective-permute-start(bf16[192,1280]{1,0:T(8,128)(2,1)} %collective-permute-done.k_ref), channel_id=1, source_target_pairs={{0,1},{1,0},{2,3},{3,2},{4,5},{5,4},{6,7},{7,6},{8,9},{9,8},{10,11... | collective-permute-start | bytes 1474568 | tf_op jit(solution)/shard_map/ppermute | solution.py:203
  42.5 18.7 %collective-permute-start.3 = (bf16[192,1280]{1,0:T(8,128)(2,1)}, bf16[192,1280]{1,0:T(8,128)(2,1)S(1)}, u32[]{:S(2)}, u32[]{:S(2)}) collective-permute-start(bf16[192,1280]{1,0:T(8,128)(2,1)} %collective-permute-done.2.v_ref), channel_id=1, source_target_pairs={{0,1},{1,0},{2,3},{3,2},{4,5},{5,4},{6,7},{7,6},{8,9},{9,8},{10,11... | collective-permute-start | bytes 1474568 | tf_op jit(solution)/shard_map/ppermute | solution.py:203

commit v4 on v2

v4 whole, which is shorter than its diff:
```python
import functools

import jax
import jax.numpy as jnp
from jax import lax
from jax.experimental import pallas as pl
from jax.experimental.pallas import tpu as pltpu
from jax.sharding import PartitionSpec as P

HEADS = 20
HEAD_DIM = 64
VIEWS = 6
ADJ = 3
SCALE = 0.125
LANES = 128


def tree_broadcast(value, axis, source):
    count = lax.axis_size(axis)
    index = lax.axis_index(axis)
    if count & (count - 1):
        kept = jnp.where(index == source, value, jnp.zeros_like(value))
        return lax.psum(kept, axis)
    distance = 1
    while distance < count:
        pairs = [(i, i ^ distance) for i in range(count)]
        received = lax.ppermute(value, axis, pairs)
        partner_has = ((index ^ distance) // distance) == (source // distance)
        value = jnp.where(partner_has, received, value)
        distance *= 2
    return value


def gather_rows(value, axis):
    count = lax.axis_size(axis)
    if count == 4:
        across = lax.ppermute(value, axis, [(i, i ^ 2) for i in range(count)])
        both = jnp.concatenate([value, across], axis=0)
        near = lax.ppermute(both, axis, [(i, i ^ 1) for i in range(count)])
        return jnp.concatenate([both, near], axis=0)
    return lax.all_gather(value, axis, axis=0, tiled=True)


def attention_kernel(piece_count, pairs, q_ref, *refs):
    key_refs = refs[:piece_count]
    value_refs = refs[piece_count : 2 * piece_count]
    bias_refs = refs[2 * piece_count : 3 * piece_count]
    rk_ref, rv_ref, out_ref = refs[3 * piece_count :]
    lane = lax.broadcasted_iota(jnp.int32, (1, LANES), 1)
    dims = (((1,), (1,)), ((), ()))
    for pair in range(pairs):
        cols = slice(pair * LANES, (pair + 1) * LANES)
        queries = q_ref[:, cols]
        results = []
        for head in range(LANES // HEAD_DIM):
            own = (lane // HEAD_DIM) == head
            q_head = jnp.where(own, queries, jnp.zeros_like(queries))
            scores = [
                lax.dot_general(q_head, key_refs[p][:, cols], dims, preferred_element_type=jnp.float32)
                * SCALE
                + bias_refs[p][...]
                for p in range(piece_count)
            ]
            peak = jnp.max(scores[0], axis=1, keepdims=True)
            for p in range(1, piece_count):
                peak = jnp.maximum(peak, jnp.max(scores[p], axis=1, keepdims=True))
            total = None
            summed = None
            for p in range(piece_count):
                weights = jnp.exp(scores[p] - peak)
                part_total = jnp.sum(weights, axis=1, keepdims=True)
                part = jnp.dot(
                    weights.astype(jnp.bfloat16), value_refs[p][:, cols], preferred_element_type=jnp.float32
                )
                total = part_total if total is None else total + part_total
                summed = part if summed is None else summed + part
            view_part = summed / total
            ref_scores = (
                lax.dot_general(q_head, rk_ref[:, cols], dims, preferred_element_type=jnp.float32) * SCALE
            )
            ref_peak = jnp.max(ref_scores, axis=1, keepdims=True)
            ref_weights = jnp.exp(ref_scores - ref_peak)
            ref_total = jnp.sum(ref_weights, axis=1, keepdims=True)
            ref_summed = jnp.dot(
                ref_weights.astype(jnp.bfloat16), rv_ref[:, cols], preferred_element_type=jnp.float32
            )
            results.append((own, view_part + ref_summed / ref_total))
        mixed = results[-1][1]
        for own, value in results[:-1]:
            mixed = jnp.where(own, value, mixed)
        out_ref[:, cols] = mixed.astype(out_ref.dtype)


def attention(queries, key_pieces, value_pieces, biases, ref_keys, ref_values, steps):
    rows, width = queries.shape
    span = width // steps
    column = lambda j: (0, j)
    fixed = lambda j: (0, 0)
    in_specs = [pl.BlockSpec((rows, span), column)]
    in_specs += [pl.BlockSpec((piece.shape[0], span), column) for piece in key_pieces]
    in_specs += [pl.BlockSpec((piece.shape[0], span), column) for piece in value_pieces]
    in_specs += [pl.BlockSpec(bias.shape, fixed) for bias in biases]
    in_specs += [pl.BlockSpec((ref_keys.shape[0], span), column)] * 2
    keys = sum(piece.shape[0] for piece in key_pieces) + ref_keys.shape[0]
    return pl.pallas_call(
        functools.partial(attention_kernel, len(key_pieces), span // LANES),
        grid=(steps,),
        in_specs=in_specs,
        out_specs=pl.BlockSpec((rows, span), column),
        out_shape=jax.ShapeDtypeStruct((rows, width), jnp.bfloat16),
        compiler_params=pltpu.CompilerParams(
            dimension_semantics=("arbitrary",), vmem_limit_bytes=48 * 1024 * 1024
        ),
        cost_estimate=pl.CostEstimate(
            flops=8 * rows * keys * width,
            transcendentals=2 * rows * keys * HEADS,
            bytes_accessed=2 * (2 * rows + 2 * keys) * width + 4 * rows * keys,
        ),
    )(queries, *key_pieces, *value_pieces, *biases, ref_keys, ref_values)


def key_bias(query_views, query_adjacent, position, rows, shard_rows, view_tok):
    key_rows = position * shard_rows + jnp.arange(rows, dtype=jnp.int32)
    key_views = key_rows // view_tok
    keep = query_views[:, None] == key_views[None, :]
    for slot in range(ADJ):
        keep = keep | (query_adjacent[:, slot : slot + 1] == key_views[None, :].astype(jnp.float32))
    return jnp.where(keep, 0.0, -jnp.inf).astype(jnp.float32)


def body(queries, keys, values, ref_keys, ref_values, out_weight, adjacency, ref_source):
    shard_rows, width = queries.shape
    view_count = lax.axis_size("view")
    view_index = lax.axis_index("view")
    view_tok = shard_rows * view_count // VIEWS

    if view_count == 4:
        across = lax.ppermute((keys, values), "view", [(i, i ^ 2) for i in range(view_count)])
        near = lax.ppermute((keys, values), "view", [(i, i ^ 1) for i in range(view_count)])
        far = lax.ppermute(across, "view", [(i, i ^ 1) for i in range(view_count)])
        pieces = [(keys, values), near, across, far]
        positions = [view_index, view_index ^ 1, view_index ^ 2, view_index ^ 3]
    else:
        pieces = [lax.all_gather((keys, values), "view", axis=0, tiled=True)]
        positions = [jnp.zeros((), jnp.int32)]

    ref_both = jnp.concatenate([ref_keys, ref_values], axis=1)
    ref_all = gather_rows(tree_broadcast(ref_both, "mesh", ref_source[0]), "view")

    view_ids = jnp.arange(VIEWS, dtype=jnp.int32)
    query_views = (view_index * shard_rows + jnp.arange(shard_rows, dtype=jnp.int32)) // view_tok
    query_onehot = (query_views[:, None] == view_ids[None, :]).astype(jnp.float32)
    query_adjacent = jnp.dot(query_onehot, adjacency.astype(jnp.float32))
    biases = [
        key_bias(query_views, query_adjacent, position, piece[0].shape[0], shard_rows, view_tok)
        for piece, position in zip(pieces, positions)
    ]

    mixed = attention(
        queries,
        [piece[0] for piece in pieces],
        [piece[1] for piece in pieces],
        biases,
        ref_all[:, :width],
        ref_all[:, width:],
        2,
    )
    return jnp.dot(mixed, out_weight, preferred_element_type=jnp.float32).astype(jnp.bfloat16)


def solution(mesh):
    return jax.shard_map(
        body,
        mesh=mesh,
        in_specs=(
            P(("mesh", "view"), None),
            P(("mesh", "view"), None),
            P(("mesh", "view"), None),
            P(("mesh", "view"), None),
            P(("mesh", "view"), None),
            P(),
            P("mesh", None),
            P(),
        ),
        out_specs=P(("mesh", "view"), None),
        check_vma=False,
    )
```

time: 58.6 us -> 50.8 us (0.87)
  Pallas kernels: 14.4 us -> 10.9 us
  local copies, waits for them, and re-layouts: 5.81 us -> 2.78 us
  waiting for transfers between devices: 21 us -> 19 us
  starting transfers between devices: 11.4 us -> 12.2 us
  other arithmetic: 3.16 us -> 2.4 us
  matrix products: 1.8 us -> 2.48 us
    ppermute x4 -> x8, waiting for transfers between devices: 17.2 us -> 8.86 us  [the longest x1 7.57 us: gather_rows(): across = lax.ppermute(value, axis, [(i, i ^ 2) for i in range(count)])]
    ppermute x3, waiting for transfers between devices: 3.8 us -> 10.2 us  [tree_broadcast(): received = lax.ppermute(value, axis, pairs)]
    pallas_call x1, Pallas kernels: 14.4 us -> 10.9 us  [attention(): pl.pallas_call(functools.partial(attention_kernel, len(key_pieces), span...]
    concatenate x1 -> x0, local copies, waits for them, and re-layouts: 1.88 us -> none  [body(): both = jnp.concatenate([keys, values], axis=1)]
    ppermute x4 -> x8, starting transfers between devices: 3.25 us -> 4.49 us  [the longest x2 2.03 us: body(): lax.ppermute((keys, values), 'view', [(i, i ^ 2) for i in range(view_coun...]
    unnamed x10 -> x11, local copies, waits for them, and re-layouts: 2.95 us -> 1.84 us
    select_n x3, other arithmetic: 0.99 us -> 0.06 us  [tree_broadcast(): value = jnp.where(partner_has, received, value)]
    dot_general x1, matrix products: 0.21 us -> 0.89 us  [body(): query_adjacent = jnp.dot(query_onehot, adjacency.astype(jnp.float32))]
  transfers between devices with their start and end apart: 7 -> 11, of which waited for: 4 -> 7; matrix products, arithmetic and copies ran while one was open for 12% -> 7% of each run, Pallas kernels for 0% -> 0%
where the time goes in v4:
time: 50.8 us; the launch traced here: 50.6 us
  waiting for transfers between devices  19 us (37%)
  starting transfers between devices  12.2 us (24%)
  Pallas kernels  10.9 us (21%)
  local copies, waits for them, and re-layouts  2.78 us (5%)
  matrix products  2.48 us (5%)
  other arithmetic  2.4 us (5%)
  between operations  0.87 us (2%)
    pallas_call x1, Pallas kernels, attention(): pl.pallas_call(functools.partial(attention_kernel, len(key_pieces), span...  10.9 us
    ppermute x3, waiting for transfers between devices, tree_broadcast(): received = lax.ppermute(value, axis, pairs)  10.2 us
    ppermute x3, starting transfers between devices, tree_broadcast(): received = lax.ppermute(value, axis, pairs)  7.67 us
    ppermute x1, waiting for transfers between devices, gather_rows(): across = lax.ppermute(value, axis, [(i, i ^ 2) for i in range(count)])  7.57 us
    ppermute x2, starting transfers between devices, body(): lax.ppermute((keys, values), 'view', [(i, i ^ 2) for i in range(view_coun...  2.03 us
    unnamed x11, local copies, waits for them, and re-layouts  1.84 us
    dot_general x1, matrix products, body(): jnp.dot(mixed, out_weight, preferred_element_type=jnp.float32)  1.59 us
    ppermute x1, starting transfers between devices, gather_rows(): across = lax.ppermute(value, axis, [(i, i ^ 2) for i in range(count)])  1.52 us
  transfers between devices with their start and end apart: 11, of which 7 were waited for; matrix products, arithmetic and copies ran while one was open for 7% of the time, Pallas kernels for 0%

profile of v4, /device:TPU:0, one launch (start us, length us, event | category | flops | bytes accessed | tf_op | source)
XLA Modules:
  0.0 50.6 jit_solution(7151723856929614838)
XLA Ops:
  0.0 1.0 %constant_dynamic-update-slice_fusion.1 = bf16[32,2560]{1,0:T(8,128)(2,1)S(1)} fusion(bf16[32,1280]{1,0:T(8,128)(2,1)} %param.11), kind=kLoop, calls=%fused_computation.14 | loop fusion | bytes 163840
  1.0 0.9 %constant_dynamic-update-slice_fusion = bf16[32,2560]{1,0:T(8,128)(2,1)S(1)} fusion(bf16[32,2560]{1,0:T(8,128)(2,1)S(1)} %constant_dynamic-update-slice_fusion.1, bf16[32,1280]{1,0:T(8,128)(2,1)} %param.12), kind=kLoop, calls=%fused_computation.13 | loop fusion | bytes 163840 | tf_op jit(solution)/shard_map/concatenate | solution.py:147
  1.9 2.9 %collective-permute-start.6 = (bf16[32,2560]{1,0:T(8,128)(2,1)S(1)}, bf16[32,2560]{1,0:T(8,128)(2,1)}, u32[]{:S(2)}, u32[]{:S(2)}) collective-permute-start(bf16[32,2560]{1,0:T(8,128)(2,1)S(1)} %constant_dynamic-update-slice_fusion), channel_id=1, source_target_pairs={{0,4},{4,0},{8,12},{12,8},{16,20},{20,16},{24,28},{28,24},{1,5},{5... | collective-permute-start | bytes 491528 | tf_op jit(solution)/shard_map/ppermute | solution.py:27
  4.9 1.5 %collective-permute-start.1 = (bf16[192,1280]{1,0:T(8,128)(2,1)}, bf16[192,1280]{1,0:T(8,128)(2,1)}, u32[]{:S(2)}, u32[]{:S(2)}) collective-permute-start(bf16[192,1280]{1,0:T(8,128)(2,1)} %refs_0_.1), channel_id=1, source_target_pairs={{0,2},{1,3},{2,0},{3,1},{4,6},{5,7},{6,4},{7,5},{8,10},{9,11},{10,... | collective-permute-start | bytes 1474568 | tf_op jit(solution)/shard_map/ppermute | solution.py:138
  6.4 0.2 collective-permute-start.3
  6.6 0.5 collective-permute-start.4
  7.9 1.3 %collective-permute-done.6 = bf16[32,2560]{1,0:T(8,128)(2,1)} collective-permute-done((bf16[32,2560]{1,0:T(8,128)(2,1)S(1)}, bf16[32,2560]{1,0:T(8,128)(2,1)}, u32[]{:S(2)}, u32[]{:S(2)}) %collective-permute-start.6) | collective-permute-done | bytes 163872 | tf_op jit(solution)/shard_map/ppermute | solution.py:27
  9.2 1.9 %collective-permute-start.7 = (bf16[32,2560]{1,0:T(8,128)(2,1)S(1)}, bf16[32,2560]{1,0:T(8,128)(2,1)S(1)}, u32[]{:S(2)}, u32[]{:S(2)}) collective-permute-start(bf16[32,2560]{1,0:T(8,128)(2,1)S(1)} %broadcast_select_fusion), channel_id=1, source_target_pairs={{0,8},{4,12},{8,0},{12,4},{16,24},{20,28},{24,16},{28,20},{1,9},{5... | collective-permute-start | bytes 491528 | tf_op jit(solution)/shard_map/ppermute | solution.py:27
  11.1 0.9 %fusion = f32[192,3]{0,1:T(4,128)S(1)} fusion(s32[192]{0:T(256)S(1)} %get-tuple-element.14, s32[6,3]{0,1:T(4,128)} %param.14), kind=kOutput, calls=%fused_computation.11 | convolution fusion | flops 8082 | bytes 3144 | tf_op jit(solution)/shard_map/dot_general | solution.py:153
  12.0 2.7 %collective-permute-done.7 = bf16[32,2560]{1,0:T(8,128)(2,1)S(1)} collective-permute-done((bf16[32,2560]{1,0:T(8,128)(2,1)S(1)}, bf16[32,2560]{1,0:T(8,128)(2,1)S(1)}, u32[]{:S(2)}, u32[]{:S(2)}) %collective-permute-start.7) | collective-permute-done | bytes 163872 | tf_op jit(solution)/shard_map/ppermute | solution.py:27
  14.7 2.8 %collective-permute-start.8 = (bf16[32,2560]{1,0:T(8,128)(2,1)S(1)}, bf16[32,2560]{1,0:T(8,128)(2,1)S(1)}, u32[]{:S(2)}, u32[]{:S(2)}) collective-permute-start(bf16[32,2560]{1,0:T(8,128)(2,1)S(1)} %broadcast_select_fusion.1), channel_id=1, source_target_pairs={{0,16},{4,20},{8,24},{12,28},{16,0},{20,4},{24,8},{28,12},{1,17},{... | collective-permute-start | bytes 491528 | tf_op jit(solution)/shard_map/ppermute | solution.py:27
  17.5 6.2 %collective-permute-done.8 = bf16[32,2560]{1,0:T(8,128)(2,1)S(1)} collective-permute-done((bf16[32,2560]{1,0:T(8,128)(2,1)S(1)}, bf16[32,2560]{1,0:T(8,128)(2,1)S(1)}, u32[]{:S(2)}, u32[]{:S(2)}) %collective-permute-start.8) | collective-permute-done | bytes 163872 | tf_op jit(solution)/shard_map/ppermute | solution.py:27
  23.7 1.5 %collective-permute-start.9 = (bf16[32,2560]{1,0:T(8,128)(2,1)S(1)}, bf16[32,2560]{1,0:T(8,128)(2,1)}, u32[]{:S(2)}, u32[]{:S(2)}) collective-permute-start(bf16[32,2560]{1,0:T(8,128)(2,1)S(1)} %broadcast_select_fusion.2), channel_id=1, source_target_pairs={{0,2},{1,3},{2,0},{3,1},{4,6},{5,7},{6,4},{7,5},{8,10},{9,11},{10,... | collective-permute-start | bytes 491528 | tf_op jit(solution)/shard_map/ppermute | solution.py:37
  25.3 7.6 %collective-permute-done.9 = bf16[32,2560]{1,0:T(8,128)(2,1)} collective-permute-done((bf16[32,2560]{1,0:T(8,128)(2,1)S(1)}, bf16[32,2560]{1,0:T(8,128)(2,1)}, u32[]{:S(2)}, u32[]{:S(2)}) %collective-permute-start.9) | collective-permute-done | bytes 163872 | tf_op jit(solution)/shard_map/ppermute | solution.py:37
  32.9 0.9 %pad_maximum_fusion.1 = bf16[64,2560]{1,0:T(8,128)(2,1)S(1)} fusion(bf16[32,2560]{1,0:T(8,128)(2,1)} %collective-permute-done.9, bf16[32,2560]{1,0:T(8,128)(2,1)S(1)} %broadcast_select_fusion.2), kind=kLoop, calls=%fused_computation.2 | loop fusion | flops 655360 | bytes 655360 | tf_op jit(solution)/shard_map/concatenate | solution.py:38
  33.9 0.4 or_select_fusion
  34.4 0.6 %collective-permute-start.2 = (bf16[192,1280]{1,0:T(8,128)(2,1)}, bf16[192,1280]{1,0:T(8,128)(2,1)S(1)}, u32[]{:S(2)}, u32[]{:S(2)}) collective-permute-start(bf16[192,1280]{1,0:T(8,128)(2,1)} %collective-permute-done.1.refs_2_), channel_id=1, source_target_pairs={{0,1},{1,0},{2,3},{3,2},{4,5},{5,4},{6,7},{7,6},{8,9},{9,8},{10,11... | collective-permute-start | bytes 1474568 | tf_op jit(solution)/shard_map/ppermute | solution.py:140
  34.9 0.1 collective-permute-start.5
  35.0 0.5 collective-permute-done.10
  35.5 1.0 %pad_maximum_fusion = bf16[128,2560]{1,0:T(8,128)(2,1)S(1)} fusion(bf16[64,2560]{1,0:T(8,128)(2,1)S(1)} %collective-permute-done.10, bf16[32,2560]{1,0:T(8,128)(2,1)} %collective-permute-done.9, bf16[32,2560]{1,0:T(8,128)(2,1)S(1)} %broadcast_select_fusion.2), kind=kLoop, calls=%fused_computation.1 | loop fusion | flops 1966080 | bytes 1310720 | tf_op jit(solution)/shard_map/concatenate | solution.py:40
  36.6 0.7 %collective-permute-done.5.refs_7_ = bf16[192,1280]{1,0:T(8,128)(2,1)S(1)} collective-permute-done((bf16[192,1280]{1,0:T(8,128)(2,1)}, bf16[192,1280]{1,0:T(8,128)(2,1)S(1)}, u32[]{:S(2)}, u32[]{:S(2)}) %collective-permute-start.5) | collective-permute-done | bytes 491552 | tf_op jit(solution)/shard_map/ppermute | solution.py:140
  37.3 0.8 %copy-done.4 = bf16[192,1280]{1,0:T(8,128)(2,1)} copy-done((bf16[192,1280]{1,0:T(8,128)(2,1)}, bf16[192,1280]{1,0:T(8,128)(2,1)S(1)}, u32[]{:S(2)}) %copy-start.4) | copy-done | bytes 491544
  38.1 10.9 %shard_map.82 = bf16[192,1280]{1,0:T(8,128)(2,1)S(1)} custom-call(bf16[192,1280]{1,0:T(8,128)(2,1)S(1)} %copy-done.1, bf16[192,1280]{1,0:T(8,128)(2,1)S(1)} %copy-done.2, bf16[192,1280]{1,0:T(8,128)(2,1)} %collective-permute-done.refs_1_, bf16[192,1280]{1,0:T(8,128)(2,1)} %collective-permute-done.1.refs_2_, ...), custom_call_target="tpu_custom_call" | custom-call | flops 1761607680 | bytes 6258688 | tf_op jit(solution)/shard_map/pallas_call | solution.py:105
  49.0 1.6 %convolution_convert_fusion = bf16[192,1280]{1,0:T(8,128)(2,1)} fusion(bf16[192,1280]{1,0:T(8,128)(2,1)S(1)} %shard_map.82, bf16[1280,1280]{1,0:T(8,128)(2,1)S(1)} %copy-done), kind=kOutput, calls=%fused_computation | convolution fusion | flops 629391360 | bytes 4259840 | tf_op jit(solution)/shard_map/dot_general | solution.py:168
  (25 shorter events, 0.3 us)
Async XLA Ops:
  0.0 49.0 %copy-start = (bf16[1280,1280]{1,0:T(8,128)(2,1)S(1)}, bf16[1280,1280]{1,0:T(8,128)(2,1)}, u32[]{:S(2)}) copy-start(bf16[1280,1280]{1,0:T(8,128)(2,1)} %param.13) | copy-start | bytes 9830404
  1.9 7.2 %collective-permute-start.6 = (bf16[32,2560]{1,0:T(8,128)(2,1)S(1)}, bf16[32,2560]{1,0:T(8,128)(2,1)}, u32[]{:S(2)}, u32[]{:S(2)}) collective-permute-start(bf16[32,2560]{1,0:T(8,128)(2,1)S(1)} %constant_dynamic-update-slice_fusion), channel_id=1, source_target_pairs={{0,4},{4,0},{8,12},{12,8},{16,20},{20,16},{24,28},{28,24},{1,5},{5... | collective-permute-start | bytes 491528 | tf_op jit(solution)/shard_map/ppermute | solution.py:27
  4.9 31.7 %collective-permute-start = (bf16[192,1280]{1,0:T(8,128)(2,1)}, bf16[192,1280]{1,0:T(8,128)(2,1)}, u32[]{:S(2)}, u32[]{:S(2)}) collective-permute-start(bf16[192,1280]{1,0:T(8,128)(2,1)} %refs_0_.1), channel_id=1, source_target_pairs={{0,1},{1,0},{2,3},{3,2},{4,5},{5,4},{6,7},{7,6},{8,9},{9,8},{10,11... | collective-permute-start | bytes 1474568 | tf_op jit(solution)/shard_map/ppermute | solution.py:139
  4.9 29.5 %collective-permute-start.1 = (bf16[192,1280]{1,0:T(8,128)(2,1)}, bf16[192,1280]{1,0:T(8,128)(2,1)}, u32[]{:S(2)}, u32[]{:S(2)}) collective-permute-start(bf16[192,1280]{1,0:T(8,128)(2,1)} %refs_0_.1), channel_id=1, source_target_pairs={{0,2},{1,3},{2,0},{3,1},{4,6},{5,7},{6,4},{7,5},{8,10},{9,11},{10,... | collective-permute-start | bytes 1474568 | tf_op jit(solution)/shard_map/ppermute | solution.py:138
  6.4 30.1 %collective-permute-start.3 = (bf16[192,1280]{1,0:T(8,128)(2,1)}, bf16[192,1280]{1,0:T(8,128)(2,1)}, u32[]{:S(2)}, u32[]{:S(2)}) collective-permute-start(bf16[192,1280]{1,0:T(8,128)(2,1)} %refs_4_.1), channel_id=1, source_target_pairs={{0,1},{1,0},{2,3},{3,2},{4,5},{5,4},{6,7},{7,6},{8,9},{9,8},{10,11... | collective-permute-start | bytes 1474568 | tf_op jit(solution)/shard_map/ppermute | solution.py:139
  6.6 28.3 %collective-permute-start.4 = (bf16[192,1280]{1,0:T(8,128)(2,1)}, bf16[192,1280]{1,0:T(8,128)(2,1)}, u32[]{:S(2)}, u32[]{:S(2)}) collective-permute-start(bf16[192,1280]{1,0:T(8,128)(2,1)} %refs_4_.1), channel_id=1, source_target_pairs={{0,2},{1,3},{2,0},{3,1},{4,6},{5,7},{6,4},{7,5},{8,10},{9,11},{10,... | collective-permute-start | bytes 1474568 | tf_op jit(solution)/shard_map/ppermute | solution.py:138
  9.2 5.5 %collective-permute-start.7 = (bf16[32,2560]{1,0:T(8,128)(2,1)S(1)}, bf16[32,2560]{1,0:T(8,128)(2,1)S(1)}, u32[]{:S(2)}, u32[]{:S(2)}) collective-permute-start(bf16[32,2560]{1,0:T(8,128)(2,1)S(1)} %broadcast_select_fusion), channel_id=1, source_target_pairs={{0,8},{4,12},{8,0},{12,4},{16,24},{20,28},{24,16},{28,20},{1,9},{5... | collective-permute-start | bytes 491528 | tf_op jit(solution)/shard_map/ppermute | solution.py:27
  14.7 9.0 %collective-permute-start.8 = (bf16[32,2560]{1,0:T(8,128)(2,1)S(1)}, bf16[32,2560]{1,0:T(8,128)(2,1)S(1)}, u32[]{:S(2)}, u32[]{:S(2)}) collective-permute-start(bf16[32,2560]{1,0:T(8,128)(2,1)S(1)} %broadcast_select_fusion.1), channel_id=1, source_target_pairs={{0,16},{4,20},{8,24},{12,28},{16,0},{20,4},{24,8},{28,12},{1,17},{... | collective-permute-start | bytes 491528 | tf_op jit(solution)/shard_map/ppermute | solution.py:27
  23.7 9.1 %collective-permute-start.9 = (bf16[32,2560]{1,0:T(8,128)(2,1)S(1)}, bf16[32,2560]{1,0:T(8,128)(2,1)}, u32[]{:S(2)}, u32[]{:S(2)}) collective-permute-start(bf16[32,2560]{1,0:T(8,128)(2,1)S(1)} %broadcast_select_fusion.2), channel_id=1, source_target_pairs={{0,2},{1,3},{2,0},{3,1},{4,6},{5,7},{6,4},{7,5},{8,10},{9,11},{10,... | collective-permute-start | bytes 491528 | tf_op jit(solution)/shard_map/ppermute | solution.py:37
  33.8 1.7 %collective-permute-start.10 = (bf16[64,2560]{1,0:T(8,128)(2,1)S(1)}, bf16[64,2560]{1,0:T(8,128)(2,1)S(1)}, u32[]{:S(2)}, u32[]{:S(2)}) collective-permute-start(bf16[64,2560]{1,0:T(8,128)(2,1)S(1)} %pad_maximum_fusion.1), channel_id=1, source_target_pairs={{0,1},{1,0},{2,3},{3,2},{4,5},{5,4},{6,7},{7,6},{8,9},{9,8},{10,11... | collective-permute-start | bytes 983048 | tf_op jit(solution)/shard_map/ppermute | solution.py:39
  34.3 3.8 %copy-start.1 = (bf16[192,1280]{1,0:T(8,128)(2,1)S(1)}, bf16[192,1280]{1,0:T(8,128)(2,1)}, u32[]{:S(2)}) copy-start(bf16[192,1280]{1,0:T(8,128)(2,1)} %q_ref.1) | copy-start | bytes 1474564
  34.3 3.8 %copy-start.2 = (bf16[192,1280]{1,0:T(8,128)(2,1)S(1)}, bf16[192,1280]{1,0:T(8,128)(2,1)}, u32[]{:S(2)}) copy-start(bf16[192,1280]{1,0:T(8,128)(2,1)} %refs_0_.1) | copy-start | bytes 1474564
  34.3 3.8 %copy-start.3 = (bf16[192,1280]{1,0:T(8,128)(2,1)S(1)}, bf16[192,1280]{1,0:T(8,128)(2,1)}, u32[]{:S(2)}) copy-start(bf16[192,1280]{1,0:T(8,128)(2,1)} %refs_4_.1) | copy-start | bytes 1474564
  34.4 2.3 %collective-permute-start.2 = (bf16[192,1280]{1,0:T(8,128)(2,1)}, bf16[192,1280]{1,0:T(8,128)(2,1)S(1)}, u32[]{:S(2)}, u32[]{:S(2)}) collective-permute-start(bf16[192,1280]{1,0:T(8,128)(2,1)} %collective-permute-done.1.refs_2_), channel_id=1, source_target_pairs={{0,1},{1,0},{2,3},{3,2},{4,5},{5,4},{6,7},{7,6},{8,9},{9,8},{10,11... | collective-permute-start | bytes 1474568 | tf_op jit(solution)/shard_map/ppermute | solution.py:140
  34.9 2.4 %collective-permute-start.5 = (bf16[192,1280]{1,0:T(8,128)(2,1)}, bf16[192,1280]{1,0:T(8,128)(2,1)S(1)}, u32[]{:S(2)}, u32[]{:S(2)}) collective-permute-start(bf16[192,1280]{1,0:T(8,128)(2,1)} %collective-permute-done.4.refs_6_), channel_id=1, source_target_pairs={{0,1},{1,0},{2,3},{3,2},{4,5},{5,4},{6,7},{7,6},{8,9},{9,8},{10,11... | collective-permute-start | bytes 1474568 | tf_op jit(solution)/shard_map/ppermute | solution.py:140
  37.3 0.8 %copy-start.4 = (bf16[192,1280]{1,0:T(8,128)(2,1)}, bf16[192,1280]{1,0:T(8,128)(2,1)S(1)}, u32[]{:S(2)}) copy-start(bf16[192,1280]{1,0:T(8,128)(2,1)S(1)} %collective-permute-done.5.refs_7_) | copy-start | bytes 1474564

commit v5 on v4

--- a/solution.py
+++ b/solution.py
@@ -18,13 +18,17 @@
 def tree_broadcast(value, axis, source):
     count = lax.axis_size(axis)
     index = lax.axis_index(axis)
-    if count & (count - 1):
+    if count & (count - 1) or count < 4:
         kept = jnp.where(index == source, value, jnp.zeros_like(value))
         return lax.psum(kept, axis)
-    distance = 1
+    gathered = value
+    for distance in (1, 2, 3):
+        received = lax.ppermute(value, axis, [(i, i ^ distance) for i in range(count)])
+        gathered = jnp.where((index ^ distance) == source, received, gathered)
+    value = gathered
+    distance = 4
     while distance < count:
-        pairs = [(i, i ^ distance) for i in range(count)]
-        received = lax.ppermute(value, axis, pairs)
+        received = lax.ppermute(value, axis, [(i, i ^ distance) for i in range(count)])
         partner_has = ((index ^ distance) // distance) == (source // distance)
         value = jnp.where(partner_has, received, value)
         distance *= 2

time: 50.8 us -> 52.6 us (1.035)
  starting transfers between devices: 12.2 us -> 14.3 us
    ppermute x2, starting transfers between devices: 2.03 us -> 3.46 us  [body(): lax.ppermute((keys, values), 'view', [(i, i ^ 2) for i in range(view_coun...]
    ppermute x3 -> x4, waiting for transfers between devices: 10.2 us -> 8.82 us  [tree_broadcast(): lax.ppermute(value, axis, [(i, i ^ distance) for i in range(count)])]
    ppermute x1, waiting for transfers between devices: 7.57 us -> 8.6 us  [gather_rows(): across = lax.ppermute(value, axis, [(i, i ^ 2) for i in range(count)])]
    ppermute x3 -> x4, starting transfers between devices: 7.67 us -> 8.25 us  [tree_broadcast(): lax.ppermute(value, axis, [(i, i ^ distance) for i in range(count)])]
  transfers between devices with their start and end apart: 11 -> 12, of which waited for: 7 -> 7; matrix products, arithmetic and copies ran while one was open for 7% -> 6% of each run, Pallas kernels for 0% -> 0%
where the time goes in v5:
time: 52.6 us; the launch traced here: 52.4 us
  waiting for transfers between devices  18.7 us (36%)
  starting transfers between devices  14.3 us (27%)
  Pallas kernels  10.9 us (21%)
  local copies, waits for them, and re-layouts  2.78 us (5%)
  matrix products  2.49 us (5%)
  other arithmetic  2.4 us (5%)
  between operations  0.86 us (2%)
    pallas_call x1, Pallas kernels, attention(): pl.pallas_call(functools.partial(attention_kernel, len(key_pieces), span...  10.9 us
    ppermute x4, waiting for transfers between devices, tree_broadcast(): lax.ppermute(value, axis, [(i, i ^ distance) for i in range(count)])  8.82 us
    ppermute x1, waiting for transfers between devices, gather_rows(): across = lax.ppermute(value, axis, [(i, i ^ 2) for i in range(count)])  8.6 us
    ppermute x4, starting transfers between devices, tree_broadcast(): lax.ppermute(value, axis, [(i, i ^ distance) for i in range(count)])  8.25 us
    ppermute x2, starting transfers between devices, body(): lax.ppermute((keys, values), 'view', [(i, i ^ 2) for i in range(view_coun...  3.46 us
    unnamed x11, local copies, waits for them, and re-layouts  1.84 us
    dot_general x1, matrix products, body(): jnp.dot(mixed, out_weight, preferred_element_type=jnp.float32)  1.59 us
    ppermute x1, starting transfers between devices, gather_rows(): across = lax.ppermute(value, axis, [(i, i ^ 2) for i in range(count)])  1.58 us
  transfers between devices with their start and end apart: 12, of which 7 were waited for; matrix products, arithmetic and copies ran while one was open for 6% of the time, Pallas kernels for 0%

profile of v5, /device:TPU:0, one launch (start us, length us, event | category | flops | bytes accessed | tf_op | source)
XLA Modules:
  0.0 52.4 jit_solution(521753409882638303)
XLA Ops:
  0.0 1.0 %constant_dynamic-update-slice_fusion.1 = bf16[32,2560]{1,0:T(8,128)(2,1)S(1)} fusion(bf16[32,1280]{1,0:T(8,128)(2,1)} %param.11), kind=kLoop, calls=%fused_computation.13 | loop fusion | bytes 163840
  1.0 0.9 %constant_dynamic-update-slice_fusion = bf16[32,2560]{1,0:T(8,128)(2,1)S(1)} fusion(bf16[32,2560]{1,0:T(8,128)(2,1)S(1)} %constant_dynamic-update-slice_fusion.1, bf16[32,1280]{1,0:T(8,128)(2,1)} %param.12), kind=kLoop, calls=%fused_computation.12 | loop fusion | bytes 163840 | tf_op jit(solution)/shard_map/concatenate | solution.py:151
  1.9 2.9 %collective-permute-start.8 = (bf16[32,2560]{1,0:T(8,128)(2,1)S(1)}, bf16[32,2560]{1,0:T(8,128)(2,1)}, u32[]{:S(2)}, u32[]{:S(2)}) collective-permute-start(bf16[32,2560]{1,0:T(8,128)(2,1)S(1)} %constant_dynamic-update-slice_fusion), channel_id=1, source_target_pairs={{0,4},{4,0},{8,12},{12,8},{16,20},{20,16},{24,28},{28,24},{1,5},{5... | collective-permute-start | bytes 491528 | tf_op jit(solution)/shard_map/ppermute | solution.py:26
  4.9 1.6 %collective-permute-start.7 = (bf16[32,2560]{1,0:T(8,128)(2,1)S(1)}, bf16[32,2560]{1,0:T(8,128)(2,1)}, u32[]{:S(2)}, u32[]{:S(2)}) collective-permute-start(bf16[32,2560]{1,0:T(8,128)(2,1)S(1)} %constant_dynamic-update-slice_fusion), channel_id=1, source_target_pairs={{0,8},{4,12},{8,0},{12,4},{16,24},{20,28},{24,16},{28,20},{1,9},{5... | collective-permute-start | bytes 491528 | tf_op jit(solution)/shard_map/ppermute | solution.py:26
  6.5 1.9 %collective-permute-start.1 = (bf16[192,1280]{1,0:T(8,128)(2,1)}, bf16[192,1280]{1,0:T(8,128)(2,1)}, u32[]{:S(2)}, u32[]{:S(2)}) collective-permute-start(bf16[192,1280]{1,0:T(8,128)(2,1)} %refs_0_.1), channel_id=1, source_target_pairs={{0,2},{1,3},{2,0},{3,1},{4,6},{5,7},{6,4},{7,5},{8,10},{9,11},{10,... | collective-permute-start | bytes 1474568 | tf_op jit(solution)/shard_map/ppermute | solution.py:142
  9.1 0.9 %fusion = f32[192,3]{0,1:T(4,128)S(1)} fusion(s32[192]{0:T(256)S(1)} %get-tuple-element.14, s32[6,3]{0,1:T(4,128)} %param.14), kind=kOutput, calls=%fused_computation.10 | convolution fusion | flops 8082 | bytes 3144 | tf_op jit(solution)/shard_map/dot_general | solution.py:157
  10.0 0.3 collective-permute-start.3
  10.3 1.8 %collective-permute-done.7 = bf16[32,2560]{1,0:T(8,128)(2,1)} collective-permute-done((bf16[32,2560]{1,0:T(8,128)(2,1)S(1)}, bf16[32,2560]{1,0:T(8,128)(2,1)}, u32[]{:S(2)}, u32[]{:S(2)}) %collective-permute-start.7) | collective-permute-done | bytes 163872 | tf_op jit(solution)/shard_map/ppermute | solution.py:26
  12.1 1.5 %collective-permute-start.4 = (bf16[192,1280]{1,0:T(8,128)(2,1)}, bf16[192,1280]{1,0:T(8,128)(2,1)}, u32[]{:S(2)}, u32[]{:S(2)}) collective-permute-start(bf16[192,1280]{1,0:T(8,128)(2,1)} %refs_4_.1), channel_id=1, source_target_pairs={{0,2},{1,3},{2,0},{3,1},{4,6},{5,7},{6,4},{7,5},{8,10},{9,11},{10,... | collective-permute-start | bytes 1474568 | tf_op jit(solution)/shard_map/ppermute | solution.py:142
  13.6 0.3 collective-permute-done.6
  14.0 3.7 %collective-permute-start.9 = (bf16[32,2560]{1,0:T(8,128)(2,1)S(1)}, bf16[32,2560]{1,0:T(8,128)(2,1)S(1)}, u32[]{:S(2)}, u32[]{:S(2)}) collective-permute-start(bf16[32,2560]{1,0:T(8,128)(2,1)S(1)} %select_select_fusion), channel_id=1, source_target_pairs={{0,16},{4,20},{8,24},{12,28},{16,0},{20,4},{24,8},{28,12},{1,17},{... | collective-permute-start | bytes 491528 | tf_op jit(solution)/shard_map/ppermute | solution.py:31
  17.7 6.7 %collective-permute-done.9 = bf16[32,2560]{1,0:T(8,128)(2,1)S(1)} collective-permute-done((bf16[32,2560]{1,0:T(8,128)(2,1)S(1)}, bf16[32,2560]{1,0:T(8,128)(2,1)S(1)}, u32[]{:S(2)}, u32[]{:S(2)}) %collective-permute-start.9) | collective-permute-done | bytes 163872 | tf_op jit(solution)/shard_map/ppermute | solution.py:31
  24.4 1.6 %collective-permute-start.10 = (bf16[32,2560]{1,0:T(8,128)(2,1)S(1)}, bf16[32,2560]{1,0:T(8,128)(2,1)}, u32[]{:S(2)}, u32[]{:S(2)}) collective-permute-start(bf16[32,2560]{1,0:T(8,128)(2,1)S(1)} %broadcast_select_fusion), channel_id=1, source_target_pairs={{0,2},{1,3},{2,0},{3,1},{4,6},{5,7},{6,4},{7,5},{8,10},{9,11},{10,... | collective-permute-start | bytes 491528 | tf_op jit(solution)/shard_map/ppermute | solution.py:41
  26.0 8.6 %collective-permute-done.10 = bf16[32,2560]{1,0:T(8,128)(2,1)} collective-permute-done((bf16[32,2560]{1,0:T(8,128)(2,1)S(1)}, bf16[32,2560]{1,0:T(8,128)(2,1)}, u32[]{:S(2)}, u32[]{:S(2)}) %collective-permute-start.10) | collective-permute-done | bytes 163872 | tf_op jit(solution)/shard_map/ppermute | solution.py:41
  34.6 0.9 %pad_maximum_fusion.1 = bf16[64,2560]{1,0:T(8,128)(2,1)S(1)} fusion(bf16[32,2560]{1,0:T(8,128)(2,1)} %collective-permute-done.10, bf16[32,2560]{1,0:T(8,128)(2,1)S(1)} %broadcast_select_fusion), kind=kLoop, calls=%fused_computation.2 | loop fusion | flops 655360 | bytes 655360 | tf_op jit(solution)/shard_map/concatenate | solution.py:42
  35.7 0.4 or_select_fusion
  36.1 0.6 %collective-permute-start.2 = (bf16[192,1280]{1,0:T(8,128)(2,1)}, bf16[192,1280]{1,0:T(8,128)(2,1)S(1)}, u32[]{:S(2)}, u32[]{:S(2)}) collective-permute-start(bf16[192,1280]{1,0:T(8,128)(2,1)} %collective-permute-done.1.refs_2_), channel_id=1, source_target_pairs={{0,1},{1,0},{2,3},{3,2},{4,5},{5,4},{6,7},{7,6},{8,9},{9,8},{10,11... | collective-permute-start | bytes 1474568 | tf_op jit(solution)/shard_map/ppermute | solution.py:144
  36.7 0.1 collective-permute-start.5
  36.8 0.5 collective-permute-done.11
  37.3 1.0 %pad_maximum_fusion = bf16[128,2560]{1,0:T(8,128)(2,1)S(1)} fusion(bf16[64,2560]{1,0:T(8,128)(2,1)S(1)} %collective-permute-done.11, bf16[32,2560]{1,0:T(8,128)(2,1)} %collective-permute-done.10, bf16[32,2560]{1,0:T(8,128)(2,1)S(1)} %broadcast_select_fusion), kind=kLoop, calls=%fused_computation.1 | loop fusion | flops 1966080 | bytes 1310720 | tf_op jit(solution)/shard_map/concatenate | solution.py:44
  38.4 0.7 %collective-permute-done.5.refs_7_ = bf16[192,1280]{1,0:T(8,128)(2,1)S(1)} collective-permute-done((bf16[192,1280]{1,0:T(8,128)(2,1)}, bf16[192,1280]{1,0:T(8,128)(2,1)S(1)}, u32[]{:S(2)}, u32[]{:S(2)}) %collective-permute-start.5) | collective-permute-done | bytes 491552 | tf_op jit(solution)/shard_map/ppermute | solution.py:144
  39.1 0.8 %copy-done.4 = bf16[192,1280]{1,0:T(8,128)(2,1)} copy-done((bf16[192,1280]{1,0:T(8,128)(2,1)}, bf16[192,1280]{1,0:T(8,128)(2,1)S(1)}, u32[]{:S(2)}) %copy-start.4) | copy-done | bytes 491544
  39.9 10.9 %shard_map.82 = bf16[192,1280]{1,0:T(8,128)(2,1)S(1)} custom-call(bf16[192,1280]{1,0:T(8,128)(2,1)S(1)} %copy-done.1, bf16[192,1280]{1,0:T(8,128)(2,1)S(1)} %copy-done.2, bf16[192,1280]{1,0:T(8,128)(2,1)} %collective-permute-done.refs_1_, bf16[192,1280]{1,0:T(8,128)(2,1)} %collective-permute-done.1.refs_2_, ...), custom_call_target="tpu_custom_call" | custom-call | flops 1761607680 | bytes 6258688 | tf_op jit(solution)/shard_map/pallas_call | solution.py:109
  50.8 1.6 %convolution_convert_fusion = bf16[192,1280]{1,0:T(8,128)(2,1)} fusion(bf16[192,1280]{1,0:T(8,128)(2,1)S(1)} %shard_map.82, bf16[1280,1280]{1,0:T(8,128)(2,1)S(1)} %copy-done), kind=kOutput, calls=%fused_computation | convolution fusion | flops 629391360 | bytes 4259840 | tf_op jit(solution)/shard_map/dot_general | solution.py:172
  (26 shorter events, 0.3 us)
Async XLA Ops:
  0.0 50.8 %copy-start = (bf16[1280,1280]{1,0:T(8,128)(2,1)S(1)}, bf16[1280,1280]{1,0:T(8,128)(2,1)}, u32[]{:S(2)}) copy-start(bf16[1280,1280]{1,0:T(8,128)(2,1)} %param.13) | copy-start | bytes 9830404
  1.9 8.1 %collective-permute-start.8 = (bf16[32,2560]{1,0:T(8,128)(2,1)S(1)}, bf16[32,2560]{1,0:T(8,128)(2,1)}, u32[]{:S(2)}, u32[]{:S(2)}) collective-permute-start(bf16[32,2560]{1,0:T(8,128)(2,1)S(1)} %constant_dynamic-update-slice_fusion), channel_id=1, source_target_pairs={{0,4},{4,0},{8,12},{12,8},{16,20},{20,16},{24,28},{28,24},{1,5},{5... | collective-permute-start | bytes 491528 | tf_op jit(solution)/shard_map/ppermute | solution.py:26
  4.9 7.2 %collective-permute-start.7 = (bf16[32,2560]{1,0:T(8,128)(2,1)S(1)}, bf16[32,2560]{1,0:T(8,128)(2,1)}, u32[]{:S(2)}, u32[]{:S(2)}) collective-permute-start(bf16[32,2560]{1,0:T(8,128)(2,1)S(1)} %constant_dynamic-update-slice_fusion), channel_id=1, source_target_pairs={{0,8},{4,12},{8,0},{12,4},{16,24},{20,28},{24,16},{28,20},{1,9},{5... | collective-permute-start | bytes 491528 | tf_op jit(solution)/shard_map/ppermute | solution.py:26
  6.5 7.5 %collective-permute-start.6 = (bf16[32,2560]{1,0:T(8,128)(2,1)S(1)}, bf16[32,2560]{1,0:T(8,128)(2,1)}, u32[]{:S(2)}, u32[]{:S(2)}) collective-permute-start(bf16[32,2560]{1,0:T(8,128)(2,1)S(1)} %constant_dynamic-update-slice_fusion), channel_id=1, source_target_pairs={{0,12},{4,8},{8,4},{12,0},{16,28},{20,24},{24,20},{28,16},{1,13},{... | collective-permute-start | bytes 491528 | tf_op jit(solution)/shard_map/ppermute | solution.py:26
  6.5 31.8 %collective-permute-start = (bf16[192,1280]{1,0:T(8,128)(2,1)}, bf16[192,1280]{1,0:T(8,128)(2,1)}, u32[]{:S(2)}, u32[]{:S(2)}) collective-permute-start(bf16[192,1280]{1,0:T(8,128)(2,1)} %refs_0_.1), channel_id=1, source_target_pairs={{0,1},{1,0},{2,3},{3,2},{4,5},{5,4},{6,7},{7,6},{8,9},{9,8},{10,11... | collective-permute-start | bytes 1474568 | tf_op jit(solution)/shard_map/ppermute | solution.py:143
  6.5 29.7 %collective-permute-start.1 = (bf16[192,1280]{1,0:T(8,128)(2,1)}, bf16[192,1280]{1,0:T(8,128)(2,1)}, u32[]{:S(2)}, u32[]{:S(2)}) collective-permute-start(bf16[192,1280]{1,0:T(8,128)(2,1)} %refs_0_.1), channel_id=1, source_target_pairs={{0,2},{1,3},{2,0},{3,1},{4,6},{5,7},{6,4},{7,5},{8,10},{9,11},{10,... | collective-permute-start | bytes 1474568 | tf_op jit(solution)/shard_map/ppermute | solution.py:142
  10.0 28.3 %collective-permute-start.3 = (bf16[192,1280]{1,0:T(8,128)(2,1)}, bf16[192,1280]{1,0:T(8,128)(2,1)}, u32[]{:S(2)}, u32[]{:S(2)}) collective-permute-start(bf16[192,1280]{1,0:T(8,128)(2,1)} %refs_4_.1), channel_id=1, source_target_pairs={{0,1},{1,0},{2,3},{3,2},{4,5},{5,4},{6,7},{7,6},{8,9},{9,8},{10,11... | collective-permute-start | bytes 1474568 | tf_op jit(solution)/shard_map/ppermute | solution.py:143
  12.1 24.6 %collective-permute-start.4 = (bf16[192,1280]{1,0:T(8,128)(2,1)}, bf16[192,1280]{1,0:T(8,128)(2,1)}, u32[]{:S(2)}, u32[]{:S(2)}) collective-permute-start(bf16[192,1280]{1,0:T(8,128)(2,1)} %refs_4_.1), channel_id=1, source_target_pairs={{0,2},{1,3},{2,0},{3,1},{4,6},{5,7},{6,4},{7,5},{8,10},{9,11},{10,... | collective-permute-start | bytes 1474568 | tf_op jit(solution)/shard_map/ppermute | solution.py:142
  14.0 10.4 %collective-permute-start.9 = (bf16[32,2560]{1,0:T(8,128)(2,1)S(1)}, bf16[32,2560]{1,0:T(8,128)(2,1)S(1)}, u32[]{:S(2)}, u32[]{:S(2)}) collective-permute-start(bf16[32,2560]{1,0:T(8,128)(2,1)S(1)} %select_select_fusion), channel_id=1, source_target_pairs={{0,16},{4,20},{8,24},{12,28},{16,0},{20,4},{24,8},{28,12},{1,17},{... | collective-permute-start | bytes 491528 | tf_op jit(solution)/shard_map/ppermute | solution.py:31
  24.4 10.2 %collective-permute-start.10 = (bf16[32,2560]{1,0:T(8,128)(2,1)S(1)}, bf16[32,2560]{1,0:T(8,128)(2,1)}, u32[]{:S(2)}, u32[]{:S(2)}) collective-permute-start(bf16[32,2560]{1,0:T(8,128)(2,1)S(1)} %broadcast_select_fusion), channel_id=1, source_target_pairs={{0,2},{1,3},{2,0},{3,1},{4,6},{5,7},{6,4},{7,5},{8,10},{9,11},{10,... | collective-permute-start | bytes 491528 | tf_op jit(solution)/shard_map/ppermute | solution.py:41
  35.6 1.7 %collective-permute-start.11 = (bf16[64,2560]{1,0:T(8,128)(2,1)S(1)}, bf16[64,2560]{1,0:T(8,128)(2,1)S(1)}, u32[]{:S(2)}, u32[]{:S(2)}) collective-permute-start(bf16[64,2560]{1,0:T(8,128)(2,1)S(1)} %pad_maximum_fusion.1), channel_id=1, source_target_pairs={{0,1},{1,0},{2,3},{3,2},{4,5},{5,4},{6,7},{7,6},{8,9},{9,8},{10,11... | collective-permute-start | bytes 983048 | tf_op jit(solution)/shard_map/ppermute | solution.py:43
  36.1 3.8 %copy-start.1 = (bf16[192,1280]{1,0:T(8,128)(2,1)S(1)}, bf16[192,1280]{1,0:T(8,128)(2,1)}, u32[]{:S(2)}) copy-start(bf16[192,1280]{1,0:T(8,128)(2,1)} %q_ref.1) | copy-start | bytes 1474564
  36.1 3.8 %copy-start.2 = (bf16[192,1280]{1,0:T(8,128)(2,1)S(1)}, bf16[192,1280]{1,0:T(8,128)(2,1)}, u32[]{:S(2)}) copy-start(bf16[192,1280]{1,0:T(8,128)(2,1)} %refs_0_.1) | copy-start | bytes 1474564
  36.1 3.8 %copy-start.3 = (bf16[192,1280]{1,0:T(8,128)(2,1)S(1)}, bf16[192,1280]{1,0:T(8,128)(2,1)}, u32[]{:S(2)}) copy-start(bf16[192,1280]{1,0:T(8,128)(2,1)} %refs_4_.1) | copy-start | bytes 1474564
  36.1 2.3 %collective-permute-start.2 = (bf16[192,1280]{1,0:T(8,128)(2,1)}, bf16[192,1280]{1,0:T(8,128)(2,1)S(1)}, u32[]{:S(2)}, u32[]{:S(2)}) collective-permute-start(bf16[192,1280]{1,0:T(8,128)(2,1)} %collective-permute-done.1.refs_2_), channel_id=1, source_target_pairs={{0,1},{1,0},{2,3},{3,2},{4,5},{5,4},{6,7},{7,6},{8,9},{9,8},{10,11... | collective-permute-start | bytes 1474568 | tf_op jit(solution)/shard_map/ppermute | solution.py:144
  36.7 2.4 %collective-permute-start.5 = (bf16[192,1280]{1,0:T(8,128)(2,1)}, bf16[192,1280]{1,0:T(8,128)(2,1)S(1)}, u32[]{:S(2)}, u32[]{:S(2)}) collective-permute-start(bf16[192,1280]{1,0:T(8,128)(2,1)} %collective-permute-done.4.refs_6_), channel_id=1, source_target_pairs={{0,1},{1,0},{2,3},{3,2},{4,5},{5,4},{6,7},{7,6},{8,9},{9,8},{10,11... | collective-permute-start | bytes 1474568 | tf_op jit(solution)/shard_map/ppermute | solution.py:144
  39.1 0.8 %copy-start.4 = (bf16[192,1280]{1,0:T(8,128)(2,1)}, bf16[192,1280]{1,0:T(8,128)(2,1)S(1)}, u32[]{:S(2)}) copy-start(bf16[192,1280]{1,0:T(8,128)(2,1)S(1)} %collective-permute-done.5.refs_7_) | copy-start | bytes 1474564

commit v6 on v4

--- a/solution.py
+++ b/solution.py
@@ -134,6 +134,16 @@
     view_index = lax.axis_index("view")
     view_tok = shard_rows * view_count // VIEWS
 
+    ref_both = jnp.concatenate([ref_keys, ref_values], axis=1)
+    if view_count == 4:
+        ref_across = lax.ppermute(ref_both, "view", [(i, i ^ 2) for i in range(view_count)])
+        ref_half = jnp.concatenate([ref_both, ref_across], axis=0)
+        ref_shared = tree_broadcast(ref_half, "mesh", ref_source[0])
+        ref_near = lax.ppermute(ref_shared, "view", [(i, i ^ 1) for i in range(view_count)])
+        ref_all = jnp.concatenate([ref_shared, ref_near], axis=0)
+    else:
+        ref_all = gather_rows(tree_broadcast(ref_both, "mesh", ref_source[0]), "view")
+
     if view_count == 4:
         across = lax.ppermute((keys, values), "view", [(i, i ^ 2) for i in range(view_count)])
         near = lax.ppermute((keys, values), "view", [(i, i ^ 1) for i in range(view_count)])
@@ -144,8 +154,6 @@
         pieces = [lax.all_gather((keys, values), "view", axis=0, tiled=True)]
         positions = [jnp.zeros((), jnp.int32)]
 
-    ref_both = jnp.concatenate([ref_keys, ref_values], axis=1)
-    ref_all = gather_rows(tree_broadcast(ref_both, "mesh", ref_source[0]), "view")
 
     view_ids = jnp.arange(VIEWS, dtype=jnp.int32)
     query_views = (view_index * shard_rows + jnp.arange(shard_rows, dtype=jnp.int32)) // view_tok

time: 50.8 us -> 60.8 us (1.20)
  waiting for transfers between devices: 19 us -> 29.1 us
  local copies, waits for them, and re-layouts: 2.78 us -> 3.4 us
    ppermute x3, waiting for transfers between devices: 10.2 us -> 22.8 us  [tree_broadcast(): received = lax.ppermute(value, axis, pairs)]
    ppermute x2, waiting for transfers between devices: 8.07 us -> 4.73 us  [the longest x1 4.2 us: body(): lax.ppermute(ref_both, 'view', [(i, i ^ 2) for i in range(view_count)])]
    ppermute x3, starting transfers between devices: 7.67 us -> 5.62 us  [tree_broadcast(): received = lax.ppermute(value, axis, pairs)]
    ppermute x2, starting transfers between devices: 1.59 us -> 3.04 us  [the longest x1 2.97 us: body(): lax.ppermute(ref_both, 'view', [(i, i ^ 2) for i in range(view_count)])]
    concatenate x2, other arithmetic: 1.9 us -> 0.79 us  [the longest x1 0.75 us: body(): ref_half = jnp.concatenate([ref_both, ref_across], axis=0)]
    select_n x3, other arithmetic: 0.06 us -> 1.07 us  [tree_broadcast(): value = jnp.where(partner_has, received, value)]
    ppermute x2, waiting for transfers between devices: 0.78 us -> 1.55 us  [body(): far = lax.ppermute(across, 'view', [(i, i ^ 1) for i in range(view_count)])]
    unnamed x11 -> x13, local copies, waits for them, and re-layouts: 1.84 us -> 2.5 us
  transfers between devices with their start and end apart: 11 -> 11, of which waited for: 7 -> 7; matrix products, arithmetic and copies ran while one was open for 7% -> 4% of each run, Pallas kernels for 0% -> 0%
where the time goes in v6:
time: 60.8 us; the launch traced here: 60.6 us
  waiting for transfers between devices  29.1 us (48%)
  starting transfers between devices  11.6 us (19%)
  Pallas kernels  10.9 us (18%)
  local copies, waits for them, and re-layouts  3.4 us (6%)
  matrix products  2.49 us (4%)
  other arithmetic  2.3 us (4%)
  between operations  0.85 us (1%)
    ppermute x3, waiting for transfers between devices, tree_broadcast(): received = lax.ppermute(value, axis, pairs)  22.8 us
    pallas_call x1, Pallas kernels, attention(): pl.pallas_call(functools.partial(attention_kernel, len(key_pieces), span...  10.9 us
    ppermute x3, starting transfers between devices, tree_broadcast(): received = lax.ppermute(value, axis, pairs)  5.62 us
    ppermute x1, waiting for transfers between devices, body(): lax.ppermute(ref_both, 'view', [(i, i ^ 2) for i in range(view_count)])  4.2 us
    ppermute x1, starting transfers between devices, body(): lax.ppermute(ref_both, 'view', [(i, i ^ 2) for i in range(view_count)])  2.97 us
    unnamed x13, local copies, waits for them, and re-layouts  2.5 us
    ppermute x2, starting transfers between devices, body(): lax.ppermute((keys, values), 'view', [(i, i ^ 2) for i in range(view_coun...  2.03 us
    dot_general x1, matrix products, body(): jnp.dot(mixed, out_weight, preferred_element_type=jnp.float32)  1.59 us
  transfers between devices with their start and end apart: 11, of which 7 were waited for; matrix products, arithmetic and copies ran while one was open for 4% of the time, Pallas kernels for 0%

profile of v6, /device:TPU:0, one launch (start us, length us, event | category | flops | bytes accessed | tf_op | source)
XLA Modules:
  0.0 60.6 jit_solution(1343499353488088500)
XLA Ops:
  0.0 1.0 %constant_dynamic-update-slice_fusion.1 = bf16[32,2560]{1,0:T(8,128)(2,1)S(1)} fusion(bf16[32,1280]{1,0:T(8,128)(2,1)} %param.11), kind=kLoop, calls=%fused_computation.17 | loop fusion | bytes 163840
  1.0 0.9 %constant_dynamic-update-slice_fusion = bf16[32,2560]{1,0:T(8,128)(2,1)S(1)} fusion(bf16[32,2560]{1,0:T(8,128)(2,1)S(1)} %constant_dynamic-update-slice_fusion.1, bf16[32,1280]{1,0:T(8,128)(2,1)} %param.12), kind=kLoop, calls=%fused_computation.16 | loop fusion | bytes 163840 | tf_op jit(solution)/shard_map/concatenate | solution.py:137
  1.9 3.0 %collective-permute-start.6 = (bf16[32,2560]{1,0:T(8,128)(2,1)S(1)}, bf16[32,2560]{1,0:T(8,128)(2,1)S(1)}, u32[]{:S(2)}, u32[]{:S(2)}) collective-permute-start(bf16[32,2560]{1,0:T(8,128)(2,1)S(1)} %constant_dynamic-update-slice_fusion), channel_id=1, source_target_pairs={{0,2},{1,3},{2,0},{3,1},{4,6},{5,7},{6,4},{7,5},{8,10},{9,11},{10,... | collective-permute-start | bytes 491528 | tf_op jit(solution)/shard_map/ppermute | solution.py:139
  4.9 4.2 %collective-permute-done.6 = bf16[32,2560]{1,0:T(8,128)(2,1)S(1)} collective-permute-done((bf16[32,2560]{1,0:T(8,128)(2,1)S(1)}, bf16[32,2560]{1,0:T(8,128)(2,1)S(1)}, u32[]{:S(2)}, u32[]{:S(2)}) %collective-permute-start.6) | collective-permute-done | bytes 163872 | tf_op jit(solution)/shard_map/ppermute | solution.py:139
  9.1 0.7 %copy-done.4 = bf16[32,2560]{1,0:T(8,128)(2,1)} copy-done((bf16[32,2560]{1,0:T(8,128)(2,1)}, bf16[32,2560]{1,0:T(8,128)(2,1)S(1)}, u32[]{:S(2)}) %copy-start.4) | copy-done | bytes 163864
  9.8 0.7 %pad_maximum_fusion.1 = bf16[64,2560]{1,0:T(8,128)(2,1)} fusion(bf16[32,2560]{1,0:T(8,128)(2,1)S(1)} %collective-permute-done.6, bf16[32,2560]{1,0:T(8,128)(2,1)S(1)} %constant_dynamic-update-slice_fusion), kind=kLoop, calls=%fused_computation.5 | loop fusion | flops 655360 | bytes 655360 | tf_op jit(solution)/shard_map/concatenate | solution.py:140
  10.5 1.7 %collective-permute-start.7 = (bf16[64,2560]{1,0:T(8,128)(2,1)}, bf16[64,2560]{1,0:T(8,128)(2,1)}, u32[]{:S(2)}, u32[]{:S(2)}) collective-permute-start(bf16[64,2560]{1,0:T(8,128)(2,1)} %pad_maximum_fusion.1), channel_id=1, source_target_pairs={{0,4},{4,0},{8,12},{12,8},{16,20},{20,16},{24,28},{28,24},{1,5},{5... | collective-permute-start | bytes 983048 | tf_op jit(solution)/shard_map/ppermute | solution.py:27
  12.2 1.5 %collective-permute-start.1 = (bf16[192,1280]{1,0:T(8,128)(2,1)}, bf16[192,1280]{1,0:T(8,128)(2,1)}, u32[]{:S(2)}, u32[]{:S(2)}) collective-permute-start(bf16[192,1280]{1,0:T(8,128)(2,1)} %refs_0_.1), channel_id=1, source_target_pairs={{0,2},{1,3},{2,0},{3,1},{4,6},{5,7},{6,4},{7,5},{8,10},{9,11},{10,... | collective-permute-start | bytes 1474568 | tf_op jit(solution)/shard_map/ppermute | solution.py:148
  14.0 0.5 collective-permute-start.4
  15.3 4.5 %collective-permute-done.7 = bf16[64,2560]{1,0:T(8,128)(2,1)} collective-permute-done((bf16[64,2560]{1,0:T(8,128)(2,1)}, bf16[64,2560]{1,0:T(8,128)(2,1)}, u32[]{:S(2)}, u32[]{:S(2)}) %collective-permute-start.7) | collective-permute-done | bytes 327712 | tf_op jit(solution)/shard_map/ppermute | solution.py:27
  19.7 1.0 %broadcast_select_fusion = bf16[64,2560]{1,0:T(8,128)(2,1)S(1)} fusion(bf16[64,2560]{1,0:T(8,128)(2,1)} %collective-permute-done.7, pred[]{:T(512)S(6)} %eq.110, bf16[32,2560]{1,0:T(8,128)(2,1)} %copy-done.4, bf16[32,2560]{1,0:T(8,128)(2,1)S(1)} %constant_dynamic-update-slice_fusion), kind=kLoop, calls=%fused_computation.6 | loop fusion | flops 819200 | bytes 983041 | tf_op jit(solution)/shard_map/jit(_where)/select_n | solution.py:29
  20.7 1.5 %collective-permute-start.8 = (bf16[64,2560]{1,0:T(8,128)(2,1)S(1)}, bf16[64,2560]{1,0:T(8,128)(2,1)S(1)}, u32[]{:S(2)}, u32[]{:S(2)}) collective-permute-start(bf16[64,2560]{1,0:T(8,128)(2,1)S(1)} %broadcast_select_fusion), channel_id=1, source_target_pairs={{0,8},{4,12},{8,0},{12,4},{16,24},{20,28},{24,16},{28,20},{1,9},{5... | collective-permute-start | bytes 983048 | tf_op jit(solution)/shard_map/ppermute | solution.py:27
  22.3 0.9 %fusion.1 = f32[192,3]{0,1:T(4,128)S(1)} fusion(s32[192]{0:T(256)S(1)} %get-tuple-element.14, s32[6,3]{0,1:T(4,128)} %param.14), kind=kOutput, calls=%fused_computation.14 | convolution fusion | flops 8082 | bytes 3144 | tf_op jit(solution)/shard_map/dot_general | solution.py:161
  23.2 5.6 %collective-permute-done.8 = bf16[64,2560]{1,0:T(8,128)(2,1)S(1)} collective-permute-done((bf16[64,2560]{1,0:T(8,128)(2,1)S(1)}, bf16[64,2560]{1,0:T(8,128)(2,1)S(1)}, u32[]{:S(2)}, u32[]{:S(2)}) %collective-permute-start.8) | collective-permute-done | bytes 327712 | tf_op jit(solution)/shard_map/ppermute | solution.py:27
  28.8 2.4 %collective-permute-start.9 = (bf16[64,2560]{1,0:T(8,128)(2,1)S(1)}, bf16[64,2560]{1,0:T(8,128)(2,1)S(1)}, u32[]{:S(2)}, u32[]{:S(2)}) collective-permute-start(bf16[64,2560]{1,0:T(8,128)(2,1)S(1)} %broadcast_select_fusion.1), channel_id=1, source_target_pairs={{0,16},{4,20},{8,24},{12,28},{16,0},{20,4},{24,8},{28,12},{1,17},{... | collective-permute-start | bytes 983048 | tf_op jit(solution)/shard_map/ppermute | solution.py:27
  31.2 12.8 %collective-permute-done.9 = bf16[64,2560]{1,0:T(8,128)(2,1)S(1)} collective-permute-done((bf16[64,2560]{1,0:T(8,128)(2,1)S(1)}, bf16[64,2560]{1,0:T(8,128)(2,1)S(1)}, u32[]{:S(2)}, u32[]{:S(2)}) %collective-permute-start.9) | collective-permute-done | bytes 327712 | tf_op jit(solution)/shard_map/ppermute | solution.py:27
  44.1 0.6 collective-permute-start.2
  44.7 0.4 or_select_fusion
  45.1 0.5 collective-permute-done.10
  45.7 0.8 %collective-permute-done.2.refs_3_ = bf16[192,1280]{1,0:T(8,128)(2,1)S(1)} collective-permute-done((bf16[192,1280]{1,0:T(8,128)(2,1)}, bf16[192,1280]{1,0:T(8,128)(2,1)S(1)}, u32[]{:S(2)}, u32[]{:S(2)}) %collective-permute-start.2) | collective-permute-done | bytes 491552 | tf_op jit(solution)/shard_map/ppermute | solution.py:150
  46.6 0.7 %collective-permute-done.5.refs_7_ = bf16[192,1280]{1,0:T(8,128)(2,1)S(1)} collective-permute-done((bf16[192,1280]{1,0:T(8,128)(2,1)}, bf16[192,1280]{1,0:T(8,128)(2,1)S(1)}, u32[]{:S(2)}, u32[]{:S(2)}) %collective-permute-start.5) | collective-permute-done | bytes 491552 | tf_op jit(solution)/shard_map/ppermute | solution.py:150
  47.3 0.8 %copy-done.5 = bf16[192,1280]{1,0:T(8,128)(2,1)} copy-done((bf16[192,1280]{1,0:T(8,128)(2,1)}, bf16[192,1280]{1,0:T(8,128)(2,1)S(1)}, u32[]{:S(2)}) %copy-start.5) | copy-done | bytes 491544
  48.1 10.9 %shard_map.82 = bf16[192,1280]{1,0:T(8,128)(2,1)S(1)} custom-call(bf16[192,1280]{1,0:T(8,128)(2,1)S(1)} %copy-done.1, bf16[192,1280]{1,0:T(8,128)(2,1)S(1)} %copy-done.2, bf16[192,1280]{1,0:T(8,128)(2,1)} %collective-permute-done.refs_1_, bf16[192,1280]{1,0:T(8,128)(2,1)} %collective-permute-done.1.refs_2_, ...), custom_call_target="tpu_custom_call" | custom-call | flops 1761607680 | bytes 6258688 | tf_op jit(solution)/shard_map/pallas_call | solution.py:105
  59.0 1.6 %convolution_convert_fusion = bf16[192,1280]{1,0:T(8,128)(2,1)} fusion(bf16[192,1280]{1,0:T(8,128)(2,1)S(1)} %shard_map.82, bf16[1280,1280]{1,0:T(8,128)(2,1)S(1)} %copy-done), kind=kOutput, calls=%fused_computation | convolution fusion | flops 629391360 | bytes 4259840 | tf_op jit(solution)/shard_map/dot_general | solution.py:176
  (26 shorter events, 0.6 us)
Async XLA Ops:
  0.0 59.0 %copy-start = (bf16[1280,1280]{1,0:T(8,128)(2,1)S(1)}, bf16[1280,1280]{1,0:T(8,128)(2,1)}, u32[]{:S(2)}) copy-start(bf16[1280,1280]{1,0:T(8,128)(2,1)} %param.13) | copy-start | bytes 9830404
  1.9 7.2 %collective-permute-start.6 = (bf16[32,2560]{1,0:T(8,128)(2,1)S(1)}, bf16[32,2560]{1,0:T(8,128)(2,1)S(1)}, u32[]{:S(2)}, u32[]{:S(2)}) collective-permute-start(bf16[32,2560]{1,0:T(8,128)(2,1)S(1)} %constant_dynamic-update-slice_fusion), channel_id=1, source_target_pairs={{0,2},{1,3},{2,0},{3,1},{4,6},{5,7},{6,4},{7,5},{8,10},{9,11},{10,... | collective-permute-start | bytes 491528 | tf_op jit(solution)/shard_map/ppermute | solution.py:139
  9.1 0.7 %copy-start.4 = (bf16[32,2560]{1,0:T(8,128)(2,1)}, bf16[32,2560]{1,0:T(8,128)(2,1)S(1)}, u32[]{:S(2)}) copy-start(bf16[32,2560]{1,0:T(8,128)(2,1)S(1)} %collective-permute-done.6) | copy-start | bytes 491524
  10.5 9.2 %collective-permute-start.7 = (bf16[64,2560]{1,0:T(8,128)(2,1)}, bf16[64,2560]{1,0:T(8,128)(2,1)}, u32[]{:S(2)}, u32[]{:S(2)}) collective-permute-start(bf16[64,2560]{1,0:T(8,128)(2,1)} %pad_maximum_fusion.1), channel_id=1, source_target_pairs={{0,4},{4,0},{8,12},{12,8},{16,20},{20,16},{24,28},{28,24},{1,5},{5... | collective-permute-start | bytes 983048 | tf_op jit(solution)/shard_map/ppermute | solution.py:27
  12.2 33.5 %collective-permute-start = (bf16[192,1280]{1,0:T(8,128)(2,1)}, bf16[192,1280]{1,0:T(8,128)(2,1)}, u32[]{:S(2)}, u32[]{:S(2)}) collective-permute-start(bf16[192,1280]{1,0:T(8,128)(2,1)} %refs_0_.1), channel_id=1, source_target_pairs={{0,1},{1,0},{2,3},{3,2},{4,5},{5,4},{6,7},{7,6},{8,9},{9,8},{10,11... | collective-permute-start | bytes 1474568 | tf_op jit(solution)/shard_map/ppermute | solution.py:149
  12.2 31.9 %collective-permute-start.1 = (bf16[192,1280]{1,0:T(8,128)(2,1)}, bf16[192,1280]{1,0:T(8,128)(2,1)}, u32[]{:S(2)}, u32[]{:S(2)}) collective-permute-start(bf16[192,1280]{1,0:T(8,128)(2,1)} %refs_0_.1), channel_id=1, source_target_pairs={{0,2},{1,3},{2,0},{3,1},{4,6},{5,7},{6,4},{7,5},{8,10},{9,11},{10,... | collective-permute-start | bytes 1474568 | tf_op jit(solution)/shard_map/ppermute | solution.py:148
  13.7 32.0 %collective-permute-start.3 = (bf16[192,1280]{1,0:T(8,128)(2,1)}, bf16[192,1280]{1,0:T(8,128)(2,1)}, u32[]{:S(2)}, u32[]{:S(2)}) collective-permute-start(bf16[192,1280]{1,0:T(8,128)(2,1)} %refs_4_.1), channel_id=1, source_target_pairs={{0,1},{1,0},{2,3},{3,2},{4,5},{5,4},{6,7},{7,6},{8,9},{9,8},{10,11... | collective-permute-start | bytes 1474568 | tf_op jit(solution)/shard_map/ppermute | solution.py:149
  14.0 30.7 %collective-permute-start.4 = (bf16[192,1280]{1,0:T(8,128)(2,1)}, bf16[192,1280]{1,0:T(8,128)(2,1)}, u32[]{:S(2)}, u32[]{:S(2)}) collective-permute-start(bf16[192,1280]{1,0:T(8,128)(2,1)} %refs_4_.1), channel_id=1, source_target_pairs={{0,2},{1,3},{2,0},{3,1},{4,6},{5,7},{6,4},{7,5},{8,10},{9,11},{10,... | collective-permute-start | bytes 1474568 | tf_op jit(solution)/shard_map/ppermute | solution.py:148
  15.2 32.9 %copy-start.1 = (bf16[192,1280]{1,0:T(8,128)(2,1)S(1)}, bf16[192,1280]{1,0:T(8,128)(2,1)}, u32[]{:S(2)}) copy-start(bf16[192,1280]{1,0:T(8,128)(2,1)} %q_ref.1) | copy-start | bytes 1474564
  15.2 32.9 %copy-start.2 = (bf16[192,1280]{1,0:T(8,128)(2,1)S(1)}, bf16[192,1280]{1,0:T(8,128)(2,1)}, u32[]{:S(2)}) copy-start(bf16[192,1280]{1,0:T(8,128)(2,1)} %refs_0_.1) | copy-start | bytes 1474564
  15.2 32.9 %copy-start.3 = (bf16[192,1280]{1,0:T(8,128)(2,1)S(1)}, bf16[192,1280]{1,0:T(8,128)(2,1)}, u32[]{:S(2)}) copy-start(bf16[192,1280]{1,0:T(8,128)(2,1)} %refs_4_.1) | copy-start | bytes 1474564
  20.7 8.0 %collective-permute-start.8 = (bf16[64,2560]{1,0:T(8,128)(2,1)S(1)}, bf16[64,2560]{1,0:T(8,128)(2,1)S(1)}, u32[]{:S(2)}, u32[]{:S(2)}) collective-permute-start(bf16[64,2560]{1,0:T(8,128)(2,1)S(1)} %broadcast_select_fusion), channel_id=1, source_target_pairs={{0,8},{4,12},{8,0},{12,4},{16,24},{20,28},{24,16},{28,20},{1,9},{5... | collective-permute-start | bytes 983048 | tf_op jit(solution)/shard_map/ppermute | solution.py:27
  28.8 15.1 %collective-permute-start.9 = (bf16[64,2560]{1,0:T(8,128)(2,1)S(1)}, bf16[64,2560]{1,0:T(8,128)(2,1)S(1)}, u32[]{:S(2)}, u32[]{:S(2)}) collective-permute-start(bf16[64,2560]{1,0:T(8,128)(2,1)S(1)} %broadcast_select_fusion.1), channel_id=1, source_target_pairs={{0,16},{4,20},{8,24},{12,28},{16,0},{20,4},{24,8},{28,12},{1,17},{... | collective-permute-start | bytes 983048 | tf_op jit(solution)/shard_map/ppermute | solution.py:27
  44.0 1.7 %collective-permute-start.10 = (bf16[64,2560]{1,0:T(8,128)(2,1)S(1)}, bf16[64,2560]{1,0:T(8,128)(2,1)S(1)}, u32[]{:S(2)}, u32[]{:S(2)}) collective-permute-start(bf16[64,2560]{1,0:T(8,128)(2,1)S(1)} %broadcast_select_fusion.2), channel_id=1, source_target_pairs={{0,1},{1,0},{2,3},{3,2},{4,5},{5,4},{6,7},{7,6},{8,9},{9,8},{10,11... | collective-permute-start | bytes 983048 | tf_op jit(solution)/shard_map/ppermute | solution.py:142
  44.1 2.5 %collective-permute-start.2 = (bf16[192,1280]{1,0:T(8,128)(2,1)}, bf16[192,1280]{1,0:T(8,128)(2,1)S(1)}, u32[]{:S(2)}, u32[]{:S(2)}) collective-permute-start(bf16[192,1280]{1,0:T(8,128)(2,1)} %collective-permute-done.1.refs_2_), channel_id=1, source_target_pairs={{0,1},{1,0},{2,3},{3,2},{4,5},{5,4},{6,7},{7,6},{8,9},{9,8},{10,11... | collective-permute-start | bytes 1474568 | tf_op jit(solution)/shard_map/ppermute | solution.py:150
  44.7 2.6 %collective-permute-start.5 = (bf16[192,1280]{1,0:T(8,128)(2,1)}, bf16[192,1280]{1,0:T(8,128)(2,1)S(1)}, u32[]{:S(2)}, u32[]{:S(2)}) collective-permute-start(bf16[192,1280]{1,0:T(8,128)(2,1)} %collective-permute-done.4.refs_6_), channel_id=1, source_target_pairs={{0,1},{1,0},{2,3},{3,2},{4,5},{5,4},{6,7},{7,6},{8,9},{9,8},{10,11... | collective-permute-start | bytes 1474568 | tf_op jit(solution)/shard_map/ppermute | solution.py:150
  47.3 0.8 %copy-start.5 = (bf16[192,1280]{1,0:T(8,128)(2,1)}, bf16[192,1280]{1,0:T(8,128)(2,1)S(1)}, u32[]{:S(2)}) copy-start(bf16[192,1280]{1,0:T(8,128)(2,1)S(1)} %collective-permute-done.5.refs_7_) | copy-start | bytes 1474564

commit v7 on v4

--- a/solution.py
+++ b/solution.py
@@ -21,13 +21,13 @@
     if count & (count - 1):
         kept = jnp.where(index == source, value, jnp.zeros_like(value))
         return lax.psum(kept, axis)
-    distance = 1
-    while distance < count:
+    distance = count // 2
+    while distance >= 1:
         pairs = [(i, i ^ distance) for i in range(count)]
         received = lax.ppermute(value, axis, pairs)
-        partner_has = ((index ^ distance) // distance) == (source // distance)
+        partner_has = ((index ^ distance) % (2 * distance)) == (source % (2 * distance))
         value = jnp.where(partner_has, received, value)
-        distance *= 2
+        distance //= 2
     return value
 
 

time: 50.8 us -> 51.9 us (1.022)
  waiting for transfers between devices: 19 us -> 20.9 us
  starting transfers between devices: 12.2 us -> 11.4 us
    ppermute x3, waiting for transfers between devices: 10.2 us -> 12 us  [tree_broadcast(): received = lax.ppermute(value, axis, pairs)]
    ppermute x3, starting transfers between devices: 7.67 us -> 6.8 us  [tree_broadcast(): received = lax.ppermute(value, axis, pairs)]
  transfers between devices with their start and end apart: 11 -> 11, of which waited for: 7 -> 7; matrix products, arithmetic and copies ran while one was open for 7% -> 6% of each run, Pallas kernels for 0% -> 0%
where the time goes in v7:
time: 51.9 us; the launch traced here: 51.7 us
  waiting for transfers between devices  20.9 us (40%)
  starting transfers between devices  11.4 us (22%)
  Pallas kernels  10.9 us (21%)
  local copies, waits for them, and re-layouts  2.78 us (5%)
  matrix products  2.48 us (5%)
  other arithmetic  2.41 us (5%)
  between operations  0.85 us (2%)
    ppermute x3, waiting for transfers between devices, tree_broadcast(): received = lax.ppermute(value, axis, pairs)  12 us
    pallas_call x1, Pallas kernels, attention(): pl.pallas_call(functools.partial(attention_kernel, len(key_pieces), span...  10.9 us
    ppermute x1, waiting for transfers between devices, gather_rows(): across = lax.ppermute(value, axis, [(i, i ^ 2) for i in range(count)])  7.62 us
    ppermute x3, starting transfers between devices, tree_broadcast(): received = lax.ppermute(value, axis, pairs)  6.8 us
    ppermute x2, starting transfers between devices, body(): lax.ppermute((keys, values), 'view', [(i, i ^ 2) for i in range(view_coun...  2.03 us
    unnamed x11, local copies, waits for them, and re-layouts  1.84 us
    dot_general x1, matrix products, body(): jnp.dot(mixed, out_weight, preferred_element_type=jnp.float32)  1.59 us
    ppermute x1, starting transfers between devices, gather_rows(): across = lax.ppermute(value, axis, [(i, i ^ 2) for i in range(count)])  1.58 us
  transfers between devices with their start and end apart: 11, of which 7 were waited for; matrix products, arithmetic and copies ran while one was open for 6% of the time, Pallas kernels for 0%

profile of v7, /device:TPU:0, one launch (start us, length us, event | category | flops | bytes accessed | tf_op | source)
XLA Modules:
  0.0 51.7 jit_solution(1707856019218533689)
XLA Ops:
  0.0 1.0 %constant_dynamic-update-slice_fusion.1 = bf16[32,2560]{1,0:T(8,128)(2,1)S(1)} fusion(bf16[32,1280]{1,0:T(8,128)(2,1)} %param.11), kind=kLoop, calls=%fused_computation.14 | loop fusion | bytes 163840
  1.0 0.9 %constant_dynamic-update-slice_fusion = bf16[32,2560]{1,0:T(8,128)(2,1)S(1)} fusion(bf16[32,2560]{1,0:T(8,128)(2,1)S(1)} %constant_dynamic-update-slice_fusion.1, bf16[32,1280]{1,0:T(8,128)(2,1)} %param.12), kind=kLoop, calls=%fused_computation.13 | loop fusion | bytes 163840 | tf_op jit(solution)/shard_map/concatenate | solution.py:147
  1.9 4.0 %collective-permute-start.6 = (bf16[32,2560]{1,0:T(8,128)(2,1)S(1)}, bf16[32,2560]{1,0:T(8,128)(2,1)}, u32[]{:S(2)}, u32[]{:S(2)}) collective-permute-start(bf16[32,2560]{1,0:T(8,128)(2,1)S(1)} %constant_dynamic-update-slice_fusion), channel_id=1, source_target_pairs={{0,16},{4,20},{8,24},{12,28},{16,0},{20,4},{24,8},{28,12},{1,17},{... | collective-permute-start | bytes 491528 | tf_op jit(solution)/shard_map/ppermute | solution.py:27
  6.0 1.5 %collective-permute-start.1 = (bf16[192,1280]{1,0:T(8,128)(2,1)}, bf16[192,1280]{1,0:T(8,128)(2,1)}, u32[]{:S(2)}, u32[]{:S(2)}) collective-permute-start(bf16[192,1280]{1,0:T(8,128)(2,1)} %refs_0_.1), channel_id=1, source_target_pairs={{0,2},{1,3},{2,0},{3,1},{4,6},{5,7},{6,4},{7,5},{8,10},{9,11},{10,... | collective-permute-start | bytes 1474568 | tf_op jit(solution)/shard_map/ppermute | solution.py:138
  7.5 0.2 collective-permute-start.3
  7.7 0.5 collective-permute-start.4
  9.0 4.8 %collective-permute-done.6 = bf16[32,2560]{1,0:T(8,128)(2,1)} collective-permute-done((bf16[32,2560]{1,0:T(8,128)(2,1)S(1)}, bf16[32,2560]{1,0:T(8,128)(2,1)}, u32[]{:S(2)}, u32[]{:S(2)}) %collective-permute-start.6) | collective-permute-done | bytes 163872 | tf_op jit(solution)/shard_map/ppermute | solution.py:27
  13.8 0.7 %collective-permute-start.7 = (bf16[32,2560]{1,0:T(8,128)(2,1)S(1)}, bf16[32,2560]{1,0:T(8,128)(2,1)S(1)}, u32[]{:S(2)}, u32[]{:S(2)}) collective-permute-start(bf16[32,2560]{1,0:T(8,128)(2,1)S(1)} %broadcast_select_fusion), channel_id=1, source_target_pairs={{0,8},{4,12},{8,0},{12,4},{16,24},{20,28},{24,16},{28,20},{1,9},{5... | collective-permute-start | bytes 491528 | tf_op jit(solution)/shard_map/ppermute | solution.py:27
  14.5 0.9 %fusion = f32[192,3]{0,1:T(4,128)S(1)} fusion(s32[192]{0:T(256)S(1)} %get-tuple-element.14, s32[6,3]{0,1:T(4,128)} %param.14), kind=kOutput, calls=%fused_computation.11 | convolution fusion | flops 8082 | bytes 3144 | tf_op jit(solution)/shard_map/dot_general | solution.py:153
  15.4 3.9 %collective-permute-done.7 = bf16[32,2560]{1,0:T(8,128)(2,1)S(1)} collective-permute-done((bf16[32,2560]{1,0:T(8,128)(2,1)S(1)}, bf16[32,2560]{1,0:T(8,128)(2,1)S(1)}, u32[]{:S(2)}, u32[]{:S(2)}) %collective-permute-start.7) | collective-permute-done | bytes 163872 | tf_op jit(solution)/shard_map/ppermute | solution.py:27
  19.3 2.1 %collective-permute-start.8 = (bf16[32,2560]{1,0:T(8,128)(2,1)S(1)}, bf16[32,2560]{1,0:T(8,128)(2,1)S(1)}, u32[]{:S(2)}, u32[]{:S(2)}) collective-permute-start(bf16[32,2560]{1,0:T(8,128)(2,1)S(1)} %broadcast_select_fusion.1), channel_id=1, source_target_pairs={{0,4},{4,0},{8,12},{12,8},{16,20},{20,16},{24,28},{28,24},{1,5},{5... | collective-permute-start | bytes 491528 | tf_op jit(solution)/shard_map/ppermute | solution.py:27
  21.4 3.3 %collective-permute-done.8 = bf16[32,2560]{1,0:T(8,128)(2,1)S(1)} collective-permute-done((bf16[32,2560]{1,0:T(8,128)(2,1)S(1)}, bf16[32,2560]{1,0:T(8,128)(2,1)S(1)}, u32[]{:S(2)}, u32[]{:S(2)}) %collective-permute-start.8) | collective-permute-done | bytes 163872 | tf_op jit(solution)/shard_map/ppermute | solution.py:27
  24.7 1.6 %collective-permute-start.9 = (bf16[32,2560]{1,0:T(8,128)(2,1)S(1)}, bf16[32,2560]{1,0:T(8,128)(2,1)}, u32[]{:S(2)}, u32[]{:S(2)}) collective-permute-start(bf16[32,2560]{1,0:T(8,128)(2,1)S(1)} %broadcast_select_fusion.2), channel_id=1, source_target_pairs={{0,2},{1,3},{2,0},{3,1},{4,6},{5,7},{6,4},{7,5},{8,10},{9,11},{10,... | collective-permute-start | bytes 491528 | tf_op jit(solution)/shard_map/ppermute | solution.py:37
  26.4 7.6 %collective-permute-done.9 = bf16[32,2560]{1,0:T(8,128)(2,1)} collective-permute-done((bf16[32,2560]{1,0:T(8,128)(2,1)S(1)}, bf16[32,2560]{1,0:T(8,128)(2,1)}, u32[]{:S(2)}, u32[]{:S(2)}) %collective-permute-start.9) | collective-permute-done | bytes 163872 | tf_op jit(solution)/shard_map/ppermute | solution.py:37
  34.0 0.9 %pad_maximum_fusion.1 = bf16[64,2560]{1,0:T(8,128)(2,1)S(1)} fusion(bf16[32,2560]{1,0:T(8,128)(2,1)} %collective-permute-done.9, bf16[32,2560]{1,0:T(8,128)(2,1)S(1)} %broadcast_select_fusion.2), kind=kLoop, calls=%fused_computation.2 | loop fusion | flops 655360 | bytes 655360 | tf_op jit(solution)/shard_map/concatenate | solution.py:38
  35.0 0.4 or_select_fusion
  35.5 0.6 %collective-permute-start.2 = (bf16[192,1280]{1,0:T(8,128)(2,1)}, bf16[192,1280]{1,0:T(8,128)(2,1)S(1)}, u32[]{:S(2)}, u32[]{:S(2)}) collective-permute-start(bf16[192,1280]{1,0:T(8,128)(2,1)} %collective-permute-done.1.refs_2_), channel_id=1, source_target_pairs={{0,1},{1,0},{2,3},{3,2},{4,5},{5,4},{6,7},{7,6},{8,9},{9,8},{10,11... | collective-permute-start | bytes 1474568 | tf_op jit(solution)/shard_map/ppermute | solution.py:140
  36.0 0.1 collective-permute-start.5
  36.1 0.5 collective-permute-done.10
  36.6 1.0 %pad_maximum_fusion = bf16[128,2560]{1,0:T(8,128)(2,1)S(1)} fusion(bf16[64,2560]{1,0:T(8,128)(2,1)S(1)} %collective-permute-done.10, bf16[32,2560]{1,0:T(8,128)(2,1)} %collective-permute-done.9, bf16[32,2560]{1,0:T(8,128)(2,1)S(1)} %broadcast_select_fusion.2), kind=kLoop, calls=%fused_computation.1 | loop fusion | flops 1966080 | bytes 1310720 | tf_op jit(solution)/shard_map/concatenate | solution.py:40
  37.7 0.7 %collective-permute-done.5.refs_7_ = bf16[192,1280]{1,0:T(8,128)(2,1)S(1)} collective-permute-done((bf16[192,1280]{1,0:T(8,128)(2,1)}, bf16[192,1280]{1,0:T(8,128)(2,1)S(1)}, u32[]{:S(2)}, u32[]{:S(2)}) %collective-permute-start.5) | collective-permute-done | bytes 491552 | tf_op jit(solution)/shard_map/ppermute | solution.py:140
  38.4 0.8 %copy-done.4 = bf16[192,1280]{1,0:T(8,128)(2,1)} copy-done((bf16[192,1280]{1,0:T(8,128)(2,1)}, bf16[192,1280]{1,0:T(8,128)(2,1)S(1)}, u32[]{:S(2)}) %copy-start.4) | copy-done | bytes 491544
  39.2 10.9 %shard_map.82 = bf16[192,1280]{1,0:T(8,128)(2,1)S(1)} custom-call(bf16[192,1280]{1,0:T(8,128)(2,1)S(1)} %copy-done.1, bf16[192,1280]{1,0:T(8,128)(2,1)S(1)} %copy-done.2, bf16[192,1280]{1,0:T(8,128)(2,1)} %collective-permute-done.refs_1_, bf16[192,1280]{1,0:T(8,128)(2,1)} %collective-permute-done.1.refs_2_, ...), custom_call_target="tpu_custom_call" | custom-call | flops 1761607680 | bytes 6258688 | tf_op jit(solution)/shard_map/pallas_call | solution.py:105
  50.1 1.6 %convolution_convert_fusion = bf16[192,1280]{1,0:T(8,128)(2,1)} fusion(bf16[192,1280]{1,0:T(8,128)(2,1)S(1)} %shard_map.82, bf16[1280,1280]{1,0:T(8,128)(2,1)S(1)} %copy-done), kind=kOutput, calls=%fused_computation | convolution fusion | flops 629391360 | bytes 4259840 | tf_op jit(solution)/shard_map/dot_general | solution.py:168
  (25 shorter events, 0.3 us)
Async XLA Ops:
  0.0 50.1 %copy-start = (bf16[1280,1280]{1,0:T(8,128)(2,1)S(1)}, bf16[1280,1280]{1,0:T(8,128)(2,1)}, u32[]{:S(2)}) copy-start(bf16[1280,1280]{1,0:T(8,128)(2,1)} %param.13) | copy-start | bytes 9830404
  1.9 11.8 %collective-permute-start.6 = (bf16[32,2560]{1,0:T(8,128)(2,1)S(1)}, bf16[32,2560]{1,0:T(8,128)(2,1)}, u32[]{:S(2)}, u32[]{:S(2)}) collective-permute-start(bf16[32,2560]{1,0:T(8,128)(2,1)S(1)} %constant_dynamic-update-slice_fusion), channel_id=1, source_target_pairs={{0,16},{4,20},{8,24},{12,28},{16,0},{20,4},{24,8},{28,12},{1,17},{... | collective-permute-start | bytes 491528 | tf_op jit(solution)/shard_map/ppermute | solution.py:27
  6.0 31.7 %collective-permute-start = (bf16[192,1280]{1,0:T(8,128)(2,1)}, bf16[192,1280]{1,0:T(8,128)(2,1)}, u32[]{:S(2)}, u32[]{:S(2)}) collective-permute-start(bf16[192,1280]{1,0:T(8,128)(2,1)} %refs_0_.1), channel_id=1, source_target_pairs={{0,1},{1,0},{2,3},{3,2},{4,5},{5,4},{6,7},{7,6},{8,9},{9,8},{10,11... | collective-permute-start | bytes 1474568 | tf_op jit(solution)/shard_map/ppermute | solution.py:139
  6.0 29.5 %collective-permute-start.1 = (bf16[192,1280]{1,0:T(8,128)(2,1)}, bf16[192,1280]{1,0:T(8,128)(2,1)}, u32[]{:S(2)}, u32[]{:S(2)}) collective-permute-start(bf16[192,1280]{1,0:T(8,128)(2,1)} %refs_0_.1), channel_id=1, source_target_pairs={{0,2},{1,3},{2,0},{3,1},{4,6},{5,7},{6,4},{7,5},{8,10},{9,11},{10,... | collective-permute-start | bytes 1474568 | tf_op jit(solution)/shard_map/ppermute | solution.py:138
  7.5 30.1 %collective-permute-start.3 = (bf16[192,1280]{1,0:T(8,128)(2,1)}, bf16[192,1280]{1,0:T(8,128)(2,1)}, u32[]{:S(2)}, u32[]{:S(2)}) collective-permute-start(bf16[192,1280]{1,0:T(8,128)(2,1)} %refs_4_.1), channel_id=1, source_target_pairs={{0,1},{1,0},{2,3},{3,2},{4,5},{5,4},{6,7},{7,6},{8,9},{9,8},{10,11... | collective-permute-start | bytes 1474568 | tf_op jit(solution)/shard_map/ppermute | solution.py:139
  7.7 28.3 %collective-permute-start.4 = (bf16[192,1280]{1,0:T(8,128)(2,1)}, bf16[192,1280]{1,0:T(8,128)(2,1)}, u32[]{:S(2)}, u32[]{:S(2)}) collective-permute-start(bf16[192,1280]{1,0:T(8,128)(2,1)} %refs_4_.1), channel_id=1, source_target_pairs={{0,2},{1,3},{2,0},{3,1},{4,6},{5,7},{6,4},{7,5},{8,10},{9,11},{10,... | collective-permute-start | bytes 1474568 | tf_op jit(solution)/shard_map/ppermute | solution.py:138
  13.8 5.5 %collective-permute-start.7 = (bf16[32,2560]{1,0:T(8,128)(2,1)S(1)}, bf16[32,2560]{1,0:T(8,128)(2,1)S(1)}, u32[]{:S(2)}, u32[]{:S(2)}) collective-permute-start(bf16[32,2560]{1,0:T(8,128)(2,1)S(1)} %broadcast_select_fusion), channel_id=1, source_target_pairs={{0,8},{4,12},{8,0},{12,4},{16,24},{20,28},{24,16},{28,20},{1,9},{5... | collective-permute-start | bytes 491528 | tf_op jit(solution)/shard_map/ppermute | solution.py:27
  19.3 5.4 %collective-permute-start.8 = (bf16[32,2560]{1,0:T(8,128)(2,1)S(1)}, bf16[32,2560]{1,0:T(8,128)(2,1)S(1)}, u32[]{:S(2)}, u32[]{:S(2)}) collective-permute-start(bf16[32,2560]{1,0:T(8,128)(2,1)S(1)} %broadcast_select_fusion.1), channel_id=1, source_target_pairs={{0,4},{4,0},{8,12},{12,8},{16,20},{20,16},{24,28},{28,24},{1,5},{5... | collective-permute-start | bytes 491528 | tf_op jit(solution)/shard_map/ppermute | solution.py:27
  24.7 9.2 %collective-permute-start.9 = (bf16[32,2560]{1,0:T(8,128)(2,1)S(1)}, bf16[32,2560]{1,0:T(8,128)(2,1)}, u32[]{:S(2)}, u32[]{:S(2)}) collective-permute-start(bf16[32,2560]{1,0:T(8,128)(2,1)S(1)} %broadcast_select_fusion.2), channel_id=1, source_target_pairs={{0,2},{1,3},{2,0},{3,1},{4,6},{5,7},{6,4},{7,5},{8,10},{9,11},{10,... | collective-permute-start | bytes 491528 | tf_op jit(solution)/shard_map/ppermute | solution.py:37
  34.9 1.7 %collective-permute-start.10 = (bf16[64,2560]{1,0:T(8,128)(2,1)S(1)}, bf16[64,2560]{1,0:T(8,128)(2,1)S(1)}, u32[]{:S(2)}, u32[]{:S(2)}) collective-permute-start(bf16[64,2560]{1,0:T(8,128)(2,1)S(1)} %pad_maximum_fusion.1), channel_id=1, source_target_pairs={{0,1},{1,0},{2,3},{3,2},{4,5},{5,4},{6,7},{7,6},{8,9},{9,8},{10,11... | collective-permute-start | bytes 983048 | tf_op jit(solution)/shard_map/ppermute | solution.py:39
  35.4 3.8 %copy-start.1 = (bf16[192,1280]{1,0:T(8,128)(2,1)S(1)}, bf16[192,1280]{1,0:T(8,128)(2,1)}, u32[]{:S(2)}) copy-start(bf16[192,1280]{1,0:T(8,128)(2,1)} %q_ref.1) | copy-start | bytes 1474564
  35.4 3.8 %copy-start.2 = (bf16[192,1280]{1,0:T(8,128)(2,1)S(1)}, bf16[192,1280]{1,0:T(8,128)(2,1)}, u32[]{:S(2)}) copy-start(bf16[192,1280]{1,0:T(8,128)(2,1)} %refs_0_.1) | copy-start | bytes 1474564
  35.4 3.8 %copy-start.3 = (bf16[192,1280]{1,0:T(8,128)(2,1)S(1)}, bf16[192,1280]{1,0:T(8,128)(2,1)}, u32[]{:S(2)}) copy-start(bf16[192,1280]{1,0:T(8,128)(2,1)} %refs_4_.1) | copy-start | bytes 1474564
  35.5 2.3 %collective-permute-start.2 = (bf16[192,1280]{1,0:T(8,128)(2,1)}, bf16[192,1280]{1,0:T(8,128)(2,1)S(1)}, u32[]{:S(2)}, u32[]{:S(2)}) collective-permute-start(bf16[192,1280]{1,0:T(8,128)(2,1)} %collective-permute-done.1.refs_2_), channel_id=1, source_target_pairs={{0,1},{1,0},{2,3},{3,2},{4,5},{5,4},{6,7},{7,6},{8,9},{9,8},{10,11... | collective-permute-start | bytes 1474568 | tf_op jit(solution)/shard_map/ppermute | solution.py:140
  36.0 2.4 %collective-permute-start.5 = (bf16[192,1280]{1,0:T(8,128)(2,1)}, bf16[192,1280]{1,0:T(8,128)(2,1)S(1)}, u32[]{:S(2)}, u32[]{:S(2)}) collective-permute-start(bf16[192,1280]{1,0:T(8,128)(2,1)} %collective-permute-done.4.refs_6_), channel_id=1, source_target_pairs={{0,1},{1,0},{2,3},{3,2},{4,5},{5,4},{6,7},{7,6},{8,9},{9,8},{10,11... | collective-permute-start | bytes 1474568 | tf_op jit(solution)/shard_map/ppermute | solution.py:140
  38.4 0.8 %copy-start.4 = (bf16[192,1280]{1,0:T(8,128)(2,1)}, bf16[192,1280]{1,0:T(8,128)(2,1)S(1)}, u32[]{:S(2)}) copy-start(bf16[192,1280]{1,0:T(8,128)(2,1)S(1)} %collective-permute-done.5.refs_7_) | copy-start | bytes 1474564

commit v8 on v4

--- a/solution.py
+++ b/solution.py
@@ -41,19 +41,40 @@
     return lax.all_gather(value, axis, axis=0, tiled=True)
 
 
-def attention_kernel(piece_count, pairs, q_ref, *refs):
+def attention_kernel(piece_count, pairs, has_state, final, q_ref, *refs):
     key_refs = refs[:piece_count]
     value_refs = refs[piece_count : 2 * piece_count]
     bias_refs = refs[2 * piece_count : 3 * piece_count]
-    rk_ref, rv_ref, out_ref = refs[3 * piece_count :]
+    rest = list(refs[3 * piece_count :])
+    if has_state:
+        m_in, t_in, acc_in = rest[:3]
+        rest = rest[3:]
+    if final:
+        rk_ref, rv_ref, out_ref = rest
+    else:
+        m_out, t_out, acc_out = rest
+    step = pl.program_id(0)
+    rows = q_ref.shape[0]
     lane = lax.broadcasted_iota(jnp.int32, (1, LANES), 1)
     dims = (((1,), (1,)), ((), ()))
+    per_pair = LANES // HEAD_DIM
+    if not final:
+
+        @pl.when(step == 0)
+        def _():
+            m_out[...] = jnp.zeros((rows, LANES), jnp.float32)
+            t_out[...] = jnp.zeros((rows, LANES), jnp.float32)
+
+    if has_state:
+        m_state = m_in[...]
+        t_state = t_in[...]
     for pair in range(pairs):
         cols = slice(pair * LANES, (pair + 1) * LANES)
         queries = q_ref[:, cols]
         results = []
-        for head in range(LANES // HEAD_DIM):
+        for head in range(per_pair):
             own = (lane // HEAD_DIM) == head
+            picked = lane == (step * pairs + pair) * per_pair + head
             q_head = jnp.where(own, queries, jnp.zeros_like(queries))
             scores = [
                 lax.dot_general(q_head, key_refs[p][:, cols], dims, preferred_element_type=jnp.float32)
@@ -61,9 +82,14 @@
                 + bias_refs[p][...]
                 for p in range(piece_count)
             ]
-            peak = jnp.max(scores[0], axis=1, keepdims=True)
-            for p in range(1, piece_count):
+            peak = jnp.full((rows, 1), -1e30, jnp.float32)
+            for p in range(piece_count):
                 peak = jnp.maximum(peak, jnp.max(scores[p], axis=1, keepdims=True))
+            if has_state:
+                m_old = jnp.sum(jnp.where(picked, m_state, 0.0), axis=1, keepdims=True)
+                t_old = jnp.sum(jnp.where(picked, t_state, 0.0), axis=1, keepdims=True)
+                peak = jnp.maximum(peak, m_old)
+                alpha = jnp.exp(m_old - peak)
             total = None
             summed = None
             for p in range(piece_count):
@@ -74,24 +100,35 @@
                 )
                 total = part_total if total is None else total + part_total
                 summed = part if summed is None else summed + part
-            view_part = summed / total
-            ref_scores = (
-                lax.dot_general(q_head, rk_ref[:, cols], dims, preferred_element_type=jnp.float32) * SCALE
-            )
-            ref_peak = jnp.max(ref_scores, axis=1, keepdims=True)
-            ref_weights = jnp.exp(ref_scores - ref_peak)
-            ref_total = jnp.sum(ref_weights, axis=1, keepdims=True)
-            ref_summed = jnp.dot(
-                ref_weights.astype(jnp.bfloat16), rv_ref[:, cols], preferred_element_type=jnp.float32
-            )
-            results.append((own, view_part + ref_summed / ref_total))
-        mixed = results[-1][1]
+            if has_state:
+                total = alpha * t_old + total
+                summed = alpha * acc_in[:, cols] + summed
+            if final:
+                ref_scores = (
+                    lax.dot_general(q_head, rk_ref[:, cols], dims, preferred_element_type=jnp.float32)
+                    * SCALE
+                )
+                ref_peak = jnp.max(ref_scores, axis=1, keepdims=True)
+                ref_weights = jnp.exp(ref_scores - ref_peak)
+                ref_total = jnp.sum(ref_weights, axis=1, keepdims=True)
+                ref_summed = jnp.dot(
+                    ref_weights.astype(jnp.bfloat16), rv_ref[:, cols], preferred_element_type=jnp.float32
+                )
+                results.append((own, summed / total + ref_summed / ref_total))
+            else:
+                m_out[...] = jnp.where(picked, peak, m_out[...])
+                t_out[...] = jnp.where(picked, total, t_out[...])
+                results.append((own, summed))
+        merged = results[-1][1]
         for own, value in results[:-1]:
-            mixed = jnp.where(own, value, mixed)
-        out_ref[:, cols] = mixed.astype(out_ref.dtype)
-
-
-def attention(queries, key_pieces, value_pieces, biases, ref_keys, ref_values, steps):
+            merged = jnp.where(own, value, merged)
+        if final:
+            out_ref[:, cols] = merged.astype(out_ref.dtype)
+        else:
+            acc_out[:, cols] = merged
+
+
+def attention(queries, key_pieces, value_pieces, biases, state, ref, steps):
     rows, width = queries.shape
     span = width // steps
     column = lambda j: (0, j)
@@ -100,23 +137,45 @@
     in_specs += [pl.BlockSpec((piece.shape[0], span), column) for piece in key_pieces]
     in_specs += [pl.BlockSpec((piece.shape[0], span), column) for piece in value_pieces]
     in_specs += [pl.BlockSpec(bias.shape, fixed) for bias in biases]
-    in_specs += [pl.BlockSpec((ref_keys.shape[0], span), column)] * 2
-    keys = sum(piece.shape[0] for piece in key_pieces) + ref_keys.shape[0]
+    operands = [queries, *key_pieces, *value_pieces, *biases]
+    keys = sum(piece.shape[0] for piece in key_pieces)
+    if state is not None:
+        in_specs += [pl.BlockSpec((rows, LANES), fixed)] * 2 + [pl.BlockSpec((rows, span), column)]
+        operands += list(state)
+    final = ref is not None
+    if final:
+        ref_keys, ref_values = ref
+        keys += ref_keys.shape[0]
+        in_specs += [pl.BlockSpec((ref_keys.shape[0], span), column)] * 2
+        operands += [ref_keys, ref_values]
+        out_specs = pl.BlockSpec((rows, span), column)
+        out_shape = jax.ShapeDtypeStruct((rows, width), jnp.bfloat16)
+    else:
+        out_specs = (
+            pl.BlockSpec((rows, LANES), fixed),
+            pl.BlockSpec((rows, LANES), fixed),
+            pl.BlockSpec((rows, span), column),
+        )
+        out_shape = (
+            jax.ShapeDtypeStruct((rows, LANES), jnp.float32),
+            jax.ShapeDtypeStruct((rows, LANES), jnp.float32),
+            jax.ShapeDtypeStruct((rows, width), jnp.float32),
+        )
     return pl.pallas_call(
-        functools.partial(attention_kernel, len(key_pieces), span // LANES),
+        functools.partial(attention_kernel, len(key_pieces), span // LANES, state is not None, final),
         grid=(steps,),
         in_specs=in_specs,
-        out_specs=pl.BlockSpec((rows, span), column),
-        out_shape=jax.ShapeDtypeStruct((rows, width), jnp.bfloat16),
+        out_specs=out_specs,
+        out_shape=out_shape,
         compiler_params=pltpu.CompilerParams(
             dimension_semantics=("arbitrary",), vmem_limit_bytes=48 * 1024 * 1024
         ),
         cost_estimate=pl.CostEstimate(
             flops=8 * rows * keys * width,
             transcendentals=2 * rows * keys * HEADS,
-            bytes_accessed=2 * (2 * rows + 2 * keys) * width + 4 * rows * keys,
+            bytes_accessed=2 * (2 * rows + 2 * keys) * width + 4 * rows * (keys + width),
         ),
-    )(queries, *key_pieces, *value_pieces, *biases, ref_keys, ref_values)
+    )(*operands)
 
 
 def key_bias(query_views, query_adjacent, position, rows, shard_rows, view_tok):
@@ -156,15 +215,14 @@
         for piece, position in zip(pieces, positions)
     ]
 
-    mixed = attention(
-        queries,
-        [piece[0] for piece in pieces],
-        [piece[1] for piece in pieces],
-        biases,
-        ref_all[:, :width],
-        ref_all[:, width:],
-        2,
-    )
+    ref = (ref_all[:, :width], ref_all[:, width:])
+    key_pieces = [piece[0] for piece in pieces]
+    value_pieces = [piece[1] for piece in pieces]
+    if view_count == 4:
+        state = attention(queries, key_pieces[:2], value_pieces[:2], biases[:2], None, None, 2)
+        mixed = attention(queries, key_pieces[2:], value_pieces[2:], biases[2:], state, ref, 2)
+    else:
+        mixed = attention(queries, key_pieces, value_pieces, biases, None, ref, 2)
     return jnp.dot(mixed, out_weight, preferred_element_type=jnp.float32).astype(jnp.bfloat16)
 
 

time: 50.8 us -> 54.9 us (1.081)
  Pallas kernels: 10.9 us -> 17 us
  waiting for transfers between devices: 19 us -> 17.4 us
  local copies, waits for them, and re-layouts: 2.78 us -> 2.01 us
    pallas_call x1 -> x2, Pallas kernels: 10.9 us -> 17 us  [attention(): pl.pallas_call(functools.partial(attention_kernel, len(key_pieces), span...]
    ppermute x1, waiting for transfers between devices: 7.57 us -> 6.79 us  [gather_rows(): across = lax.ppermute(value, axis, [(i, i ^ 2) for i in range(count)])]
    unnamed x11 -> x9, local copies, waits for them, and re-layouts: 1.84 us -> 1.07 us
    ppermute x2, waiting for transfers between devices: 0.78 us -> 0.01 us  [body(): far = lax.ppermute(across, 'view', [(i, i ^ 1) for i in range(view_count)])]
  transfers between devices with their start and end apart: 11 -> 11, of which waited for: 7 -> 4; matrix products, arithmetic and copies ran while one was open for 7% -> 6% of each run, Pallas kernels for 0% -> 9%
where the time goes in v8:
time: 54.9 us; the launch traced here: 54.7 us
  waiting for transfers between devices  17.4 us (32%)
  Pallas kernels  17 us (31%)
  starting transfers between devices  12.5 us (23%)
  matrix products  2.48 us (5%)
  other arithmetic  2.4 us (4%)
  local copies, waits for them, and re-layouts  2.01 us (4%)
  between operations  0.9 us (2%)
    pallas_call x2, Pallas kernels, attention(): pl.pallas_call(functools.partial(attention_kernel, len(key_pieces), span...  17 us
    ppermute x3, waiting for transfers between devices, tree_broadcast(): received = lax.ppermute(value, axis, pairs)  10.6 us
    ppermute x3, starting transfers between devices, tree_broadcast(): received = lax.ppermute(value, axis, pairs)  7.9 us
    ppermute x1, waiting for transfers between devices, gather_rows(): across = lax.ppermute(value, axis, [(i, i ^ 2) for i in range(count)])  6.79 us
    ppermute x2, starting transfers between devices, body(): lax.ppermute((keys, values), 'view', [(i, i ^ 2) for i in range(view_coun...  2.03 us
    dot_general x1, matrix products, body(): jnp.dot(mixed, out_weight, preferred_element_type=jnp.float32)  1.59 us
    ppermute x1, starting transfers between devices, gather_rows(): across = lax.ppermute(value, axis, [(i, i ^ 2) for i in range(count)])  1.58 us
  transfers between devices with their start and end apart: 11, of which 4 were waited for; matrix products, arithmetic and copies ran while one was open for 6% of the time, Pallas kernels for 9%

profile of v8, /device:TPU:0, one launch (start us, length us, event | category | flops | bytes accessed | tf_op | source)
XLA Modules:
  0.0 54.7 jit_solution(17947783070692487242)
XLA Ops:
  0.0 1.0 %constant_dynamic-update-slice_fusion.1 = bf16[32,2560]{1,0:T(8,128)(2,1)S(1)} fusion(bf16[32,1280]{1,0:T(8,128)(2,1)} %param.11), kind=kLoop, calls=%fused_computation.14 | loop fusion | bytes 163840
  1.0 0.9 %constant_dynamic-update-slice_fusion = bf16[32,2560]{1,0:T(8,128)(2,1)S(1)} fusion(bf16[32,2560]{1,0:T(8,128)(2,1)S(1)} %constant_dynamic-update-slice_fusion.1, bf16[32,1280]{1,0:T(8,128)(2,1)} %param.12), kind=kLoop, calls=%fused_computation.13 | loop fusion | bytes 163840 | tf_op jit(solution)/shard_map/concatenate | solution.py:206
  1.9 2.9 %collective-permute-start.6 = (bf16[32,2560]{1,0:T(8,128)(2,1)S(1)}, bf16[32,2560]{1,0:T(8,128)(2,1)}, u32[]{:S(2)}, u32[]{:S(2)}) collective-permute-start(bf16[32,2560]{1,0:T(8,128)(2,1)S(1)} %constant_dynamic-update-slice_fusion), channel_id=1, source_target_pairs={{0,4},{4,0},{8,12},{12,8},{16,20},{20,16},{24,28},{28,24},{1,5},{5... | collective-permute-start | bytes 491528 | tf_op jit(solution)/shard_map/ppermute | solution.py:27
  4.9 1.5 %collective-permute-start = (bf16[192,1280]{1,0:T(8,128)(2,1)}, bf16[192,1280]{1,0:T(8,128)(2,1)}, u32[]{:S(2)}, u32[]{:S(2)}) collective-permute-start(bf16[192,1280]{1,0:T(8,128)(2,1)} %refs_0_.1), channel_id=1, source_target_pairs={{0,2},{1,3},{2,0},{3,1},{4,6},{5,7},{6,4},{7,5},{8,10},{9,11},{10,... | collective-permute-start | bytes 1474568 | tf_op jit(solution)/shard_map/ppermute | solution.py:197
  6.4 0.2 collective-permute-start.5
  6.6 0.5 collective-permute-start.2
  7.9 1.3 %collective-permute-done.6 = bf16[32,2560]{1,0:T(8,128)(2,1)} collective-permute-done((bf16[32,2560]{1,0:T(8,128)(2,1)S(1)}, bf16[32,2560]{1,0:T(8,128)(2,1)}, u32[]{:S(2)}, u32[]{:S(2)}) %collective-permute-start.6) | collective-permute-done | bytes 163872 | tf_op jit(solution)/shard_map/ppermute | solution.py:27
  9.2 2.8 %collective-permute-start.7 = (bf16[32,2560]{1,0:T(8,128)(2,1)S(1)}, bf16[32,2560]{1,0:T(8,128)(2,1)S(1)}, u32[]{:S(2)}, u32[]{:S(2)}) collective-permute-start(bf16[32,2560]{1,0:T(8,128)(2,1)S(1)} %broadcast_select_fusion), channel_id=1, source_target_pairs={{0,8},{4,12},{8,0},{12,4},{16,24},{20,28},{24,16},{28,20},{1,9},{5... | collective-permute-start | bytes 491528 | tf_op jit(solution)/shard_map/ppermute | solution.py:27
  12.0 0.9 %fusion = f32[192,3]{0,1:T(4,128)S(1)} fusion(s32[192]{0:T(256)S(1)} %get-tuple-element.20, s32[6,3]{0,1:T(4,128)} %param.14), kind=kOutput, calls=%fused_computation.11 | convolution fusion | flops 8082 | bytes 3144 | tf_op jit(solution)/shard_map/dot_general | solution.py:212
  12.9 2.4 %collective-permute-done.7 = bf16[32,2560]{1,0:T(8,128)(2,1)S(1)} collective-permute-done((bf16[32,2560]{1,0:T(8,128)(2,1)S(1)}, bf16[32,2560]{1,0:T(8,128)(2,1)S(1)}, u32[]{:S(2)}, u32[]{:S(2)}) %collective-permute-start.7) | collective-permute-done | bytes 163872 | tf_op jit(solution)/shard_map/ppermute | solution.py:27
  15.4 2.2 %collective-permute-start.8 = (bf16[32,2560]{1,0:T(8,128)(2,1)S(1)}, bf16[32,2560]{1,0:T(8,128)(2,1)S(1)}, u32[]{:S(2)}, u32[]{:S(2)}) collective-permute-start(bf16[32,2560]{1,0:T(8,128)(2,1)S(1)} %broadcast_select_fusion.1), channel_id=1, source_target_pairs={{0,16},{4,20},{8,24},{12,28},{16,0},{20,4},{24,8},{28,12},{1,17},{... | collective-permute-start | bytes 491528 | tf_op jit(solution)/shard_map/ppermute | solution.py:27
  17.5 6.9 %collective-permute-done.8 = bf16[32,2560]{1,0:T(8,128)(2,1)S(1)} collective-permute-done((bf16[32,2560]{1,0:T(8,128)(2,1)S(1)}, bf16[32,2560]{1,0:T(8,128)(2,1)S(1)}, u32[]{:S(2)}, u32[]{:S(2)}) %collective-permute-start.8) | collective-permute-done | bytes 163872 | tf_op jit(solution)/shard_map/ppermute | solution.py:27
  24.4 1.6 %collective-permute-start.9 = (bf16[32,2560]{1,0:T(8,128)(2,1)S(1)}, bf16[32,2560]{1,0:T(8,128)(2,1)}, u32[]{:S(2)}, u32[]{:S(2)}) collective-permute-start(bf16[32,2560]{1,0:T(8,128)(2,1)S(1)} %broadcast_select_fusion.2), channel_id=1, source_target_pairs={{0,2},{1,3},{2,0},{3,1},{4,6},{5,7},{6,4},{7,5},{8,10},{9,11},{10,... | collective-permute-start | bytes 491528 | tf_op jit(solution)/shard_map/ppermute | solution.py:37
  26.1 0.0 copy-start.3
  26.1 6.8 %collective-permute-done.9 = bf16[32,2560]{1,0:T(8,128)(2,1)} collective-permute-done((bf16[32,2560]{1,0:T(8,128)(2,1)S(1)}, bf16[32,2560]{1,0:T(8,128)(2,1)}, u32[]{:S(2)}, u32[]{:S(2)}) %collective-permute-start.9) | collective-permute-done | bytes 163872 | tf_op jit(solution)/shard_map/ppermute | solution.py:37
  32.9 0.9 %pad_maximum_fusion.1 = bf16[64,2560]{1,0:T(8,128)(2,1)S(1)} fusion(bf16[32,2560]{1,0:T(8,128)(2,1)} %collective-permute-done.9, bf16[32,2560]{1,0:T(8,128)(2,1)S(1)} %broadcast_select_fusion.2), kind=kLoop, calls=%fused_computation.2 | loop fusion | flops 655360 | bytes 655360 | tf_op jit(solution)/shard_map/concatenate | solution.py:38
  33.8 0.1 collective-permute-start.10
  33.9 0.4 or_select_fusion
  34.3 0.6 %collective-permute-start.1 = (bf16[192,1280]{1,0:T(8,128)(2,1)}, bf16[192,1280]{1,0:T(8,128)(2,1)S(1)}, u32[]{:S(2)}, u32[]{:S(2)}) collective-permute-start(bf16[192,1280]{1,0:T(8,128)(2,1)} %collective-permute-done.refs_0_), channel_id=1, source_target_pairs={{0,1},{1,0},{2,3},{3,2},{4,5},{5,4},{6,7},{7,6},{8,9},{9,8},{10,11... | collective-permute-start | bytes 1474568 | tf_op jit(solution)/shard_map/ppermute | solution.py:199
  34.9 0.1 collective-permute-start.3
  35.0 4.7 %shard_map.82 = (f32[192,128]{1,0:T(8,128)S(1)}, f32[192,128]{1,0:T(8,128)S(1)}, f32[192,1280]{1,0:T(8,128)S(1)}) custom-call(bf16[192,1280]{1,0:T(8,128)(2,1)S(1)} %copy-done.3, bf16[192,1280]{1,0:T(8,128)(2,1)S(1)} %copy-done.1, bf16[192,1280]{1,0:T(8,128)(2,1)} %collective-permute-done.4.refs_1_, bf16[192,1280]{1,0:T(8,128)(2,1)S(1)} %copy-done.2, ...), custom_call_target="tpu_custom_call" | custom-call | flops 754974720 | bytes 4227072 | tf_op jit(solution)/shard_map/pallas_call | solution.py:164
  39.7 1.0 %pad_maximum_fusion = bf16[128,2560]{1,0:T(8,128)(2,1)S(1)} fusion(bf16[64,2560]{1,0:T(8,128)(2,1)S(1)} %collective-permute-done.10, bf16[32,2560]{1,0:T(8,128)(2,1)} %collective-permute-done.9, bf16[32,2560]{1,0:T(8,128)(2,1)S(1)} %broadcast_select_fusion.2), kind=kLoop, calls=%fused_computation.1 | loop fusion | flops 1966080 | bytes 1310720 | tf_op jit(solution)/shard_map/concatenate | solution.py:40
  40.8 12.3 %shard_map.83 = bf16[192,1280]{1,0:T(8,128)(2,1)S(1)} custom-call(bf16[192,1280]{1,0:T(8,128)(2,1)S(1)} %copy-done.3, bf16[192,1280]{1,0:T(8,128)(2,1)} %collective-permute-done.refs_0_, bf16[192,1280]{1,0:T(8,128)(2,1)S(1)} %collective-permute-done.1.refs_1_, bf16[192,1280]{1,0:T(8,128)(2,1)} %collective-permute-done.2.refs_2_, ...), custom_call_target="tpu_custom_call" | custom-call | flops 1006632960 | bytes 4980736 | tf_op jit(solution)/shard_map/pallas_call | solution.py:164
  53.1 1.6 %convolution_convert_fusion = bf16[192,1280]{1,0:T(8,128)(2,1)} fusion(bf16[192,1280]{1,0:T(8,128)(2,1)S(1)} %shard_map.83, bf16[1280,1280]{1,0:T(8,128)(2,1)S(1)} %copy-done), kind=kOutput, calls=%fused_computation | convolution fusion | flops 629391360 | bytes 4259840 | tf_op jit(solution)/shard_map/dot_general | solution.py:226
  (24 shorter events, 0.2 us)
Async XLA Ops:
  0.0 53.1 %copy-start = (bf16[1280,1280]{1,0:T(8,128)(2,1)S(1)}, bf16[1280,1280]{1,0:T(8,128)(2,1)}, u32[]{:S(2)}) copy-start(bf16[1280,1280]{1,0:T(8,128)(2,1)} %param.13) | copy-start | bytes 9830404
  1.9 7.2 %collective-permute-start.6 = (bf16[32,2560]{1,0:T(8,128)(2,1)S(1)}, bf16[32,2560]{1,0:T(8,128)(2,1)}, u32[]{:S(2)}, u32[]{:S(2)}) collective-permute-start(bf16[32,2560]{1,0:T(8,128)(2,1)S(1)} %constant_dynamic-update-slice_fusion), channel_id=1, source_target_pairs={{0,4},{4,0},{8,12},{12,8},{16,20},{20,16},{24,28},{28,24},{1,5},{5... | collective-permute-start | bytes 491528 | tf_op jit(solution)/shard_map/ppermute | solution.py:27
  4.9 30.1 %collective-permute-start.4 = (bf16[192,1280]{1,0:T(8,128)(2,1)}, bf16[192,1280]{1,0:T(8,128)(2,1)}, u32[]{:S(2)}, u32[]{:S(2)}) collective-permute-start(bf16[192,1280]{1,0:T(8,128)(2,1)} %refs_0_.1), channel_id=1, source_target_pairs={{0,1},{1,0},{2,3},{3,2},{4,5},{5,4},{6,7},{7,6},{8,9},{9,8},{10,11... | collective-permute-start | bytes 1474568 | tf_op jit(solution)/shard_map/ppermute | solution.py:198
  4.9 29.4 %collective-permute-start = (bf16[192,1280]{1,0:T(8,128)(2,1)}, bf16[192,1280]{1,0:T(8,128)(2,1)}, u32[]{:S(2)}, u32[]{:S(2)}) collective-permute-start(bf16[192,1280]{1,0:T(8,128)(2,1)} %refs_0_.1), channel_id=1, source_target_pairs={{0,2},{1,3},{2,0},{3,1},{4,6},{5,7},{6,4},{7,5},{8,10},{9,11},{10,... | collective-permute-start | bytes 1474568 | tf_op jit(solution)/shard_map/ppermute | solution.py:197
  6.4 28.6 %collective-permute-start.5 = (bf16[192,1280]{1,0:T(8,128)(2,1)}, bf16[192,1280]{1,0:T(8,128)(2,1)}, u32[]{:S(2)}, u32[]{:S(2)}) collective-permute-start(bf16[192,1280]{1,0:T(8,128)(2,1)} %refs_2_.1), channel_id=1, source_target_pairs={{0,1},{1,0},{2,3},{3,2},{4,5},{5,4},{6,7},{7,6},{8,9},{9,8},{10,11... | collective-permute-start | bytes 1474568 | tf_op jit(solution)/shard_map/ppermute | solution.py:198
  6.6 28.3 %collective-permute-start.2 = (bf16[192,1280]{1,0:T(8,128)(2,1)}, bf16[192,1280]{1,0:T(8,128)(2,1)}, u32[]{:S(2)}, u32[]{:S(2)}) collective-permute-start(bf16[192,1280]{1,0:T(8,128)(2,1)} %refs_2_.1), channel_id=1, source_target_pairs={{0,2},{1,3},{2,0},{3,1},{4,6},{5,7},{6,4},{7,5},{8,10},{9,11},{10,... | collective-permute-start | bytes 1474568 | tf_op jit(solution)/shard_map/ppermute | solution.py:197
  9.2 6.1 %collective-permute-start.7 = (bf16[32,2560]{1,0:T(8,128)(2,1)S(1)}, bf16[32,2560]{1,0:T(8,128)(2,1)S(1)}, u32[]{:S(2)}, u32[]{:S(2)}) collective-permute-start(bf16[32,2560]{1,0:T(8,128)(2,1)S(1)} %broadcast_select_fusion), channel_id=1, source_target_pairs={{0,8},{4,12},{8,0},{12,4},{16,24},{20,28},{24,16},{28,20},{1,9},{5... | collective-permute-start | bytes 491528 | tf_op jit(solution)/shard_map/ppermute | solution.py:27
  15.4 9.0 %collective-permute-start.8 = (bf16[32,2560]{1,0:T(8,128)(2,1)S(1)}, bf16[32,2560]{1,0:T(8,128)(2,1)S(1)}, u32[]{:S(2)}, u32[]{:S(2)}) collective-permute-start(bf16[32,2560]{1,0:T(8,128)(2,1)S(1)} %broadcast_select_fusion.1), channel_id=1, source_target_pairs={{0,16},{4,20},{8,24},{12,28},{16,0},{20,4},{24,8},{28,12},{1,17},{... | collective-permute-start | bytes 491528 | tf_op jit(solution)/shard_map/ppermute | solution.py:27
  24.4 8.4 %collective-permute-start.9 = (bf16[32,2560]{1,0:T(8,128)(2,1)S(1)}, bf16[32,2560]{1,0:T(8,128)(2,1)}, u32[]{:S(2)}, u32[]{:S(2)}) collective-permute-start(bf16[32,2560]{1,0:T(8,128)(2,1)S(1)} %broadcast_select_fusion.2), channel_id=1, source_target_pairs={{0,2},{1,3},{2,0},{3,1},{4,6},{5,7},{6,4},{7,5},{8,10},{9,11},{10,... | collective-permute-start | bytes 491528 | tf_op jit(solution)/shard_map/ppermute | solution.py:37
  26.0 9.0 %copy-start.1 = (bf16[192,1280]{1,0:T(8,128)(2,1)S(1)}, bf16[192,1280]{1,0:T(8,128)(2,1)}, u32[]{:S(2)}) copy-start(bf16[192,1280]{1,0:T(8,128)(2,1)} %refs_0_.1) | copy-start | bytes 1474564
  26.0 8.9 %copy-start.2 = (bf16[192,1280]{1,0:T(8,128)(2,1)S(1)}, bf16[192,1280]{1,0:T(8,128)(2,1)}, u32[]{:S(2)}) copy-start(bf16[192,1280]{1,0:T(8,128)(2,1)} %refs_2_.1) | copy-start | bytes 1474564
  26.1 8.9 %copy-start.3 = (bf16[192,1280]{1,0:T(8,128)(2,1)S(1)}, bf16[192,1280]{1,0:T(8,128)(2,1)}, u32[]{:S(2)}) copy-start(bf16[192,1280]{1,0:T(8,128)(2,1)} %q_ref.3) | copy-start | bytes 1474564
  33.8 5.9 %collective-permute-start.10 = (bf16[64,2560]{1,0:T(8,128)(2,1)S(1)}, bf16[64,2560]{1,0:T(8,128)(2,1)S(1)}, u32[]{:S(2)}, u32[]{:S(2)}) collective-permute-start(bf16[64,2560]{1,0:T(8,128)(2,1)S(1)} %pad_maximum_fusion.1), channel_id=1, source_target_pairs={{0,1},{1,0},{2,3},{3,2},{4,5},{5,4},{6,7},{7,6},{8,9},{9,8},{10,11... | collective-permute-start | bytes 983048 | tf_op jit(solution)/shard_map/ppermute | solution.py:39
  34.3 6.4 %collective-permute-start.1 = (bf16[192,1280]{1,0:T(8,128)(2,1)}, bf16[192,1280]{1,0:T(8,128)(2,1)S(1)}, u32[]{:S(2)}, u32[]{:S(2)}) collective-permute-start(bf16[192,1280]{1,0:T(8,128)(2,1)} %collective-permute-done.refs_0_), channel_id=1, source_target_pairs={{0,1},{1,0},{2,3},{3,2},{4,5},{5,4},{6,7},{7,6},{8,9},{9,8},{10,11... | collective-permute-start | bytes 1474568 | tf_op jit(solution)/shard_map/ppermute | solution.py:199
  34.9 5.9 %collective-permute-start.3 = (bf16[192,1280]{1,0:T(8,128)(2,1)}, bf16[192,1280]{1,0:T(8,128)(2,1)S(1)}, u32[]{:S(2)}, u32[]{:S(2)}) collective-permute-start(bf16[192,1280]{1,0:T(8,128)(2,1)} %collective-permute-done.2.refs_2_), channel_id=1, source_target_pairs={{0,1},{1,0},{2,3},{3,2},{4,5},{5,4},{6,7},{7,6},{8,9},{9,8},{10,11... | collective-permute-start | bytes 1474568 | tf_op jit(solution)/shard_map/ppermute | solution.py:199

commit v9 on v4

--- a/solution.py
+++ b/solution.py
@@ -44,36 +44,27 @@
 def attention_kernel(piece_count, pairs, q_ref, *refs):
     key_refs = refs[:piece_count]
     value_refs = refs[piece_count : 2 * piece_count]
-    bias_refs = refs[2 * piece_count : 3 * piece_count]
-    rk_ref, rv_ref, out_ref = refs[3 * piece_count :]
+    bias_refs = refs[2 * piece_count : 2 * piece_count + 1]
+    rk_ref, rv_ref, out_ref = refs[2 * piece_count + 1 :]
     lane = lax.broadcasted_iota(jnp.int32, (1, LANES), 1)
     dims = (((1,), (1,)), ((), ()))
     for pair in range(pairs):
         cols = slice(pair * LANES, (pair + 1) * LANES)
         queries = q_ref[:, cols]
         results = []
+        keys = jnp.concatenate([key_refs[p][:, cols] for p in range(piece_count)], axis=0)
+        values = jnp.concatenate([value_refs[p][:, cols] for p in range(piece_count)], axis=0)
+        bias = bias_refs[0][...]
         for head in range(LANES // HEAD_DIM):
             own = (lane // HEAD_DIM) == head
             q_head = jnp.where(own, queries, jnp.zeros_like(queries))
-            scores = [
-                lax.dot_general(q_head, key_refs[p][:, cols], dims, preferred_element_type=jnp.float32)
-                * SCALE
-                + bias_refs[p][...]
-                for p in range(piece_count)
-            ]
-            peak = jnp.max(scores[0], axis=1, keepdims=True)
-            for p in range(1, piece_count):
-                peak = jnp.maximum(peak, jnp.max(scores[p], axis=1, keepdims=True))
-            total = None
-            summed = None
-            for p in range(piece_count):
-                weights = jnp.exp(scores[p] - peak)
-                part_total = jnp.sum(weights, axis=1, keepdims=True)
-                part = jnp.dot(
-                    weights.astype(jnp.bfloat16), value_refs[p][:, cols], preferred_element_type=jnp.float32
-                )
-                total = part_total if total is None else total + part_total
-                summed = part if summed is None else summed + part
+            scores = (
+                lax.dot_general(q_head, keys, dims, preferred_element_type=jnp.float32) * SCALE + bias
+            )
+            peak = jnp.max(scores, axis=1, keepdims=True)
+            weights = jnp.exp(scores - peak)
+            total = jnp.sum(weights, axis=1, keepdims=True)
+            summed = jnp.dot(weights.astype(jnp.bfloat16), values, preferred_element_type=jnp.float32)
             view_part = summed / total
             ref_scores = (
                 lax.dot_general(q_head, rk_ref[:, cols], dims, preferred_element_type=jnp.float32) * SCALE
@@ -152,8 +143,13 @@
     query_onehot = (query_views[:, None] == view_ids[None, :]).astype(jnp.float32)
     query_adjacent = jnp.dot(query_onehot, adjacency.astype(jnp.float32))
     biases = [
-        key_bias(query_views, query_adjacent, position, piece[0].shape[0], shard_rows, view_tok)
-        for piece, position in zip(pieces, positions)
+        jnp.concatenate(
+            [
+                key_bias(query_views, query_adjacent, position, piece[0].shape[0], shard_rows, view_tok)
+                for piece, position in zip(pieces, positions)
+            ],
+            axis=1,
+        )
     ]
 
     mixed = attention(

time: 50.8 us -> 51 us (level)
  waiting for transfers between devices: 19 us -> 17.2 us
  Pallas kernels: 10.9 us -> 12.6 us
  other arithmetic: 2.4 us -> 3.52 us
  local copies, waits for them, and re-layouts: 2.78 us -> 2.01 us
    ppermute x1, waiting for transfers between devices: 7.57 us -> 5.59 us  [gather_rows(): across = lax.ppermute(value, axis, [(i, i ^ 2) for i in range(count)])]
    pallas_call x1, Pallas kernels: 10.9 us -> 12.6 us  [attention(): pl.pallas_call(functools.partial(attention_kernel, len(key_pieces), span...]
    select_n x3, other arithmetic: 0.06 us -> 0.98 us  [tree_broadcast(): value = jnp.where(partner_has, received, value)]
    unnamed x11, local copies, waits for them, and re-layouts: 1.84 us -> 1.07 us
  transfers between devices with their start and end apart: 11 -> 11, of which waited for: 7 -> 7; matrix products, arithmetic and copies ran while one was open for 7% -> 9% of each run, Pallas kernels for 0% -> 0%
where the time goes in v9:
time: 51 us; the launch traced here: 50.8 us
  waiting for transfers between devices  17.2 us (34%)
  Pallas kernels  12.6 us (25%)
  starting transfers between devices  12.2 us (24%)
  other arithmetic  3.52 us (7%)
  matrix products  2.48 us (5%)
  local copies, waits for them, and re-layouts  2.01 us (4%)
  between operations  0.85 us (2%)
    pallas_call x1, Pallas kernels, attention(): pl.pallas_call(functools.partial(attention_kernel, len(key_pieces), span...  12.6 us
    ppermute x3, waiting for transfers between devices, tree_broadcast(): received = lax.ppermute(value, axis, pairs)  10.3 us
    ppermute x3, starting transfers between devices, tree_broadcast(): received = lax.ppermute(value, axis, pairs)  7.67 us
    ppermute x1, waiting for transfers between devices, gather_rows(): across = lax.ppermute(value, axis, [(i, i ^ 2) for i in range(count)])  5.59 us
    ppermute x2, starting transfers between devices, body(): lax.ppermute((keys, values), 'view', [(i, i ^ 2) for i in range(view_coun...  2.03 us
    dot_general x1, matrix products, body(): jnp.dot(mixed, out_weight, preferred_element_type=jnp.float32)  1.59 us
    ppermute x1, starting transfers between devices, gather_rows(): across = lax.ppermute(value, axis, [(i, i ^ 2) for i in range(count)])  1.52 us
    unnamed x11, local copies, waits for them, and re-layouts  1.07 us
  transfers between devices with their start and end apart: 11, of which 7 were waited for; matrix products, arithmetic and copies ran while one was open for 9% of the time, Pallas kernels for 0%

profile of v9, /device:TPU:0, one launch (start us, length us, event | category | flops | bytes accessed | tf_op | source)
XLA Modules:
  0.0 50.8 jit_solution(1325688009469404913)
XLA Ops:
  0.0 1.0 %constant_dynamic-update-slice_fusion.1 = bf16[32,2560]{1,0:T(8,128)(2,1)S(1)} fusion(bf16[32,1280]{1,0:T(8,128)(2,1)} %param.11), kind=kLoop, calls=%fused_computation.15 | loop fusion | bytes 163840
  1.0 0.9 %constant_dynamic-update-slice_fusion = bf16[32,2560]{1,0:T(8,128)(2,1)S(1)} fusion(bf16[32,2560]{1,0:T(8,128)(2,1)S(1)} %constant_dynamic-update-slice_fusion.1, bf16[32,1280]{1,0:T(8,128)(2,1)} %param.12), kind=kLoop, calls=%fused_computation.14 | loop fusion | bytes 163840 | tf_op jit(solution)/shard_map/concatenate | solution.py:138
  1.9 2.9 %collective-permute-start.6 = (bf16[32,2560]{1,0:T(8,128)(2,1)S(1)}, bf16[32,2560]{1,0:T(8,128)(2,1)}, u32[]{:S(2)}, u32[]{:S(2)}) collective-permute-start(bf16[32,2560]{1,0:T(8,128)(2,1)S(1)} %constant_dynamic-update-slice_fusion), channel_id=1, source_target_pairs={{0,4},{4,0},{8,12},{12,8},{16,20},{20,16},{24,28},{28,24},{1,5},{5... | collective-permute-start | bytes 491528 | tf_op jit(solution)/shard_map/ppermute | solution.py:27
  4.9 1.5 %collective-permute-start.1 = (bf16[192,1280]{1,0:T(8,128)(2,1)}, bf16[192,1280]{1,0:T(8,128)(2,1)}, u32[]{:S(2)}, u32[]{:S(2)}) collective-permute-start(bf16[192,1280]{1,0:T(8,128)(2,1)} %refs_0_.1), channel_id=1, source_target_pairs={{0,2},{1,3},{2,0},{3,1},{4,6},{5,7},{6,4},{7,5},{8,10},{9,11},{10,... | collective-permute-start | bytes 1474568 | tf_op jit(solution)/shard_map/ppermute | solution.py:129
  6.4 0.5 collective-permute-start.4
  6.9 0.2 collective-permute-start.3
  7.9 1.3 %collective-permute-done.6 = bf16[32,2560]{1,0:T(8,128)(2,1)} collective-permute-done((bf16[32,2560]{1,0:T(8,128)(2,1)S(1)}, bf16[32,2560]{1,0:T(8,128)(2,1)}, u32[]{:S(2)}, u32[]{:S(2)}) %collective-permute-start.6) | collective-permute-done | bytes 163872 | tf_op jit(solution)/shard_map/ppermute | solution.py:27
  9.2 1.9 %collective-permute-start.7 = (bf16[32,2560]{1,0:T(8,128)(2,1)S(1)}, bf16[32,2560]{1,0:T(8,128)(2,1)S(1)}, u32[]{:S(2)}, u32[]{:S(2)}) collective-permute-start(bf16[32,2560]{1,0:T(8,128)(2,1)S(1)} %broadcast_select_fusion), channel_id=1, source_target_pairs={{0,8},{4,12},{8,0},{12,4},{16,24},{20,28},{24,16},{28,20},{1,9},{5... | collective-permute-start | bytes 491528 | tf_op jit(solution)/shard_map/ppermute | solution.py:27
  11.1 0.9 %fusion = f32[192,3]{0,1:T(4,128)S(1)} fusion(s32[192]{0:T(256)S(1)} %get-tuple-element.14, s32[6,3]{0,1:T(4,128)} %param.14), kind=kOutput, calls=%fused_computation.12 | convolution fusion | flops 8082 | bytes 3144 | tf_op jit(solution)/shard_map/dot_general | solution.py:144
  12.0 2.7 %collective-permute-done.7 = bf16[32,2560]{1,0:T(8,128)(2,1)S(1)} collective-permute-done((bf16[32,2560]{1,0:T(8,128)(2,1)S(1)}, bf16[32,2560]{1,0:T(8,128)(2,1)S(1)}, u32[]{:S(2)}, u32[]{:S(2)}) %collective-permute-start.7) | collective-permute-done | bytes 163872 | tf_op jit(solution)/shard_map/ppermute | solution.py:27
  14.7 2.8 %collective-permute-start.8 = (bf16[32,2560]{1,0:T(8,128)(2,1)S(1)}, bf16[32,2560]{1,0:T(8,128)(2,1)}, u32[]{:S(2)}, u32[]{:S(2)}) collective-permute-start(bf16[32,2560]{1,0:T(8,128)(2,1)S(1)} %broadcast_select_fusion.1), channel_id=1, source_target_pairs={{0,16},{4,20},{8,24},{12,28},{16,0},{20,4},{24,8},{28,12},{1,17},{... | collective-permute-start | bytes 491528 | tf_op jit(solution)/shard_map/ppermute | solution.py:27
  17.6 6.3 %collective-permute-done.8 = bf16[32,2560]{1,0:T(8,128)(2,1)} collective-permute-done((bf16[32,2560]{1,0:T(8,128)(2,1)S(1)}, bf16[32,2560]{1,0:T(8,128)(2,1)}, u32[]{:S(2)}, u32[]{:S(2)}) %collective-permute-start.8) | collective-permute-done | bytes 163872 | tf_op jit(solution)/shard_map/ppermute | solution.py:27
  23.8 0.9 %broadcast_select_fusion.2 = bf16[32,2560]{1,0:T(8,128)(2,1)S(1)} fusion(bf16[32,2560]{1,0:T(8,128)(2,1)} %collective-permute-done.8, bf16[32,2560]{1,0:T(8,128)(2,1)} %copy-done.4, pred[]{:T(512)S(6)} %eq.108), kind=kLoop, calls=%fused_computation.10 | loop fusion | flops 81920 | bytes 491521 | tf_op jit(solution)/shard_map/jit(_where)/select_n | solution.py:29
  24.8 1.5 %collective-permute-start.9 = (bf16[32,2560]{1,0:T(8,128)(2,1)S(1)}, bf16[32,2560]{1,0:T(8,128)(2,1)}, u32[]{:S(2)}, u32[]{:S(2)}) collective-permute-start(bf16[32,2560]{1,0:T(8,128)(2,1)S(1)} %broadcast_select_fusion.2), channel_id=1, source_target_pairs={{0,2},{1,3},{2,0},{3,1},{4,6},{5,7},{6,4},{7,5},{8,10},{9,11},{10,... | collective-permute-start | bytes 491528 | tf_op jit(solution)/shard_map/ppermute | solution.py:37
  26.3 5.6 %collective-permute-done.9 = bf16[32,2560]{1,0:T(8,128)(2,1)} collective-permute-done((bf16[32,2560]{1,0:T(8,128)(2,1)S(1)}, bf16[32,2560]{1,0:T(8,128)(2,1)}, u32[]{:S(2)}, u32[]{:S(2)}) %collective-permute-start.9) | collective-permute-done | bytes 163872 | tf_op jit(solution)/shard_map/ppermute | solution.py:37
  31.9 0.9 %pad_maximum_fusion.2 = bf16[64,2560]{1,0:T(8,128)(2,1)S(1)} fusion(bf16[32,2560]{1,0:T(8,128)(2,1)} %collective-permute-done.9, bf16[32,2560]{1,0:T(8,128)(2,1)S(1)} %broadcast_select_fusion.2), kind=kLoop, calls=%fused_computation.3 | loop fusion | flops 655360 | bytes 655360 | tf_op jit(solution)/shard_map/concatenate | solution.py:38
  32.9 0.4 or_select_fusion.3
  33.6 0.6 %collective-permute-start.2 = (bf16[192,1280]{1,0:T(8,128)(2,1)}, bf16[192,1280]{1,0:T(8,128)(2,1)S(1)}, u32[]{:S(2)}, u32[]{:S(2)}) collective-permute-start(bf16[192,1280]{1,0:T(8,128)(2,1)} %collective-permute-done.1.refs_2_), channel_id=1, source_target_pairs={{0,1},{1,0},{2,3},{3,2},{4,5},{5,4},{6,7},{7,6},{8,9},{9,8},{10,11... | collective-permute-start | bytes 1474568 | tf_op jit(solution)/shard_map/ppermute | solution.py:131
  34.2 0.3 collective-permute-done.10
  34.6 1.0 %pad_maximum_fusion = bf16[128,2560]{1,0:T(8,128)(2,1)S(1)} fusion(bf16[64,2560]{1,0:T(8,128)(2,1)S(1)} %collective-permute-done.10, bf16[32,2560]{1,0:T(8,128)(2,1)} %collective-permute-done.9, bf16[32,2560]{1,0:T(8,128)(2,1)S(1)} %broadcast_select_fusion.2), kind=kLoop, calls=%fused_computation.1 | loop fusion | flops 1966080 | bytes 1310720 | tf_op jit(solution)/shard_map/concatenate | solution.py:40
  35.6 0.3 collective-permute-done.2.refs_3_
  35.8 0.7 %collective-permute-done.5.refs_7_ = bf16[192,1280]{1,0:T(8,128)(2,1)S(1)} collective-permute-done((bf16[192,1280]{1,0:T(8,128)(2,1)}, bf16[192,1280]{1,0:T(8,128)(2,1)S(1)}, u32[]{:S(2)}, u32[]{:S(2)}) %collective-permute-start.5) | collective-permute-done | bytes 491552 | tf_op jit(solution)/shard_map/ppermute | solution.py:131
  36.6 12.6 %shard_map.82 = bf16[192,1280]{1,0:T(8,128)(2,1)S(1)} custom-call(bf16[192,1280]{1,0:T(8,128)(2,1)S(1)} %copy-done.1, bf16[192,1280]{1,0:T(8,128)(2,1)S(1)} %copy-done.2, bf16[192,1280]{1,0:T(8,128)(2,1)} %collective-permute-done.refs_1_, bf16[192,1280]{1,0:T(8,128)(2,1)} %collective-permute-done.1.refs_2_, ...), custom_call_target="tpu_custom_call" | custom-call | flops 1761607680 | bytes 6258688 | tf_op jit(solution)/shard_map/pallas_call | solution.py:96
  49.2 1.6 %convolution_convert_fusion = bf16[192,1280]{1,0:T(8,128)(2,1)} fusion(bf16[192,1280]{1,0:T(8,128)(2,1)S(1)} %shard_map.82, bf16[1280,1280]{1,0:T(8,128)(2,1)S(1)} %copy-done), kind=kOutput, calls=%fused_computation | convolution fusion | flops 629391360 | bytes 4259840 | tf_op jit(solution)/shard_map/dot_general | solution.py:164
  (26 shorter events, 0.5 us)
Async XLA Ops:
  0.0 49.2 %copy-start = (bf16[1280,1280]{1,0:T(8,128)(2,1)S(1)}, bf16[1280,1280]{1,0:T(8,128)(2,1)}, u32[]{:S(2)}) copy-start(bf16[1280,1280]{1,0:T(8,128)(2,1)} %param.13) | copy-start | bytes 9830404
  1.9 7.2 %collective-permute-start.6 = (bf16[32,2560]{1,0:T(8,128)(2,1)S(1)}, bf16[32,2560]{1,0:T(8,128)(2,1)}, u32[]{:S(2)}, u32[]{:S(2)}) collective-permute-start(bf16[32,2560]{1,0:T(8,128)(2,1)S(1)} %constant_dynamic-update-slice_fusion), channel_id=1, source_target_pairs={{0,4},{4,0},{8,12},{12,8},{16,20},{20,16},{24,28},{28,24},{1,5},{5... | collective-permute-start | bytes 491528 | tf_op jit(solution)/shard_map/ppermute | solution.py:27
  4.9 28.7 %collective-permute-start.1 = (bf16[192,1280]{1,0:T(8,128)(2,1)}, bf16[192,1280]{1,0:T(8,128)(2,1)}, u32[]{:S(2)}, u32[]{:S(2)}) collective-permute-start(bf16[192,1280]{1,0:T(8,128)(2,1)} %refs_0_.1), channel_id=1, source_target_pairs={{0,2},{1,3},{2,0},{3,1},{4,6},{5,7},{6,4},{7,5},{8,10},{9,11},{10,... | collective-permute-start | bytes 1474568 | tf_op jit(solution)/shard_map/ppermute | solution.py:129
  6.4 29.2 %collective-permute-start = (bf16[192,1280]{1,0:T(8,128)(2,1)}, bf16[192,1280]{1,0:T(8,128)(2,1)}, u32[]{:S(2)}, u32[]{:S(2)}) collective-permute-start(bf16[192,1280]{1,0:T(8,128)(2,1)} %refs_0_.1), channel_id=1, source_target_pairs={{0,1},{1,0},{2,3},{3,2},{4,5},{5,4},{6,7},{7,6},{8,9},{9,8},{10,11... | collective-permute-start | bytes 1474568 | tf_op jit(solution)/shard_map/ppermute | solution.py:130
  6.4 27.7 %collective-permute-start.4 = (bf16[192,1280]{1,0:T(8,128)(2,1)}, bf16[192,1280]{1,0:T(8,128)(2,1)}, u32[]{:S(2)}, u32[]{:S(2)}) collective-permute-start(bf16[192,1280]{1,0:T(8,128)(2,1)} %refs_4_.1), channel_id=1, source_target_pairs={{0,2},{1,3},{2,0},{3,1},{4,6},{5,7},{6,4},{7,5},{8,10},{9,11},{10,... | collective-permute-start | bytes 1474568 | tf_op jit(solution)/shard_map/ppermute | solution.py:129
  6.9 28.7 %collective-permute-start.3 = (bf16[192,1280]{1,0:T(8,128)(2,1)}, bf16[192,1280]{1,0:T(8,128)(2,1)}, u32[]{:S(2)}, u32[]{:S(2)}) collective-permute-start(bf16[192,1280]{1,0:T(8,128)(2,1)} %refs_4_.1), channel_id=1, source_target_pairs={{0,1},{1,0},{2,3},{3,2},{4,5},{5,4},{6,7},{7,6},{8,9},{9,8},{10,11... | collective-permute-start | bytes 1474568 | tf_op jit(solution)/shard_map/ppermute | solution.py:130
  9.2 5.5 %collective-permute-start.7 = (bf16[32,2560]{1,0:T(8,128)(2,1)S(1)}, bf16[32,2560]{1,0:T(8,128)(2,1)S(1)}, u32[]{:S(2)}, u32[]{:S(2)}) collective-permute-start(bf16[32,2560]{1,0:T(8,128)(2,1)S(1)} %broadcast_select_fusion), channel_id=1, source_target_pairs={{0,8},{4,12},{8,0},{12,4},{16,24},{20,28},{24,16},{28,20},{1,9},{5... | collective-permute-start | bytes 491528 | tf_op jit(solution)/shard_map/ppermute | solution.py:27
  14.7 2.9 %copy-start.4 = (bf16[32,2560]{1,0:T(8,128)(2,1)}, bf16[32,2560]{1,0:T(8,128)(2,1)S(1)}, u32[]{:S(2)}) copy-start(bf16[32,2560]{1,0:T(8,128)(2,1)S(1)} %broadcast_select_fusion.1) | copy-start | bytes 491524
  14.7 9.2 %collective-permute-start.8 = (bf16[32,2560]{1,0:T(8,128)(2,1)S(1)}, bf16[32,2560]{1,0:T(8,128)(2,1)}, u32[]{:S(2)}, u32[]{:S(2)}) collective-permute-start(bf16[32,2560]{1,0:T(8,128)(2,1)S(1)} %broadcast_select_fusion.1), channel_id=1, source_target_pairs={{0,16},{4,20},{8,24},{12,28},{16,0},{20,4},{24,8},{28,12},{1,17},{... | collective-permute-start | bytes 491528 | tf_op jit(solution)/shard_map/ppermute | solution.py:27
  24.8 7.1 %collective-permute-start.9 = (bf16[32,2560]{1,0:T(8,128)(2,1)S(1)}, bf16[32,2560]{1,0:T(8,128)(2,1)}, u32[]{:S(2)}, u32[]{:S(2)}) collective-permute-start(bf16[32,2560]{1,0:T(8,128)(2,1)S(1)} %broadcast_select_fusion.2), channel_id=1, source_target_pairs={{0,2},{1,3},{2,0},{3,1},{4,6},{5,7},{6,4},{7,5},{8,10},{9,11},{10,... | collective-permute-start | bytes 491528 | tf_op jit(solution)/shard_map/ppermute | solution.py:37
  32.9 1.7 %collective-permute-start.10 = (bf16[64,2560]{1,0:T(8,128)(2,1)S(1)}, bf16[64,2560]{1,0:T(8,128)(2,1)S(1)}, u32[]{:S(2)}, u32[]{:S(2)}) collective-permute-start(bf16[64,2560]{1,0:T(8,128)(2,1)S(1)} %pad_maximum_fusion.2), channel_id=1, source_target_pairs={{0,1},{1,0},{2,3},{3,2},{4,5},{5,4},{6,7},{7,6},{8,9},{9,8},{10,11... | collective-permute-start | bytes 983048 | tf_op jit(solution)/shard_map/ppermute | solution.py:39
  33.5 3.0 %copy-start.1 = (bf16[192,1280]{1,0:T(8,128)(2,1)S(1)}, bf16[192,1280]{1,0:T(8,128)(2,1)}, u32[]{:S(2)}) copy-start(bf16[192,1280]{1,0:T(8,128)(2,1)} %q_ref.1) | copy-start | bytes 1474564
  33.6 3.0 %copy-start.2 = (bf16[192,1280]{1,0:T(8,128)(2,1)S(1)}, bf16[192,1280]{1,0:T(8,128)(2,1)}, u32[]{:S(2)}) copy-start(bf16[192,1280]{1,0:T(8,128)(2,1)} %refs_0_.1) | copy-start | bytes 1474564
  33.6 3.0 %copy-start.3 = (bf16[192,1280]{1,0:T(8,128)(2,1)S(1)}, bf16[192,1280]{1,0:T(8,128)(2,1)}, u32[]{:S(2)}) copy-start(bf16[192,1280]{1,0:T(8,128)(2,1)} %refs_4_.1) | copy-start | bytes 1474564
  33.6 2.3 %collective-permute-start.2 = (bf16[192,1280]{1,0:T(8,128)(2,1)}, bf16[192,1280]{1,0:T(8,128)(2,1)S(1)}, u32[]{:S(2)}, u32[]{:S(2)}) collective-permute-start(bf16[192,1280]{1,0:T(8,128)(2,1)} %collective-permute-done.1.refs_2_), channel_id=1, source_target_pairs={{0,1},{1,0},{2,3},{3,2},{4,5},{5,4},{6,7},{7,6},{8,9},{9,8},{10,11... | collective-permute-start | bytes 1474568 | tf_op jit(solution)/shard_map/ppermute | solution.py:131
  34.1 2.4 %collective-permute-start.5 = (bf16[192,1280]{1,0:T(8,128)(2,1)}, bf16[192,1280]{1,0:T(8,128)(2,1)S(1)}, u32[]{:S(2)}, u32[]{:S(2)}) collective-permute-start(bf16[192,1280]{1,0:T(8,128)(2,1)} %collective-permute-done.4.refs_6_), channel_id=1, source_target_pairs={{0,1},{1,0},{2,3},{3,2},{4,5},{5,4},{6,7},{7,6},{8,9},{9,8},{10,11... | collective-permute-start | bytes 1474568 | tf_op jit(solution)/shard_map/ppermute | solution.py:131

commit v10 on v4

--- a/solution.py
+++ b/solution.py
@@ -48,46 +48,41 @@
     rk_ref, rv_ref, out_ref = refs[3 * piece_count :]
     lane = lax.broadcasted_iota(jnp.int32, (1, LANES), 1)
     dims = (((1,), (1,)), ((), ()))
+    rows = q_ref.shape[0]
+    per_pair = LANES // HEAD_DIM
     for pair in range(pairs):
         cols = slice(pair * LANES, (pair + 1) * LANES)
         queries = q_ref[:, cols]
-        results = []
-        for head in range(LANES // HEAD_DIM):
-            own = (lane // HEAD_DIM) == head
-            q_head = jnp.where(own, queries, jnp.zeros_like(queries))
-            scores = [
-                lax.dot_general(q_head, key_refs[p][:, cols], dims, preferred_element_type=jnp.float32)
-                * SCALE
-                + bias_refs[p][...]
-                for p in range(piece_count)
-            ]
-            peak = jnp.max(scores[0], axis=1, keepdims=True)
-            for p in range(1, piece_count):
-                peak = jnp.maximum(peak, jnp.max(scores[p], axis=1, keepdims=True))
-            total = None
-            summed = None
-            for p in range(piece_count):
-                weights = jnp.exp(scores[p] - peak)
-                part_total = jnp.sum(weights, axis=1, keepdims=True)
-                part = jnp.dot(
-                    weights.astype(jnp.bfloat16), value_refs[p][:, cols], preferred_element_type=jnp.float32
-                )
-                total = part_total if total is None else total + part_total
-                summed = part if summed is None else summed + part
-            view_part = summed / total
-            ref_scores = (
-                lax.dot_general(q_head, rk_ref[:, cols], dims, preferred_element_type=jnp.float32) * SCALE
-            )
-            ref_peak = jnp.max(ref_scores, axis=1, keepdims=True)
-            ref_weights = jnp.exp(ref_scores - ref_peak)
-            ref_total = jnp.sum(ref_weights, axis=1, keepdims=True)
-            ref_summed = jnp.dot(
-                ref_weights.astype(jnp.bfloat16), rv_ref[:, cols], preferred_element_type=jnp.float32
-            )
-            results.append((own, view_part + ref_summed / ref_total))
-        mixed = results[-1][1]
-        for own, value in results[:-1]:
-            mixed = jnp.where(own, value, mixed)
+        stacked = jnp.concatenate(
+            [jnp.where((lane // HEAD_DIM) == head, queries, jnp.zeros_like(queries)) for head in range(per_pair)],
+            axis=0,
+        )
+        scores = [
+            lax.dot_general(stacked, key_refs[p][:, cols], dims, preferred_element_type=jnp.float32) * SCALE
+            + jnp.concatenate([bias_refs[p][...]] * per_pair, axis=0)
+            for p in range(piece_count)
+        ]
+        peak = jnp.max(scores[0], axis=1, keepdims=True)
+        for p in range(1, piece_count):
+            peak = jnp.maximum(peak, jnp.max(scores[p], axis=1, keepdims=True))
+        total = None
+        summed = None
+        for p in range(piece_count):
+            weights = jnp.exp(scores[p] - peak)
+            part_total = jnp.sum(weights, axis=1, keepdims=True)
+            part = jnp.dot(weights.astype(jnp.bfloat16), value_refs[p][:, cols], preferred_element_type=jnp.float32)
+            total = part_total if total is None else total + part_total
+            summed = part if summed is None else summed + part
+        view_part = summed / total
+        ref_scores = lax.dot_general(stacked, rk_ref[:, cols], dims, preferred_element_type=jnp.float32) * SCALE
+        ref_peak = jnp.max(ref_scores, axis=1, keepdims=True)
+        ref_weights = jnp.exp(ref_scores - ref_peak)
+        ref_total = jnp.sum(ref_weights, axis=1, keepdims=True)
+        ref_summed = jnp.dot(ref_weights.astype(jnp.bfloat16), rv_ref[:, cols], preferred_element_type=jnp.float32)
+        both = view_part + ref_summed / ref_total
+        mixed = both[(per_pair - 1) * rows :]
+        for head in range(per_pair - 1):
+            mixed = jnp.where((lane // HEAD_DIM) == head, both[head * rows : (head + 1) * rows], mixed)
         out_ref[:, cols] = mixed.astype(out_ref.dtype)
 
 
@@ -163,7 +158,7 @@
         biases,
         ref_all[:, :width],
         ref_all[:, width:],
-        2,
+        1,
     )
     return jnp.dot(mixed, out_weight, preferred_element_type=jnp.float32).astype(jnp.bfloat16)
 

time: 50.8 us -> 49.1 us (0.967)
  Pallas kernels: 10.9 us -> 9.16 us
    pallas_call x1, Pallas kernels: 10.9 us -> 9.16 us  [attention(): pl.pallas_call(functools.partial(attention_kernel, len(key_pieces), span...]
where the time goes in v10:
time: 49.1 us; the launch traced here: 48.9 us
  waiting for transfers between devices  19 us (39%)
  starting transfers between devices  12.2 us (25%)
  Pallas kernels  9.16 us (19%)
  local copies, waits for them, and re-layouts  2.78 us (6%)
  matrix products  2.48 us (5%)
  other arithmetic  2.4 us (5%)
  between operations  0.86 us (2%)
    ppermute x3, waiting for transfers between devices, tree_broadcast(): received = lax.ppermute(value, axis, pairs)  10.2 us
    pallas_call x1, Pallas kernels, attention(): pl.pallas_call(functools.partial(attention_kernel, len(key_pieces), span...  9.16 us
    ppermute x3, starting transfers between devices, tree_broadcast(): received = lax.ppermute(value, axis, pairs)  7.67 us
    ppermute x1, waiting for transfers between devices, gather_rows(): across = lax.ppermute(value, axis, [(i, i ^ 2) for i in range(count)])  7.57 us
    ppermute x2, starting transfers between devices, body(): lax.ppermute((keys, values), 'view', [(i, i ^ 2) for i in range(view_coun...  2.03 us
    unnamed x11, local copies, waits for them, and re-layouts  1.84 us
    dot_general x1, matrix products, body(): jnp.dot(mixed, out_weight, preferred_element_type=jnp.float32)  1.59 us
    ppermute x1, starting transfers between devices, gather_rows(): across = lax.ppermute(value, axis, [(i, i ^ 2) for i in range(count)])  1.52 us
  transfers between devices with their start and end apart: 11, of which 7 were waited for; matrix products, arithmetic and copies ran while one was open for 7% of the time, Pallas kernels for 0%

profile of v10, /device:TPU:0, one launch (start us, length us, event | category | flops | bytes accessed | tf_op | source)
XLA Modules:
  0.0 48.9 jit_solution(12671218144232423177)
XLA Ops:
  0.0 1.0 %constant_dynamic-update-slice_fusion.1 = bf16[32,2560]{1,0:T(8,128)(2,1)S(1)} fusion(bf16[32,1280]{1,0:T(8,128)(2,1)} %param.11), kind=kLoop, calls=%fused_computation.14 | loop fusion | bytes 163840
  1.0 0.9 %constant_dynamic-update-slice_fusion = bf16[32,2560]{1,0:T(8,128)(2,1)S(1)} fusion(bf16[32,2560]{1,0:T(8,128)(2,1)S(1)} %constant_dynamic-update-slice_fusion.1, bf16[32,1280]{1,0:T(8,128)(2,1)} %param.12), kind=kLoop, calls=%fused_computation.13 | loop fusion | bytes 163840 | tf_op jit(solution)/shard_map/concatenate | solution.py:142
  1.9 2.9 %collective-permute-start.6 = (bf16[32,2560]{1,0:T(8,128)(2,1)S(1)}, bf16[32,2560]{1,0:T(8,128)(2,1)}, u32[]{:S(2)}, u32[]{:S(2)}) collective-permute-start(bf16[32,2560]{1,0:T(8,128)(2,1)S(1)} %constant_dynamic-update-slice_fusion), channel_id=1, source_target_pairs={{0,4},{4,0},{8,12},{12,8},{16,20},{20,16},{24,28},{28,24},{1,5},{5... | collective-permute-start | bytes 491528 | tf_op jit(solution)/shard_map/ppermute | solution.py:27
  4.9 1.5 %collective-permute-start.1 = (bf16[192,1280]{1,0:T(8,128)(2,1)}, bf16[192,1280]{1,0:T(8,128)(2,1)}, u32[]{:S(2)}, u32[]{:S(2)}) collective-permute-start(bf16[192,1280]{1,0:T(8,128)(2,1)} %refs_0_.1), channel_id=1, source_target_pairs={{0,2},{1,3},{2,0},{3,1},{4,6},{5,7},{6,4},{7,5},{8,10},{9,11},{10,... | collective-permute-start | bytes 1474568 | tf_op jit(solution)/shard_map/ppermute | solution.py:133
  6.4 0.2 collective-permute-start.3
  6.6 0.5 %collective-permute-start.4 = (bf16[192,1280]{1,0:T(8,128)(2,1)}, bf16[192,1280]{1,0:T(8,128)(2,1)}, u32[]{:S(2)}, u32[]{:S(2)}) collective-permute-start(bf16[192,1280]{1,0:T(8,128)(2,1)} %refs_4_.1), channel_id=1, source_target_pairs={{0,2},{1,3},{2,0},{3,1},{4,6},{5,7},{6,4},{7,5},{8,10},{9,11},{10,... | collective-permute-start | bytes 1474568 | tf_op jit(solution)/shard_map/ppermute | solution.py:133
  7.9 1.3 %collective-permute-done.6 = bf16[32,2560]{1,0:T(8,128)(2,1)} collective-permute-done((bf16[32,2560]{1,0:T(8,128)(2,1)S(1)}, bf16[32,2560]{1,0:T(8,128)(2,1)}, u32[]{:S(2)}, u32[]{:S(2)}) %collective-permute-start.6) | collective-permute-done | bytes 163872 | tf_op jit(solution)/shard_map/ppermute | solution.py:27
  9.2 1.9 %collective-permute-start.7 = (bf16[32,2560]{1,0:T(8,128)(2,1)S(1)}, bf16[32,2560]{1,0:T(8,128)(2,1)S(1)}, u32[]{:S(2)}, u32[]{:S(2)}) collective-permute-start(bf16[32,2560]{1,0:T(8,128)(2,1)S(1)} %broadcast_select_fusion), channel_id=1, source_target_pairs={{0,8},{4,12},{8,0},{12,4},{16,24},{20,28},{24,16},{28,20},{1,9},{5... | collective-permute-start | bytes 491528 | tf_op jit(solution)/shard_map/ppermute | solution.py:27
  11.1 0.9 %fusion = f32[192,3]{0,1:T(4,128)S(1)} fusion(s32[192]{0:T(256)S(1)} %get-tuple-element.14, s32[6,3]{0,1:T(4,128)} %param.14), kind=kOutput, calls=%fused_computation.11 | convolution fusion | flops 8082 | bytes 3144 | tf_op jit(solution)/shard_map/dot_general | solution.py:148
  12.0 2.7 %collective-permute-done.7 = bf16[32,2560]{1,0:T(8,128)(2,1)S(1)} collective-permute-done((bf16[32,2560]{1,0:T(8,128)(2,1)S(1)}, bf16[32,2560]{1,0:T(8,128)(2,1)S(1)}, u32[]{:S(2)}, u32[]{:S(2)}) %collective-permute-start.7) | collective-permute-done | bytes 163872 | tf_op jit(solution)/shard_map/ppermute | solution.py:27
  14.7 2.8 %collective-permute-start.8 = (bf16[32,2560]{1,0:T(8,128)(2,1)S(1)}, bf16[32,2560]{1,0:T(8,128)(2,1)S(1)}, u32[]{:S(2)}, u32[]{:S(2)}) collective-permute-start(bf16[32,2560]{1,0:T(8,128)(2,1)S(1)} %broadcast_select_fusion.1), channel_id=1, source_target_pairs={{0,16},{4,20},{8,24},{12,28},{16,0},{20,4},{24,8},{28,12},{1,17},{... | collective-permute-start | bytes 491528 | tf_op jit(solution)/shard_map/ppermute | solution.py:27
  17.5 6.2 %collective-permute-done.8 = bf16[32,2560]{1,0:T(8,128)(2,1)S(1)} collective-permute-done((bf16[32,2560]{1,0:T(8,128)(2,1)S(1)}, bf16[32,2560]{1,0:T(8,128)(2,1)S(1)}, u32[]{:S(2)}, u32[]{:S(2)}) %collective-permute-start.8) | collective-permute-done | bytes 163872 | tf_op jit(solution)/shard_map/ppermute | solution.py:27
  23.7 1.5 %collective-permute-start.9 = (bf16[32,2560]{1,0:T(8,128)(2,1)S(1)}, bf16[32,2560]{1,0:T(8,128)(2,1)}, u32[]{:S(2)}, u32[]{:S(2)}) collective-permute-start(bf16[32,2560]{1,0:T(8,128)(2,1)S(1)} %broadcast_select_fusion.2), channel_id=1, source_target_pairs={{0,2},{1,3},{2,0},{3,1},{4,6},{5,7},{6,4},{7,5},{8,10},{9,11},{10,... | collective-permute-start | bytes 491528 | tf_op jit(solution)/shard_map/ppermute | solution.py:37
  25.3 7.6 %collective-permute-done.9 = bf16[32,2560]{1,0:T(8,128)(2,1)} collective-permute-done((bf16[32,2560]{1,0:T(8,128)(2,1)S(1)}, bf16[32,2560]{1,0:T(8,128)(2,1)}, u32[]{:S(2)}, u32[]{:S(2)}) %collective-permute-start.9) | collective-permute-done | bytes 163872 | tf_op jit(solution)/shard_map/ppermute | solution.py:37
  32.9 0.9 %pad_maximum_fusion.1 = bf16[64,2560]{1,0:T(8,128)(2,1)S(1)} fusion(bf16[32,2560]{1,0:T(8,128)(2,1)} %collective-permute-done.9, bf16[32,2560]{1,0:T(8,128)(2,1)S(1)} %broadcast_select_fusion.2), kind=kLoop, calls=%fused_computation.2 | loop fusion | flops 655360 | bytes 655360 | tf_op jit(solution)/shard_map/concatenate | solution.py:38
  33.9 0.4 or_select_fusion
  34.4 0.6 %collective-permute-start.2 = (bf16[192,1280]{1,0:T(8,128)(2,1)}, bf16[192,1280]{1,0:T(8,128)(2,1)S(1)}, u32[]{:S(2)}, u32[]{:S(2)}) collective-permute-start(bf16[192,1280]{1,0:T(8,128)(2,1)} %collective-permute-done.1.refs_2_), channel_id=1, source_target_pairs={{0,1},{1,0},{2,3},{3,2},{4,5},{5,4},{6,7},{7,6},{8,9},{9,8},{10,11... | collective-permute-start | bytes 1474568 | tf_op jit(solution)/shard_map/ppermute | solution.py:135
  34.9 0.1 collective-permute-start.5
  35.0 0.5 %collective-permute-done.10 = bf16[64,2560]{1,0:T(8,128)(2,1)S(1)} collective-permute-done((bf16[64,2560]{1,0:T(8,128)(2,1)S(1)}, bf16[64,2560]{1,0:T(8,128)(2,1)S(1)}, u32[]{:S(2)}, u32[]{:S(2)}) %collective-permute-start.10) | collective-permute-done | bytes 327712 | tf_op jit(solution)/shard_map/ppermute | solution.py:39
  35.5 1.0 %pad_maximum_fusion = bf16[128,2560]{1,0:T(8,128)(2,1)S(1)} fusion(bf16[64,2560]{1,0:T(8,128)(2,1)S(1)} %collective-permute-done.10, bf16[32,2560]{1,0:T(8,128)(2,1)} %collective-permute-done.9, bf16[32,2560]{1,0:T(8,128)(2,1)S(1)} %broadcast_select_fusion.2), kind=kLoop, calls=%fused_computation.1 | loop fusion | flops 1966080 | bytes 1310720 | tf_op jit(solution)/shard_map/concatenate | solution.py:40
  36.6 0.7 %collective-permute-done.5.refs_7_ = bf16[192,1280]{1,0:T(8,128)(2,1)S(1)} collective-permute-done((bf16[192,1280]{1,0:T(8,128)(2,1)}, bf16[192,1280]{1,0:T(8,128)(2,1)S(1)}, u32[]{:S(2)}, u32[]{:S(2)}) %collective-permute-start.5) | collective-permute-done | bytes 491552 | tf_op jit(solution)/shard_map/ppermute | solution.py:135
  37.3 0.8 %copy-done.4 = bf16[192,1280]{1,0:T(8,128)(2,1)} copy-done((bf16[192,1280]{1,0:T(8,128)(2,1)}, bf16[192,1280]{1,0:T(8,128)(2,1)S(1)}, u32[]{:S(2)}) %copy-start.4) | copy-done | bytes 491544
  38.1 9.2 %shard_map.82 = bf16[192,1280]{1,0:T(8,128)(2,1)S(1)} custom-call(bf16[192,1280]{1,0:T(8,128)(2,1)S(1)} %copy-done.1, bf16[192,1280]{1,0:T(8,128)(2,1)S(1)} %copy-done.2, bf16[192,1280]{1,0:T(8,128)(2,1)} %collective-permute-done.refs_1_, bf16[192,1280]{1,0:T(8,128)(2,1)} %collective-permute-done.1.refs_2_, ...), custom_call_target="tpu_custom_call" | custom-call | flops 1761607680 | bytes 6258688 | tf_op jit(solution)/shard_map/pallas_call | solution.py:100
  47.3 1.6 %convolution_convert_fusion = bf16[192,1280]{1,0:T(8,128)(2,1)} fusion(bf16[192,1280]{1,0:T(8,128)(2,1)S(1)} %shard_map.82, bf16[1280,1280]{1,0:T(8,128)(2,1)S(1)} %copy-done), kind=kOutput, calls=%fused_computation | convolution fusion | flops 629391360 | bytes 4259840 | tf_op jit(solution)/shard_map/dot_general | solution.py:163
  (25 shorter events, 0.3 us)
Async XLA Ops:
  0.0 47.3 %copy-start = (bf16[1280,1280]{1,0:T(8,128)(2,1)S(1)}, bf16[1280,1280]{1,0:T(8,128)(2,1)}, u32[]{:S(2)}) copy-start(bf16[1280,1280]{1,0:T(8,128)(2,1)} %param.13) | copy-start | bytes 9830404
  1.9 7.2 %collective-permute-start.6 = (bf16[32,2560]{1,0:T(8,128)(2,1)S(1)}, bf16[32,2560]{1,0:T(8,128)(2,1)}, u32[]{:S(2)}, u32[]{:S(2)}) collective-permute-start(bf16[32,2560]{1,0:T(8,128)(2,1)S(1)} %constant_dynamic-update-slice_fusion), channel_id=1, source_target_pairs={{0,4},{4,0},{8,12},{12,8},{16,20},{20,16},{24,28},{28,24},{1,5},{5... | collective-permute-start | bytes 491528 | tf_op jit(solution)/shard_map/ppermute | solution.py:27
  4.9 31.7 %collective-permute-start = (bf16[192,1280]{1,0:T(8,128)(2,1)}, bf16[192,1280]{1,0:T(8,128)(2,1)}, u32[]{:S(2)}, u32[]{:S(2)}) collective-permute-start(bf16[192,1280]{1,0:T(8,128)(2,1)} %refs_0_.1), channel_id=1, source_target_pairs={{0,1},{1,0},{2,3},{3,2},{4,5},{5,4},{6,7},{7,6},{8,9},{9,8},{10,11... | collective-permute-start | bytes 1474568 | tf_op jit(solution)/shard_map/ppermute | solution.py:134
  4.9 29.5 %collective-permute-start.1 = (bf16[192,1280]{1,0:T(8,128)(2,1)}, bf16[192,1280]{1,0:T(8,128)(2,1)}, u32[]{:S(2)}, u32[]{:S(2)}) collective-permute-start(bf16[192,1280]{1,0:T(8,128)(2,1)} %refs_0_.1), channel_id=1, source_target_pairs={{0,2},{1,3},{2,0},{3,1},{4,6},{5,7},{6,4},{7,5},{8,10},{9,11},{10,... | collective-permute-start | bytes 1474568 | tf_op jit(solution)/shard_map/ppermute | solution.py:133
  6.4 30.1 %collective-permute-start.3 = (bf16[192,1280]{1,0:T(8,128)(2,1)}, bf16[192,1280]{1,0:T(8,128)(2,1)}, u32[]{:S(2)}, u32[]{:S(2)}) collective-permute-start(bf16[192,1280]{1,0:T(8,128)(2,1)} %refs_4_.1), channel_id=1, source_target_pairs={{0,1},{1,0},{2,3},{3,2},{4,5},{5,4},{6,7},{7,6},{8,9},{9,8},{10,11... | collective-permute-start | bytes 1474568 | tf_op jit(solution)/shard_map/ppermute | solution.py:134
  6.6 28.3 %collective-permute-start.4 = (bf16[192,1280]{1,0:T(8,128)(2,1)}, bf16[192,1280]{1,0:T(8,128)(2,1)}, u32[]{:S(2)}, u32[]{:S(2)}) collective-permute-start(bf16[192,1280]{1,0:T(8,128)(2,1)} %refs_4_.1), channel_id=1, source_target_pairs={{0,2},{1,3},{2,0},{3,1},{4,6},{5,7},{6,4},{7,5},{8,10},{9,11},{10,... | collective-permute-start | bytes 1474568 | tf_op jit(solution)/shard_map/ppermute | solution.py:133
  9.2 5.5 %collective-permute-start.7 = (bf16[32,2560]{1,0:T(8,128)(2,1)S(1)}, bf16[32,2560]{1,0:T(8,128)(2,1)S(1)}, u32[]{:S(2)}, u32[]{:S(2)}) collective-permute-start(bf16[32,2560]{1,0:T(8,128)(2,1)S(1)} %broadcast_select_fusion), channel_id=1, source_target_pairs={{0,8},{4,12},{8,0},{12,4},{16,24},{20,28},{24,16},{28,20},{1,9},{5... | collective-permute-start | bytes 491528 | tf_op jit(solution)/shard_map/ppermute | solution.py:27
  14.7 9.0 %collective-permute-start.8 = (bf16[32,2560]{1,0:T(8,128)(2,1)S(1)}, bf16[32,2560]{1,0:T(8,128)(2,1)S(1)}, u32[]{:S(2)}, u32[]{:S(2)}) collective-permute-start(bf16[32,2560]{1,0:T(8,128)(2,1)S(1)} %broadcast_select_fusion.1), channel_id=1, source_target_pairs={{0,16},{4,20},{8,24},{12,28},{16,0},{20,4},{24,8},{28,12},{1,17},{... | collective-permute-start | bytes 491528 | tf_op jit(solution)/shard_map/ppermute | solution.py:27
  23.7 9.1 %collective-permute-start.9 = (bf16[32,2560]{1,0:T(8,128)(2,1)S(1)}, bf16[32,2560]{1,0:T(8,128)(2,1)}, u32[]{:S(2)}, u32[]{:S(2)}) collective-permute-start(bf16[32,2560]{1,0:T(8,128)(2,1)S(1)} %broadcast_select_fusion.2), channel_id=1, source_target_pairs={{0,2},{1,3},{2,0},{3,1},{4,6},{5,7},{6,4},{7,5},{8,10},{9,11},{10,... | collective-permute-start | bytes 491528 | tf_op jit(solution)/shard_map/ppermute | solution.py:37
  33.8 1.7 %collective-permute-start.10 = (bf16[64,2560]{1,0:T(8,128)(2,1)S(1)}, bf16[64,2560]{1,0:T(8,128)(2,1)S(1)}, u32[]{:S(2)}, u32[]{:S(2)}) collective-permute-start(bf16[64,2560]{1,0:T(8,128)(2,1)S(1)} %pad_maximum_fusion.1), channel_id=1, source_target_pairs={{0,1},{1,0},{2,3},{3,2},{4,5},{5,4},{6,7},{7,6},{8,9},{9,8},{10,11... | collective-permute-start | bytes 983048 | tf_op jit(solution)/shard_map/ppermute | solution.py:39
  34.3 3.8 %copy-start.1 = (bf16[192,1280]{1,0:T(8,128)(2,1)S(1)}, bf16[192,1280]{1,0:T(8,128)(2,1)}, u32[]{:S(2)}) copy-start(bf16[192,1280]{1,0:T(8,128)(2,1)} %q_ref.1) | copy-start | bytes 1474564
  34.3 3.8 %copy-start.2 = (bf16[192,1280]{1,0:T(8,128)(2,1)S(1)}, bf16[192,1280]{1,0:T(8,128)(2,1)}, u32[]{:S(2)}) copy-start(bf16[192,1280]{1,0:T(8,128)(2,1)} %refs_0_.1) | copy-start | bytes 1474564
  34.3 3.8 %copy-start.3 = (bf16[192,1280]{1,0:T(8,128)(2,1)S(1)}, bf16[192,1280]{1,0:T(8,128)(2,1)}, u32[]{:S(2)}) copy-start(bf16[192,1280]{1,0:T(8,128)(2,1)} %refs_4_.1) | copy-start | bytes 1474564
  34.4 2.3 %collective-permute-start.2 = (bf16[192,1280]{1,0:T(8,128)(2,1)}, bf16[192,1280]{1,0:T(8,128)(2,1)S(1)}, u32[]{:S(2)}, u32[]{:S(2)}) collective-permute-start(bf16[192,1280]{1,0:T(8,128)(2,1)} %collective-permute-done.1.refs_2_), channel_id=1, source_target_pairs={{0,1},{1,0},{2,3},{3,2},{4,5},{5,4},{6,7},{7,6},{8,9},{9,8},{10,11... | collective-permute-start | bytes 1474568 | tf_op jit(solution)/shard_map/ppermute | solution.py:135
  34.9 2.4 %collective-permute-start.5 = (bf16[192,1280]{1,0:T(8,128)(2,1)}, bf16[192,1280]{1,0:T(8,128)(2,1)S(1)}, u32[]{:S(2)}, u32[]{:S(2)}) collective-permute-start(bf16[192,1280]{1,0:T(8,128)(2,1)} %collective-permute-done.4.refs_6_), channel_id=1, source_target_pairs={{0,1},{1,0},{2,3},{3,2},{4,5},{5,4},{6,7},{7,6},{8,9},{9,8},{10,11... | collective-permute-start | bytes 1474568 | tf_op jit(solution)/shard_map/ppermute | solution.py:135
  37.3 0.8 %copy-start.4 = (bf16[192,1280]{1,0:T(8,128)(2,1)}, bf16[192,1280]{1,0:T(8,128)(2,1)S(1)}, u32[]{:S(2)}) copy-start(bf16[192,1280]{1,0:T(8,128)(2,1)S(1)} %collective-permute-done.5.refs_7_) | copy-start | bytes 1474564

commit v11 on v10

--- a/solution.py
+++ b/solution.py
@@ -41,11 +41,13 @@
     return lax.all_gather(value, axis, axis=0, tiled=True)
 
 
-def attention_kernel(piece_count, pairs, q_ref, *refs):
+def attention_kernel(piece_count, ref_count, pairs, q_ref, *refs):
     key_refs = refs[:piece_count]
     value_refs = refs[piece_count : 2 * piece_count]
     bias_refs = refs[2 * piece_count : 3 * piece_count]
-    rk_ref, rv_ref, out_ref = refs[3 * piece_count :]
+    rk_refs = refs[3 * piece_count : 3 * piece_count + ref_count]
+    rv_refs = refs[3 * piece_count + ref_count : 3 * piece_count + 2 * ref_count]
+    out_ref = refs[-1]
     lane = lax.broadcasted_iota(jnp.int32, (1, LANES), 1)
     dims = (((1,), (1,)), ((), ()))
     rows = q_ref.shape[0]
@@ -59,7 +61,7 @@
         )
         scores = [
             lax.dot_general(stacked, key_refs[p][:, cols], dims, preferred_element_type=jnp.float32) * SCALE
-            + jnp.concatenate([bias_refs[p][...]] * per_pair, axis=0)
+            + bias_refs[p][...]
             for p in range(piece_count)
         ]
         peak = jnp.max(scores[0], axis=1, keepdims=True)
@@ -74,11 +76,13 @@
             total = part_total if total is None else total + part_total
             summed = part if summed is None else summed + part
         view_part = summed / total
-        ref_scores = lax.dot_general(stacked, rk_ref[:, cols], dims, preferred_element_type=jnp.float32) * SCALE
+        ref_keys = jnp.concatenate([r[:, cols] for r in rk_refs], axis=0)
+        ref_values = jnp.concatenate([r[:, cols] for r in rv_refs], axis=0)
+        ref_scores = lax.dot_general(stacked, ref_keys, dims, preferred_element_type=jnp.float32) * SCALE
         ref_peak = jnp.max(ref_scores, axis=1, keepdims=True)
         ref_weights = jnp.exp(ref_scores - ref_peak)
         ref_total = jnp.sum(ref_weights, axis=1, keepdims=True)
-        ref_summed = jnp.dot(ref_weights.astype(jnp.bfloat16), rv_ref[:, cols], preferred_element_type=jnp.float32)
+        ref_summed = jnp.dot(ref_weights.astype(jnp.bfloat16), ref_values, preferred_element_type=jnp.float32)
         both = view_part + ref_summed / ref_total
         mixed = both[(per_pair - 1) * rows :]
         for head in range(per_pair - 1):
@@ -86,32 +90,34 @@
         out_ref[:, cols] = mixed.astype(out_ref.dtype)
 
 
-def attention(queries, key_pieces, value_pieces, biases, ref_keys, ref_values, steps):
+def attention(queries, key_pieces, value_pieces, biases, ref_pieces, steps):
     rows, width = queries.shape
     span = width // steps
     column = lambda j: (0, j)
+    second = lambda j: (0, j + steps)
     fixed = lambda j: (0, 0)
     in_specs = [pl.BlockSpec((rows, span), column)]
     in_specs += [pl.BlockSpec((piece.shape[0], span), column) for piece in key_pieces]
     in_specs += [pl.BlockSpec((piece.shape[0], span), column) for piece in value_pieces]
     in_specs += [pl.BlockSpec(bias.shape, fixed) for bias in biases]
-    in_specs += [pl.BlockSpec((ref_keys.shape[0], span), column)] * 2
-    keys = sum(piece.shape[0] for piece in key_pieces) + ref_keys.shape[0]
+    in_specs += [pl.BlockSpec((piece.shape[0], span), column) for piece in ref_pieces]
+    in_specs += [pl.BlockSpec((piece.shape[0], span), second) for piece in ref_pieces]
+    keys = sum(piece.shape[0] for piece in key_pieces) + sum(piece.shape[0] for piece in ref_pieces)
     return pl.pallas_call(
-        functools.partial(attention_kernel, len(key_pieces), span // LANES),
+        functools.partial(attention_kernel, len(key_pieces), len(ref_pieces), span // LANES),
         grid=(steps,),
         in_specs=in_specs,
         out_specs=pl.BlockSpec((rows, span), column),
         out_shape=jax.ShapeDtypeStruct((rows, width), jnp.bfloat16),
         compiler_params=pltpu.CompilerParams(
-            dimension_semantics=("arbitrary",), vmem_limit_bytes=48 * 1024 * 1024
+            dimension_semantics=("arbitrary",), vmem_limit_bytes=64 * 1024 * 1024
         ),
         cost_estimate=pl.CostEstimate(
             flops=8 * rows * keys * width,
             transcendentals=2 * rows * keys * HEADS,
-            bytes_accessed=2 * (2 * rows + 2 * keys) * width + 4 * rows * keys,
+            bytes_accessed=2 * (2 * rows + 2 * keys) * width + 8 * rows * keys,
         ),
-    )(queries, *key_pieces, *value_pieces, *biases, ref_keys, ref_values)
+    )(queries, *key_pieces, *value_pieces, *biases, *ref_pieces, *ref_pieces)
 
 
 def key_bias(query_views, query_adjacent, position, rows, shard_rows, view_tok):
@@ -129,36 +135,35 @@
     view_index = lax.axis_index("view")
     view_tok = shard_rows * view_count // VIEWS
 
+    ref_both = jnp.concatenate([ref_keys, ref_values], axis=1)
+    ref_shared = tree_broadcast(ref_both, "mesh", ref_source[0])
     if view_count == 4:
         across = lax.ppermute((keys, values), "view", [(i, i ^ 2) for i in range(view_count)])
         near = lax.ppermute((keys, values), "view", [(i, i ^ 1) for i in range(view_count)])
+        ref_shared, across = lax.optimization_barrier((ref_shared, across))
         far = lax.ppermute(across, "view", [(i, i ^ 1) for i in range(view_count)])
+        ref_across = lax.ppermute(ref_shared, "view", [(i, i ^ 2) for i in range(view_count)])
+        ref_near = lax.ppermute((ref_shared, ref_across), "view", [(i, i ^ 1) for i in range(view_count)])
         pieces = [(keys, values), near, across, far]
         positions = [view_index, view_index ^ 1, view_index ^ 2, view_index ^ 3]
+        ref_pieces = [ref_shared, ref_across, *ref_near]
     else:
         pieces = [lax.all_gather((keys, values), "view", axis=0, tiled=True)]
         positions = [jnp.zeros((), jnp.int32)]
-
-    ref_both = jnp.concatenate([ref_keys, ref_values], axis=1)
-    ref_all = gather_rows(tree_broadcast(ref_both, "mesh", ref_source[0]), "view")
+        ref_pieces = [lax.all_gather(ref_shared, "view", axis=0, tiled=True)]
 
     view_ids = jnp.arange(VIEWS, dtype=jnp.int32)
     query_views = (view_index * shard_rows + jnp.arange(shard_rows, dtype=jnp.int32)) // view_tok
     query_onehot = (query_views[:, None] == view_ids[None, :]).astype(jnp.float32)
     query_adjacent = jnp.dot(query_onehot, adjacency.astype(jnp.float32))
     biases = [
-        key_bias(query_views, query_adjacent, position, piece[0].shape[0], shard_rows, view_tok)
+        jnp.concatenate(
+            [key_bias(query_views, query_adjacent, position, piece[0].shape[0], shard_rows, view_tok)] * 2, axis=0
+        )
         for piece, position in zip(pieces, positions)
     ]
-
     mixed = attention(
-        queries,
-        [piece[0] for piece in pieces],
-        [piece[1] for piece in pieces],
-        biases,
-        ref_all[:, :width],
-        ref_all[:, width:],
-        1,
+        queries, [piece[0] for piece in pieces], [piece[1] for piece in pieces], biases, ref_pieces, 1 if view_count == 4 else 2
     )
     return jnp.dot(mixed, out_weight, preferred_element_type=jnp.float32).astype(jnp.bfloat16)
 

time: 49.1 us -> 52.9 us (1.077)
  matrix products: 2.48 us -> 4.57 us
  Pallas kernels: 9.16 us -> 11.2 us
  waiting for transfers between devices: 19 us -> 17 us
  other arithmetic: 2.4 us -> 3.67 us
  local copies, waits for them, and re-layouts: 2.78 us -> 3.42 us
    ppermute x2 -> x3, waiting for transfers between devices: 8.07 us -> 3.02 us  [the longest x1 3.02 us: body(): lax.ppermute(ref_shared, 'view', [(i, i ^ 2) for i in range(view_count)])]
    ppermute x3, waiting for transfers between devices: 10.2 us -> 14 us  [tree_broadcast(): received = lax.ppermute(value, axis, pairs)]
    dot_general x1, matrix products: 1.59 us -> 3.68 us  [body(): jnp.dot(mixed, out_weight, preferred_element_type=jnp.float32)]
    pallas_call x1, Pallas kernels: 9.16 us -> 11.2 us  [attention(): pl.pallas_call(functools.partial(attention_kernel, len(key_pieces), len(r...]
    concatenate x2 -> x4, other arithmetic: 1.9 us -> 3.17 us  [body(): jnp.concatenate([key_bias(query_views, query_adjacent, position, piece[0]...]
    ppermute x3, starting transfers between devices: 7.67 us -> 6.45 us  [tree_broadcast(): received = lax.ppermute(value, axis, pairs)]
    ppermute x2, waiting for transfers between devices: 0.78 us -> 0.01 us  [body(): far = lax.ppermute(across, 'view', [(i, i ^ 1) for i in range(view_count)])]
    unnamed x11 -> x19, local copies, waits for them, and re-layouts: 1.84 us -> 2.52 us
  transfers between devices with their start and end apart: 11 -> 12, of which waited for: 7 -> 4; matrix products, arithmetic and copies ran while one was open for 7% -> 12% of each run, Pallas kernels for 0% -> 0%
where the time goes in v11:
time: 52.9 us; the launch traced here: 52.6 us
  waiting for transfers between devices  17 us (32%)
  starting transfers between devices  11.9 us (22%)
  Pallas kernels  11.2 us (21%)
  matrix products  4.57 us (9%)
  other arithmetic  3.67 us (7%)
  local copies, waits for them, and re-layouts  3.42 us (6%)
  between operations  0.88 us (2%)
    ppermute x3, waiting for transfers between devices, tree_broadcast(): received = lax.ppermute(value, axis, pairs)  14 us
    pallas_call x1, Pallas kernels, attention(): pl.pallas_call(functools.partial(attention_kernel, len(key_pieces), len(r...  11.2 us
    ppermute x3, starting transfers between devices, tree_broadcast(): received = lax.ppermute(value, axis, pairs)  6.45 us
    dot_general x1, matrix products, body(): jnp.dot(mixed, out_weight, preferred_element_type=jnp.float32)  3.68 us
    concatenate x4, other arithmetic, body(): jnp.concatenate([key_bias(query_views, query_adjacent, position, piece[0]...  3.17 us
    ppermute x1, waiting for transfers between devices, body(): lax.ppermute(ref_shared, 'view', [(i, i ^ 2) for i in range(view_count)])  3.02 us
    ppermute x2, starting transfers between devices, body(): lax.ppermute((keys, values), 'view', [(i, i ^ 2) for i in range(view_coun...  2.59 us
    unnamed x19, local copies, waits for them, and re-layouts  2.52 us
  transfers between devices with their start and end apart: 12, of which 4 were waited for; matrix products, arithmetic and copies ran while one was open for 12% of the time, Pallas kernels for 0%

profile of v11, /device:TPU:0, one launch (start us, length us, event | category | flops | bytes accessed | tf_op | source)
XLA Modules:
  0.0 52.6 jit_solution(11899150743281409577)
XLA Ops:
  0.0 0.5 collective-permute-start
  0.5 2.5 %collective-permute-start.4 = (bf16[192,1280]{1,0:T(8,128)(2,1)}, bf16[192,1280]{1,0:T(8,128)(2,1)S(1)}, u32[]{:S(2)}, u32[]{:S(2)}) collective-permute-start(bf16[192,1280]{1,0:T(8,128)(2,1)} %refs_0_.1), channel_id=1, source_target_pairs={{0,2},{1,3},{2,0},{3,1},{4,6},{5,7},{6,4},{7,5},{8,10},{9,11},{10,... | collective-permute-start | bytes 1474568 | tf_op jit(solution)/shard_map/ppermute | solution.py:141
  3.0 0.2 collective-permute-start.7
  3.2 0.9 %constant_dynamic-update-slice_fusion.1 = bf16[32,2560]{1,0:T(8,128)(2,1)S(1)} fusion(bf16[32,1280]{1,0:T(8,128)(2,1)} %param.11), kind=kLoop, calls=%fused_computation.16 | loop fusion | bytes 163840
  4.1 0.9 %constant_dynamic-update-slice_fusion = bf16[32,2560]{1,0:T(8,128)(2,1)S(1)} fusion(bf16[32,2560]{1,0:T(8,128)(2,1)S(1)} %constant_dynamic-update-slice_fusion.1, bf16[32,1280]{1,0:T(8,128)(2,1)} %param.12), kind=kLoop, calls=%fused_computation.15 | loop fusion | bytes 163840 | tf_op jit(solution)/shard_map/concatenate | solution.py:138
  5.0 1.7 %collective-permute-start.1 = (bf16[32,2560]{1,0:T(8,128)(2,1)S(1)}, bf16[32,2560]{1,0:T(8,128)(2,1)S(1)}, u32[]{:S(2)}, u32[]{:S(2)}) collective-permute-start(bf16[32,2560]{1,0:T(8,128)(2,1)S(1)} %constant_dynamic-update-slice_fusion), channel_id=1, source_target_pairs={{0,4},{4,0},{8,12},{12,8},{16,20},{20,16},{24,28},{28,24},{1,5},{5... | collective-permute-start | bytes 491528 | tf_op jit(solution)/shard_map/ppermute | solution.py:27
  7.4 0.9 %fusion = f32[192,3]{0,1:T(4,128)S(1)} fusion(s32[192]{0:T(256)S(1)} %get-tuple-element.18, s32[6,3]{0,1:T(4,128)} %param.14), kind=kOutput, calls=%fused_computation.13 | convolution fusion | flops 8082 | bytes 3144 | tf_op jit(solution)/shard_map/dot_general | solution.py:158
  8.3 3.3 %collective-permute-done.1 = bf16[32,2560]{1,0:T(8,128)(2,1)S(1)} collective-permute-done((bf16[32,2560]{1,0:T(8,128)(2,1)S(1)}, bf16[32,2560]{1,0:T(8,128)(2,1)S(1)}, u32[]{:S(2)}, u32[]{:S(2)}) %collective-permute-start.1) | collective-permute-done | bytes 163872 | tf_op jit(solution)/shard_map/ppermute | solution.py:27
  11.6 1.9 %collective-permute-start.2 = (bf16[32,2560]{1,0:T(8,128)(2,1)S(1)}, bf16[32,2560]{1,0:T(8,128)(2,1)S(1)}, u32[]{:S(2)}, u32[]{:S(2)}) collective-permute-start(bf16[32,2560]{1,0:T(8,128)(2,1)S(1)} %broadcast_select_fusion), channel_id=1, source_target_pairs={{0,8},{4,12},{8,0},{12,4},{16,24},{20,28},{24,16},{28,20},{1,9},{5... | collective-permute-start | bytes 491528 | tf_op jit(solution)/shard_map/ppermute | solution.py:27
  13.6 4.1 %collective-permute-done.2 = bf16[32,2560]{1,0:T(8,128)(2,1)S(1)} collective-permute-done((bf16[32,2560]{1,0:T(8,128)(2,1)S(1)}, bf16[32,2560]{1,0:T(8,128)(2,1)S(1)}, u32[]{:S(2)}, u32[]{:S(2)}) %collective-permute-start.2) | collective-permute-done | bytes 163872 | tf_op jit(solution)/shard_map/ppermute | solution.py:27
  17.7 2.8 %collective-permute-start.3 = (bf16[32,2560]{1,0:T(8,128)(2,1)S(1)}, bf16[32,2560]{1,0:T(8,128)(2,1)S(1)}, u32[]{:S(2)}, u32[]{:S(2)}) collective-permute-start(bf16[32,2560]{1,0:T(8,128)(2,1)S(1)} %broadcast_select_fusion.1), channel_id=1, source_target_pairs={{0,16},{4,20},{8,24},{12,28},{16,0},{20,4},{24,8},{28,12},{1,17},{... | collective-permute-start | bytes 491528 | tf_op jit(solution)/shard_map/ppermute | solution.py:27
  20.6 6.6 %collective-permute-done.3 = bf16[32,2560]{1,0:T(8,128)(2,1)S(1)} collective-permute-done((bf16[32,2560]{1,0:T(8,128)(2,1)S(1)}, bf16[32,2560]{1,0:T(8,128)(2,1)S(1)}, u32[]{:S(2)}, u32[]{:S(2)}) %collective-permute-start.3) | collective-permute-done | bytes 163872 | tf_op jit(solution)/shard_map/ppermute | solution.py:27
  27.3 0.5 collective-permute-start.8
  27.8 0.4 or_select_fusion
  28.2 1.6 %collective-permute-start.9 = (bf16[32,2560]{1,0:T(8,128)(2,1)S(1)}, bf16[32,2560]{1,0:T(8,128)(2,1)S(1)}, u32[]{:S(2)}, u32[]{:S(2)}) collective-permute-start(bf16[32,2560]{1,0:T(8,128)(2,1)S(1)} %broadcast_select_fusion.2.refs_12_.refs_16_), channel_id=1, source_target_pairs={{0,2},{1,3},{2,0},{3,1},{4,6},{5,7},{6,4},{7,5},{8,10},{9,11},{10,... | collective-permute-start | bytes 491528 | tf_op jit(solution)/shard_map/ppermute | solution.py:145
  29.9 0.8 %pad_maximum_fusion.3.refs_11_ = f32[384,192]{1,0:T(8,128)} fusion(f32[192,192]{1,0:T(8,128)S(1)} %get-tuple-element.11), kind=kLoop, calls=%fused_computation.4 | loop fusion | flops 73728 | bytes 442368 | tf_op jit(solution)/shard_map/concatenate | solution.py:160
  30.7 0.8 %pad_maximum_fusion.1.refs_9_ = f32[384,192]{1,0:T(8,128)} fusion(f32[192,192]{1,0:T(8,128)S(1)} %get-tuple-element.12), kind=kLoop, calls=%fused_computation.2 | loop fusion | flops 73728 | bytes 442368 | tf_op jit(solution)/shard_map/concatenate | solution.py:160
  31.5 3.0 %collective-permute-done.9.refs_13_.refs_17_ = bf16[32,2560]{1,0:T(8,128)(2,1)S(1)} collective-permute-done((bf16[32,2560]{1,0:T(8,128)(2,1)S(1)}, bf16[32,2560]{1,0:T(8,128)(2,1)S(1)}, u32[]{:S(2)}, u32[]{:S(2)}) %collective-permute-start.9) | collective-permute-done | bytes 163872 | tf_op jit(solution)/shard_map/ppermute | solution.py:145
  34.5 0.8 %pad_maximum_fusion.2.refs_10_ = f32[384,192]{1,0:T(8,128)} fusion(f32[192,192]{1,0:T(8,128)S(1)} %get-tuple-element.13), kind=kLoop, calls=%fused_computation.3 | loop fusion | flops 73728 | bytes 442368 | tf_op jit(solution)/shard_map/concatenate | solution.py:160
  35.3 0.8 %pad_maximum_fusion.refs_8_ = f32[384,192]{1,0:T(8,128)} fusion(f32[192,192]{1,0:T(8,128)S(1)} %get-tuple-element.14), kind=kLoop, calls=%fused_computation.1 | loop fusion | flops 73728 | bytes 442368 | tf_op jit(solution)/shard_map/concatenate | solution.py:160
  36.2 0.7 %copy-done.4 = bf16[192,1280]{1,0:T(8,128)(2,1)} copy-done((bf16[192,1280]{1,0:T(8,128)(2,1)}, bf16[192,1280]{1,0:T(8,128)(2,1)S(1)}, u32[]{:S(2)}) %copy-start.4) | copy-done | bytes 491544
  37.0 0.8 %copy-done.5 = bf16[192,1280]{1,0:T(8,128)(2,1)} copy-done((bf16[192,1280]{1,0:T(8,128)(2,1)}, bf16[192,1280]{1,0:T(8,128)(2,1)S(1)}, u32[]{:S(2)}) %copy-start.5) | copy-done | bytes 491544
  37.8 11.2 %shard_map.82 = bf16[192,1280]{1,0:T(8,128)(2,1)} custom-call(bf16[192,1280]{1,0:T(8,128)(2,1)} %q_ref.1, bf16[192,1280]{1,0:T(8,128)(2,1)} %refs_0_.1, bf16[192,1280]{1,0:T(8,128)(2,1)} %copy-done.1, bf16[192,1280]{1,0:T(8,128)(2,1)} %copy-done.2, bf16[192,1280]{1,0:T(8,128)(2,1)} %copy-done.5, bf16[192,1280]{1,0:T(8,128)(2,1)} %refs_4_.1, ...), custom_call_target="tpu_custom_call" | custom-call | flops 1761607680 | bytes 6946816 | tf_op jit(solution)/shard_map/pallas_call | solution.py:106
  48.9 3.7 %convolution_convert_fusion = bf16[192,1280]{1,0:T(8,128)(2,1)} fusion(bf16[192,1280]{1,0:T(8,128)(2,1)} %shard_map.82, bf16[1280,1280]{1,0:T(8,128)(2,1)} %param.13), kind=kOutput, calls=%fused_computation | convolution fusion | flops 629391360 | bytes 4259840 | tf_op jit(solution)/shard_map/dot_general | solution.py:168
  (36 shorter events, 0.4 us)
Async XLA Ops:
  0.0 31.5 %collective-permute-start = (bf16[192,1280]{1,0:T(8,128)(2,1)}, bf16[192,1280]{1,0:T(8,128)(2,1)S(1)}, u32[]{:S(2)}, u32[]{:S(2)}) collective-permute-start(bf16[192,1280]{1,0:T(8,128)(2,1)} %refs_0_.1), channel_id=1, source_target_pairs={{0,1},{1,0},{2,3},{3,2},{4,5},{5,4},{6,7},{7,6},{8,9},{9,8},{10,11... | collective-permute-start | bytes 1474568 | tf_op jit(solution)/shard_map/ppermute | solution.py:142
  0.5 26.8 %collective-permute-start.4 = (bf16[192,1280]{1,0:T(8,128)(2,1)}, bf16[192,1280]{1,0:T(8,128)(2,1)S(1)}, u32[]{:S(2)}, u32[]{:S(2)}) collective-permute-start(bf16[192,1280]{1,0:T(8,128)(2,1)} %refs_0_.1), channel_id=1, source_target_pairs={{0,2},{1,3},{2,0},{3,1},{4,6},{5,7},{6,4},{7,5},{8,10},{9,11},{10,... | collective-permute-start | bytes 1474568 | tf_op jit(solution)/shard_map/ppermute | solution.py:141
  3.0 24.3 %collective-permute-start.5 = (bf16[192,1280]{1,0:T(8,128)(2,1)}, bf16[192,1280]{1,0:T(8,128)(2,1)S(1)}, u32[]{:S(2)}, u32[]{:S(2)}) collective-permute-start(bf16[192,1280]{1,0:T(8,128)(2,1)} %refs_4_.1), channel_id=1, source_target_pairs={{0,2},{1,3},{2,0},{3,1},{4,6},{5,7},{6,4},{7,5},{8,10},{9,11},{10,... | collective-permute-start | bytes 1474568 | tf_op jit(solution)/shard_map/ppermute | solution.py:141
  3.0 33.0 %collective-permute-start.7 = (bf16[192,1280]{1,0:T(8,128)(2,1)}, bf16[192,1280]{1,0:T(8,128)(2,1)S(1)}, u32[]{:S(2)}, u32[]{:S(2)}) collective-permute-start(bf16[192,1280]{1,0:T(8,128)(2,1)} %refs_4_.1), channel_id=1, source_target_pairs={{0,1},{1,0},{2,3},{3,2},{4,5},{5,4},{6,7},{7,6},{8,9},{9,8},{10,11... | collective-permute-start | bytes 1474568 | tf_op jit(solution)/shard_map/ppermute | solution.py:142
  5.0 6.6 %collective-permute-start.1 = (bf16[32,2560]{1,0:T(8,128)(2,1)S(1)}, bf16[32,2560]{1,0:T(8,128)(2,1)S(1)}, u32[]{:S(2)}, u32[]{:S(2)}) collective-permute-start(bf16[32,2560]{1,0:T(8,128)(2,1)S(1)} %constant_dynamic-update-slice_fusion), channel_id=1, source_target_pairs={{0,4},{4,0},{8,12},{12,8},{16,20},{20,16},{24,28},{28,24},{1,5},{5... | collective-permute-start | bytes 491528 | tf_op jit(solution)/shard_map/ppermute | solution.py:27
  11.6 6.0 %collective-permute-start.2 = (bf16[32,2560]{1,0:T(8,128)(2,1)S(1)}, bf16[32,2560]{1,0:T(8,128)(2,1)S(1)}, u32[]{:S(2)}, u32[]{:S(2)}) collective-permute-start(bf16[32,2560]{1,0:T(8,128)(2,1)S(1)} %broadcast_select_fusion), channel_id=1, source_target_pairs={{0,8},{4,12},{8,0},{12,4},{16,24},{20,28},{24,16},{28,20},{1,9},{5... | collective-permute-start | bytes 491528 | tf_op jit(solution)/shard_map/ppermute | solution.py:27
  17.7 9.5 %collective-permute-start.3 = (bf16[32,2560]{1,0:T(8,128)(2,1)S(1)}, bf16[32,2560]{1,0:T(8,128)(2,1)S(1)}, u32[]{:S(2)}, u32[]{:S(2)}) collective-permute-start(bf16[32,2560]{1,0:T(8,128)(2,1)S(1)} %broadcast_select_fusion.1), channel_id=1, source_target_pairs={{0,16},{4,20},{8,24},{12,28},{16,0},{20,4},{24,8},{28,12},{1,17},{... | collective-permute-start | bytes 491528 | tf_op jit(solution)/shard_map/ppermute | solution.py:27
  27.2 8.9 %copy-start = (bf16[32,2560]{1,0:T(8,128)(2,1)}, bf16[32,2560]{1,0:T(8,128)(2,1)S(1)}, u32[]{:S(2)}) copy-start(bf16[32,2560]{1,0:T(8,128)(2,1)S(1)} %broadcast_select_fusion.2.refs_12_.refs_16_) | copy-start | bytes 491524
  27.2 8.9 %copy-start.2 = (bf16[192,1280]{1,0:T(8,128)(2,1)}, bf16[192,1280]{1,0:T(8,128)(2,1)S(1)}, u32[]{:S(2)}) copy-start(bf16[192,1280]{1,0:T(8,128)(2,1)S(1)} %collective-permute-done.4.refs_2_) | copy-start | bytes 1474564
  27.2 8.9 %copy-start.3 = (bf16[192,1280]{1,0:T(8,128)(2,1)}, bf16[192,1280]{1,0:T(8,128)(2,1)S(1)}, u32[]{:S(2)}) copy-start(bf16[192,1280]{1,0:T(8,128)(2,1)S(1)} %collective-permute-done.5.refs_6_) | copy-start | bytes 1474564
  27.3 8.9 %collective-permute-start.6 = (bf16[192,1280]{1,0:T(8,128)(2,1)S(1)}, bf16[192,1280]{1,0:T(8,128)(2,1)S(1)}, u32[]{:S(2)}, u32[]{:S(2)}) collective-permute-start(bf16[192,1280]{1,0:T(8,128)(2,1)S(1)} %collective-permute-done.4.refs_2_), channel_id=1, source_target_pairs={{0,1},{1,0},{2,3},{3,2},{4,5},{5,4},{6,7},{7,6},{8,9},{9,8},{10,11... | collective-permute-start | bytes 1474568 | tf_op jit(solution)/shard_map/ppermute | solution.py:144
  27.3 10.4 %collective-permute-start.8 = (bf16[192,1280]{1,0:T(8,128)(2,1)S(1)}, bf16[192,1280]{1,0:T(8,128)(2,1)}, u32[]{:S(2)}, u32[]{:S(2)}) collective-permute-start(bf16[192,1280]{1,0:T(8,128)(2,1)S(1)} %collective-permute-done.5.refs_6_), channel_id=1, source_target_pairs={{0,1},{1,0},{2,3},{3,2},{4,5},{5,4},{6,7},{7,6},{8,9},{9,8},{10,11... | collective-permute-start | bytes 1474568 | tf_op jit(solution)/shard_map/ppermute | solution.py:144
  28.2 6.2 %collective-permute-start.9 = (bf16[32,2560]{1,0:T(8,128)(2,1)S(1)}, bf16[32,2560]{1,0:T(8,128)(2,1)S(1)}, u32[]{:S(2)}, u32[]{:S(2)}) collective-permute-start(bf16[32,2560]{1,0:T(8,128)(2,1)S(1)} %broadcast_select_fusion.2.refs_12_.refs_16_), channel_id=1, source_target_pairs={{0,2},{1,3},{2,0},{3,1},{4,6},{5,7},{6,4},{7,5},{8,10},{9,11},{10,... | collective-permute-start | bytes 491528 | tf_op jit(solution)/shard_map/ppermute | solution.py:145
  31.5 4.6 %copy-start.1 = (bf16[192,1280]{1,0:T(8,128)(2,1)}, bf16[192,1280]{1,0:T(8,128)(2,1)S(1)}, u32[]{:S(2)}) copy-start(bf16[192,1280]{1,0:T(8,128)(2,1)S(1)} %collective-permute-done.refs_1_) | copy-start | bytes 1474564
  31.5 4.6 %collective-permute-start.10 = (bf16[32,2560]{1,0:T(8,128)(2,1)S(1)}, bf16[32,2560]{1,0:T(8,128)(2,1)S(1)}, u32[]{:S(2)}, u32[]{:S(2)}) collective-permute-start(bf16[32,2560]{1,0:T(8,128)(2,1)S(1)} %broadcast_select_fusion.2.refs_12_.refs_16_), channel_id=1, source_target_pairs={{0,1},{1,0},{2,3},{3,2},{4,5},{5,4},{6,7},{7,6},{8,9},{9,8},{10,11... | collective-permute-start | bytes 491528 | tf_op jit(solution)/shard_map/ppermute | solution.py:146
  34.5 1.7 %copy-start.6 = (bf16[32,2560]{1,0:T(8,128)(2,1)}, bf16[32,2560]{1,0:T(8,128)(2,1)S(1)}, u32[]{:S(2)}) copy-start(bf16[32,2560]{1,0:T(8,128)(2,1)S(1)} %collective-permute-done.9.refs_13_.refs_17_) | copy-start | bytes 491524
  34.5 1.6 %collective-permute-start.11 = (bf16[32,2560]{1,0:T(8,128)(2,1)S(1)}, bf16[32,2560]{1,0:T(8,128)(2,1)S(1)}, u32[]{:S(2)}, u32[]{:S(2)}) collective-permute-start(bf16[32,2560]{1,0:T(8,128)(2,1)S(1)} %collective-permute-done.9.refs_13_.refs_17_), channel_id=1, source_target_pairs={{0,1},{1,0},{2,3},{3,2},{4,5},{5,4},{6,7},{7,6},{8,9},{9,8},{10,11... | collective-permute-start | bytes 491528 | tf_op jit(solution)/shard_map/ppermute | solution.py:146
  36.1 0.8 %copy-start.4 = (bf16[192,1280]{1,0:T(8,128)(2,1)}, bf16[192,1280]{1,0:T(8,128)(2,1)S(1)}, u32[]{:S(2)}) copy-start(bf16[192,1280]{1,0:T(8,128)(2,1)S(1)} %collective-permute-done.7.refs_5_) | copy-start | bytes 1474564
  36.1 0.8 %copy-start.7 = (bf16[32,2560]{1,0:T(8,128)(2,1)}, bf16[32,2560]{1,0:T(8,128)(2,1)S(1)}, u32[]{:S(2)}) copy-start(bf16[32,2560]{1,0:T(8,128)(2,1)S(1)} %collective-permute-done.10.refs_14_.refs_18_) | copy-start | bytes 491524
  36.1 0.9 %copy-start.8 = (bf16[32,2560]{1,0:T(8,128)(2,1)}, bf16[32,2560]{1,0:T(8,128)(2,1)S(1)}, u32[]{:S(2)}) copy-start(bf16[32,2560]{1,0:T(8,128)(2,1)S(1)} %collective-permute-done.11.refs_15_.refs_19_) | copy-start | bytes 491524
  37.0 0.8 %copy-start.5 = (bf16[192,1280]{1,0:T(8,128)(2,1)}, bf16[192,1280]{1,0:T(8,128)(2,1)S(1)}, u32[]{:S(2)}) copy-start(bf16[192,1280]{1,0:T(8,128)(2,1)S(1)} %collective-permute-done.6.refs_3_) | copy-start | bytes 1474564

commit v12 on v10

--- a/solution.py
+++ b/solution.py
@@ -129,18 +129,19 @@
     view_index = lax.axis_index("view")
     view_tok = shard_rows * view_count // VIEWS
 
+    ref_both = jnp.concatenate([ref_keys, ref_values], axis=1)
+    ref_shared = tree_broadcast(ref_both, "mesh", ref_source[0])
     if view_count == 4:
         across = lax.ppermute((keys, values), "view", [(i, i ^ 2) for i in range(view_count)])
         near = lax.ppermute((keys, values), "view", [(i, i ^ 1) for i in range(view_count)])
+        ref_shared, across = lax.optimization_barrier((ref_shared, across))
         far = lax.ppermute(across, "view", [(i, i ^ 1) for i in range(view_count)])
         pieces = [(keys, values), near, across, far]
         positions = [view_index, view_index ^ 1, view_index ^ 2, view_index ^ 3]
     else:
         pieces = [lax.all_gather((keys, values), "view", axis=0, tiled=True)]
         positions = [jnp.zeros((), jnp.int32)]
-
-    ref_both = jnp.concatenate([ref_keys, ref_values], axis=1)
-    ref_all = gather_rows(tree_broadcast(ref_both, "mesh", ref_source[0]), "view")
+    ref_all = gather_rows(ref_shared, "view")
 
     view_ids = jnp.arange(VIEWS, dtype=jnp.int32)
     query_views = (view_index * shard_rows + jnp.arange(shard_rows, dtype=jnp.int32)) // view_tok

time: 49.1 us -> 47.7 us (0.971)
  other arithmetic: 2.4 us -> 1.44 us
    ppermute x1, waiting for transfers between devices: 7.57 us -> 3.21 us  [gather_rows(): across = lax.ppermute(value, axis, [(i, i ^ 2) for i in range(count)])]
    ppermute x3, waiting for transfers between devices: 10.2 us -> 13.9 us  [tree_broadcast(): received = lax.ppermute(value, axis, pairs)]
    ppermute x3, starting transfers between devices: 7.67 us -> 6.52 us  [tree_broadcast(): received = lax.ppermute(value, axis, pairs)]
    ppermute x1, waiting for transfers between devices: 0.5 us -> 1.59 us  [gather_rows(): near = lax.ppermute(both, axis, [(i, i ^ 1) for i in range(count)])]
    concatenate x1 -> x0, other arithmetic: 0.96 us -> none  [gather_rows(): return jnp.concatenate([both, near], axis=0)]
    select_n x3, other arithmetic: 0.06 us -> 0.98 us  [tree_broadcast(): value = jnp.where(partner_has, received, value)]
    concatenate x1, other arithmetic: 0.94 us -> 0.02 us  [gather_rows(): both = jnp.concatenate([value, across], axis=0)]
    ppermute x2, waiting for transfers between devices: 0.78 us -> 0.01 us  [body(): far = lax.ppermute(across, 'view', [(i, i ^ 1) for i in range(view_count)])]
  transfers between devices with their start and end apart: 11 -> 11, of which waited for: 7 -> 5; matrix products, arithmetic and copies ran while one was open for 7% -> 9% of each run, Pallas kernels for 0% -> 0%
where the time goes in v12:
time: 47.7 us; the launch traced here: 47.5 us
  waiting for transfers between devices  18.7 us (39%)
  starting transfers between devices  12 us (25%)
  Pallas kernels  9.18 us (19%)
  local copies, waits for them, and re-layouts  2.68 us (6%)
  matrix products  2.49 us (5%)
  other arithmetic  1.44 us (3%)
  between operations  0.96 us (2%)
    ppermute x3, waiting for transfers between devices, tree_broadcast(): received = lax.ppermute(value, axis, pairs)  13.9 us
    pallas_call x1, Pallas kernels, attention(): pl.pallas_call(functools.partial(attention_kernel, len(key_pieces), span...  9.18 us
    ppermute x3, starting transfers between devices, tree_broadcast(): received = lax.ppermute(value, axis, pairs)  6.52 us
    ppermute x1, waiting for transfers between devices, gather_rows(): across = lax.ppermute(value, axis, [(i, i ^ 2) for i in range(count)])  3.21 us
    ppermute x2, starting transfers between devices, body(): lax.ppermute((keys, values), 'view', [(i, i ^ 2) for i in range(view_coun...  2.68 us
    unnamed x15, local copies, waits for them, and re-layouts  1.72 us
    ppermute x1, waiting for transfers between devices, gather_rows(): near = lax.ppermute(both, axis, [(i, i ^ 1) for i in range(count)])  1.59 us
    dot_general x1, matrix products, body(): jnp.dot(mixed, out_weight, preferred_element_type=jnp.float32)  1.59 us
  transfers between devices with their start and end apart: 11, of which 5 were waited for; matrix products, arithmetic and copies ran while one was open for 9% of the time, Pallas kernels for 0%

profile of v12, /device:TPU:0, one launch (start us, length us, event | category | flops | bytes accessed | tf_op | source)
XLA Modules:
  0.0 47.5 jit_solution(10646428018998959419)
XLA Ops:
  0.0 0.5 collective-permute-start
  0.5 2.6 %collective-permute-start.4 = (bf16[192,1280]{1,0:T(8,128)(2,1)}, bf16[192,1280]{1,0:T(8,128)(2,1)}, u32[]{:S(2)}, u32[]{:S(2)}) collective-permute-start(bf16[192,1280]{1,0:T(8,128)(2,1)} %refs_0_.1), channel_id=1, source_target_pairs={{0,2},{1,3},{2,0},{3,1},{4,6},{5,7},{6,4},{7,5},{8,10},{9,11},{10,... | collective-permute-start | bytes 1474568 | tf_op jit(solution)/shard_map/ppermute | solution.py:135
  3.0 0.1 collective-permute-start.5
  3.1 0.1 collective-permute-start.7
  3.2 0.9 %constant_dynamic-update-slice_fusion.1 = bf16[32,2560]{1,0:T(8,128)(2,1)S(1)} fusion(bf16[32,1280]{1,0:T(8,128)(2,1)} %param.11), kind=kLoop, calls=%fused_computation.13 | loop fusion | bytes 163840
  4.1 0.9 %constant_dynamic-update-slice_fusion = bf16[32,2560]{1,0:T(8,128)(2,1)S(1)} fusion(bf16[32,2560]{1,0:T(8,128)(2,1)S(1)} %constant_dynamic-update-slice_fusion.1, bf16[32,1280]{1,0:T(8,128)(2,1)} %param.12), kind=kLoop, calls=%fused_computation.12 | loop fusion | bytes 163840 | tf_op jit(solution)/shard_map/concatenate | solution.py:132
  5.0 1.8 %collective-permute-start.1 = (bf16[32,2560]{1,0:T(8,128)(2,1)S(1)}, bf16[32,2560]{1,0:T(8,128)(2,1)}, u32[]{:S(2)}, u32[]{:S(2)}) collective-permute-start(bf16[32,2560]{1,0:T(8,128)(2,1)S(1)} %constant_dynamic-update-slice_fusion), channel_id=1, source_target_pairs={{0,4},{4,0},{8,12},{12,8},{16,20},{20,16},{24,28},{28,24},{1,5},{5... | collective-permute-start | bytes 491528 | tf_op jit(solution)/shard_map/ppermute | solution.py:27
  6.8 0.9 %fusion = f32[192,3]{0,1:T(4,128)S(1)} fusion(s32[192]{0:T(256)S(1)} %get-tuple-element.20, s32[6,3]{0,1:T(4,128)} %param.14), kind=kOutput, calls=%fused_computation.10 | convolution fusion | flops 8082 | bytes 3144 | tf_op jit(solution)/shard_map/dot_general | solution.py:149
  8.5 3.4 %collective-permute-done.1 = bf16[32,2560]{1,0:T(8,128)(2,1)} collective-permute-done((bf16[32,2560]{1,0:T(8,128)(2,1)S(1)}, bf16[32,2560]{1,0:T(8,128)(2,1)}, u32[]{:S(2)}, u32[]{:S(2)}) %collective-permute-start.1) | collective-permute-done | bytes 163872 | tf_op jit(solution)/shard_map/ppermute | solution.py:27
  11.8 0.9 %broadcast_select_fusion = bf16[32,2560]{1,0:T(8,128)(2,1)S(1)} fusion(bf16[32,2560]{1,0:T(8,128)(2,1)} %collective-permute-done.1, bf16[32,2560]{1,0:T(8,128)(2,1)} %copy-done.4, pred[]{:T(512)S(6)} %eq.76), kind=kLoop, calls=%fused_computation.6 | loop fusion | flops 81920 | bytes 491521 | tf_op jit(solution)/shard_map/jit(_where)/select_n | solution.py:29
  12.7 1.9 %collective-permute-start.2 = (bf16[32,2560]{1,0:T(8,128)(2,1)S(1)}, bf16[32,2560]{1,0:T(8,128)(2,1)}, u32[]{:S(2)}, u32[]{:S(2)}) collective-permute-start(bf16[32,2560]{1,0:T(8,128)(2,1)S(1)} %broadcast_select_fusion), channel_id=1, source_target_pairs={{0,8},{4,12},{8,0},{12,4},{16,24},{20,28},{24,16},{28,20},{1,9},{5... | collective-permute-start | bytes 491528 | tf_op jit(solution)/shard_map/ppermute | solution.py:27
  14.8 4.0 %collective-permute-done.2 = bf16[32,2560]{1,0:T(8,128)(2,1)} collective-permute-done((bf16[32,2560]{1,0:T(8,128)(2,1)S(1)}, bf16[32,2560]{1,0:T(8,128)(2,1)}, u32[]{:S(2)}, u32[]{:S(2)}) %collective-permute-start.2) | collective-permute-done | bytes 163872 | tf_op jit(solution)/shard_map/ppermute | solution.py:27
  18.9 2.8 %collective-permute-start.3 = (bf16[32,2560]{1,0:T(8,128)(2,1)S(1)}, bf16[32,2560]{1,0:T(8,128)(2,1)S(1)}, u32[]{:S(2)}, u32[]{:S(2)}) collective-permute-start(bf16[32,2560]{1,0:T(8,128)(2,1)S(1)} %broadcast_select_fusion.1), channel_id=1, source_target_pairs={{0,16},{4,20},{8,24},{12,28},{16,0},{20,4},{24,8},{28,12},{1,17},{... | collective-permute-start | bytes 491528 | tf_op jit(solution)/shard_map/ppermute | solution.py:27
  21.7 0.4 or_select_fusion
  22.1 6.5 %collective-permute-done.3 = bf16[32,2560]{1,0:T(8,128)(2,1)S(1)} collective-permute-done((bf16[32,2560]{1,0:T(8,128)(2,1)S(1)}, bf16[32,2560]{1,0:T(8,128)(2,1)S(1)}, u32[]{:S(2)}, u32[]{:S(2)}) %collective-permute-start.3) | collective-permute-done | bytes 163872 | tf_op jit(solution)/shard_map/ppermute | solution.py:27
  28.7 1.6 %collective-permute-start.9 = (bf16[32,2560]{1,0:T(8,128)(2,1)S(1)}, bf16[32,2560]{1,0:T(8,128)(2,1)S(1)}, u32[]{:S(2)}, u32[]{:S(2)}) collective-permute-start(bf16[32,2560]{1,0:T(8,128)(2,1)S(1)} %broadcast_select_fusion.2), channel_id=1, source_target_pairs={{0,2},{1,3},{2,0},{3,1},{4,6},{5,7},{6,4},{7,5},{8,10},{9,11},{10,... | collective-permute-start | bytes 491528 | tf_op jit(solution)/shard_map/ppermute | solution.py:37
  30.3 0.1 collective-permute-start.6
  30.3 0.5 %collective-permute-start.8 = (bf16[192,1280]{1,0:T(8,128)(2,1)}, bf16[192,1280]{1,0:T(8,128)(2,1)S(1)}, u32[]{:S(2)}, u32[]{:S(2)}) collective-permute-start(bf16[192,1280]{1,0:T(8,128)(2,1)} %collective-permute-done.5.refs_6_), channel_id=1, source_target_pairs={{0,1},{1,0},{2,3},{3,2},{4,5},{5,4},{6,7},{7,6},{8,9},{9,8},{10,11... | collective-permute-start | bytes 1474568 | tf_op jit(solution)/shard_map/ppermute | solution.py:138
  30.8 3.2 %collective-permute-done.9 = bf16[32,2560]{1,0:T(8,128)(2,1)S(1)} collective-permute-done((bf16[32,2560]{1,0:T(8,128)(2,1)S(1)}, bf16[32,2560]{1,0:T(8,128)(2,1)S(1)}, u32[]{:S(2)}, u32[]{:S(2)}) %collective-permute-start.9) | collective-permute-done | bytes 163872 | tf_op jit(solution)/shard_map/ppermute | solution.py:37
  34.1 0.1 collective-permute-start.10
  34.2 1.6 %collective-permute-done.10 = bf16[64,2560]{1,0:T(8,128)(2,1)S(1)} collective-permute-done((bf16[64,2560]{1,0:T(8,128)(2,1)S(1)}, bf16[64,2560]{1,0:T(8,128)(2,1)S(1)}, u32[]{:S(2)}, u32[]{:S(2)}) %collective-permute-start.10) | collective-permute-done | bytes 327712 | tf_op jit(solution)/shard_map/ppermute | solution.py:39
  35.9 0.8 %copy-done.5 = bf16[192,1280]{1,0:T(8,128)(2,1)} copy-done((bf16[192,1280]{1,0:T(8,128)(2,1)}, bf16[192,1280]{1,0:T(8,128)(2,1)S(1)}, u32[]{:S(2)}) %copy-start.5) | copy-done | bytes 491544
  36.7 9.2 %shard_map.82 = bf16[192,1280]{1,0:T(8,128)(2,1)S(1)} custom-call(bf16[192,1280]{1,0:T(8,128)(2,1)S(1)} %copy-done.1, bf16[192,1280]{1,0:T(8,128)(2,1)S(1)} %copy-done.2, bf16[192,1280]{1,0:T(8,128)(2,1)} %collective-permute-done.refs_1_, bf16[192,1280]{1,0:T(8,128)(2,1)} %collective-permute-done.4.refs_2_, ...), custom_call_target="tpu_custom_call" | custom-call | flops 1761607680 | bytes 6258688 | tf_op jit(solution)/shard_map/pallas_call | solution.py:100
  45.9 1.6 %convolution_convert_fusion = bf16[192,1280]{1,0:T(8,128)(2,1)} fusion(bf16[192,1280]{1,0:T(8,128)(2,1)S(1)} %shard_map.82, bf16[1280,1280]{1,0:T(8,128)(2,1)S(1)} %copy-done), kind=kOutput, calls=%fused_computation | convolution fusion | flops 629391360 | bytes 4259840 | tf_op jit(solution)/shard_map/dot_general | solution.py:164
  (29 shorter events, 0.3 us)
Async XLA Ops:
  0.0 45.9 %copy-start = (bf16[1280,1280]{1,0:T(8,128)(2,1)S(1)}, bf16[1280,1280]{1,0:T(8,128)(2,1)}, u32[]{:S(2)}) copy-start(bf16[1280,1280]{1,0:T(8,128)(2,1)} %param.13) | copy-start | bytes 9830404
  0.0 35.8 %collective-permute-start = (bf16[192,1280]{1,0:T(8,128)(2,1)}, bf16[192,1280]{1,0:T(8,128)(2,1)}, u32[]{:S(2)}, u32[]{:S(2)}) collective-permute-start(bf16[192,1280]{1,0:T(8,128)(2,1)} %refs_0_.1), channel_id=1, source_target_pairs={{0,1},{1,0},{2,3},{3,2},{4,5},{5,4},{6,7},{7,6},{8,9},{9,8},{10,11... | collective-permute-start | bytes 1474568 | tf_op jit(solution)/shard_map/ppermute | solution.py:136
  0.5 28.2 %collective-permute-start.4 = (bf16[192,1280]{1,0:T(8,128)(2,1)}, bf16[192,1280]{1,0:T(8,128)(2,1)}, u32[]{:S(2)}, u32[]{:S(2)}) collective-permute-start(bf16[192,1280]{1,0:T(8,128)(2,1)} %refs_0_.1), channel_id=1, source_target_pairs={{0,2},{1,3},{2,0},{3,1},{4,6},{5,7},{6,4},{7,5},{8,10},{9,11},{10,... | collective-permute-start | bytes 1474568 | tf_op jit(solution)/shard_map/ppermute | solution.py:135
  3.0 25.6 %collective-permute-start.5 = (bf16[192,1280]{1,0:T(8,128)(2,1)}, bf16[192,1280]{1,0:T(8,128)(2,1)}, u32[]{:S(2)}, u32[]{:S(2)}) collective-permute-start(bf16[192,1280]{1,0:T(8,128)(2,1)} %refs_4_.1), channel_id=1, source_target_pairs={{0,2},{1,3},{2,0},{3,1},{4,6},{5,7},{6,4},{7,5},{8,10},{9,11},{10,... | collective-permute-start | bytes 1474568 | tf_op jit(solution)/shard_map/ppermute | solution.py:135
  3.1 32.7 %collective-permute-start.7 = (bf16[192,1280]{1,0:T(8,128)(2,1)}, bf16[192,1280]{1,0:T(8,128)(2,1)}, u32[]{:S(2)}, u32[]{:S(2)}) collective-permute-start(bf16[192,1280]{1,0:T(8,128)(2,1)} %refs_4_.1), channel_id=1, source_target_pairs={{0,1},{1,0},{2,3},{3,2},{4,5},{5,4},{6,7},{7,6},{8,9},{9,8},{10,11... | collective-permute-start | bytes 1474568 | tf_op jit(solution)/shard_map/ppermute | solution.py:136
  5.0 3.4 %copy-start.4 = (bf16[32,2560]{1,0:T(8,128)(2,1)}, bf16[32,2560]{1,0:T(8,128)(2,1)S(1)}, u32[]{:S(2)}) copy-start(bf16[32,2560]{1,0:T(8,128)(2,1)S(1)} %constant_dynamic-update-slice_fusion) | copy-start | bytes 491524
  5.0 6.8 %collective-permute-start.1 = (bf16[32,2560]{1,0:T(8,128)(2,1)S(1)}, bf16[32,2560]{1,0:T(8,128)(2,1)}, u32[]{:S(2)}, u32[]{:S(2)}) collective-permute-start(bf16[32,2560]{1,0:T(8,128)(2,1)S(1)} %constant_dynamic-update-slice_fusion), channel_id=1, source_target_pairs={{0,4},{4,0},{8,12},{12,8},{16,20},{20,16},{24,28},{28,24},{1,5},{5... | collective-permute-start | bytes 491528 | tf_op jit(solution)/shard_map/ppermute | solution.py:27
  12.7 6.1 %collective-permute-start.2 = (bf16[32,2560]{1,0:T(8,128)(2,1)S(1)}, bf16[32,2560]{1,0:T(8,128)(2,1)}, u32[]{:S(2)}, u32[]{:S(2)}) collective-permute-start(bf16[32,2560]{1,0:T(8,128)(2,1)S(1)} %broadcast_select_fusion), channel_id=1, source_target_pairs={{0,8},{4,12},{8,0},{12,4},{16,24},{20,28},{24,16},{28,20},{1,9},{5... | collective-permute-start | bytes 491528 | tf_op jit(solution)/shard_map/ppermute | solution.py:27
  14.7 21.9 %copy-start.1 = (bf16[192,1280]{1,0:T(8,128)(2,1)S(1)}, bf16[192,1280]{1,0:T(8,128)(2,1)}, u32[]{:S(2)}) copy-start(bf16[192,1280]{1,0:T(8,128)(2,1)} %q_ref.1) | copy-start | bytes 1474564
  14.8 21.9 %copy-start.2 = (bf16[192,1280]{1,0:T(8,128)(2,1)S(1)}, bf16[192,1280]{1,0:T(8,128)(2,1)}, u32[]{:S(2)}) copy-start(bf16[192,1280]{1,0:T(8,128)(2,1)} %refs_0_.1) | copy-start | bytes 1474564
  14.8 21.9 %copy-start.3 = (bf16[192,1280]{1,0:T(8,128)(2,1)S(1)}, bf16[192,1280]{1,0:T(8,128)(2,1)}, u32[]{:S(2)}) copy-start(bf16[192,1280]{1,0:T(8,128)(2,1)} %refs_4_.1) | copy-start | bytes 1474564
  18.9 9.7 %collective-permute-start.3 = (bf16[32,2560]{1,0:T(8,128)(2,1)S(1)}, bf16[32,2560]{1,0:T(8,128)(2,1)S(1)}, u32[]{:S(2)}, u32[]{:S(2)}) collective-permute-start(bf16[32,2560]{1,0:T(8,128)(2,1)S(1)} %broadcast_select_fusion.1), channel_id=1, source_target_pairs={{0,16},{4,20},{8,24},{12,28},{16,0},{20,4},{24,8},{28,12},{1,17},{... | collective-permute-start | bytes 491528 | tf_op jit(solution)/shard_map/ppermute | solution.py:27
  28.7 5.4 %collective-permute-start.9 = (bf16[32,2560]{1,0:T(8,128)(2,1)S(1)}, bf16[32,2560]{1,0:T(8,128)(2,1)S(1)}, u32[]{:S(2)}, u32[]{:S(2)}) collective-permute-start(bf16[32,2560]{1,0:T(8,128)(2,1)S(1)} %broadcast_select_fusion.2), channel_id=1, source_target_pairs={{0,2},{1,3},{2,0},{3,1},{4,6},{5,7},{6,4},{7,5},{8,10},{9,11},{10,... | collective-permute-start | bytes 491528 | tf_op jit(solution)/shard_map/ppermute | solution.py:37
  30.3 5.6 %collective-permute-start.6 = (bf16[192,1280]{1,0:T(8,128)(2,1)}, bf16[192,1280]{1,0:T(8,128)(2,1)S(1)}, u32[]{:S(2)}, u32[]{:S(2)}) collective-permute-start(bf16[192,1280]{1,0:T(8,128)(2,1)} %collective-permute-done.4.refs_2_), channel_id=1, source_target_pairs={{0,1},{1,0},{2,3},{3,2},{4,5},{5,4},{6,7},{7,6},{8,9},{9,8},{10,11... | collective-permute-start | bytes 1474568 | tf_op jit(solution)/shard_map/ppermute | solution.py:138
  30.3 5.5 %collective-permute-start.8 = (bf16[192,1280]{1,0:T(8,128)(2,1)}, bf16[192,1280]{1,0:T(8,128)(2,1)S(1)}, u32[]{:S(2)}, u32[]{:S(2)}) collective-permute-start(bf16[192,1280]{1,0:T(8,128)(2,1)} %collective-permute-done.5.refs_6_), channel_id=1, source_target_pairs={{0,1},{1,0},{2,3},{3,2},{4,5},{5,4},{6,7},{7,6},{8,9},{9,8},{10,11... | collective-permute-start | bytes 1474568 | tf_op jit(solution)/shard_map/ppermute | solution.py:138
  34.1 1.7 %collective-permute-start.10 = (bf16[64,2560]{1,0:T(8,128)(2,1)S(1)}, bf16[64,2560]{1,0:T(8,128)(2,1)S(1)}, u32[]{:S(2)}, u32[]{:S(2)}) collective-permute-start(bf16[64,2560]{1,0:T(8,128)(2,1)S(1)} %pad_maximum_fusion), channel_id=1, source_target_pairs={{0,1},{1,0},{2,3},{3,2},{4,5},{5,4},{6,7},{7,6},{8,9},{9,8},{10,11... | collective-permute-start | bytes 983048 | tf_op jit(solution)/shard_map/ppermute | solution.py:39
  35.9 0.8 %copy-start.5 = (bf16[192,1280]{1,0:T(8,128)(2,1)}, bf16[192,1280]{1,0:T(8,128)(2,1)S(1)}, u32[]{:S(2)}) copy-start(bf16[192,1280]{1,0:T(8,128)(2,1)S(1)} %collective-permute-done.8.refs_7_) | copy-start | bytes 1474564

commit v13 on v12

--- a/solution.py
+++ b/solution.py
@@ -21,13 +21,13 @@
     if count & (count - 1):
         kept = jnp.where(index == source, value, jnp.zeros_like(value))
         return lax.psum(kept, axis)
-    distance = 1
-    while distance < count:
+    distance = count // 2
+    while distance >= 1:
         pairs = [(i, i ^ distance) for i in range(count)]
         received = lax.ppermute(value, axis, pairs)
-        partner_has = ((index ^ distance) // distance) == (source // distance)
+        partner_has = ((index ^ distance) % (2 * distance)) == (source % (2 * distance))
         value = jnp.where(partner_has, received, value)
-        distance *= 2
+        distance //= 2
     return value
 
 

time: 47.7 us -> 48.5 us (1.017)
  waiting for transfers between devices: 18.7 us -> 20.7 us
  starting transfers between devices: 12 us -> 10.4 us
    ppermute x3, waiting for transfers between devices: 13.9 us -> 15.7 us  [tree_broadcast(): received = lax.ppermute(value, axis, pairs)]
    ppermute x3, starting transfers between devices: 6.52 us -> 5.03 us  [tree_broadcast(): received = lax.ppermute(value, axis, pairs)]
where the time goes in v13:
time: 48.5 us; the launch traced here: 47.8 us
  waiting for transfers between devices  20.7 us (43%)
  starting transfers between devices  10.4 us (21%)
  Pallas kernels  9.16 us (19%)
  local copies, waits for them, and re-layouts  2.68 us (6%)
  matrix products  2.48 us (5%)
  other arithmetic  1.44 us (3%)
  between operations  0.97 us (2%)
    ppermute x3, waiting for transfers between devices, tree_broadcast(): received = lax.ppermute(value, axis, pairs)  15.7 us
    pallas_call x1, Pallas kernels, attention(): pl.pallas_call(functools.partial(attention_kernel, len(key_pieces), span...  9.16 us
    ppermute x3, starting transfers between devices, tree_broadcast(): received = lax.ppermute(value, axis, pairs)  5.03 us
    ppermute x1, waiting for transfers between devices, gather_rows(): across = lax.ppermute(value, axis, [(i, i ^ 2) for i in range(count)])  3.34 us
    ppermute x2, starting transfers between devices, body(): lax.ppermute((keys, values), 'view', [(i, i ^ 2) for i in range(view_coun...  2.68 us
    unnamed x15, local copies, waits for them, and re-layouts  1.72 us
    ppermute x1, waiting for transfers between devices, gather_rows(): near = lax.ppermute(both, axis, [(i, i ^ 1) for i in range(count)])  1.59 us
    dot_general x1, matrix products, body(): jnp.dot(mixed, out_weight, preferred_element_type=jnp.float32)  1.59 us
  transfers between devices with their start and end apart: 11, of which 5 were waited for; matrix products, arithmetic and copies ran while one was open for 9% of the time, Pallas kernels for 0%

profile of v13, /device:TPU:0, one launch (start us, length us, event | category | flops | bytes accessed | tf_op | source)
XLA Modules:
  0.0 47.8 jit_solution(8203009876145085168)
XLA Ops:
  0.0 0.5 collective-permute-start
  0.5 2.6 %collective-permute-start.4 = (bf16[192,1280]{1,0:T(8,128)(2,1)}, bf16[192,1280]{1,0:T(8,128)(2,1)}, u32[]{:S(2)}, u32[]{:S(2)}) collective-permute-start(bf16[192,1280]{1,0:T(8,128)(2,1)} %refs_0_.1), channel_id=1, source_target_pairs={{0,2},{1,3},{2,0},{3,1},{4,6},{5,7},{6,4},{7,5},{8,10},{9,11},{10,... | collective-permute-start | bytes 1474568 | tf_op jit(solution)/shard_map/ppermute | solution.py:135
  3.0 0.1 collective-permute-start.5
  3.1 0.1 collective-permute-start.7
  3.2 0.9 %constant_dynamic-update-slice_fusion.1 = bf16[32,2560]{1,0:T(8,128)(2,1)S(1)} fusion(bf16[32,1280]{1,0:T(8,128)(2,1)} %param.11), kind=kLoop, calls=%fused_computation.13 | loop fusion | bytes 163840
  4.1 0.9 %constant_dynamic-update-slice_fusion = bf16[32,2560]{1,0:T(8,128)(2,1)S(1)} fusion(bf16[32,2560]{1,0:T(8,128)(2,1)S(1)} %constant_dynamic-update-slice_fusion.1, bf16[32,1280]{1,0:T(8,128)(2,1)} %param.12), kind=kLoop, calls=%fused_computation.12 | loop fusion | bytes 163840 | tf_op jit(solution)/shard_map/concatenate | solution.py:132
  5.0 2.9 %collective-permute-start.1 = (bf16[32,2560]{1,0:T(8,128)(2,1)S(1)}, bf16[32,2560]{1,0:T(8,128)(2,1)}, u32[]{:S(2)}, u32[]{:S(2)}) collective-permute-start(bf16[32,2560]{1,0:T(8,128)(2,1)S(1)} %constant_dynamic-update-slice_fusion), channel_id=1, source_target_pairs={{0,16},{4,20},{8,24},{12,28},{16,0},{20,4},{24,8},{28,12},{1,17},{... | collective-permute-start | bytes 491528 | tf_op jit(solution)/shard_map/ppermute | solution.py:27
  7.9 0.9 %fusion = f32[192,3]{0,1:T(4,128)S(1)} fusion(s32[192]{0:T(256)S(1)} %get-tuple-element.20, s32[6,3]{0,1:T(4,128)} %param.14), kind=kOutput, calls=%fused_computation.10 | convolution fusion | flops 8082 | bytes 3144 | tf_op jit(solution)/shard_map/dot_general | solution.py:149
  9.6 6.8 %collective-permute-done.1 = bf16[32,2560]{1,0:T(8,128)(2,1)} collective-permute-done((bf16[32,2560]{1,0:T(8,128)(2,1)S(1)}, bf16[32,2560]{1,0:T(8,128)(2,1)}, u32[]{:S(2)}, u32[]{:S(2)}) %collective-permute-start.1) | collective-permute-done | bytes 163872 | tf_op jit(solution)/shard_map/ppermute | solution.py:27
  16.4 0.9 %broadcast_select_fusion = bf16[32,2560]{1,0:T(8,128)(2,1)S(1)} fusion(bf16[32,2560]{1,0:T(8,128)(2,1)} %collective-permute-done.1, bf16[32,2560]{1,0:T(8,128)(2,1)} %copy-done.4, pred[]{:T(512)S(6)} %eq.83), kind=kLoop, calls=%fused_computation.6 | loop fusion | flops 81920 | bytes 491521 | tf_op jit(solution)/shard_map/jit(_where)/select_n | solution.py:29
  17.4 0.7 %collective-permute-start.2 = (bf16[32,2560]{1,0:T(8,128)(2,1)S(1)}, bf16[32,2560]{1,0:T(8,128)(2,1)}, u32[]{:S(2)}, u32[]{:S(2)}) collective-permute-start(bf16[32,2560]{1,0:T(8,128)(2,1)S(1)} %broadcast_select_fusion), channel_id=1, source_target_pairs={{0,8},{4,12},{8,0},{12,4},{16,24},{20,28},{24,16},{28,20},{1,9},{5... | collective-permute-start | bytes 491528 | tf_op jit(solution)/shard_map/ppermute | solution.py:27
  18.2 5.3 %collective-permute-done.2 = bf16[32,2560]{1,0:T(8,128)(2,1)} collective-permute-done((bf16[32,2560]{1,0:T(8,128)(2,1)S(1)}, bf16[32,2560]{1,0:T(8,128)(2,1)}, u32[]{:S(2)}, u32[]{:S(2)}) %collective-permute-start.2) | collective-permute-done | bytes 163872 | tf_op jit(solution)/shard_map/ppermute | solution.py:27
  23.6 1.4 %collective-permute-start.3 = (bf16[32,2560]{1,0:T(8,128)(2,1)S(1)}, bf16[32,2560]{1,0:T(8,128)(2,1)S(1)}, u32[]{:S(2)}, u32[]{:S(2)}) collective-permute-start(bf16[32,2560]{1,0:T(8,128)(2,1)S(1)} %broadcast_select_fusion.1), channel_id=1, source_target_pairs={{0,4},{4,0},{8,12},{12,8},{16,20},{20,16},{24,28},{28,24},{1,5},{5... | collective-permute-start | bytes 491528 | tf_op jit(solution)/shard_map/ppermute | solution.py:27
  25.0 0.4 or_select_fusion
  25.4 3.6 %collective-permute-done.3 = bf16[32,2560]{1,0:T(8,128)(2,1)S(1)} collective-permute-done((bf16[32,2560]{1,0:T(8,128)(2,1)S(1)}, bf16[32,2560]{1,0:T(8,128)(2,1)S(1)}, u32[]{:S(2)}, u32[]{:S(2)}) %collective-permute-start.3) | collective-permute-done | bytes 163872 | tf_op jit(solution)/shard_map/ppermute | solution.py:27
  29.0 1.5 %collective-permute-start.9 = (bf16[32,2560]{1,0:T(8,128)(2,1)S(1)}, bf16[32,2560]{1,0:T(8,128)(2,1)S(1)}, u32[]{:S(2)}, u32[]{:S(2)}) collective-permute-start(bf16[32,2560]{1,0:T(8,128)(2,1)S(1)} %broadcast_select_fusion.2), channel_id=1, source_target_pairs={{0,2},{1,3},{2,0},{3,1},{4,6},{5,7},{6,4},{7,5},{8,10},{9,11},{10,... | collective-permute-start | bytes 491528 | tf_op jit(solution)/shard_map/ppermute | solution.py:37
  30.5 0.1 collective-permute-start.6
  30.5 0.5 %collective-permute-start.8 = (bf16[192,1280]{1,0:T(8,128)(2,1)}, bf16[192,1280]{1,0:T(8,128)(2,1)S(1)}, u32[]{:S(2)}, u32[]{:S(2)}) collective-permute-start(bf16[192,1280]{1,0:T(8,128)(2,1)} %collective-permute-done.5.refs_6_), channel_id=1, source_target_pairs={{0,1},{1,0},{2,3},{3,2},{4,5},{5,4},{6,7},{7,6},{8,9},{9,8},{10,11... | collective-permute-start | bytes 1474568 | tf_op jit(solution)/shard_map/ppermute | solution.py:138
  31.0 3.3 %collective-permute-done.9 = bf16[32,2560]{1,0:T(8,128)(2,1)S(1)} collective-permute-done((bf16[32,2560]{1,0:T(8,128)(2,1)S(1)}, bf16[32,2560]{1,0:T(8,128)(2,1)S(1)}, u32[]{:S(2)}, u32[]{:S(2)}) %collective-permute-start.9) | collective-permute-done | bytes 163872 | tf_op jit(solution)/shard_map/ppermute | solution.py:37
  34.4 0.1 collective-permute-start.10
  34.5 1.6 %collective-permute-done.10 = bf16[64,2560]{1,0:T(8,128)(2,1)S(1)} collective-permute-done((bf16[64,2560]{1,0:T(8,128)(2,1)S(1)}, bf16[64,2560]{1,0:T(8,128)(2,1)S(1)}, u32[]{:S(2)}, u32[]{:S(2)}) %collective-permute-start.10) | collective-permute-done | bytes 327712 | tf_op jit(solution)/shard_map/ppermute | solution.py:39
  36.2 0.8 %copy-done.5 = bf16[192,1280]{1,0:T(8,128)(2,1)} copy-done((bf16[192,1280]{1,0:T(8,128)(2,1)}, bf16[192,1280]{1,0:T(8,128)(2,1)S(1)}, u32[]{:S(2)}) %copy-start.5) | copy-done | bytes 491544
  37.0 9.2 %shard_map.82 = bf16[192,1280]{1,0:T(8,128)(2,1)S(1)} custom-call(bf16[192,1280]{1,0:T(8,128)(2,1)S(1)} %copy-done.1, bf16[192,1280]{1,0:T(8,128)(2,1)S(1)} %copy-done.2, bf16[192,1280]{1,0:T(8,128)(2,1)} %collective-permute-done.refs_1_, bf16[192,1280]{1,0:T(8,128)(2,1)} %collective-permute-done.4.refs_2_, ...), custom_call_target="tpu_custom_call" | custom-call | flops 1761607680 | bytes 6258688 | tf_op jit(solution)/shard_map/pallas_call | solution.py:100
  46.2 1.6 %convolution_convert_fusion = bf16[192,1280]{1,0:T(8,128)(2,1)} fusion(bf16[192,1280]{1,0:T(8,128)(2,1)S(1)} %shard_map.82, bf16[1280,1280]{1,0:T(8,128)(2,1)S(1)} %copy-done), kind=kOutput, calls=%fused_computation | convolution fusion | flops 629391360 | bytes 4259840 | tf_op jit(solution)/shard_map/dot_general | solution.py:164
  (29 shorter events, 0.3 us)
Async XLA Ops:
  0.0 46.2 %copy-start = (bf16[1280,1280]{1,0:T(8,128)(2,1)S(1)}, bf16[1280,1280]{1,0:T(8,128)(2,1)}, u32[]{:S(2)}) copy-start(bf16[1280,1280]{1,0:T(8,128)(2,1)} %param.13) | copy-start | bytes 9830404
  0.0 36.2 %collective-permute-start = (bf16[192,1280]{1,0:T(8,128)(2,1)}, bf16[192,1280]{1,0:T(8,128)(2,1)}, u32[]{:S(2)}, u32[]{:S(2)}) collective-permute-start(bf16[192,1280]{1,0:T(8,128)(2,1)} %refs_0_.1), channel_id=1, source_target_pairs={{0,1},{1,0},{2,3},{3,2},{4,5},{5,4},{6,7},{7,6},{8,9},{9,8},{10,11... | collective-permute-start | bytes 1474568 | tf_op jit(solution)/shard_map/ppermute | solution.py:136
  0.5 28.5 %collective-permute-start.4 = (bf16[192,1280]{1,0:T(8,128)(2,1)}, bf16[192,1280]{1,0:T(8,128)(2,1)}, u32[]{:S(2)}, u32[]{:S(2)}) collective-permute-start(bf16[192,1280]{1,0:T(8,128)(2,1)} %refs_0_.1), channel_id=1, source_target_pairs={{0,2},{1,3},{2,0},{3,1},{4,6},{5,7},{6,4},{7,5},{8,10},{9,11},{10,... | collective-permute-start | bytes 1474568 | tf_op jit(solution)/shard_map/ppermute | solution.py:135
  3.0 25.9 %collective-permute-start.5 = (bf16[192,1280]{1,0:T(8,128)(2,1)}, bf16[192,1280]{1,0:T(8,128)(2,1)}, u32[]{:S(2)}, u32[]{:S(2)}) collective-permute-start(bf16[192,1280]{1,0:T(8,128)(2,1)} %refs_4_.1), channel_id=1, source_target_pairs={{0,2},{1,3},{2,0},{3,1},{4,6},{5,7},{6,4},{7,5},{8,10},{9,11},{10,... | collective-permute-start | bytes 1474568 | tf_op jit(solution)/shard_map/ppermute | solution.py:135
  3.1 33.1 %collective-permute-start.7 = (bf16[192,1280]{1,0:T(8,128)(2,1)}, bf16[192,1280]{1,0:T(8,128)(2,1)}, u32[]{:S(2)}, u32[]{:S(2)}) collective-permute-start(bf16[192,1280]{1,0:T(8,128)(2,1)} %refs_4_.1), channel_id=1, source_target_pairs={{0,1},{1,0},{2,3},{3,2},{4,5},{5,4},{6,7},{7,6},{8,9},{9,8},{10,11... | collective-permute-start | bytes 1474568 | tf_op jit(solution)/shard_map/ppermute | solution.py:136
  5.0 4.6 %copy-start.4 = (bf16[32,2560]{1,0:T(8,128)(2,1)}, bf16[32,2560]{1,0:T(8,128)(2,1)S(1)}, u32[]{:S(2)}) copy-start(bf16[32,2560]{1,0:T(8,128)(2,1)S(1)} %constant_dynamic-update-slice_fusion) | copy-start | bytes 491524
  5.0 11.4 %collective-permute-start.1 = (bf16[32,2560]{1,0:T(8,128)(2,1)S(1)}, bf16[32,2560]{1,0:T(8,128)(2,1)}, u32[]{:S(2)}, u32[]{:S(2)}) collective-permute-start(bf16[32,2560]{1,0:T(8,128)(2,1)S(1)} %constant_dynamic-update-slice_fusion), channel_id=1, source_target_pairs={{0,16},{4,20},{8,24},{12,28},{16,0},{20,4},{24,8},{28,12},{1,17},{... | collective-permute-start | bytes 491528 | tf_op jit(solution)/shard_map/ppermute | solution.py:27
  17.4 6.2 %collective-permute-start.2 = (bf16[32,2560]{1,0:T(8,128)(2,1)S(1)}, bf16[32,2560]{1,0:T(8,128)(2,1)}, u32[]{:S(2)}, u32[]{:S(2)}) collective-permute-start(bf16[32,2560]{1,0:T(8,128)(2,1)S(1)} %broadcast_select_fusion), channel_id=1, source_target_pairs={{0,8},{4,12},{8,0},{12,4},{16,24},{20,28},{24,16},{28,20},{1,9},{5... | collective-permute-start | bytes 491528 | tf_op jit(solution)/shard_map/ppermute | solution.py:27
  18.1 18.9 %copy-start.1 = (bf16[192,1280]{1,0:T(8,128)(2,1)S(1)}, bf16[192,1280]{1,0:T(8,128)(2,1)}, u32[]{:S(2)}) copy-start(bf16[192,1280]{1,0:T(8,128)(2,1)} %q_ref.1) | copy-start | bytes 1474564
  18.2 18.9 %copy-start.2 = (bf16[192,1280]{1,0:T(8,128)(2,1)S(1)}, bf16[192,1280]{1,0:T(8,128)(2,1)}, u32[]{:S(2)}) copy-start(bf16[192,1280]{1,0:T(8,128)(2,1)} %refs_0_.1) | copy-start | bytes 1474564
  18.2 18.8 %copy-start.3 = (bf16[192,1280]{1,0:T(8,128)(2,1)S(1)}, bf16[192,1280]{1,0:T(8,128)(2,1)}, u32[]{:S(2)}) copy-start(bf16[192,1280]{1,0:T(8,128)(2,1)} %refs_4_.1) | copy-start | bytes 1474564
  23.6 5.4 %collective-permute-start.3 = (bf16[32,2560]{1,0:T(8,128)(2,1)S(1)}, bf16[32,2560]{1,0:T(8,128)(2,1)S(1)}, u32[]{:S(2)}, u32[]{:S(2)}) collective-permute-start(bf16[32,2560]{1,0:T(8,128)(2,1)S(1)} %broadcast_select_fusion.1), channel_id=1, source_target_pairs={{0,4},{4,0},{8,12},{12,8},{16,20},{20,16},{24,28},{28,24},{1,5},{5... | collective-permute-start | bytes 491528 | tf_op jit(solution)/shard_map/ppermute | solution.py:27
  29.0 5.4 %collective-permute-start.9 = (bf16[32,2560]{1,0:T(8,128)(2,1)S(1)}, bf16[32,2560]{1,0:T(8,128)(2,1)S(1)}, u32[]{:S(2)}, u32[]{:S(2)}) collective-permute-start(bf16[32,2560]{1,0:T(8,128)(2,1)S(1)} %broadcast_select_fusion.2), channel_id=1, source_target_pairs={{0,2},{1,3},{2,0},{3,1},{4,6},{5,7},{6,4},{7,5},{8,10},{9,11},{10,... | collective-permute-start | bytes 491528 | tf_op jit(solution)/shard_map/ppermute | solution.py:37
  30.5 5.7 %collective-permute-start.6 = (bf16[192,1280]{1,0:T(8,128)(2,1)}, bf16[192,1280]{1,0:T(8,128)(2,1)S(1)}, u32[]{:S(2)}, u32[]{:S(2)}) collective-permute-start(bf16[192,1280]{1,0:T(8,128)(2,1)} %collective-permute-done.4.refs_2_), channel_id=1, source_target_pairs={{0,1},{1,0},{2,3},{3,2},{4,5},{5,4},{6,7},{7,6},{8,9},{9,8},{10,11... | collective-permute-start | bytes 1474568 | tf_op jit(solution)/shard_map/ppermute | solution.py:138
  30.5 5.7 %collective-permute-start.8 = (bf16[192,1280]{1,0:T(8,128)(2,1)}, bf16[192,1280]{1,0:T(8,128)(2,1)S(1)}, u32[]{:S(2)}, u32[]{:S(2)}) collective-permute-start(bf16[192,1280]{1,0:T(8,128)(2,1)} %collective-permute-done.5.refs_6_), channel_id=1, source_target_pairs={{0,1},{1,0},{2,3},{3,2},{4,5},{5,4},{6,7},{7,6},{8,9},{9,8},{10,11... | collective-permute-start | bytes 1474568 | tf_op jit(solution)/shard_map/ppermute | solution.py:138
  34.4 1.7 %collective-permute-start.10 = (bf16[64,2560]{1,0:T(8,128)(2,1)S(1)}, bf16[64,2560]{1,0:T(8,128)(2,1)S(1)}, u32[]{:S(2)}, u32[]{:S(2)}) collective-permute-start(bf16[64,2560]{1,0:T(8,128)(2,1)S(1)} %pad_maximum_fusion), channel_id=1, source_target_pairs={{0,1},{1,0},{2,3},{3,2},{4,5},{5,4},{6,7},{7,6},{8,9},{9,8},{10,11... | collective-permute-start | bytes 983048 | tf_op jit(solution)/shard_map/ppermute | solution.py:39
  36.2 0.8 %copy-start.5 = (bf16[192,1280]{1,0:T(8,128)(2,1)}, bf16[192,1280]{1,0:T(8,128)(2,1)S(1)}, u32[]{:S(2)}) copy-start(bf16[192,1280]{1,0:T(8,128)(2,1)S(1)} %collective-permute-done.8.refs_7_) | copy-start | bytes 1474564

commit v14 on v12

--- a/solution.py
+++ b/solution.py
@@ -129,7 +129,7 @@
     view_index = lax.axis_index("view")
     view_tok = shard_rows * view_count // VIEWS
 
-    ref_both = jnp.concatenate([ref_keys, ref_values], axis=1)
+    ref_both = jnp.concatenate([ref_keys, ref_values], axis=0)
     ref_shared = tree_broadcast(ref_both, "mesh", ref_source[0])
     if view_count == 4:
         across = lax.ppermute((keys, values), "view", [(i, i ^ 2) for i in range(view_count)])
@@ -142,6 +142,9 @@
         pieces = [lax.all_gather((keys, values), "view", axis=0, tiled=True)]
         positions = [jnp.zeros((), jnp.int32)]
     ref_all = gather_rows(ref_shared, "view")
+    ref_blocks = ref_all.reshape(-1, 2, ref_keys.shape[0], width)
+    ref_key_rows = ref_blocks[:, 0].reshape(-1, width)
+    ref_value_rows = ref_blocks[:, 1].reshape(-1, width)
 
     view_ids = jnp.arange(VIEWS, dtype=jnp.int32)
     query_views = (view_index * shard_rows + jnp.arange(shard_rows, dtype=jnp.int32)) // view_tok
@@ -157,8 +160,8 @@
         [piece[0] for piece in pieces],
         [piece[1] for piece in pieces],
         biases,
-        ref_all[:, :width],
-        ref_all[:, width:],
+        ref_key_rows,
+        ref_value_rows,
         1,
     )
     return jnp.dot(mixed, out_weight, preferred_element_type=jnp.float32).astype(jnp.bfloat16)

time: 47.7 us -> 51.5 us (1.080)
  other arithmetic: 1.44 us -> 3.32 us
  waiting for transfers between devices: 18.7 us -> 19.8 us
  starting transfers between devices: 12 us -> 12.9 us
    ppermute x2, waiting for transfers between devices: 0.01 us -> 3.78 us  [body(): lax.ppermute((keys, values), 'view', [(i, i ^ 2) for i in range(view_coun...]
    ppermute x3, waiting for transfers between devices: 13.9 us -> 10.4 us  [tree_broadcast(): received = lax.ppermute(value, axis, pairs)]
    ppermute x3, starting transfers between devices: 6.52 us -> 8.63 us  [tree_broadcast(): received = lax.ppermute(value, axis, pairs)]
    ppermute x1, waiting for transfers between devices: 3.21 us -> 4.38 us  [gather_rows(): across = lax.ppermute(value, axis, [(i, i ^ 2) for i in range(count)])]
    ppermute x1, waiting for transfers between devices: 1.59 us -> 0.52 us  [gather_rows(): near = lax.ppermute(both, axis, [(i, i ^ 1) for i in range(count)])]
    concatenate x0 -> x1, other arithmetic: none -> 0.96 us  [gather_rows(): return jnp.concatenate([both, near], axis=0)]
    concatenate x1, other arithmetic: 0.02 us -> 0.94 us  [gather_rows(): both = jnp.concatenate([value, across], axis=0)]
    ppermute x2, waiting for transfers between devices: 0.01 us -> 0.77 us  [body(): far = lax.ppermute(across, 'view', [(i, i ^ 1) for i in range(view_count)])]
  transfers between devices with their start and end apart: 11 -> 11, of which waited for: 5 -> 8; matrix products, arithmetic and copies ran while one was open for 9% -> 8% of each run, Pallas kernels for 0% -> 0%
where the time goes in v14:
time: 51.5 us; the launch traced here: 51.3 us
  waiting for transfers between devices  19.8 us (38%)
  starting transfers between devices  12.9 us (25%)
  Pallas kernels  9.17 us (18%)
  other arithmetic  3.32 us (6%)
  local copies, waits for them, and re-layouts  2.79 us (5%)
  matrix products  2.48 us (5%)
  between operations  0.85 us (2%)
    ppermute x3, waiting for transfers between devices, tree_broadcast(): received = lax.ppermute(value, axis, pairs)  10.4 us
    pallas_call x1, Pallas kernels, attention(): pl.pallas_call(functools.partial(attention_kernel, len(key_pieces), span...  9.17 us
    ppermute x3, starting transfers between devices, tree_broadcast(): received = lax.ppermute(value, axis, pairs)  8.63 us
    ppermute x1, waiting for transfers between devices, gather_rows(): across = lax.ppermute(value, axis, [(i, i ^ 2) for i in range(count)])  4.38 us
    ppermute x2, waiting for transfers between devices, body(): lax.ppermute((keys, values), 'view', [(i, i ^ 2) for i in range(view_coun...  3.78 us
    ppermute x2, starting transfers between devices, body(): lax.ppermute((keys, values), 'view', [(i, i ^ 2) for i in range(view_coun...  2.03 us
    unnamed x13, local copies, waits for them, and re-layouts  1.85 us
    dot_general x1, matrix products, body(): jnp.dot(mixed, out_weight, preferred_element_type=jnp.float32)  1.59 us
  transfers between devices with their start and end apart: 11, of which 8 were waited for; matrix products, arithmetic and copies ran while one was open for 8% of the time, Pallas kernels for 0%

profile of v14, /device:TPU:0, one launch (start us, length us, event | category | flops | bytes accessed | tf_op | source)
XLA Modules:
  0.0 51.3 jit_solution(13411264915724224813)
XLA Ops:
  0.0 1.0 %constant_dynamic-update-slice_fusion.1 = bf16[64,1280]{1,0:T(8,128)(2,1)S(1)} fusion(bf16[32,1280]{1,0:T(8,128)(2,1)} %param.11), kind=kLoop, calls=%fused_computation.14 | loop fusion | bytes 163840
  1.0 0.9 %constant_dynamic-update-slice_fusion = bf16[64,1280]{1,0:T(8,128)(2,1)S(1)} fusion(bf16[64,1280]{1,0:T(8,128)(2,1)S(1)} %constant_dynamic-update-slice_fusion.1, bf16[32,1280]{1,0:T(8,128)(2,1)} %param.12), kind=kLoop, calls=%fused_computation.13 | loop fusion | bytes 163840 | tf_op jit(solution)/shard_map/concatenate | solution.py:132
  1.9 2.9 %collective-permute-start.1 = (bf16[64,1280]{1,0:T(8,128)(2,1)S(1)}, bf16[64,1280]{1,0:T(8,128)(2,1)}, u32[]{:S(2)}, u32[]{:S(2)}) collective-permute-start(bf16[64,1280]{1,0:T(8,128)(2,1)S(1)} %constant_dynamic-update-slice_fusion), channel_id=1, source_target_pairs={{0,4},{4,0},{8,12},{12,8},{16,20},{20,16},{24,28},{28,24},{1,5},{5... | collective-permute-start | bytes 491528 | tf_op jit(solution)/shard_map/ppermute | solution.py:27
  4.9 1.5 %collective-permute-start.4 = (bf16[192,1280]{1,0:T(8,128)(2,1)}, bf16[192,1280]{1,0:T(8,128)(2,1)}, u32[]{:S(2)}, u32[]{:S(2)}) collective-permute-start(bf16[192,1280]{1,0:T(8,128)(2,1)} %refs_0_.1), channel_id=1, source_target_pairs={{0,2},{1,3},{2,0},{3,1},{4,6},{5,7},{6,4},{7,5},{8,10},{9,11},{10,... | collective-permute-start | bytes 1474568 | tf_op jit(solution)/shard_map/ppermute | solution.py:135
  6.4 0.5 collective-permute-start.5
  7.6 1.6 %collective-permute-done.1 = bf16[64,1280]{1,0:T(8,128)(2,1)} collective-permute-done((bf16[64,1280]{1,0:T(8,128)(2,1)S(1)}, bf16[64,1280]{1,0:T(8,128)(2,1)}, u32[]{:S(2)}, u32[]{:S(2)}) %collective-permute-start.1) | collective-permute-done | bytes 163872 | tf_op jit(solution)/shard_map/ppermute | solution.py:27
  9.2 1.9 %collective-permute-start.2 = (bf16[64,1280]{1,0:T(8,128)(2,1)S(1)}, bf16[64,1280]{1,0:T(8,128)(2,1)S(1)}, u32[]{:S(2)}, u32[]{:S(2)}) collective-permute-start(bf16[64,1280]{1,0:T(8,128)(2,1)S(1)} %broadcast_select_fusion), channel_id=1, source_target_pairs={{0,8},{4,12},{8,0},{12,4},{16,24},{20,28},{24,16},{28,20},{1,9},{5... | collective-permute-start | bytes 491528 | tf_op jit(solution)/shard_map/ppermute | solution.py:27
  11.1 0.9 %fusion = f32[192,3]{0,1:T(4,128)S(1)} fusion(s32[192]{0:T(256)S(1)} %get-tuple-element.20, s32[6,3]{0,1:T(4,128)} %param.14), kind=kOutput, calls=%fused_computation.11 | convolution fusion | flops 8082 | bytes 3144 | tf_op jit(solution)/shard_map/dot_general | solution.py:152
  12.0 2.7 %collective-permute-done.2 = bf16[64,1280]{1,0:T(8,128)(2,1)S(1)} collective-permute-done((bf16[64,1280]{1,0:T(8,128)(2,1)S(1)}, bf16[64,1280]{1,0:T(8,128)(2,1)S(1)}, u32[]{:S(2)}, u32[]{:S(2)}) %collective-permute-start.2) | collective-permute-done | bytes 163872 | tf_op jit(solution)/shard_map/ppermute | solution.py:27
  14.7 3.8 %collective-permute-start.3 = (bf16[64,1280]{1,0:T(8,128)(2,1)S(1)}, bf16[64,1280]{1,0:T(8,128)(2,1)}, u32[]{:S(2)}, u32[]{:S(2)}) collective-permute-start(bf16[64,1280]{1,0:T(8,128)(2,1)S(1)} %broadcast_select_fusion.1), channel_id=1, source_target_pairs={{0,16},{4,20},{8,24},{12,28},{16,0},{20,4},{24,8},{28,12},{1,17},{... | collective-permute-start | bytes 491528 | tf_op jit(solution)/shard_map/ppermute | solution.py:27
  18.5 6.1 %collective-permute-done.3 = bf16[64,1280]{1,0:T(8,128)(2,1)} collective-permute-done((bf16[64,1280]{1,0:T(8,128)(2,1)S(1)}, bf16[64,1280]{1,0:T(8,128)(2,1)}, u32[]{:S(2)}, u32[]{:S(2)}) %collective-permute-start.3) | collective-permute-done | bytes 163872 | tf_op jit(solution)/shard_map/ppermute | solution.py:27
  24.6 0.9 %broadcast_select_fusion.2 = bf16[64,1280]{1,0:T(8,128)(2,1)S(1)} fusion(bf16[64,1280]{1,0:T(8,128)(2,1)} %collective-permute-done.3, bf16[64,1280]{1,0:T(8,128)(2,1)} %copy-done.4, pred[]{:T(512)S(6)} %eq.74), kind=kLoop, calls=%fused_computation.9 | loop fusion | flops 81920 | bytes 491521 | tf_op jit(solution)/shard_map/jit(_where)/select_n | solution.py:29
  25.6 3.8 %collective-permute-done.5.refs_6_ = bf16[192,1280]{1,0:T(8,128)(2,1)} collective-permute-done((bf16[192,1280]{1,0:T(8,128)(2,1)}, bf16[192,1280]{1,0:T(8,128)(2,1)}, u32[]{:S(2)}, u32[]{:S(2)}) %collective-permute-start.5) | collective-permute-done | bytes 491552 | tf_op jit(solution)/shard_map/ppermute | solution.py:135
  29.4 1.5 %collective-permute-start.9 = (bf16[64,1280]{1,0:T(8,128)(2,1)S(1)}, bf16[64,1280]{1,0:T(8,128)(2,1)}, u32[]{:S(2)}, u32[]{:S(2)}) collective-permute-start(bf16[64,1280]{1,0:T(8,128)(2,1)S(1)} %broadcast_select_fusion.2), channel_id=1, source_target_pairs={{0,2},{1,3},{2,0},{3,1},{4,6},{5,7},{6,4},{7,5},{8,10},{9,11},{10,... | collective-permute-start | bytes 491528 | tf_op jit(solution)/shard_map/ppermute | solution.py:37
  30.9 4.4 %collective-permute-done.9 = bf16[64,1280]{1,0:T(8,128)(2,1)} collective-permute-done((bf16[64,1280]{1,0:T(8,128)(2,1)S(1)}, bf16[64,1280]{1,0:T(8,128)(2,1)}, u32[]{:S(2)}, u32[]{:S(2)}) %collective-permute-start.9) | collective-permute-done | bytes 163872 | tf_op jit(solution)/shard_map/ppermute | solution.py:37
  35.3 0.9 %pad_maximum_fusion.1 = bf16[128,1280]{1,0:T(8,128)(2,1)S(1)} fusion(bf16[64,1280]{1,0:T(8,128)(2,1)} %collective-permute-done.9, bf16[64,1280]{1,0:T(8,128)(2,1)S(1)} %broadcast_select_fusion.2), kind=kLoop, calls=%fused_computation.2 | loop fusion | flops 655360 | bytes 655360 | tf_op jit(solution)/shard_map/concatenate | solution.py:38
  36.3 0.4 or_select_fusion
  36.8 0.6 %collective-permute-start.6 = (bf16[192,1280]{1,0:T(8,128)(2,1)}, bf16[192,1280]{1,0:T(8,128)(2,1)S(1)}, u32[]{:S(2)}, u32[]{:S(2)}) collective-permute-start(bf16[192,1280]{1,0:T(8,128)(2,1)} %collective-permute-done.4.refs_2_), channel_id=1, source_target_pairs={{0,1},{1,0},{2,3},{3,2},{4,5},{5,4},{6,7},{7,6},{8,9},{9,8},{10,11... | collective-permute-start | bytes 1474568 | tf_op jit(solution)/shard_map/ppermute | solution.py:138
  37.4 0.5 %collective-permute-done.10 = bf16[128,1280]{1,0:T(8,128)(2,1)S(1)} collective-permute-done((bf16[128,1280]{1,0:T(8,128)(2,1)S(1)}, bf16[128,1280]{1,0:T(8,128)(2,1)S(1)}, u32[]{:S(2)}, u32[]{:S(2)}) %collective-permute-start.10) | collective-permute-done | bytes 327712 | tf_op jit(solution)/shard_map/ppermute | solution.py:39
  37.9 1.0 %pad_maximum_fusion = bf16[256,1280]{1,0:T(8,128)(2,1)S(1)} fusion(bf16[128,1280]{1,0:T(8,128)(2,1)S(1)} %collective-permute-done.10, bf16[64,1280]{1,0:T(8,128)(2,1)} %collective-permute-done.9, bf16[64,1280]{1,0:T(8,128)(2,1)S(1)} %broadcast_select_fusion.2), kind=kLoop, calls=%fused_computation.1 | loop fusion | flops 1966080 | bytes 1310720 | tf_op jit(solution)/shard_map/concatenate | solution.py:40
  39.0 0.7 %collective-permute-done.8.refs_7_ = bf16[192,1280]{1,0:T(8,128)(2,1)S(1)} collective-permute-done((bf16[192,1280]{1,0:T(8,128)(2,1)}, bf16[192,1280]{1,0:T(8,128)(2,1)S(1)}, u32[]{:S(2)}, u32[]{:S(2)}) %collective-permute-start.8) | collective-permute-done | bytes 491552 | tf_op jit(solution)/shard_map/ppermute | solution.py:138
  39.7 0.8 %copy-done.5 = bf16[192,1280]{1,0:T(8,128)(2,1)} copy-done((bf16[192,1280]{1,0:T(8,128)(2,1)}, bf16[192,1280]{1,0:T(8,128)(2,1)S(1)}, u32[]{:S(2)}) %copy-start.5) | copy-done | bytes 491544
  40.5 9.2 %shard_map.82 = bf16[192,1280]{1,0:T(8,128)(2,1)S(1)} custom-call(bf16[192,1280]{1,0:T(8,128)(2,1)S(1)} %copy-done.1, bf16[192,1280]{1,0:T(8,128)(2,1)S(1)} %copy-done.2, bf16[192,1280]{1,0:T(8,128)(2,1)} %collective-permute-done.refs_1_, bf16[192,1280]{1,0:T(8,128)(2,1)} %collective-permute-done.4.refs_2_, ...), custom_call_target="tpu_custom_call" | custom-call | flops 1761607680 | bytes 6258688 | tf_op jit(solution)/shard_map/pallas_call | solution.py:100
  49.7 1.6 %convolution_convert_fusion = bf16[192,1280]{1,0:T(8,128)(2,1)} fusion(bf16[192,1280]{1,0:T(8,128)(2,1)S(1)} %shard_map.82, bf16[1280,1280]{1,0:T(8,128)(2,1)S(1)} %copy-done), kind=kOutput, calls=%fused_computation | convolution fusion | flops 629391360 | bytes 4259840 | tf_op jit(solution)/shard_map/dot_general | solution.py:167
  (27 shorter events, 0.4 us)
Async XLA Ops:
  0.0 49.7 %copy-start = (bf16[1280,1280]{1,0:T(8,128)(2,1)S(1)}, bf16[1280,1280]{1,0:T(8,128)(2,1)}, u32[]{:S(2)}) copy-start(bf16[1280,1280]{1,0:T(8,128)(2,1)} %param.13) | copy-start | bytes 9830404
  1.9 7.2 %collective-permute-start.1 = (bf16[64,1280]{1,0:T(8,128)(2,1)S(1)}, bf16[64,1280]{1,0:T(8,128)(2,1)}, u32[]{:S(2)}, u32[]{:S(2)}) collective-permute-start(bf16[64,1280]{1,0:T(8,128)(2,1)S(1)} %constant_dynamic-update-slice_fusion), channel_id=1, source_target_pairs={{0,4},{4,0},{8,12},{12,8},{16,20},{20,16},{24,28},{28,24},{1,5},{5... | collective-permute-start | bytes 491528 | tf_op jit(solution)/shard_map/ppermute | solution.py:27
  4.9 34.1 %collective-permute-start = (bf16[192,1280]{1,0:T(8,128)(2,1)}, bf16[192,1280]{1,0:T(8,128)(2,1)}, u32[]{:S(2)}, u32[]{:S(2)}) collective-permute-start(bf16[192,1280]{1,0:T(8,128)(2,1)} %refs_0_.1), channel_id=1, source_target_pairs={{0,1},{1,0},{2,3},{3,2},{4,5},{5,4},{6,7},{7,6},{8,9},{9,8},{10,11... | collective-permute-start | bytes 1474568 | tf_op jit(solution)/shard_map/ppermute | solution.py:136
  4.9 20.7 %collective-permute-start.4 = (bf16[192,1280]{1,0:T(8,128)(2,1)}, bf16[192,1280]{1,0:T(8,128)(2,1)}, u32[]{:S(2)}, u32[]{:S(2)}) collective-permute-start(bf16[192,1280]{1,0:T(8,128)(2,1)} %refs_0_.1), channel_id=1, source_target_pairs={{0,2},{1,3},{2,0},{3,1},{4,6},{5,7},{6,4},{7,5},{8,10},{9,11},{10,... | collective-permute-start | bytes 1474568 | tf_op jit(solution)/shard_map/ppermute | solution.py:135
  6.4 23.0 %collective-permute-start.5 = (bf16[192,1280]{1,0:T(8,128)(2,1)}, bf16[192,1280]{1,0:T(8,128)(2,1)}, u32[]{:S(2)}, u32[]{:S(2)}) collective-permute-start(bf16[192,1280]{1,0:T(8,128)(2,1)} %refs_4_.1), channel_id=1, source_target_pairs={{0,2},{1,3},{2,0},{3,1},{4,6},{5,7},{6,4},{7,5},{8,10},{9,11},{10,... | collective-permute-start | bytes 1474568 | tf_op jit(solution)/shard_map/ppermute | solution.py:135
  6.9 32.1 %collective-permute-start.7 = (bf16[192,1280]{1,0:T(8,128)(2,1)}, bf16[192,1280]{1,0:T(8,128)(2,1)}, u32[]{:S(2)}, u32[]{:S(2)}) collective-permute-start(bf16[192,1280]{1,0:T(8,128)(2,1)} %refs_4_.1), channel_id=1, source_target_pairs={{0,1},{1,0},{2,3},{3,2},{4,5},{5,4},{6,7},{7,6},{8,9},{9,8},{10,11... | collective-permute-start | bytes 1474568 | tf_op jit(solution)/shard_map/ppermute | solution.py:136
  9.2 5.5 %collective-permute-start.2 = (bf16[64,1280]{1,0:T(8,128)(2,1)S(1)}, bf16[64,1280]{1,0:T(8,128)(2,1)S(1)}, u32[]{:S(2)}, u32[]{:S(2)}) collective-permute-start(bf16[64,1280]{1,0:T(8,128)(2,1)S(1)} %broadcast_select_fusion), channel_id=1, source_target_pairs={{0,8},{4,12},{8,0},{12,4},{16,24},{20,28},{24,16},{28,20},{1,9},{5... | collective-permute-start | bytes 491528 | tf_op jit(solution)/shard_map/ppermute | solution.py:27
  14.7 3.8 %copy-start.4 = (bf16[64,1280]{1,0:T(8,128)(2,1)}, bf16[64,1280]{1,0:T(8,128)(2,1)S(1)}, u32[]{:S(2)}) copy-start(bf16[64,1280]{1,0:T(8,128)(2,1)S(1)} %broadcast_select_fusion.1) | copy-start | bytes 491524
  14.7 9.9 %collective-permute-start.3 = (bf16[64,1280]{1,0:T(8,128)(2,1)S(1)}, bf16[64,1280]{1,0:T(8,128)(2,1)}, u32[]{:S(2)}, u32[]{:S(2)}) collective-permute-start(bf16[64,1280]{1,0:T(8,128)(2,1)S(1)} %broadcast_select_fusion.1), channel_id=1, source_target_pairs={{0,16},{4,20},{8,24},{12,28},{16,0},{20,4},{24,8},{28,12},{1,17},{... | collective-permute-start | bytes 491528 | tf_op jit(solution)/shard_map/ppermute | solution.py:27
  29.4 5.9 %collective-permute-start.9 = (bf16[64,1280]{1,0:T(8,128)(2,1)S(1)}, bf16[64,1280]{1,0:T(8,128)(2,1)}, u32[]{:S(2)}, u32[]{:S(2)}) collective-permute-start(bf16[64,1280]{1,0:T(8,128)(2,1)S(1)} %broadcast_select_fusion.2), channel_id=1, source_target_pairs={{0,2},{1,3},{2,0},{3,1},{4,6},{5,7},{6,4},{7,5},{8,10},{9,11},{10,... | collective-permute-start | bytes 491528 | tf_op jit(solution)/shard_map/ppermute | solution.py:37
  36.2 1.7 %collective-permute-start.10 = (bf16[128,1280]{1,0:T(8,128)(2,1)S(1)}, bf16[128,1280]{1,0:T(8,128)(2,1)S(1)}, u32[]{:S(2)}, u32[]{:S(2)}) collective-permute-start(bf16[128,1280]{1,0:T(8,128)(2,1)S(1)} %pad_maximum_fusion.1), channel_id=1, source_target_pairs={{0,1},{1,0},{2,3},{3,2},{4,5},{5,4},{6,7},{7,6},{8,9},{9,8},{10,11... | collective-permute-start | bytes 983048 | tf_op jit(solution)/shard_map/ppermute | solution.py:39
  36.7 3.8 %copy-start.1 = (bf16[192,1280]{1,0:T(8,128)(2,1)S(1)}, bf16[192,1280]{1,0:T(8,128)(2,1)}, u32[]{:S(2)}) copy-start(bf16[192,1280]{1,0:T(8,128)(2,1)} %q_ref.1) | copy-start | bytes 1474564
  36.8 3.8 %copy-start.2 = (bf16[192,1280]{1,0:T(8,128)(2,1)S(1)}, bf16[192,1280]{1,0:T(8,128)(2,1)}, u32[]{:S(2)}) copy-start(bf16[192,1280]{1,0:T(8,128)(2,1)} %refs_0_.1) | copy-start | bytes 1474564
  36.8 3.8 %copy-start.3 = (bf16[192,1280]{1,0:T(8,128)(2,1)S(1)}, bf16[192,1280]{1,0:T(8,128)(2,1)}, u32[]{:S(2)}) copy-start(bf16[192,1280]{1,0:T(8,128)(2,1)} %refs_4_.1) | copy-start | bytes 1474564
  36.8 2.3 %collective-permute-start.6 = (bf16[192,1280]{1,0:T(8,128)(2,1)}, bf16[192,1280]{1,0:T(8,128)(2,1)S(1)}, u32[]{:S(2)}, u32[]{:S(2)}) collective-permute-start(bf16[192,1280]{1,0:T(8,128)(2,1)} %collective-permute-done.4.refs_2_), channel_id=1, source_target_pairs={{0,1},{1,0},{2,3},{3,2},{4,5},{5,4},{6,7},{7,6},{8,9},{9,8},{10,11... | collective-permute-start | bytes 1474568 | tf_op jit(solution)/shard_map/ppermute | solution.py:138
  37.3 2.4 %collective-permute-start.8 = (bf16[192,1280]{1,0:T(8,128)(2,1)}, bf16[192,1280]{1,0:T(8,128)(2,1)S(1)}, u32[]{:S(2)}, u32[]{:S(2)}) collective-permute-start(bf16[192,1280]{1,0:T(8,128)(2,1)} %collective-permute-done.5.refs_6_), channel_id=1, source_target_pairs={{0,1},{1,0},{2,3},{3,2},{4,5},{5,4},{6,7},{7,6},{8,9},{9,8},{10,11... | collective-permute-start | bytes 1474568 | tf_op jit(solution)/shard_map/ppermute | solution.py:138
  39.7 0.8 %copy-start.5 = (bf16[192,1280]{1,0:T(8,128)(2,1)}, bf16[192,1280]{1,0:T(8,128)(2,1)S(1)}, u32[]{:S(2)}) copy-start(bf16[192,1280]{1,0:T(8,128)(2,1)S(1)} %collective-permute-done.8.refs_7_) | copy-start | bytes 1474564

commit v15 on v12

--- a/solution.py
+++ b/solution.py
@@ -45,7 +45,7 @@
     key_refs = refs[:piece_count]
     value_refs = refs[piece_count : 2 * piece_count]
     bias_refs = refs[2 * piece_count : 3 * piece_count]
-    rk_ref, rv_ref, out_ref = refs[3 * piece_count :]
+    rk_ref, rv_ref, w_ref, out_ref, mixed_ref = refs[3 * piece_count :]
     lane = lax.broadcasted_iota(jnp.int32, (1, LANES), 1)
     dims = (((1,), (1,)), ((), ()))
     rows = q_ref.shape[0]
@@ -83,12 +83,13 @@
         mixed = both[(per_pair - 1) * rows :]
         for head in range(per_pair - 1):
             mixed = jnp.where((lane // HEAD_DIM) == head, both[head * rows : (head + 1) * rows], mixed)
-        out_ref[:, cols] = mixed.astype(out_ref.dtype)
+        mixed_ref[:, cols] = mixed.astype(mixed_ref.dtype)
+    out_ref[...] = jnp.dot(mixed_ref[...], w_ref[...], preferred_element_type=jnp.float32).astype(out_ref.dtype)
 
 
-def attention(queries, key_pieces, value_pieces, biases, ref_keys, ref_values, steps):
+def attention(queries, key_pieces, value_pieces, biases, ref_keys, ref_values, out_weight):
     rows, width = queries.shape
-    span = width // steps
+    span = width
     column = lambda j: (0, j)
     fixed = lambda j: (0, 0)
     in_specs = [pl.BlockSpec((rows, span), column)]
@@ -96,22 +97,24 @@
     in_specs += [pl.BlockSpec((piece.shape[0], span), column) for piece in value_pieces]
     in_specs += [pl.BlockSpec(bias.shape, fixed) for bias in biases]
     in_specs += [pl.BlockSpec((ref_keys.shape[0], span), column)] * 2
+    in_specs.append(pl.BlockSpec(out_weight.shape, fixed))
     keys = sum(piece.shape[0] for piece in key_pieces) + ref_keys.shape[0]
     return pl.pallas_call(
         functools.partial(attention_kernel, len(key_pieces), span // LANES),
-        grid=(steps,),
+        grid=(1,),
+        scratch_shapes=[pltpu.VMEM((rows, width), jnp.bfloat16)],
         in_specs=in_specs,
         out_specs=pl.BlockSpec((rows, span), column),
         out_shape=jax.ShapeDtypeStruct((rows, width), jnp.bfloat16),
         compiler_params=pltpu.CompilerParams(
-            dimension_semantics=("arbitrary",), vmem_limit_bytes=48 * 1024 * 1024
+            dimension_semantics=("arbitrary",), vmem_limit_bytes=60 * 1024 * 1024
         ),
         cost_estimate=pl.CostEstimate(
-            flops=8 * rows * keys * width,
+            flops=8 * rows * keys * width + 2 * rows * width * width,
             transcendentals=2 * rows * keys * HEADS,
             bytes_accessed=2 * (2 * rows + 2 * keys) * width + 4 * rows * keys,
         ),
-    )(queries, *key_pieces, *value_pieces, *biases, ref_keys, ref_values)
+    )(queries, *key_pieces, *value_pieces, *biases, ref_keys, ref_values, out_weight)
 
 
 def key_bias(query_views, query_adjacent, position, rows, shard_rows, view_tok):
@@ -159,9 +162,9 @@
         biases,
         ref_all[:, :width],
         ref_all[:, width:],
-        1,
+        out_weight,
     )
-    return jnp.dot(mixed, out_weight, preferred_element_type=jnp.float32).astype(jnp.bfloat16)
+    return mixed
 
 
 def solution(mesh):

time: 47.7 us -> 49.3 us (1.034)
  Pallas kernels: 9.18 us -> 12.5 us
  matrix products: 2.49 us -> 0.9 us
  waiting for transfers between devices: 18.7 us -> 17.4 us
  local copies, waits for them, and re-layouts: 2.68 us -> 3.93 us
    pallas_call x1, Pallas kernels: 9.18 us -> 12.5 us  [attention(): pl.pallas_call(functools.partial(attention_kernel, len(key_pieces), span...]
    dot_general x1 -> x0, matrix products: 1.59 us -> none  [body(): jnp.dot(mixed, out_weight, preferred_element_type=jnp.float32)]
    ppermute x3, waiting for transfers between devices: 13.9 us -> 12.6 us  [tree_broadcast(): received = lax.ppermute(value, axis, pairs)]
    select_n x3, other arithmetic: 0.98 us -> 0.06 us  [tree_broadcast(): value = jnp.where(partner_has, received, value)]
    select_n x1, other arithmetic: 0.4 us -> 1.29 us  [key_bias(): return jnp.where(keep, 0.0, -jnp.inf).astype(jnp.float32)]
    slice x1, local copies, waits for them, and re-layouts: 0.04 us -> 0.88 us  [body(): ref_all[:, width:]]
  transfers between devices with their start and end apart: 11 -> 11, of which waited for: 5 -> 5; matrix products, arithmetic and copies ran while one was open for 9% -> 10% of each run, Pallas kernels for 0% -> 0%
where the time goes in v15:
time: 49.3 us; the launch traced here: 49.1 us
  waiting for transfers between devices  17.4 us (35%)
  Pallas kernels  12.5 us (25%)
  starting transfers between devices  12 us (24%)
  local copies, waits for them, and re-layouts  3.93 us (8%)
  other arithmetic  1.41 us (3%)
  between operations  0.93 us (2%)
  matrix products  0.9 us (2%)
    ppermute x3, waiting for transfers between devices, tree_broadcast(): received = lax.ppermute(value, axis, pairs)  12.6 us
    pallas_call x1, Pallas kernels, attention(): pl.pallas_call(functools.partial(attention_kernel, len(key_pieces), span...  12.5 us
    ppermute x3, starting transfers between devices, tree_broadcast(): received = lax.ppermute(value, axis, pairs)  6.45 us
    ppermute x1, waiting for transfers between devices, gather_rows(): across = lax.ppermute(value, axis, [(i, i ^ 2) for i in range(count)])  3.16 us
    ppermute x2, starting transfers between devices, body(): lax.ppermute((keys, values), 'view', [(i, i ^ 2) for i in range(view_coun...  2.59 us
    unnamed x15, local copies, waits for them, and re-layouts  2.12 us
    ppermute x1, starting transfers between devices, gather_rows(): across = lax.ppermute(value, axis, [(i, i ^ 2) for i in range(count)])  1.63 us
    ppermute x1, waiting for transfers between devices, gather_rows(): near = lax.ppermute(both, axis, [(i, i ^ 1) for i in range(count)])  1.59 us
  transfers between devices with their start and end apart: 11, of which 5 were waited for; matrix products, arithmetic and copies ran while one was open for 10% of the time, Pallas kernels for 0%

profile of v15, /device:TPU:0, one launch (start us, length us, event | category | flops | bytes accessed | tf_op | source)
XLA Modules:
  0.0 49.1 jit_solution(74140022975137097)
XLA Ops:
  0.0 0.5 collective-permute-start
  0.5 2.5 %collective-permute-start.4 = (bf16[192,1280]{1,0:T(8,128)(2,1)}, bf16[192,1280]{1,0:T(8,128)(2,1)S(1)}, u32[]{:S(2)}, u32[]{:S(2)}) collective-permute-start(bf16[192,1280]{1,0:T(8,128)(2,1)} %refs_0_.1), channel_id=1, source_target_pairs={{0,2},{1,3},{2,0},{3,1},{4,6},{5,7},{6,4},{7,5},{8,10},{9,11},{10,... | collective-permute-start | bytes 1474568 | tf_op jit(solution)/shard_map/ppermute | solution.py:138
  3.0 0.2 collective-permute-start.7
  3.2 0.9 %constant_dynamic-update-slice_fusion.1 = bf16[32,2560]{1,0:T(8,128)(2,1)S(1)} fusion(bf16[32,1280]{1,0:T(8,128)(2,1)} %param.11), kind=kLoop, calls=%fused_computation.12 | loop fusion | bytes 163840
  4.1 0.9 %constant_dynamic-update-slice_fusion = bf16[32,2560]{1,0:T(8,128)(2,1)S(1)} fusion(bf16[32,2560]{1,0:T(8,128)(2,1)S(1)} %constant_dynamic-update-slice_fusion.1, bf16[32,1280]{1,0:T(8,128)(2,1)} %param.12), kind=kLoop, calls=%fused_computation.11 | loop fusion | bytes 163840 | tf_op jit(solution)/shard_map/concatenate | solution.py:135
  5.0 1.7 %collective-permute-start.1 = (bf16[32,2560]{1,0:T(8,128)(2,1)S(1)}, bf16[32,2560]{1,0:T(8,128)(2,1)S(1)}, u32[]{:S(2)}, u32[]{:S(2)}) collective-permute-start(bf16[32,2560]{1,0:T(8,128)(2,1)S(1)} %constant_dynamic-update-slice_fusion), channel_id=1, source_target_pairs={{0,4},{4,0},{8,12},{12,8},{16,20},{20,16},{24,28},{28,24},{1,5},{5... | collective-permute-start | bytes 491528 | tf_op jit(solution)/shard_map/ppermute | solution.py:27
  6.8 0.9 %fusion = f32[192,3]{0,1:T(4,128)S(1)} fusion(s32[192]{0:T(256)S(1)} %get-tuple-element.22, s32[6,3]{0,1:T(4,128)} %param.14), kind=kOutput, calls=%fused_computation.9 | convolution fusion | flops 8082 | bytes 3144 | tf_op jit(solution)/shard_map/dot_general | solution.py:152
  8.4 3.3 %collective-permute-done.1 = bf16[32,2560]{1,0:T(8,128)(2,1)S(1)} collective-permute-done((bf16[32,2560]{1,0:T(8,128)(2,1)S(1)}, bf16[32,2560]{1,0:T(8,128)(2,1)S(1)}, u32[]{:S(2)}, u32[]{:S(2)}) %collective-permute-start.1) | collective-permute-done | bytes 163872 | tf_op jit(solution)/shard_map/ppermute | solution.py:27
  11.6 1.9 %collective-permute-start.2 = (bf16[32,2560]{1,0:T(8,128)(2,1)S(1)}, bf16[32,2560]{1,0:T(8,128)(2,1)S(1)}, u32[]{:S(2)}, u32[]{:S(2)}) collective-permute-start(bf16[32,2560]{1,0:T(8,128)(2,1)S(1)} %broadcast_select_fusion), channel_id=1, source_target_pairs={{0,8},{4,12},{8,0},{12,4},{16,24},{20,28},{24,16},{28,20},{1,9},{5... | collective-permute-start | bytes 491528 | tf_op jit(solution)/shard_map/ppermute | solution.py:27
  13.7 4.0 %collective-permute-done.2 = bf16[32,2560]{1,0:T(8,128)(2,1)S(1)} collective-permute-done((bf16[32,2560]{1,0:T(8,128)(2,1)S(1)}, bf16[32,2560]{1,0:T(8,128)(2,1)S(1)}, u32[]{:S(2)}, u32[]{:S(2)}) %collective-permute-start.2) | collective-permute-done | bytes 163872 | tf_op jit(solution)/shard_map/ppermute | solution.py:27
  17.7 2.8 %collective-permute-start.3 = (bf16[32,2560]{1,0:T(8,128)(2,1)S(1)}, bf16[32,2560]{1,0:T(8,128)(2,1)S(1)}, u32[]{:S(2)}, u32[]{:S(2)}) collective-permute-start(bf16[32,2560]{1,0:T(8,128)(2,1)S(1)} %broadcast_select_fusion.1), channel_id=1, source_target_pairs={{0,16},{4,20},{8,24},{12,28},{16,0},{20,4},{24,8},{28,12},{1,17},{... | collective-permute-start | bytes 491528 | tf_op jit(solution)/shard_map/ppermute | solution.py:27
  20.5 1.3 %or_select_fusion = (f32[192,192]{1,0:T(8,128)}, f32[192,192]{1,0:T(8,128)}, f32[192,192]{1,0:T(8,128)}, f32[192,192]{1,0:T(8,128)}) fusion(f32[192]{0:T(256)S(1)} %get-tuple-element.21, s32[192]{0:T(256)S(1)} %get-tuple-element.20, f32[192]{0:T(256)S(1)} %bitcast.10, f32[192]{0:T(256)S(1)} %bitcast.11, f32[192]{0:T(256)S(1)} %bitcast.9, ...), kind=kLoop, calls=%fused_computation.1 | loop fusion | flops 1179648 | bytes 598272 | tf_op jit(solution)/shard_map/jit(_where)/select_n | solution.py:126
  21.8 5.4 %collective-permute-done.3 = bf16[32,2560]{1,0:T(8,128)(2,1)S(1)} collective-permute-done((bf16[32,2560]{1,0:T(8,128)(2,1)S(1)}, bf16[32,2560]{1,0:T(8,128)(2,1)S(1)}, u32[]{:S(2)}, u32[]{:S(2)}) %collective-permute-start.3) | collective-permute-done | bytes 163872 | tf_op jit(solution)/shard_map/ppermute | solution.py:27
  27.2 1.6 %collective-permute-start.9 = (bf16[32,2560]{1,0:T(8,128)(2,1)S(1)}, bf16[32,2560]{1,0:T(8,128)(2,1)S(1)}, u32[]{:S(2)}, u32[]{:S(2)}) collective-permute-start(bf16[32,2560]{1,0:T(8,128)(2,1)S(1)} %broadcast_select_fusion.2), channel_id=1, source_target_pairs={{0,2},{1,3},{2,0},{3,1},{4,6},{5,7},{6,4},{7,5},{8,10},{9,11},{10,... | collective-permute-start | bytes 491528 | tf_op jit(solution)/shard_map/ppermute | solution.py:37
  28.9 0.1 collective-permute-start.6
  29.0 0.5 %collective-permute-start.8 = (bf16[192,1280]{1,0:T(8,128)(2,1)S(1)}, bf16[192,1280]{1,0:T(8,128)(2,1)S(1)}, u32[]{:S(2)}, u32[]{:S(2)}) collective-permute-start(bf16[192,1280]{1,0:T(8,128)(2,1)S(1)} %collective-permute-done.5.refs_6_), channel_id=1, source_target_pairs={{0,1},{1,0},{2,3},{3,2},{4,5},{5,4},{6,7},{7,6},{8,9},{9,8},{10,11... | collective-permute-start | bytes 1474568 | tf_op jit(solution)/shard_map/ppermute | solution.py:141
  29.5 3.2 %collective-permute-done.9 = bf16[32,2560]{1,0:T(8,128)(2,1)S(1)} collective-permute-done((bf16[32,2560]{1,0:T(8,128)(2,1)S(1)}, bf16[32,2560]{1,0:T(8,128)(2,1)S(1)}, u32[]{:S(2)}, u32[]{:S(2)}) %collective-permute-start.9) | collective-permute-done | bytes 163872 | tf_op jit(solution)/shard_map/ppermute | solution.py:37
  32.8 1.6 %collective-permute-done.10 = bf16[64,2560]{1,0:T(8,128)(2,1)S(1)} collective-permute-done((bf16[64,2560]{1,0:T(8,128)(2,1)S(1)}, bf16[64,2560]{1,0:T(8,128)(2,1)S(1)}, u32[]{:S(2)}, u32[]{:S(2)}) %collective-permute-start.10) | collective-permute-done | bytes 327712 | tf_op jit(solution)/shard_map/ppermute | solution.py:39
  34.4 0.9 %fusion.7 = (bf16[128,1280]{1,0:T(8,128)(2,1)}, bf16[128,1280]{1,0:T(8,128)(2,1)}) fusion(bf16[128,2560]{1,0:T(8,128)(2,1)S(1)} %constant_dynamic-update-slice_fusion.2), kind=kLoop, calls=%fused_computation.37 | loop fusion | bytes 1310720 | tf_op jit(solution)/shard_map/slice | solution.py:164
  35.3 0.7 %copy-done = bf16[192,1280]{1,0:T(8,128)(2,1)} copy-done((bf16[192,1280]{1,0:T(8,128)(2,1)}, bf16[192,1280]{1,0:T(8,128)(2,1)S(1)}, u32[]{:S(2)}) %copy-start) | copy-done | bytes 491544
  36.1 0.2 copy-done.3
  36.2 0.2 copy-done.4
  36.4 0.1 copy-done.5
  36.5 12.5 %shard_map.82 = bf16[192,1280]{1,0:T(8,128)(2,1)} custom-call(bf16[192,1280]{1,0:T(8,128)(2,1)} %q_ref.1, bf16[192,1280]{1,0:T(8,128)(2,1)} %refs_0_.1, bf16[192,1280]{1,0:T(8,128)(2,1)} %copy-done, bf16[192,1280]{1,0:T(8,128)(2,1)} %copy-done.1, bf16[192,1280]{1,0:T(8,128)(2,1)} %copy-done.4, bf16[192,1280]{1,0:T(8,128)(2,1)} %refs_4_.1, ...), custom_call_target="tpu_custom_call" | custom-call | flops 2390753280 | bytes 6258688 | tf_op jit(solution)/shard_map/pallas_call | solution.py:102
  (28 shorter events, 0.4 us)
Async XLA Ops:
  0.0 35.3 %collective-permute-start = (bf16[192,1280]{1,0:T(8,128)(2,1)}, bf16[192,1280]{1,0:T(8,128)(2,1)S(1)}, u32[]{:S(2)}, u32[]{:S(2)}) collective-permute-start(bf16[192,1280]{1,0:T(8,128)(2,1)} %refs_0_.1), channel_id=1, source_target_pairs={{0,1},{1,0},{2,3},{3,2},{4,5},{5,4},{6,7},{7,6},{8,9},{9,8},{10,11... | collective-permute-start | bytes 1474568 | tf_op jit(solution)/shard_map/ppermute | solution.py:139
  0.5 26.8 %collective-permute-start.4 = (bf16[192,1280]{1,0:T(8,128)(2,1)}, bf16[192,1280]{1,0:T(8,128)(2,1)S(1)}, u32[]{:S(2)}, u32[]{:S(2)}) collective-permute-start(bf16[192,1280]{1,0:T(8,128)(2,1)} %refs_0_.1), channel_id=1, source_target_pairs={{0,2},{1,3},{2,0},{3,1},{4,6},{5,7},{6,4},{7,5},{8,10},{9,11},{10,... | collective-permute-start | bytes 1474568 | tf_op jit(solution)/shard_map/ppermute | solution.py:138
  3.0 24.3 %collective-permute-start.5 = (bf16[192,1280]{1,0:T(8,128)(2,1)}, bf16[192,1280]{1,0:T(8,128)(2,1)S(1)}, u32[]{:S(2)}, u32[]{:S(2)}) collective-permute-start(bf16[192,1280]{1,0:T(8,128)(2,1)} %refs_4_.1), channel_id=1, source_target_pairs={{0,2},{1,3},{2,0},{3,1},{4,6},{5,7},{6,4},{7,5},{8,10},{9,11},{10,... | collective-permute-start | bytes 1474568 | tf_op jit(solution)/shard_map/ppermute | solution.py:138
  3.0 32.2 %collective-permute-start.7 = (bf16[192,1280]{1,0:T(8,128)(2,1)}, bf16[192,1280]{1,0:T(8,128)(2,1)S(1)}, u32[]{:S(2)}, u32[]{:S(2)}) collective-permute-start(bf16[192,1280]{1,0:T(8,128)(2,1)} %refs_4_.1), channel_id=1, source_target_pairs={{0,1},{1,0},{2,3},{3,2},{4,5},{5,4},{6,7},{7,6},{8,9},{9,8},{10,11... | collective-permute-start | bytes 1474568 | tf_op jit(solution)/shard_map/ppermute | solution.py:139
  5.0 6.6 %collective-permute-start.1 = (bf16[32,2560]{1,0:T(8,128)(2,1)S(1)}, bf16[32,2560]{1,0:T(8,128)(2,1)S(1)}, u32[]{:S(2)}, u32[]{:S(2)}) collective-permute-start(bf16[32,2560]{1,0:T(8,128)(2,1)S(1)} %constant_dynamic-update-slice_fusion), channel_id=1, source_target_pairs={{0,4},{4,0},{8,12},{12,8},{16,20},{20,16},{24,28},{28,24},{1,5},{5... | collective-permute-start | bytes 491528 | tf_op jit(solution)/shard_map/ppermute | solution.py:27
  11.6 6.0 %collective-permute-start.2 = (bf16[32,2560]{1,0:T(8,128)(2,1)S(1)}, bf16[32,2560]{1,0:T(8,128)(2,1)S(1)}, u32[]{:S(2)}, u32[]{:S(2)}) collective-permute-start(bf16[32,2560]{1,0:T(8,128)(2,1)S(1)} %broadcast_select_fusion), channel_id=1, source_target_pairs={{0,8},{4,12},{8,0},{12,4},{16,24},{20,28},{24,16},{28,20},{1,9},{5... | collective-permute-start | bytes 491528 | tf_op jit(solution)/shard_map/ppermute | solution.py:27
  17.7 9.5 %collective-permute-start.3 = (bf16[32,2560]{1,0:T(8,128)(2,1)S(1)}, bf16[32,2560]{1,0:T(8,128)(2,1)S(1)}, u32[]{:S(2)}, u32[]{:S(2)}) collective-permute-start(bf16[32,2560]{1,0:T(8,128)(2,1)S(1)} %broadcast_select_fusion.1), channel_id=1, source_target_pairs={{0,16},{4,20},{8,24},{12,28},{16,0},{20,4},{24,8},{28,12},{1,17},{... | collective-permute-start | bytes 491528 | tf_op jit(solution)/shard_map/ppermute | solution.py:27
  27.2 8.1 %copy-start.1 = (bf16[192,1280]{1,0:T(8,128)(2,1)}, bf16[192,1280]{1,0:T(8,128)(2,1)S(1)}, u32[]{:S(2)}) copy-start(bf16[192,1280]{1,0:T(8,128)(2,1)S(1)} %collective-permute-done.4.refs_2_) | copy-start | bytes 1474564
  27.2 8.1 %copy-start.2 = (bf16[192,1280]{1,0:T(8,128)(2,1)}, bf16[192,1280]{1,0:T(8,128)(2,1)S(1)}, u32[]{:S(2)}) copy-start(bf16[192,1280]{1,0:T(8,128)(2,1)S(1)} %collective-permute-done.5.refs_6_) | copy-start | bytes 1474564
  27.2 5.4 %collective-permute-start.9 = (bf16[32,2560]{1,0:T(8,128)(2,1)S(1)}, bf16[32,2560]{1,0:T(8,128)(2,1)S(1)}, u32[]{:S(2)}, u32[]{:S(2)}) collective-permute-start(bf16[32,2560]{1,0:T(8,128)(2,1)S(1)} %broadcast_select_fusion.2), channel_id=1, source_target_pairs={{0,2},{1,3},{2,0},{3,1},{4,6},{5,7},{6,4},{7,5},{8,10},{9,11},{10,... | collective-permute-start | bytes 491528 | tf_op jit(solution)/shard_map/ppermute | solution.py:37
  28.9 6.4 %collective-permute-start.6 = (bf16[192,1280]{1,0:T(8,128)(2,1)S(1)}, bf16[192,1280]{1,0:T(8,128)(2,1)S(1)}, u32[]{:S(2)}, u32[]{:S(2)}) collective-permute-start(bf16[192,1280]{1,0:T(8,128)(2,1)S(1)} %collective-permute-done.4.refs_2_), channel_id=1, source_target_pairs={{0,1},{1,0},{2,3},{3,2},{4,5},{5,4},{6,7},{7,6},{8,9},{9,8},{10,11... | collective-permute-start | bytes 1474568 | tf_op jit(solution)/shard_map/ppermute | solution.py:141
  29.0 6.3 %collective-permute-start.8 = (bf16[192,1280]{1,0:T(8,128)(2,1)S(1)}, bf16[192,1280]{1,0:T(8,128)(2,1)S(1)}, u32[]{:S(2)}, u32[]{:S(2)}) collective-permute-start(bf16[192,1280]{1,0:T(8,128)(2,1)S(1)} %collective-permute-done.5.refs_6_), channel_id=1, source_target_pairs={{0,1},{1,0},{2,3},{3,2},{4,5},{5,4},{6,7},{7,6},{8,9},{9,8},{10,11... | collective-permute-start | bytes 1474568 | tf_op jit(solution)/shard_map/ppermute | solution.py:141
  32.7 1.7 %collective-permute-start.10 = (bf16[64,2560]{1,0:T(8,128)(2,1)S(1)}, bf16[64,2560]{1,0:T(8,128)(2,1)S(1)}, u32[]{:S(2)}, u32[]{:S(2)}) collective-permute-start(bf16[64,2560]{1,0:T(8,128)(2,1)S(1)} %pad_maximum_fusion), channel_id=1, source_target_pairs={{0,1},{1,0},{2,3},{3,2},{4,5},{5,4},{6,7},{7,6},{8,9},{9,8},{10,11... | collective-permute-start | bytes 983048 | tf_op jit(solution)/shard_map/ppermute | solution.py:39
  35.3 0.8 %copy-start = (bf16[192,1280]{1,0:T(8,128)(2,1)}, bf16[192,1280]{1,0:T(8,128)(2,1)S(1)}, u32[]{:S(2)}) copy-start(bf16[192,1280]{1,0:T(8,128)(2,1)S(1)} %collective-permute-done.refs_1_) | copy-start | bytes 1474564
  35.3 0.9 %copy-start.3 = (bf16[192,1280]{1,0:T(8,128)(2,1)}, bf16[192,1280]{1,0:T(8,128)(2,1)S(1)}, u32[]{:S(2)}) copy-start(bf16[192,1280]{1,0:T(8,128)(2,1)S(1)} %collective-permute-done.7.refs_5_) | copy-start | bytes 1474564
  35.3 1.1 %copy-start.4 = (bf16[192,1280]{1,0:T(8,128)(2,1)}, bf16[192,1280]{1,0:T(8,128)(2,1)S(1)}, u32[]{:S(2)}) copy-start(bf16[192,1280]{1,0:T(8,128)(2,1)S(1)} %collective-permute-done.6.refs_3_) | copy-start | bytes 1474564
  35.3 1.2 %copy-start.5 = (bf16[192,1280]{1,0:T(8,128)(2,1)}, bf16[192,1280]{1,0:T(8,128)(2,1)S(1)}, u32[]{:S(2)}) copy-start(bf16[192,1280]{1,0:T(8,128)(2,1)S(1)} %collective-permute-done.8.refs_7_) | copy-start | bytes 1474564

commit v16 on v12

--- a/solution.py
+++ b/solution.py
@@ -134,7 +134,7 @@
     if view_count == 4:
         across = lax.ppermute((keys, values), "view", [(i, i ^ 2) for i in range(view_count)])
         near = lax.ppermute((keys, values), "view", [(i, i ^ 1) for i in range(view_count)])
-        ref_shared, across = lax.optimization_barrier((ref_shared, across))
+        ref_shared, unused = lax.optimization_barrier((ref_shared, across))
         far = lax.ppermute(across, "view", [(i, i ^ 1) for i in range(view_count)])
         pieces = [(keys, values), near, across, far]
         positions = [view_index, view_index ^ 1, view_index ^ 2, view_index ^ 3]

time: 47.7 us -> 46.8 us (0.981)
  waiting for transfers between devices: 18.7 us -> 17.4 us
    ppermute x3, waiting for transfers between devices: 13.9 us -> 12.5 us  [tree_broadcast(): received = lax.ppermute(value, axis, pairs)]
where the time goes in v16:
time: 46.8 us; the launch traced here: 46.2 us
  waiting for transfers between devices  17.4 us (37%)
  starting transfers between devices  12.1 us (26%)
  Pallas kernels  9.17 us (20%)
  local copies, waits for them, and re-layouts  2.68 us (6%)
  matrix products  2.48 us (5%)
  other arithmetic  1.44 us (3%)
  between operations  0.96 us (2%)
    ppermute x3, waiting for transfers between devices, tree_broadcast(): received = lax.ppermute(value, axis, pairs)  12.5 us
    pallas_call x1, Pallas kernels, attention(): pl.pallas_call(functools.partial(attention_kernel, len(key_pieces), span...  9.17 us
    ppermute x3, starting transfers between devices, tree_broadcast(): received = lax.ppermute(value, axis, pairs)  6.4 us
    ppermute x1, waiting for transfers between devices, gather_rows(): across = lax.ppermute(value, axis, [(i, i ^ 2) for i in range(count)])  3.21 us
    ppermute x2, starting transfers between devices, body(): lax.ppermute((keys, values), 'view', [(i, i ^ 2) for i in range(view_coun...  2.87 us
    unnamed x15, local copies, waits for them, and re-layouts  1.72 us
    ppermute x1, waiting for transfers between devices, gather_rows(): near = lax.ppermute(both, axis, [(i, i ^ 1) for i in range(count)])  1.59 us
    dot_general x1, matrix products, body(): jnp.dot(mixed, out_weight, preferred_element_type=jnp.float32)  1.59 us
  transfers between devices with their start and end apart: 11, of which 5 were waited for; matrix products, arithmetic and copies ran while one was open for 9% of the time, Pallas kernels for 0%

profile of v16, /device:TPU:0, one launch (start us, length us, event | category | flops | bytes accessed | tf_op | source)
XLA Modules:
  0.0 46.2 jit_solution(2258270795822437720)
XLA Ops:
  0.0 0.5 collective-permute-start
  0.5 2.6 %collective-permute-start.1 = (bf16[192,1280]{1,0:T(8,128)(2,1)}, bf16[192,1280]{1,0:T(8,128)(2,1)}, u32[]{:S(2)}, u32[]{:S(2)}) collective-permute-start(bf16[192,1280]{1,0:T(8,128)(2,1)} %refs_0_.1), channel_id=1, source_target_pairs={{0,2},{1,3},{2,0},{3,1},{4,6},{5,7},{6,4},{7,5},{8,10},{9,11},{10,... | collective-permute-start | bytes 1474568 | tf_op jit(solution)/shard_map/ppermute | solution.py:135
  3.0 0.2 collective-permute-start.3
  3.2 0.3 collective-permute-start.4
  3.5 0.9 %constant_dynamic-update-slice_fusion.1 = bf16[32,2560]{1,0:T(8,128)(2,1)S(1)} fusion(bf16[32,1280]{1,0:T(8,128)(2,1)} %param.11), kind=kLoop, calls=%fused_computation.13 | loop fusion | bytes 163840
  4.4 0.9 %constant_dynamic-update-slice_fusion = bf16[32,2560]{1,0:T(8,128)(2,1)S(1)} fusion(bf16[32,2560]{1,0:T(8,128)(2,1)S(1)} %constant_dynamic-update-slice_fusion.1, bf16[32,1280]{1,0:T(8,128)(2,1)} %param.12), kind=kLoop, calls=%fused_computation.12 | loop fusion | bytes 163840 | tf_op jit(solution)/shard_map/concatenate | solution.py:132
  5.3 1.7 %collective-permute-start.6 = (bf16[32,2560]{1,0:T(8,128)(2,1)S(1)}, bf16[32,2560]{1,0:T(8,128)(2,1)}, u32[]{:S(2)}, u32[]{:S(2)}) collective-permute-start(bf16[32,2560]{1,0:T(8,128)(2,1)S(1)} %constant_dynamic-update-slice_fusion), channel_id=1, source_target_pairs={{0,4},{4,0},{8,12},{12,8},{16,20},{20,16},{24,28},{28,24},{1,5},{5... | collective-permute-start | bytes 491528 | tf_op jit(solution)/shard_map/ppermute | solution.py:27
  7.0 0.9 %fusion = f32[192,3]{0,1:T(4,128)S(1)} fusion(s32[192]{0:T(256)S(1)} %get-tuple-element.16, s32[6,3]{0,1:T(4,128)} %param.14), kind=kOutput, calls=%fused_computation.10 | convolution fusion | flops 8082 | bytes 3144 | tf_op jit(solution)/shard_map/dot_general | solution.py:149
  8.6 2.9 %collective-permute-done.6 = bf16[32,2560]{1,0:T(8,128)(2,1)} collective-permute-done((bf16[32,2560]{1,0:T(8,128)(2,1)S(1)}, bf16[32,2560]{1,0:T(8,128)(2,1)}, u32[]{:S(2)}, u32[]{:S(2)}) %collective-permute-start.6) | collective-permute-done | bytes 163872 | tf_op jit(solution)/shard_map/ppermute | solution.py:27
  11.6 0.9 %broadcast_select_fusion = bf16[32,2560]{1,0:T(8,128)(2,1)S(1)} fusion(bf16[32,2560]{1,0:T(8,128)(2,1)} %collective-permute-done.6, bf16[32,2560]{1,0:T(8,128)(2,1)} %copy-done.4, pred[]{:T(512)S(6)} %eq.110), kind=kLoop, calls=%fused_computation.6 | loop fusion | flops 81920 | bytes 491521 | tf_op jit(solution)/shard_map/jit(_where)/select_n | solution.py:29
  12.5 1.9 %collective-permute-start.7 = (bf16[32,2560]{1,0:T(8,128)(2,1)S(1)}, bf16[32,2560]{1,0:T(8,128)(2,1)}, u32[]{:S(2)}, u32[]{:S(2)}) collective-permute-start(bf16[32,2560]{1,0:T(8,128)(2,1)S(1)} %broadcast_select_fusion), channel_id=1, source_target_pairs={{0,8},{4,12},{8,0},{12,4},{16,24},{20,28},{24,16},{28,20},{1,9},{5... | collective-permute-start | bytes 491528 | tf_op jit(solution)/shard_map/ppermute | solution.py:27
  14.5 3.5 %collective-permute-done.7 = bf16[32,2560]{1,0:T(8,128)(2,1)} collective-permute-done((bf16[32,2560]{1,0:T(8,128)(2,1)S(1)}, bf16[32,2560]{1,0:T(8,128)(2,1)}, u32[]{:S(2)}, u32[]{:S(2)}) %collective-permute-start.7) | collective-permute-done | bytes 163872 | tf_op jit(solution)/shard_map/ppermute | solution.py:27
  18.1 2.8 %collective-permute-start.8 = (bf16[32,2560]{1,0:T(8,128)(2,1)S(1)}, bf16[32,2560]{1,0:T(8,128)(2,1)S(1)}, u32[]{:S(2)}, u32[]{:S(2)}) collective-permute-start(bf16[32,2560]{1,0:T(8,128)(2,1)S(1)} %broadcast_select_fusion.1), channel_id=1, source_target_pairs={{0,16},{4,20},{8,24},{12,28},{16,0},{20,4},{24,8},{28,12},{1,17},{... | collective-permute-start | bytes 491528 | tf_op jit(solution)/shard_map/ppermute | solution.py:27
  20.9 0.4 or_select_fusion
  21.3 6.1 %collective-permute-done.8 = bf16[32,2560]{1,0:T(8,128)(2,1)S(1)} collective-permute-done((bf16[32,2560]{1,0:T(8,128)(2,1)S(1)}, bf16[32,2560]{1,0:T(8,128)(2,1)S(1)}, u32[]{:S(2)}, u32[]{:S(2)}) %collective-permute-start.8) | collective-permute-done | bytes 163872 | tf_op jit(solution)/shard_map/ppermute | solution.py:27
  27.4 1.6 %collective-permute-start.9 = (bf16[32,2560]{1,0:T(8,128)(2,1)S(1)}, bf16[32,2560]{1,0:T(8,128)(2,1)S(1)}, u32[]{:S(2)}, u32[]{:S(2)}) collective-permute-start(bf16[32,2560]{1,0:T(8,128)(2,1)S(1)} %broadcast_select_fusion.2), channel_id=1, source_target_pairs={{0,2},{1,3},{2,0},{3,1},{4,6},{5,7},{6,4},{7,5},{8,10},{9,11},{10,... | collective-permute-start | bytes 491528 | tf_op jit(solution)/shard_map/ppermute | solution.py:37
  29.0 0.1 collective-permute-start.2
  29.1 0.5 %collective-permute-start.5 = (bf16[192,1280]{1,0:T(8,128)(2,1)}, bf16[192,1280]{1,0:T(8,128)(2,1)S(1)}, u32[]{:S(2)}, u32[]{:S(2)}) collective-permute-start(bf16[192,1280]{1,0:T(8,128)(2,1)} %collective-permute-done.4.refs_6_), channel_id=1, source_target_pairs={{0,1},{1,0},{2,3},{3,2},{4,5},{5,4},{6,7},{7,6},{8,9},{9,8},{10,11... | collective-permute-start | bytes 1474568 | tf_op jit(solution)/shard_map/ppermute | solution.py:138
  29.6 3.2 %collective-permute-done.9 = bf16[32,2560]{1,0:T(8,128)(2,1)S(1)} collective-permute-done((bf16[32,2560]{1,0:T(8,128)(2,1)S(1)}, bf16[32,2560]{1,0:T(8,128)(2,1)S(1)}, u32[]{:S(2)}, u32[]{:S(2)}) %collective-permute-start.9) | collective-permute-done | bytes 163872 | tf_op jit(solution)/shard_map/ppermute | solution.py:37
  32.8 0.1 collective-permute-start.10
  32.9 1.6 %collective-permute-done.10 = bf16[64,2560]{1,0:T(8,128)(2,1)S(1)} collective-permute-done((bf16[64,2560]{1,0:T(8,128)(2,1)S(1)}, bf16[64,2560]{1,0:T(8,128)(2,1)S(1)}, u32[]{:S(2)}, u32[]{:S(2)}) %collective-permute-start.10) | collective-permute-done | bytes 327712 | tf_op jit(solution)/shard_map/ppermute | solution.py:39
  34.6 0.8 %copy-done.5 = bf16[192,1280]{1,0:T(8,128)(2,1)} copy-done((bf16[192,1280]{1,0:T(8,128)(2,1)}, bf16[192,1280]{1,0:T(8,128)(2,1)S(1)}, u32[]{:S(2)}) %copy-start.5) | copy-done | bytes 491544
  35.4 9.2 %shard_map.82 = bf16[192,1280]{1,0:T(8,128)(2,1)S(1)} custom-call(bf16[192,1280]{1,0:T(8,128)(2,1)S(1)} %copy-done.1, bf16[192,1280]{1,0:T(8,128)(2,1)S(1)} %copy-done.2, bf16[192,1280]{1,0:T(8,128)(2,1)} %collective-permute-done.refs_1_, bf16[192,1280]{1,0:T(8,128)(2,1)} %collective-permute-done.1.refs_2_, ...), custom_call_target="tpu_custom_call" | custom-call | flops 1761607680 | bytes 6258688 | tf_op jit(solution)/shard_map/pallas_call | solution.py:100
  44.6 1.6 %convolution_convert_fusion = bf16[192,1280]{1,0:T(8,128)(2,1)} fusion(bf16[192,1280]{1,0:T(8,128)(2,1)S(1)} %shard_map.82, bf16[1280,1280]{1,0:T(8,128)(2,1)S(1)} %copy-done), kind=kOutput, calls=%fused_computation | convolution fusion | flops 629391360 | bytes 4259840 | tf_op jit(solution)/shard_map/dot_general | solution.py:164
  (29 shorter events, 0.3 us)
Async XLA Ops:
  0.0 44.6 %copy-start = (bf16[1280,1280]{1,0:T(8,128)(2,1)S(1)}, bf16[1280,1280]{1,0:T(8,128)(2,1)}, u32[]{:S(2)}) copy-start(bf16[1280,1280]{1,0:T(8,128)(2,1)} %param.13) | copy-start | bytes 9830404
  0.0 34.6 %collective-permute-start = (bf16[192,1280]{1,0:T(8,128)(2,1)}, bf16[192,1280]{1,0:T(8,128)(2,1)}, u32[]{:S(2)}, u32[]{:S(2)}) collective-permute-start(bf16[192,1280]{1,0:T(8,128)(2,1)} %refs_0_.1), channel_id=1, source_target_pairs={{0,1},{1,0},{2,3},{3,2},{4,5},{5,4},{6,7},{7,6},{8,9},{9,8},{10,11... | collective-permute-start | bytes 1474568 | tf_op jit(solution)/shard_map/ppermute | solution.py:136
  0.5 26.9 %collective-permute-start.1 = (bf16[192,1280]{1,0:T(8,128)(2,1)}, bf16[192,1280]{1,0:T(8,128)(2,1)}, u32[]{:S(2)}, u32[]{:S(2)}) collective-permute-start(bf16[192,1280]{1,0:T(8,128)(2,1)} %refs_0_.1), channel_id=1, source_target_pairs={{0,2},{1,3},{2,0},{3,1},{4,6},{5,7},{6,4},{7,5},{8,10},{9,11},{10,... | collective-permute-start | bytes 1474568 | tf_op jit(solution)/shard_map/ppermute | solution.py:135
  3.0 31.6 %collective-permute-start.3 = (bf16[192,1280]{1,0:T(8,128)(2,1)}, bf16[192,1280]{1,0:T(8,128)(2,1)}, u32[]{:S(2)}, u32[]{:S(2)}) collective-permute-start(bf16[192,1280]{1,0:T(8,128)(2,1)} %refs_4_.1), channel_id=1, source_target_pairs={{0,1},{1,0},{2,3},{3,2},{4,5},{5,4},{6,7},{7,6},{8,9},{9,8},{10,11... | collective-permute-start | bytes 1474568 | tf_op jit(solution)/shard_map/ppermute | solution.py:136
  3.2 24.2 %collective-permute-start.4 = (bf16[192,1280]{1,0:T(8,128)(2,1)}, bf16[192,1280]{1,0:T(8,128)(2,1)}, u32[]{:S(2)}, u32[]{:S(2)}) collective-permute-start(bf16[192,1280]{1,0:T(8,128)(2,1)} %refs_4_.1), channel_id=1, source_target_pairs={{0,2},{1,3},{2,0},{3,1},{4,6},{5,7},{6,4},{7,5},{8,10},{9,11},{10,... | collective-permute-start | bytes 1474568 | tf_op jit(solution)/shard_map/ppermute | solution.py:135
  5.3 3.3 %copy-start.4 = (bf16[32,2560]{1,0:T(8,128)(2,1)}, bf16[32,2560]{1,0:T(8,128)(2,1)S(1)}, u32[]{:S(2)}) copy-start(bf16[32,2560]{1,0:T(8,128)(2,1)S(1)} %constant_dynamic-update-slice_fusion) | copy-start | bytes 491524
  5.3 6.3 %collective-permute-start.6 = (bf16[32,2560]{1,0:T(8,128)(2,1)S(1)}, bf16[32,2560]{1,0:T(8,128)(2,1)}, u32[]{:S(2)}, u32[]{:S(2)}) collective-permute-start(bf16[32,2560]{1,0:T(8,128)(2,1)S(1)} %constant_dynamic-update-slice_fusion), channel_id=1, source_target_pairs={{0,4},{4,0},{8,12},{12,8},{16,20},{20,16},{24,28},{28,24},{1,5},{5... | collective-permute-start | bytes 491528 | tf_op jit(solution)/shard_map/ppermute | solution.py:27
  12.5 5.6 %collective-permute-start.7 = (bf16[32,2560]{1,0:T(8,128)(2,1)S(1)}, bf16[32,2560]{1,0:T(8,128)(2,1)}, u32[]{:S(2)}, u32[]{:S(2)}) collective-permute-start(bf16[32,2560]{1,0:T(8,128)(2,1)S(1)} %broadcast_select_fusion), channel_id=1, source_target_pairs={{0,8},{4,12},{8,0},{12,4},{16,24},{20,28},{24,16},{28,20},{1,9},{5... | collective-permute-start | bytes 491528 | tf_op jit(solution)/shard_map/ppermute | solution.py:27
  14.5 21.0 %copy-start.1 = (bf16[192,1280]{1,0:T(8,128)(2,1)S(1)}, bf16[192,1280]{1,0:T(8,128)(2,1)}, u32[]{:S(2)}) copy-start(bf16[192,1280]{1,0:T(8,128)(2,1)} %q_ref.1) | copy-start | bytes 1474564
  14.5 20.9 %copy-start.2 = (bf16[192,1280]{1,0:T(8,128)(2,1)S(1)}, bf16[192,1280]{1,0:T(8,128)(2,1)}, u32[]{:S(2)}) copy-start(bf16[192,1280]{1,0:T(8,128)(2,1)} %refs_0_.1) | copy-start | bytes 1474564
  14.5 20.9 %copy-start.3 = (bf16[192,1280]{1,0:T(8,128)(2,1)S(1)}, bf16[192,1280]{1,0:T(8,128)(2,1)}, u32[]{:S(2)}) copy-start(bf16[192,1280]{1,0:T(8,128)(2,1)} %refs_4_.1) | copy-start | bytes 1474564
  18.1 9.3 %collective-permute-start.8 = (bf16[32,2560]{1,0:T(8,128)(2,1)S(1)}, bf16[32,2560]{1,0:T(8,128)(2,1)S(1)}, u32[]{:S(2)}, u32[]{:S(2)}) collective-permute-start(bf16[32,2560]{1,0:T(8,128)(2,1)S(1)} %broadcast_select_fusion.1), channel_id=1, source_target_pairs={{0,16},{4,20},{8,24},{12,28},{16,0},{20,4},{24,8},{28,12},{1,17},{... | collective-permute-start | bytes 491528 | tf_op jit(solution)/shard_map/ppermute | solution.py:27
  27.4 5.4 %collective-permute-start.9 = (bf16[32,2560]{1,0:T(8,128)(2,1)S(1)}, bf16[32,2560]{1,0:T(8,128)(2,1)S(1)}, u32[]{:S(2)}, u32[]{:S(2)}) collective-permute-start(bf16[32,2560]{1,0:T(8,128)(2,1)S(1)} %broadcast_select_fusion.2), channel_id=1, source_target_pairs={{0,2},{1,3},{2,0},{3,1},{4,6},{5,7},{6,4},{7,5},{8,10},{9,11},{10,... | collective-permute-start | bytes 491528 | tf_op jit(solution)/shard_map/ppermute | solution.py:37
  29.0 5.6 %collective-permute-start.2 = (bf16[192,1280]{1,0:T(8,128)(2,1)}, bf16[192,1280]{1,0:T(8,128)(2,1)S(1)}, u32[]{:S(2)}, u32[]{:S(2)}) collective-permute-start(bf16[192,1280]{1,0:T(8,128)(2,1)} %collective-permute-done.1.refs_2_), channel_id=1, source_target_pairs={{0,1},{1,0},{2,3},{3,2},{4,5},{5,4},{6,7},{7,6},{8,9},{9,8},{10,11... | collective-permute-start | bytes 1474568 | tf_op jit(solution)/shard_map/ppermute | solution.py:138
  29.1 5.5 %collective-permute-start.5 = (bf16[192,1280]{1,0:T(8,128)(2,1)}, bf16[192,1280]{1,0:T(8,128)(2,1)S(1)}, u32[]{:S(2)}, u32[]{:S(2)}) collective-permute-start(bf16[192,1280]{1,0:T(8,128)(2,1)} %collective-permute-done.4.refs_6_), channel_id=1, source_target_pairs={{0,1},{1,0},{2,3},{3,2},{4,5},{5,4},{6,7},{7,6},{8,9},{9,8},{10,11... | collective-permute-start | bytes 1474568 | tf_op jit(solution)/shard_map/ppermute | solution.py:138
  32.8 1.7 %collective-permute-start.10 = (bf16[64,2560]{1,0:T(8,128)(2,1)S(1)}, bf16[64,2560]{1,0:T(8,128)(2,1)S(1)}, u32[]{:S(2)}, u32[]{:S(2)}) collective-permute-start(bf16[64,2560]{1,0:T(8,128)(2,1)S(1)} %pad_maximum_fusion), channel_id=1, source_target_pairs={{0,1},{1,0},{2,3},{3,2},{4,5},{5,4},{6,7},{7,6},{8,9},{9,8},{10,11... | collective-permute-start | bytes 983048 | tf_op jit(solution)/shard_map/ppermute | solution.py:39
  34.6 0.8 %copy-start.5 = (bf16[192,1280]{1,0:T(8,128)(2,1)}, bf16[192,1280]{1,0:T(8,128)(2,1)S(1)}, u32[]{:S(2)}) copy-start(bf16[192,1280]{1,0:T(8,128)(2,1)S(1)} %collective-permute-done.5.refs_7_) | copy-start | bytes 1474564
